TPU v7x, 128 devices: a whole 4x4x4 slice. The times are simulated.
128 devices in a mesh: br: 8 (over y_lo, z), bus: 16 (over y_hi, x, core).
Axes of the slice: x: 4, y: 4 (y_hi: 2, y_lo: 2; y = y_hi * 2 + y_lo), z: 4, core: 2. Of those that a mesh axis runs over, the one named last changes fastest.
Arguments:
- shift_factors: bfloat16 [65536, 8192], P('br', 'bus'), may hold values from -0.09375 to 0.09375
- injections: float32 [8192, 384], P('bus'), may hold values from -6 to 6
- prices: float32 [65536, 384], P(('br', 'bus')), may hold values from -6 to 6
- limits: float32 [65536], P(('br', 'bus')), may hold values from 0.2 to 2
- unit_cost: float32 [8192], P('bus'), may hold values from -1 to 1
- bus_load: float32 [8192], P('bus'), may hold values from 0.5 to 3
- bus_capacity: float32 [8192], P('bus'), may hold values from 0.5 to 3
- irradiance_profile: float32 [64, 1024], replicated, may hold values from 0 to 1
- plant_group: int32 [8192], P('bus'), may hold values from 0 to 1023
- scenario_profile: int32 [384], replicated, may hold values from 0 to 63
- listed_slab: int32 [1024, 3], replicated, may hold values from 0 to 7, all different within a row; in each aligned block of 8 rows (0 to 7, 8 to 15, ...) at most 6 rows name the same one
- listed_block: int32 [1024, 3], replicated, may hold values from 0 to 15
- rent_weight: bfloat16 [1024, 1536], P(('br', 'bus')), may hold values from -0.15625 to 0.15625
Outputs:
- new_injections: float32 [8192, 384], P('bus')
- new_prices: float32 [65536, 384], P(('br', 'bus'))
- group_rent: float32 [1024, 384], P(('br', 'bus'))
Inputs may be any that keep to these rules, and one draw needn't show every extreme that they name: `listed_slab`: each plant group names 3 different slabs; among the 8 plant groups of one device (aligned blocks of 8 rows) no slab is named by more than 6 groups, and some device's groups name one slab exactly 6 times.
All inputs are finite; a program needn't handle non-finite values.
Results may differ from a plain program's by a relative error of at most 0.0052.
Values may be sent and summed in bfloat16 or wider, within the bound.
No kernel may reach another device: no remote copies, remote signals or barrier semaphores. Data moves between devices by JAX's collectives and lax.ppermute only.
A program may use at most 128 MiB of HBM per device.

v0:
```python
import jax
import jax.numpy as jnp
from jax import lax
from jax.sharding import PartitionSpec as P

BLOCK = 512
CAP = 6
GDEV = 8


step_dual = 0.5
step_primal = 0.25


def per_device(
    shift_factors,
    injections,
    prices,
    limits,
    unit_cost,
    bus_load,
    bus_capacity,
    irradiance_profile,
    plant_group,
    scenario_profile,
    listed_slab,
    listed_block,
    rent_weight,
):
    scenarios = injections.shape[1]
    bus_axis = lax.axis_size("bus")
    slab_axis = lax.axis_size("br")
    inject_half = injections.astype(jnp.bfloat16)
    flow = lax.psum_scatter(
        jnp.dot(shift_factors, inject_half, preferred_element_type=jnp.float32),
        "bus",
        scatter_dimension=0,
        tiled=True,
    )
    moved = prices + step_dual * flow
    bound = step_dual * limits[:, None]
    new_prices = moved - jnp.clip(moved, -bound, bound)
    price_half = new_prices.astype(jnp.bfloat16)
    slab_prices = lax.all_gather(price_half, "bus", axis=0, tiled=True)
    partial_grad = lax.dot_general(
        shift_factors, slab_prices, (((0,), (0,)), ((), ())), preferred_element_type=jnp.float32
    )
    gradient = lax.psum(partial_grad, "br")
    group_count = irradiance_profile.shape[1]
    profile_count = irradiance_profile.shape[0]
    pick_group = (plant_group[:, None] == jnp.arange(group_count, dtype=jnp.int32)[None, :]).astype(
        jnp.float32
    )
    bus_profile = jnp.dot(pick_group, irradiance_profile.T, precision=lax.Precision.HIGHEST)
    pick_scenario = (
        jnp.arange(profile_count, dtype=jnp.int32)[:, None] == scenario_profile[None, :]
    ).astype(jnp.float32)
    share = jnp.dot(bus_profile, pick_scenario, precision=lax.Precision.HIGHEST)
    upper = bus_capacity[:, None] * share
    trial = injections - step_primal * (unit_cost[:, None] + gradient)
    new_injections = jnp.minimum(jnp.maximum(trial, -bus_load[:, None]), upper)
    list_len = listed_slab.shape[1]
    entries = GDEV * list_len
    slab_by_device = listed_slab.reshape(-1, entries)
    block_by_device = listed_block.reshape(-1, entries)
    slab_index = lax.axis_index("br")
    column_index = lax.axis_index("bus")
    targets = jnp.arange(slab_axis, dtype=jnp.int32) * bus_axis + column_index
    wanted_slab = jnp.take(slab_by_device, targets, axis=0)
    wanted_block = jnp.take(block_by_device, targets, axis=0)
    matched = wanted_slab == slab_index
    slot_rank = jnp.cumsum(matched.astype(jnp.int32), axis=1) - 1
    slot_range = jnp.arange(CAP, dtype=jnp.int32)
    selected = matched[:, None, :] & (slot_rank[:, None, :] == slot_range[None, :, None])
    block_choice = jnp.sum(jnp.where(selected, wanted_block[:, None, :], 0), axis=2)
    filled = jnp.any(selected, axis=2)
    slab_blocks = slab_prices.reshape(-1, BLOCK, scenarios)
    outgoing = jnp.take(slab_blocks, block_choice, axis=0)
    self_device = slab_index * bus_axis + column_index
    own_slab = lax.dynamic_index_in_dim(slab_by_device, self_device, 0, keepdims=False)
    positions = jnp.arange(entries, dtype=jnp.int32)
    earlier = positions[None, :] < positions[:, None]
    same_slab = own_slab[:, None] == own_slab[None, :]
    own_slot = jnp.sum((same_slab & earlier).astype(jnp.int32), axis=1)
    lookup = own_slab * CAP + own_slot
    outgoing = jnp.where(filled[:, :, None, None], outgoing, jnp.zeros_like(outgoing))
    arrived = lax.all_to_all(outgoing, "br", split_axis=0, concat_axis=0, tiled=True)
    fetched = jnp.take(arrived.reshape(-1, BLOCK, scenarios), lookup, axis=0)
    fetched = fetched.reshape(GDEV, list_len * BLOCK, scenarios)
    group_rent = jnp.einsum("gr,grs->gs", rent_weight, fetched, preferred_element_type=jnp.float32)
    return (new_injections, new_prices, group_rent)


def solution(mesh):
    placed = (
        P("br", "bus"),
        P("bus", None),
        P(("br", "bus"), None),
        P(("br", "bus")),
        P("bus"),
        P("bus"),
        P("bus"),
        P(),
        P("bus"),
        P(),
        P(),
        P(),
        P(("br", "bus"), None),
    )
    return jax.shard_map(
        per_device,
        mesh=mesh,
        in_specs=placed,
        out_specs=(P("bus", None), P(("br", "bus"), None), P(("br", "bus"), None)),
        check_vma=False,
    )
```

profile of v0, /device:TPU:6, one launch (start us, length us, event | category | flops | bytes accessed | tf_op | source)
XLA Modules:
  0.0 526.5 jit_solution(10477733938909790546)
XLA Ops:
  7.2 12.6 %fusion.3 = f32[8192,384]{1,0:T(8,128)} fusion(bf16[8192,512]{1,0:T(8,128)(2,1)} %param.15, f32[512,384]{1,0:T(8,128)} %param.16), kind=kOutput, calls=%fused_computation.13 | convolution fusion | flops 3221422080 | bytes 21757952 | tf_op jit(solution)/shard_map/dot_general | solution.py:35
  19.9 0.6 copy-done.9
  20.5 123.5 %reduce-scatter.2.cloned.1.call-done = f32[512,384]{1,0:T(8,128)} async-done(((f32[8192,384]{1,0:T(8,128)}), f32[512,384]{1,0:T(8,128)}) %reduce-scatter.2.cloned.1.call-update) | async-done | bytes 786448 | tf_op jit(solution)/shard_map/reduce_scatter | solution.py:34
  144.0 2.4 fusion.15
  146.4 0.2 copy.39
  146.7 0.2 reshape.107
  146.9 0.2 copy.43
  147.1 0.2 reshape.108
  147.3 0.6 gather_fusion.2
  147.9 0.6 gather_fusion.3
  148.5 0.2 reduce_window_sum.11
  148.8 0.2 fusion.9
  149.0 0.1 copy.42
  149.1 0.2 select_reduce_fusion
  149.4 0.1 copy.44
  149.5 60.0 %all-gather.2.cloned.1.call-done = bf16[8192,384]{1,0:T(8,128)(2,1)} async-done(((bf16[512,384]{1,0:T(8,128)(2,1)}), bf16[8192,384]{1,0:T(8,128)(2,1)}) %all-gather.2.cloned.1.call-update) | async-done | bytes 6291472 | tf_op jit(solution)/shard_map/all_gather | solution.py:44
  209.5 11.7 %gather_fusion = bf16[48,512,384]{2,1,0:T(8,128)(2,1)} fusion(bf16[16,512,384]{2,1,0:T(8,128)(2,1)} %bitcast.33, s32[1024]{0:T(1024)S(1)} %pad_clamp_fusion.1), kind=kCustom, calls=%fused_computation.2 | custom fusion | bytes 37748928 | tf_op jit(solution)/shard_map/jit(_take)/gather | solution.py:78
  221.2 17.3 %select_select_fusion = bf16[8,6,512,384]{3,2,1,0:T(8,128)(2,1)} fusion(bf16[8,6,512,384]{3,2,1,0:T(8,128)(2,1)} %bitcast.34, pred[8,6]{1,0:T(8,128)(4,1)S(1)} %copy.44, pred[8,6]{1,0:T(8,128)(4,1)S(1)} %copy.42), kind=kLoop, calls=%fused_computation.4 | loop fusion | flops 18874368 | bytes 37748832 | tf_op jit(solution)/shard_map/jit(_where)/select_n | solution.py:86
  238.5 6.0 %all-to-all-start = ((bf16[8,6,512,384]{3,2,1,0:T(8,128)(2,1)}), bf16[8,6,512,384]{3,2,1,0:T(8,128)(2,1)}, u32[]{:S(2)}, u32[]{:S(2)}) async-start(bf16[8,6,512,384]{3,2,1,0:T(8,128)(2,1)} %select_select_fusion), calls=%async_computation.1 | async-start | bytes 37748736 | tf_op jit(solution)/shard_map/all_to_all | solution.py:87
  244.5 0.2 all-reduce.2.cloned.1.call-start
  244.8 0.3 copy.37
  245.1 0.2 convert_reduce_fusion
  245.4 0.1 copy.41
  245.6 9.6 %convolution_bitcast_fusion = f32[512,384]{0,1:T(8,128)} fusion(bf16[8192,384]{1,0:T(8,128)(2,1)} %all-gather.2.cloned.1.call-done, bf16[8192,512]{1,0:T(8,128)(2,1)} %param.15), kind=kOutput, calls=%fused_computation.8 | convolution fusion | flops 3221225472 | bytes 15466496 | tf_op jit(solution)/shard_map/dot_general | solution.py:45
  255.3 1.2 fusion
  256.5 239.7 %all-reduce.2.cloned.1.call-done = f32[512,384]{0,1:T(8,128)} async-done(((f32[512,384]{0,1:T(8,128)}), f32[512,384]{0,1:T(8,128)}) %all-reduce.2.cloned.1.call-update) | async-done | bytes 786448 | tf_op jit(solution)/shard_map/psum | solution.py:48
  496.3 1.7 fusion.1
  498.0 1.1 copy.46
  499.2 12.7 %gather_fusion.1 = bf16[24,512,384]{2,1,0:T(8,128)(2,1)} fusion(bf16[48,512,384]{2,1,0:T(8,128)(2,1)} %bitcast.6, s32[1024]{0:T(1024)S(1)} %pad_clamp_fusion), kind=kCustom, calls=%fused_computation.3 | custom fusion | bytes 18874464 | tf_op jit(solution)/shard_map/jit(_take)/gather | solution.py:88
  512.0 6.0 %bitcast_select_fusion = bf16[8,1536,384]{2,1,0:T(8,128)(2,1)S(1)} fusion(pred[8,1536]{1,0:T(8,128)(4,1)S(1)} %bitcast.37, bf16[8,1536,384]{2,1,0:T(8,128)(2,1)} %bitcast.35), kind=kLoop, calls=%fused_computation.5 | loop fusion | flops 4718592 | bytes 18886656 | tf_op jit(solution)/shard_map/jit(_take)/select_n | solution.py:88
  518.1 1.3 fusion.5
  519.4 0.6 copy.53
  (49 shorter events, 0.9 us)
Async XLA Ops:
  7.2 248.1 %copy-start = (f32[64,1024]{1,0:T(8,128)S(1)}, f32[64,1024]{1,0:T(8,128)}, u32[]{:S(2)}) copy-start(f32[64,1024]{1,0:T(8,128)} %param.22) | copy-start | bytes 786436
  7.2 136.8 %reduce-scatter.2.cloned.1.call-start = ((), (), s32[]{:S(2)}) async-start(), calls=%async_computation.2 | async-start | bytes 13369344 | tf_op jit(solution)/shard_map/reduce_scatter | solution.py:34
  19.8 0.7 copy-start.9
  19.8 124.2 %copy-start.2 = (f32[512,384]{1,0:T(8,128)S(1)}, f32[512,384]{1,0:T(8,128)}, u32[]{:S(2)}) copy-start(f32[512,384]{1,0:T(8,128)} %param.17) | copy-start | bytes 2359300
  19.8 126.6 %copy-start.4 = (s32[1024,3]{0,1:T(4,128)S(1)}, s32[1024,3]{0,1:T(4,128)}, u32[]{:S(2)}) copy-start(s32[1024,3]{0,1:T(4,128)} %param.25) | copy-start | bytes 36868
  19.8 127.0 %copy-start.5 = (s32[1024,3]{0,1:T(4,128)S(1)}, s32[1024,3]{0,1:T(4,128)}, u32[]{:S(2)}) copy-start(s32[1024,3]{0,1:T(4,128)} %param.26) | copy-start | bytes 36868
  19.9 189.6 %all-gather.2.cloned.1.call-start = ((), (), s32[]{:S(2)}) async-start(), calls=%async_computation.3 | async-start | bytes 6684672 | tf_op jit(solution)/shard_map/all_gather | solution.py:44
  238.5 6.3 %copy-start.1 = (f32[512,384]{1,0:T(8,128)S(1)}, f32[512,384]{1,0:T(8,128)}, u32[]{:S(2)}) copy-start(f32[512,384]{1,0:T(8,128)} %param.16) | copy-start | bytes 2359300
  238.5 6.6 %copy-start.10 = (f32[512]{0:T(512)S(1)}, f32[512]{0:T(512)}, u32[]{:S(2)}) copy-start(f32[512]{0:T(512)} %param.20) | copy-start | bytes 6148
  238.5 260.7 %all-to-all-start = ((bf16[8,6,512,384]{3,2,1,0:T(8,128)(2,1)}), bf16[8,6,512,384]{3,2,1,0:T(8,128)(2,1)}, u32[]{:S(2)}, u32[]{:S(2)}) async-start(bf16[8,6,512,384]{3,2,1,0:T(8,128)(2,1)} %select_select_fusion), calls=%async_computation.1 | async-start | bytes 37748736 | tf_op jit(solution)/shard_map/all_to_all | solution.py:87
  244.5 251.7 %all-reduce.2.cloned.1.call-start = ((), (), s32[]{:S(2)}) async-start(), calls=%async_computation.4 | async-start | bytes 1572864 | tf_op jit(solution)/shard_map/psum | solution.py:48
  245.6 9.7 %copy-start.11 = (s32[512]{0:T(512)S(1)}, s32[512]{0:T(512)}, u32[]{:S(2)}) copy-start(s32[512]{0:T(512)} %param.23) | copy-start | bytes 6148
  245.6 250.6 %copy-start.6 = (f32[512]{0:T(512)S(1)}, f32[512]{0:T(512)}, u32[]{:S(2)}) copy-start(f32[512]{0:T(512)} %param.21) | copy-start | bytes 6148
  245.6 250.6 %copy-start.7 = (f32[512]{0:T(512)S(1)}, f32[512]{0:T(512)}, u32[]{:S(2)}) copy-start(f32[512]{0:T(512)} %param.19) | copy-start | bytes 6148
  245.6 250.6 %copy-start.8 = (s32[384]{0:T(512)S(1)}, s32[384]{0:T(512)}, u32[]{:S(2)}) copy-start(s32[384]{0:T(512)} %param.24) | copy-start | bytes 4612
  512.0 6.0 %copy-start.3 = (bf16[8,1536]{1,0:T(8,128)(2,1)S(1)}, bf16[8,1536]{1,0:T(8,128)(2,1)}, u32[]{:S(2)}) copy-start(bf16[8,1536]{1,0:T(8,128)(2,1)} %param.27) | copy-start | bytes 73732
Sparse Core Ops, SparseCore 0:
  20.0 123.9 reduce-scatter.1
  147.0 62.4 all-gather.1
  255.3 240.8 all-reduce.1
where the time goes:
time: 527 us
  waiting for transfers between devices  423 us (80%)
  local copies, waits for them, and re-layouts  29.8 us (6%)
  other arithmetic  26.7 us (5%)
  matrix products  26.5 us (5%)
  between operations  14 us (3%)
  starting transfers between devices  6.33 us (1%)
    psum x1, waiting for transfers between devices, per_device(): gradient = lax.psum(partial_grad, 'br')  240 us
    reduce_scatter x1, waiting for transfers between devices, per_device(): lax.psum_scatter(jnp.dot(shift_factors, inject_half, preferred_element_ty...  124 us
    all_gather x1, waiting for transfers between devices, per_device(): slab_prices = lax.all_gather(price_half, 'bus', axis=0, tiled=True)  60 us
    select_n x1, other arithmetic, per_device(): jnp.where(filled[:, :, None, None], outgoing, jnp.zeros_like(outgoing))  17.3 us
    gather x1, local copies, waits for them, and re-layouts, per_device(): fetched = jnp.take(arrived.reshape(-1, BLOCK, scenarios), lookup, axis=0)  12.7 us
    dot_general x1, matrix products, per_device(): jnp.dot(shift_factors, inject_half, preferred_element_type=jnp.float32)  12.6 us
    gather x1, local copies, waits for them, and re-layouts, per_device(): outgoing = jnp.take(slab_blocks, block_choice, axis=0)  11.7 us
  transfers between devices with their start and end apart: 4, of which 3 were waited for; matrix products, arithmetic and copies ran while one was open for 3% of the time, Pallas kernels for 0%

commit v1 on v0

v1 whole, which is shorter than its diff:
```python
import jax
import jax.numpy as jnp
from jax import lax
from jax.sharding import PartitionSpec as P

BLOCK = 512
CAP = 6
GDEV = 8


step_dual = 0.5
step_primal = 0.25


def slots_of(slabs):
    positions = jnp.arange(slabs.shape[-1], dtype=jnp.int32)
    earlier = positions[None, :] < positions[:, None]
    same = slabs[..., :, None] == slabs[..., None, :]
    return jnp.sum((same & earlier).astype(jnp.int32), axis=-1)


def per_device(
    shift_factors,
    injections,
    prices,
    limits,
    unit_cost,
    bus_load,
    bus_capacity,
    irradiance_profile,
    plant_group,
    scenario_profile,
    listed_slab,
    listed_block,
    rent_weight,
):
    scenarios = injections.shape[1]
    bus_axis = lax.axis_size("bus")
    slab_axis = lax.axis_size("br")
    slab_index = lax.axis_index("br")
    column_index = lax.axis_index("bus")
    list_len = listed_slab.shape[1]
    entries = GDEV * list_len
    slab_rows = shift_factors.shape[0]
    blocks_per_slab = slab_rows // BLOCK

    slab_by_device = listed_slab.reshape(-1, entries)
    block_by_device = listed_block.reshape(-1, entries)
    self_device = slab_index * bus_axis + column_index
    own_slab = lax.dynamic_index_in_dim(slab_by_device, self_device, 0, keepdims=False)
    own_slot = slots_of(own_slab)
    slab_range = jnp.arange(slab_axis, dtype=jnp.int32)
    slot_range = jnp.arange(CAP, dtype=jnp.int32)
    pick_out = (own_slab[None, None, :] == slab_range[:, None, None]) & (
        own_slot[None, None, :] == slot_range[None, :, None]
    )
    weight_rows = rent_weight.reshape(entries, BLOCK)
    outgoing_w = jnp.einsum(
        "sce,er->scr", pick_out.astype(jnp.bfloat16), weight_rows, preferred_element_type=jnp.float32
    ).astype(jnp.bfloat16)
    arrived_w = lax.all_to_all(outgoing_w, "br", 0, 0, tiled=True)

    inject_half = injections.astype(jnp.bfloat16)
    flow = lax.psum_scatter(
        jnp.dot(shift_factors, inject_half, preferred_element_type=jnp.float32),
        "bus",
        scatter_dimension=0,
        tiled=True,
    )
    moved = prices + step_dual * flow
    bound = step_dual * limits[:, None]
    new_prices = moved - jnp.clip(moved, -bound, bound)
    price_half = new_prices.astype(jnp.bfloat16)
    slab_prices = lax.all_gather(price_half, "bus", axis=0, tiled=True)
    partial_grad = lax.dot_general(
        shift_factors, slab_prices, (((0,), (0,)), ((), ())), preferred_element_type=jnp.float32
    )

    bus_rows = partial_grad.shape[0]
    share_rows = bus_rows // slab_axis
    gathered = lax.all_to_all(partial_grad.reshape(slab_axis, share_rows, scenarios), "br", 0, 0, tiled=True)
    gradient = jnp.sum(gathered, axis=0)
    start = slab_index * share_rows
    my_inj = lax.dynamic_slice_in_dim(injections, start, share_rows, 0)
    my_cost = lax.dynamic_slice_in_dim(unit_cost, start, share_rows, 0)
    my_load = lax.dynamic_slice_in_dim(bus_load, start, share_rows, 0)
    my_cap = lax.dynamic_slice_in_dim(bus_capacity, start, share_rows, 0)
    my_group = lax.dynamic_slice_in_dim(plant_group, start, share_rows, 0)
    by_group = jnp.take(irradiance_profile, my_group, axis=1)
    share = jnp.take(by_group, scenario_profile, axis=0).T
    upper = my_cap[:, None] * share
    trial = my_inj - step_primal * (my_cost[:, None] + gradient)
    my_new = jnp.minimum(jnp.maximum(trial, -my_load[:, None]), upper)
    new_injections = lax.all_to_all(
        jnp.broadcast_to(my_new[None], (slab_axis, share_rows, scenarios)), "br", 0, 0, tiled=True
    ).reshape(bus_rows, scenarios)

    sources = slab_range * bus_axis + column_index
    src_slab = jnp.take(slab_by_device, sources, axis=0)
    src_block = jnp.take(block_by_device, sources, axis=0)
    src_slot = slots_of(src_slab)
    pick_in = (src_slab[:, None, :] == slab_index) & (src_slot[:, None, :] == slot_range[None, :, None])
    block_choice = jnp.sum(jnp.where(pick_in, src_block[:, None, :], 0), axis=2)
    block_hot = block_choice[:, :, None] == jnp.arange(blocks_per_slab, dtype=jnp.int32)[None, None, :]
    masked = jnp.where(block_hot[:, :, :, None], arrived_w[:, :, None, :], jnp.zeros((), jnp.bfloat16))
    masked = masked.reshape(slab_axis * CAP, slab_rows)
    partial_rent = jnp.dot(masked, slab_prices, preferred_element_type=jnp.float32)
    returned = lax.all_to_all(partial_rent.reshape(slab_axis, CAP, scenarios), "br", 0, 0, tiled=True)
    lookup = own_slab * CAP + own_slot
    fetched = jnp.take(returned.reshape(slab_axis * CAP, scenarios), lookup, axis=0)
    group_rent = jnp.sum(fetched.reshape(GDEV, list_len, scenarios), axis=1)
    return (new_injections, new_prices, group_rent)


def solution(mesh):
    placed = (
        P("br", "bus"),
        P("bus", None),
        P(("br", "bus"), None),
        P(("br", "bus")),
        P("bus"),
        P("bus"),
        P("bus"),
        P(),
        P("bus"),
        P(),
        P(),
        P(),
        P(("br", "bus"), None),
    )
    return jax.shard_map(
        per_device,
        mesh=mesh,
        in_specs=placed,
        out_specs=(P("bus", None), P(("br", "bus"), None), P(("br", "bus"), None)),
        check_vma=False,
    )
```

time: 527 us -> 270 us (0.51)
  waiting for transfers between devices: 423 us -> 196 us
  other arithmetic: 26.7 us -> 6.79 us
  local copies, waits for them, and re-layouts: 29.8 us -> 11.2 us
  starting transfers between devices: 6.33 us -> 16.1 us
    psum x1 -> x0, waiting for transfers between devices: 240 us -> none  [per_device(): gradient = lax.psum(partial_grad, 'br')]
    select_n x6, other arithmetic: 23.5 us -> 0.34 us  [the longest x1 0.17 us: per_device(): jnp.where(block_hot[:, :, :, None], arrived_w[:, :, None, :], jnp.zeros((...]
    all_to_all x1 -> x4, waiting for transfers between devices: 0.01 us -> 22.8 us  [the longest x1 9.65 us: per_device(): lax.all_to_all(jnp.broadcast_to(my_new[None], (slab_axis, share_rows, sce...]
    gather x4 -> x7, local copies, waits for them, and re-layouts: 25.5 us -> 3.56 us  [the longest x2 1.24 us: per_device(): share = jnp.take(by_group, scenario_profile, axis=0).T]
    all_gather x1, waiting for transfers between devices: 60 us -> 49.6 us  [per_device(): slab_prices = lax.all_gather(price_half, 'bus', axis=0, tiled=True)]
    all_to_all x1 -> x4, starting transfers between devices: 6.03 us -> 16.1 us  [the longest x1 4.45 us: per_device(): lax.all_to_all(partial_grad.reshape(slab_axis, share_rows, scenarios), 'b...]
  transfers between devices with their start and end apart: 4 -> 6, of which waited for: 3 -> 5; matrix products, arithmetic and copies ran while one was open for 3% -> 6% of each run, Pallas kernels for 0% -> 0%
where the time goes in v1:
time: 270 us; the launch traced here: 269 us
  waiting for transfers between devices  196 us (73%)
  matrix products  24.3 us (9%)
  starting transfers between devices  16.1 us (6%)
  between operations  14.4 us (5%)
  local copies, waits for them, and re-layouts  11.2 us (4%)
  other arithmetic  6.79 us (3%)
    reduce_scatter x1, waiting for transfers between devices, per_device(): lax.psum_scatter(jnp.dot(shift_factors, inject_half, preferred_element_ty...  124 us
    all_gather x1, waiting for transfers between devices, per_device(): slab_prices = lax.all_gather(price_half, 'bus', axis=0, tiled=True)  49.6 us
    dot_general x1, matrix products, per_device(): jnp.dot(shift_factors, inject_half, preferred_element_type=jnp.float32)  12.6 us
    all_to_all x1, waiting for transfers between devices, per_device(): lax.all_to_all(jnp.broadcast_to(my_new[None], (slab_axis, share_rows, sce...  9.65 us
    dot_general x1, matrix products, per_device(): lax.dot_general(shift_factors, slab_prices, (((0,), (0,)), ((), ())), pre...  7.8 us
    all_to_all x1, waiting for transfers between devices, per_device(): lax.all_to_all(partial_grad.reshape(slab_axis, share_rows, scenarios), 'b...  7.74 us
  transfers between devices with their start and end apart: 6, of which 5 were waited for; matrix products, arithmetic and copies ran while one was open for 6% of the time, Pallas kernels for 0%

profile of v1, /device:TPU:6, one launch (start us, length us, event | category | flops | bytes accessed | tf_op | source)
XLA Modules:
  0.0 268.8 jit_solution(15771404547266552700)
XLA Ops:
  7.2 12.6 %fusion.2 = f32[8192,384]{1,0:T(8,128)} fusion(bf16[8192,512]{1,0:T(8,128)(2,1)} %param.15, f32[512,384]{1,0:T(8,128)} %param.16), kind=kOutput, calls=%fused_computation.11 | convolution fusion | flops 3221422080 | bytes 21757952 | tf_op jit(solution)/shard_map/dot_general | solution.py:65
  19.9 0.6 copy-done.6
  20.5 123.6 %reduce-scatter.2.cloned.1.call-done = f32[512,384]{1,0:T(8,128)} async-done(((f32[8192,384]{1,0:T(8,128)}), f32[512,384]{1,0:T(8,128)}) %reduce-scatter.2.cloned.1.call-update) | async-done | bytes 786448 | tf_op jit(solution)/shard_map/reduce_scatter | solution.py:64
  144.1 2.4 fusion.11
  146.5 0.2 copy.56
  147.3 0.6 copy.58
  147.9 4.4 %all-to-all-start.2 = ((bf16[8,6,512]{2,1,0:T(8,128)(2,1)}), bf16[8,6,512]{2,1,0:T(8,128)(2,1)S(1)}, u32[]{:S(2)}, u32[]{:S(2)}) async-start(bf16[8,6,512]{2,1,0:T(8,128)(2,1)} %copy.58), calls=%async_computation.3 | async-start | bytes 131072 | tf_op jit(solution)/shard_map/all_to_all | solution.py:61
  153.0 0.6 gather_fusion.3
  153.6 0.6 gather_fusion.4
  154.2 0.8 compare_and_fusion.2
  154.9 0.6 gather_fusion
  155.7 0.3 convert_reduce_fusion
  156.3 0.8 dynamic-slice_negate_fusion
  157.2 1.1 gather_fusion.1
  158.4 0.8 dynamic_slice.22
  159.2 0.8 dynamic_slice.20
  159.9 49.6 %all-gather.2.cloned.1.call-done = bf16[8192,384]{1,0:T(8,128)(2,1)} async-done(((bf16[512,384]{1,0:T(8,128)(2,1)}), bf16[8192,384]{1,0:T(8,128)(2,1)}) %all-gather.2.cloned.1.call-update) | async-done | bytes 6291472 | tf_op jit(solution)/shard_map/all_gather | solution.py:74
  209.5 7.8 %convolution_bitcast_fusion = f32[512,384]{0,1:T(8,128)S(1)} fusion(bf16[8192,384]{1,0:T(8,128)(2,1)} %all-gather.2.cloned.1.call-done, bf16[8192,512]{1,0:T(8,128)(2,1)} %param.15), kind=kOutput, calls=%fused_computation.7 | convolution fusion | flops 3221225472 | bytes 15466496 | tf_op jit(solution)/shard_map/dot_general | solution.py:75
  217.4 1.1 copy.52
  218.5 4.4 %all-to-all-start = ((f32[8,64,384]{2,1,0:T(8,128)}), f32[8,64,384]{2,1,0:T(8,128)S(1)}, u32[]{:S(2)}, u32[]{:S(2)}) async-start(f32[8,64,384]{2,1,0:T(8,128)} %bitcast.1), calls=%async_computation.1 | async-start | bytes 1572864 | tf_op jit(solution)/shard_map/all_to_all | solution.py:81
  223.1 3.8 %fusion = f32[8,6,384]{2,0,1:T(8,128)S(1)} fusion(bf16[8,6,8192]{2,0,1:T(8,128)(2,1)S(1)} %bitcast.27, bf16[8192,384]{1,0:T(8,128)(2,1)} %all-gather.2.cloned.1.call-done), kind=kOutput, calls=%fused_computation.5 | convolution fusion | flops 301989888 | bytes 7151616 | tf_op jit(solution)/shard_map/dot_general | solution.py:107
  226.9 0.7 copy.60
  227.6 7.7 %all-to-all-done = f32[8,64,384]{2,1,0:T(8,128)S(1)} async-done(((f32[8,64,384]{2,1,0:T(8,128)}), f32[8,64,384]{2,1,0:T(8,128)S(1)}, u32[]{:S(2)}, u32[]{:S(2)}) %all-to-all-start) | async-done | bytes 786464 | tf_op jit(solution)/shard_map/all_to_all | solution.py:81
  235.3 3.6 %all-to-all-start.3 = ((f32[8,6,384]{2,1,0:T(8,128)}), f32[8,6,384]{2,1,0:T(8,128)S(1)}, u32[]{:S(2)}, u32[]{:S(2)}) async-start(f32[8,6,384]{2,1,0:T(8,128)} %copy.60), calls=%async_computation.4 | async-start | bytes 196608 | tf_op jit(solution)/shard_map/all_to_all | solution.py:108
  239.0 1.0 bitcast_minimum_fusion
  240.0 5.4 %all-to-all-done.3 = f32[8,6,384]{2,1,0:T(8,128)S(1)} async-done(((f32[8,6,384]{2,1,0:T(8,128)}), f32[8,6,384]{2,1,0:T(8,128)S(1)}, u32[]{:S(2)}, u32[]{:S(2)}) %all-to-all-start.3) | async-done | bytes 73760 | tf_op jit(solution)/shard_map/all_to_all | solution.py:108
  245.4 0.9 broadcast_in_dim.112
  246.3 3.5 %all-to-all-start.1 = ((f32[8,64,384]{2,1,0:T(8,128)}), f32[8,64,384]{2,1,0:T(8,128)S(1)}, u32[]{:S(2)}, u32[]{:S(2)}) async-start(f32[8,64,384]{2,1,0:T(8,128)} %broadcast_in_dim.112), calls=%async_computation.2 | async-start | bytes 1572864 | tf_op jit(solution)/shard_map/all_to_all | solution.py:94
  250.1 0.6 gather_fusion.2
  250.7 0.7 select_reduce_fusion
  251.4 9.6 %all-to-all-done.1 = f32[8,64,384]{2,1,0:T(8,128)S(1)} async-done(((f32[8,64,384]{2,1,0:T(8,128)}), f32[8,64,384]{2,1,0:T(8,128)S(1)}, u32[]{:S(2)}, u32[]{:S(2)}) %all-to-all-start.1) | async-done | bytes 786464 | tf_op jit(solution)/shard_map/all_to_all | solution.py:94
  261.1 0.9 copy.62
  (54 shorter events, 2.4 us)
Async XLA Ops:
  7.2 136.9 %reduce-scatter.2.cloned.1.call-start = ((), (), s32[]{:S(2)}) async-start(), calls=%async_computation.5 | async-start | bytes 13369344 | tf_op jit(solution)/shard_map/reduce_scatter | solution.py:64
  19.8 0.7 copy-start.6
  19.8 124.3 %copy-start = (f32[512,384]{1,0:T(8,128)S(1)}, f32[512,384]{1,0:T(8,128)}, u32[]{:S(2)}) copy-start(f32[512,384]{1,0:T(8,128)} %param.17) | copy-start | bytes 2359300
  19.8 126.6 %copy-start.3 = (s32[1024,3]{0,1:T(4,128)S(1)}, s32[1024,3]{0,1:T(4,128)}, u32[]{:S(2)}) copy-start(s32[1024,3]{0,1:T(4,128)} %param.25) | copy-start | bytes 36868
  19.8 127.1 %copy-start.2 = (bf16[8,1536]{1,0:T(8,128)(2,1)S(1)}, bf16[8,1536]{1,0:T(8,128)(2,1)}, u32[]{:S(2)}) copy-start(bf16[8,1536]{1,0:T(8,128)(2,1)} %param.27) | copy-start | bytes 73732
  19.8 132.6 %copy-start.1 = (f32[64,1024]{1,0:T(8,128)S(1)}, f32[64,1024]{1,0:T(8,128)}, u32[]{:S(2)}) copy-start(f32[64,1024]{1,0:T(8,128)} %param.22) | copy-start | bytes 786436
  19.8 132.8 %copy-start.4 = (s32[1024,3]{0,1:T(4,128)S(1)}, s32[1024,3]{0,1:T(4,128)}, u32[]{:S(2)}) copy-start(s32[1024,3]{0,1:T(4,128)} %param.26) | copy-start | bytes 36868
  19.8 135.7 %copy-start.5 = (s32[384]{0:T(512)S(1)}, s32[384]{0:T(512)}, u32[]{:S(2)}) copy-start(s32[384]{0:T(512)} %param.24) | copy-start | bytes 4612
  19.9 189.7 %all-gather.2.cloned.1.call-start = ((), (), s32[]{:S(2)}) async-start(), calls=%async_computation.6 | async-start | bytes 6684672 | tf_op jit(solution)/shard_map/all_gather | solution.py:74
  147.9 12.0 %all-to-all-start.2 = ((bf16[8,6,512]{2,1,0:T(8,128)(2,1)}), bf16[8,6,512]{2,1,0:T(8,128)(2,1)S(1)}, u32[]{:S(2)}, u32[]{:S(2)}) async-start(bf16[8,6,512]{2,1,0:T(8,128)(2,1)} %copy.58), calls=%async_computation.3 | async-start | bytes 131072 | tf_op jit(solution)/shard_map/all_to_all | solution.py:61
  218.5 16.8 %all-to-all-start = ((f32[8,64,384]{2,1,0:T(8,128)}), f32[8,64,384]{2,1,0:T(8,128)S(1)}, u32[]{:S(2)}, u32[]{:S(2)}) async-start(f32[8,64,384]{2,1,0:T(8,128)} %bitcast.1), calls=%async_computation.1 | async-start | bytes 1572864 | tf_op jit(solution)/shard_map/all_to_all | solution.py:81
  235.3 10.1 %all-to-all-start.3 = ((f32[8,6,384]{2,1,0:T(8,128)}), f32[8,6,384]{2,1,0:T(8,128)S(1)}, u32[]{:S(2)}, u32[]{:S(2)}) async-start(f32[8,6,384]{2,1,0:T(8,128)} %copy.60), calls=%async_computation.4 | async-start | bytes 196608 | tf_op jit(solution)/shard_map/all_to_all | solution.py:108
  246.3 14.8 %all-to-all-start.1 = ((f32[8,64,384]{2,1,0:T(8,128)}), f32[8,64,384]{2,1,0:T(8,128)S(1)}, u32[]{:S(2)}, u32[]{:S(2)}) async-start(f32[8,64,384]{2,1,0:T(8,128)} %broadcast_in_dim.112), calls=%async_computation.2 | async-start | bytes 1572864 | tf_op jit(solution)/shard_map/all_to_all | solution.py:94
Sparse Core Ops, SparseCore 0:
  20.0 124.0 reduce-scatter.1
  147.1 62.4 all-gather.1

commit v2 on v1

--- a/solution.py
+++ b/solution.py
@@ -10,6 +10,76 @@
 
 step_dual = 0.5
 step_primal = 0.25
+
+
+YHI, XR, CORES = 2, 4, 2
+
+
+def bus_place():
+    b = lax.axis_index("bus")
+    return b // (XR * CORES), (b // CORES) % XR, b % CORES
+
+
+def bus_perm(move):
+    pairs = []
+    for b in range(YHI * XR * CORES):
+        yh, xi, c = b // (XR * CORES), (b // CORES) % XR, b % CORES
+        ty, tx, tc = move(yh, xi, c)
+        pairs.append((b, (ty * XR + tx) * CORES + tc))
+    return pairs
+
+
+CORE_SWAP = bus_perm(lambda y, x, c: (y, x, 1 - c))
+X_UP = bus_perm(lambda y, x, c: (y, (x + 1) % XR, c))
+X_DOWN = bus_perm(lambda y, x, c: (y, (x - 1) % XR, c))
+Y_SWAP = bus_perm(lambda y, x, c: (1 - y, x, c))
+
+
+def pick(a, i, axis):
+    return lax.dynamic_index_in_dim(a, i, axis, keepdims=False)
+
+
+def ring_scatter(parts, xi, up):
+    step = 1 if up else -1
+    perm = X_UP if up else X_DOWN
+    acc = pick(parts, (xi - step) % XR, 0)
+    for k in range(XR - 1):
+        acc = lax.ppermute(acc, "bus", perm) + pick(parts, (xi - step * (k + 2)) % XR, 0)
+    return acc
+
+
+def ring_gather(own, xi, up):
+    step = 1 if up else -1
+    perm = X_UP if up else X_DOWN
+    got = [own]
+    for _ in range(XR - 1):
+        got.append(lax.ppermute(got[-1], "bus", perm))
+    stacked = jnp.stack(got)
+    order = (step * (xi - jnp.arange(XR, dtype=jnp.int32))) % XR
+    return jnp.take(stacked, order, axis=0)
+
+
+def bus_reduce_scatter(send, keep):
+    yh, xi, c = bus_place()
+    y = keep + lax.ppermute(send, "bus", CORE_SWAP)
+    half = y.shape[2] // 2
+    cw = ring_scatter(jnp.moveaxis(y[:, :, :half], 1, 0), xi, True)
+    ccw = ring_scatter(jnp.moveaxis(y[:, :, half:], 1, 0), xi, False)
+    z = jnp.concatenate([cw, ccw], axis=1)
+    return pick(z, yh, 0) + lax.ppermute(pick(z, 1 - yh, 0), "bus", Y_SWAP)
+
+
+def bus_all_gather(p):
+    yh, xi, c = bus_place()
+    other = lax.ppermute(p, "bus", Y_SWAP)
+    pair = jnp.where(yh == 0, jnp.stack([p, other]), jnp.stack([other, p]))
+    half = p.shape[0] // 2
+    cw = ring_gather(pair[:, :half], xi, True)
+    ccw = ring_gather(pair[:, half:], xi, False)
+    quad = jnp.moveaxis(jnp.concatenate([cw, ccw], axis=2), 0, 1)
+    mate = lax.ppermute(quad, "bus", CORE_SWAP)
+    full = jnp.where(c == 0, jnp.stack([quad, mate], axis=2), jnp.stack([mate, quad], axis=2))
+    return full.reshape(-1, p.shape[1])
 
 
 def slots_of(slabs):
@@ -61,17 +131,16 @@
     arrived_w = lax.all_to_all(outgoing_w, "br", 0, 0, tiled=True)
 
     inject_half = injections.astype(jnp.bfloat16)
-    flow = lax.psum_scatter(
-        jnp.dot(shift_factors, inject_half, preferred_element_type=jnp.float32),
-        "bus",
-        scatter_dimension=0,
-        tiled=True,
-    )
+    yh, xi, core = bus_place()
+    by_place = shift_factors.reshape(YHI, XR, CORES, -1, shift_factors.shape[1])
+    flow_send = jnp.dot(pick(by_place, 1 - core, 2), inject_half, preferred_element_type=jnp.float32)
+    flow_keep = jnp.dot(pick(by_place, core, 2), inject_half, preferred_element_type=jnp.float32)
+    flow = bus_reduce_scatter(flow_send, flow_keep)
     moved = prices + step_dual * flow
     bound = step_dual * limits[:, None]
     new_prices = moved - jnp.clip(moved, -bound, bound)
     price_half = new_prices.astype(jnp.bfloat16)
-    slab_prices = lax.all_gather(price_half, "bus", axis=0, tiled=True)
+    slab_prices = bus_all_gather(price_half)
     partial_grad = lax.dot_general(
         shift_factors, slab_prices, (((0,), (0,)), ((), ())), preferred_element_type=jnp.float32
     )

time: 270 us -> 257 us (0.952)
  waiting for transfers between devices: 196 us -> 121 us
  starting transfers between devices: 16.1 us -> 45.8 us
  other arithmetic: 6.79 us -> 34.9 us
  local copies, waits for them, and re-layouts: 11.2 us -> 31.4 us
  between operations: 14.4 us -> 1.18 us
  matrix products: 24.3 us -> 21.5 us
    reduce_scatter x1 -> x0, waiting for transfers between devices: 124 us -> none  [per_device(): lax.psum_scatter(jnp.dot(shift_factors, inject_half, preferred_element_ty...]
    ppermute x0 -> x16, waiting for transfers between devices: none -> 99.2 us  [the longest x6 45.9 us: ring_scatter(): lax.ppermute(acc, 'bus', perm) + pick(parts, (xi - step * (k + 2)) % XR, 0)]
    all_gather x1 -> x0, waiting for transfers between devices: 49.6 us -> none  [per_device(): slab_prices = lax.all_gather(price_half, 'bus', axis=0, tiled=True)]
    ppermute x0 -> x16, starting transfers between devices: none -> 26.6 us  [the longest x6 10.5 us: ring_gather(): got.append(lax.ppermute(got[-1], 'bus', perm))]
    add x0 -> x6, other arithmetic: none -> 11.8 us  [ring_scatter(): lax.ppermute(acc, 'bus', perm) + pick(parts, (xi - step * (k + 2)) % XR, 0)]
    select_n x0 -> x6, other arithmetic: none -> 9.83 us  [the longest x1 7.33 us: bus_all_gather(): jnp.where(c == 0, jnp.stack([quad, mate], axis=2), jnp.stack([mate, quad]...]
    unnamed x18 -> x50, local copies, waits for them, and re-layouts: 2.1 us -> 9.41 us
    dot_general x1, matrix products: 7.8 us -> 3.42 us  [per_device(): lax.dot_general(shift_factors, slab_prices, (((0,), (0,)), ((), ())), pre...]
  transfers between devices with their start and end apart: 6 -> 20, of which waited for: 5 -> 13; matrix products, arithmetic and copies ran while one was open for 6% -> 15% of each run, Pallas kernels for 0% -> 0%
where the time goes in v2:
time: 257 us; the launch traced here: 256 us
  waiting for transfers between devices  121 us (47%)
  starting transfers between devices  45.8 us (18%)
  other arithmetic  34.9 us (14%)
  local copies, waits for them, and re-layouts  31.4 us (12%)
  matrix products  21.5 us (8%)
    ppermute x6, waiting for transfers between devices, ring_scatter(): lax.ppermute(acc, 'bus', perm) + pick(parts, (xi - step * (k + 2)) % XR, 0)  45.9 us
    ppermute x6, waiting for transfers between devices, ring_gather(): got.append(lax.ppermute(got[-1], 'bus', perm))  21.3 us
    ppermute x1, waiting for transfers between devices, bus_reduce_scatter(): return pick(z, yh, 0) + lax.ppermute(pick(z, 1 - yh, 0), 'bus', Y_SWAP)  15.3 us
    add x6, other arithmetic, ring_scatter(): lax.ppermute(acc, 'bus', perm) + pick(parts, (xi - step * (k + 2)) % XR, 0)  11.8 us
    ppermute x6, starting transfers between devices, ring_gather(): got.append(lax.ppermute(got[-1], 'bus', perm))  10.5 us
    ppermute x1, waiting for transfers between devices, bus_reduce_scatter(): y = keep + lax.ppermute(send, 'bus', CORE_SWAP)  10.5 us
    ppermute x6, starting transfers between devices, ring_scatter(): lax.ppermute(acc, 'bus', perm) + pick(parts, (xi - step * (k + 2)) % XR, 0)  9.71 us
    unnamed x50, local copies, waits for them, and re-layouts  9.41 us
  transfers between devices with their start and end apart: 20, of which 13 were waited for; matrix products, arithmetic and copies ran while one was open for 15% of the time, Pallas kernels for 0%

profile of v2, /device:TPU:6, one launch (start us, length us, event | category | flops | bytes accessed | tf_op | source)
XLA Modules:
  0.0 255.8 jit_solution(2390822953001729939)
XLA Ops:
  0.7 7.5 %fusion = f32[2,4,512,384]{3,2,1,0:T(8,128)} fusion(bf16[2,4,2,512,512]{4,3,2,1,0:T(8,128)(2,1)} %bitcast.96, s32[]{:T(128)S(6)} %select_n.224, f32[512,384]{1,0:T(8,128)} %param.18), kind=kOutput, calls=%fused_computation.8 | convolution fusion | flops 1610809344 | bytes 11272196 | tf_op jit(solution)/shard_map/dot_general | solution.py:136
  8.1 10.5 %collective-permute-done = f32[2,4,512,384]{3,2,1,0:T(8,128)} collective-permute-done((f32[2,4,512,384]{3,2,1,0:T(8,128)}, f32[2,4,512,384]{3,2,1,0:T(8,128)}, u32[]{:S(2)}, u32[]{:S(2)}) %collective-permute-start) | collective-permute-done | bytes 6291488 | tf_op jit(solution)/shard_map/ppermute | solution.py:64
  18.6 6.7 %fusion.6 = f32[2,4,512,384]{3,2,1,0:T(8,128)S(1)} fusion(f32[2,4,512,384]{3,2,1,0:T(8,128)} %collective-permute-done, bf16[2,4,2,512,512]{4,3,2,1,0:T(8,128)(2,1)} %bitcast.97, s32[]{:T(128)S(6)} %select_n.223, f32[512,384]{1,0:T(8,128)S(1)} %copy-done.5), kind=kOutput, calls=%fused_computation.15 | convolution fusion | flops 1612382208 | bytes 17563652 | tf_op jit(solution)/shard_map/dot_general | solution.py:137
  32.5 16.9 %collective-permute-done.4 = f32[2,256,384]{2,1,0:T(8,128)} collective-permute-done((f32[2,256,384]{2,1,0:T(8,128)}, f32[2,256,384]{2,1,0:T(8,128)}, u32[]{:S(2)}, u32[]{:S(2)}) %collective-permute-start.4) | collective-permute-done | bytes 786464 | tf_op jit(solution)/shard_map/ppermute | solution.py:47
  53.9 3.2 %collective-permute-start.2 = (f32[2,256,384]{2,1,0:T(8,128)}, f32[2,256,384]{2,1,0:T(8,128)}, u32[]{:S(2)}, u32[]{:S(2)}) collective-permute-start(f32[2,256,384]{2,1,0:T(8,128)} %bitcast_add_fusion.5), channel_id=1, source_target_pairs={{0,2},{1,3},{2,4},{3,5},{4,6},{5,7},{6,0},{7,1},{8,10},{9,11},{10,... | collective-permute-start | bytes 2359304 | tf_op jit(solution)/shard_map/ppermute | solution.py:47
  57.1 14.9 %collective-permute-done.5 = f32[2,256,384]{2,1,0:T(8,128)} collective-permute-done((f32[2,256,384]{2,1,0:T(8,128)}, f32[2,256,384]{2,1,0:T(8,128)}, u32[]{:S(2)}, u32[]{:S(2)}) %collective-permute-start.5) | collective-permute-done | bytes 786464 | tf_op jit(solution)/shard_map/ppermute | solution.py:47
  76.5 3.2 %collective-permute-start.3 = (f32[2,256,384]{2,1,0:T(8,128)}, f32[2,256,384]{2,1,0:T(8,128)}, u32[]{:S(2)}, u32[]{:S(2)}) collective-permute-start(f32[2,256,384]{2,1,0:T(8,128)} %bitcast_add_fusion.4), channel_id=1, source_target_pairs={{0,2},{1,3},{2,4},{3,5},{4,6},{5,7},{6,0},{7,1},{8,10},{9,11},{10,... | collective-permute-start | bytes 2359304 | tf_op jit(solution)/shard_map/ppermute | solution.py:47
  79.7 14.1 %collective-permute-done.6 = f32[2,256,384]{2,1,0:T(8,128)} collective-permute-done((f32[2,256,384]{2,1,0:T(8,128)}, f32[2,256,384]{2,1,0:T(8,128)}, u32[]{:S(2)}, u32[]{:S(2)}) %collective-permute-start.6) | collective-permute-done | bytes 786464 | tf_op jit(solution)/shard_map/ppermute | solution.py:47
  97.6 3.2 %collective-permute-start.7 = (f32[512,384]{1,0:T(8,128)S(1)}, f32[512,384]{1,0:T(8,128)S(1)}, u32[]{:S(2)}, u32[]{:S(2)}) collective-permute-start(f32[512,384]{1,0:T(8,128)S(1)} %fusion.12), channel_id=1, source_target_pairs={{0,8},{1,9},{2,10},{3,11},{4,12},{5,13},{6,14},{7,15},{8,0},{9,1},... | collective-permute-start | bytes 2359304 | tf_op jit(solution)/shard_map/ppermute | solution.py:69
  100.8 15.3 %collective-permute-done.7 = f32[512,384]{1,0:T(8,128)S(1)} collective-permute-done((f32[512,384]{1,0:T(8,128)S(1)}, f32[512,384]{1,0:T(8,128)S(1)}, u32[]{:S(2)}, u32[]{:S(2)}) %collective-permute-start.7) | collective-permute-done | bytes 786464 | tf_op jit(solution)/shard_map/ppermute | solution.py:69
  116.2 2.5 fusion.33
  118.6 3.2 %collective-permute-start.8 = (bf16[512,384]{1,0:T(8,128)(2,1)S(1)}, bf16[512,384]{1,0:T(8,128)(2,1)S(1)}, u32[]{:S(2)}, u32[]{:S(2)}) collective-permute-start(bf16[512,384]{1,0:T(8,128)(2,1)S(1)} %get-tuple-element.7), channel_id=1, source_target_pairs={{0,8},{1,9},{2,10},{3,11},{4,12},{5,13},{6,14},{7,15},{8,0},{9,1},... | collective-permute-start | bytes 1179656 | tf_op jit(solution)/shard_map/ppermute | solution.py:74
  121.8 6.1 %collective-permute-done.8 = bf16[512,384]{1,0:T(8,128)(2,1)S(1)} collective-permute-done((bf16[512,384]{1,0:T(8,128)(2,1)S(1)}, bf16[512,384]{1,0:T(8,128)(2,1)S(1)}, u32[]{:S(2)}, u32[]{:S(2)}) %collective-permute-start.8) | collective-permute-done | bytes 393248 | tf_op jit(solution)/shard_map/ppermute | solution.py:74
  128.2 3.1 %collective-permute-start.9 = (bf16[2,256,384]{2,1,0:T(8,128)(2,1)S(1)}, bf16[2,256,384]{2,1,0:T(8,128)(2,1)S(1)}, u32[]{:S(2)}, u32[]{:S(2)}) collective-permute-start(bf16[2,256,384]{2,1,0:T(8,128)(2,1)S(1)} %get-tuple-element.18), channel_id=1, source_target_pairs={{0,2},{1,3},{2,4},{3,5},{4,6},{5,7},{6,0},{7,1},{8,10},{9,11},{10,... | collective-permute-start | bytes 1179656 | tf_op jit(solution)/shard_map/ppermute | solution.py:56
  131.3 7.3 %collective-permute-done.9 = bf16[2,256,384]{2,1,0:T(8,128)(2,1)S(1)} collective-permute-done((bf16[2,256,384]{2,1,0:T(8,128)(2,1)S(1)}, bf16[2,256,384]{2,1,0:T(8,128)(2,1)S(1)}, u32[]{:S(2)}, u32[]{:S(2)}) %collective-permute-start.9) | collective-permute-done | bytes 393248 | tf_op jit(solution)/shard_map/ppermute | solution.py:56
  138.6 3.7 %collective-permute-start.10 = (bf16[2,256,384]{2,1,0:T(8,128)(2,1)S(1)}, bf16[2,256,384]{2,1,0:T(8,128)(2,1)S(1)}, u32[]{:S(2)}, u32[]{:S(2)}) collective-permute-start(bf16[2,256,384]{2,1,0:T(8,128)(2,1)S(1)} %collective-permute-done.9), channel_id=1, source_target_pairs={{0,2},{1,3},{2,4},{3,5},{4,6},{5,7},{6,0},{7,1},{8,10},{9,11},{10,... | collective-permute-start | bytes 1179656 | tf_op jit(solution)/shard_map/ppermute | solution.py:56
  142.9 7.9 %collective-permute-done.10 = bf16[2,256,384]{2,1,0:T(8,128)(2,1)S(1)} collective-permute-done((bf16[2,256,384]{2,1,0:T(8,128)(2,1)S(1)}, bf16[2,256,384]{2,1,0:T(8,128)(2,1)S(1)}, u32[]{:S(2)}, u32[]{:S(2)}) %collective-permute-start.10) | collective-permute-done | bytes 393248 | tf_op jit(solution)/shard_map/ppermute | solution.py:56
  150.8 3.7 %collective-permute-start.11 = (bf16[2,256,384]{2,1,0:T(8,128)(2,1)S(1)}, bf16[2,256,384]{2,1,0:T(8,128)(2,1)S(1)}, u32[]{:S(2)}, u32[]{:S(2)}) collective-permute-start(bf16[2,256,384]{2,1,0:T(8,128)(2,1)S(1)} %collective-permute-done.10), channel_id=1, source_target_pairs={{0,2},{1,3},{2,4},{3,5},{4,6},{5,7},{6,0},{7,1},{8,10},{9,11},{10,... | collective-permute-start | bytes 1179656 | tf_op jit(solution)/shard_map/ppermute | solution.py:56
  156.5 3.3 %collective-permute-done.11 = bf16[2,256,384]{2,1,0:T(8,128)(2,1)S(1)} collective-permute-done((bf16[2,256,384]{2,1,0:T(8,128)(2,1)S(1)}, bf16[2,256,384]{2,1,0:T(8,128)(2,1)S(1)}, u32[]{:S(2)}, u32[]{:S(2)}) %collective-permute-start.11) | collective-permute-done | bytes 393248 | tf_op jit(solution)/shard_map/ppermute | solution.py:56
  163.1 2.7 %collective-permute-done.14 = bf16[2,256,384]{2,1,0:T(8,128)(2,1)} collective-permute-done((bf16[2,256,384]{2,1,0:T(8,128)(2,1)}, bf16[2,256,384]{2,1,0:T(8,128)(2,1)}, u32[]{:S(2)}, u32[]{:S(2)}) %collective-permute-start.14) | collective-permute-done | bytes 393248 | tf_op jit(solution)/shard_map/ppermute | solution.py:56
  172.8 6.3 %all-to-all-start.2 = ((bf16[8,6,512]{2,1,0:T(8,128)(2,1)}), bf16[8,6,512]{2,1,0:T(8,128)(2,1)S(1)}, u32[]{:S(2)}, u32[]{:S(2)}) async-start(bf16[8,6,512]{2,1,0:T(8,128)(2,1)} %copy.82), calls=%async_computation.2 | async-start | bytes 131072 | tf_op jit(solution)/shard_map/all_to_all | solution.py:131
  193.2 7.3 %maximum_select_fusion = bf16[2,4,2,512,384]{4,3,0,1,2:T(8,128)(2,1)} fusion(bf16[2,4,1,512,384]{4,3,0,1,2:T(8,128)(2,1)} %bitcast.28, bf16[2,4,1,512,384]{4,3,0,1,2:T(8,128)(2,1)S(1)} %get-tuple-element.13, pred[]{:T(512)S(6)} %eq.121), kind=kLoop, calls=%fused_computation.7 | loop fusion | flops 9437184 | bytes 12582913 | tf_op jit(solution)/shard_map/jit(_where)/select_n | solution.py:81
  200.5 3.7 %copy.75 = bf16[2,4,2,512,384]{4,3,2,1,0:T(8,128)(2,1)S(1)} copy(bf16[2,4,2,512,384]{4,3,0,1,2:T(8,128)(2,1)} %maximum_select_fusion) | data formatting | bytes 12582912 | tf_op jit(solution)/shard_map/jit(_where)/select_n | solution.py:81
  204.2 2.6 %copy-done = bf16[2,4,2,512,384]{4,3,2,1,0:T(8,128)(2,1)} copy-done((bf16[2,4,2,512,384]{4,3,2,1,0:T(8,128)(2,1)}, bf16[2,4,2,512,384]{4,3,2,1,0:T(8,128)(2,1)S(1)}, u32[]{:S(2)}) %copy-start) | copy-done | bytes 6291480
  206.8 3.4 %convolution_bitcast_fusion = f32[512,384]{0,1:T(8,128)S(1)} fusion(bf16[8192,384]{1,0:T(8,128)(2,1)S(1)} %bitcast.94, bf16[8192,512]{1,0:T(8,128)(2,1)S(1)} %bitcast.99), kind=kOutput, calls=%fused_computation.26 | convolution fusion | flops 3221225472 | bytes 15466496 | tf_op jit(solution)/shard_map/dot_general | solution.py:144
  211.4 5.7 %all-to-all-start = ((f32[8,64,384]{2,1,0:T(8,128)}), f32[8,64,384]{2,1,0:T(8,128)S(1)}, u32[]{:S(2)}, u32[]{:S(2)}) async-start(f32[8,64,384]{2,1,0:T(8,128)} %bitcast.32), calls=%async_computation | async-start | bytes 1572864 | tf_op jit(solution)/shard_map/all_to_all | solution.py:150
  217.3 3.8 %fusion.35 = f32[8,6,384]{2,0,1:T(8,128)S(1)} fusion(bf16[8,6,8192]{2,0,1:T(8,128)(2,1)S(1)} %bitcast.100, bf16[8192,384,1]{1,0,2:T(8,128)(2,1)} %bitcast.95), kind=kOutput, calls=%fused_computation.110 | convolution fusion | flops 301989888 | bytes 7151616 | tf_op jit(solution)/shard_map/dot_general | solution.py:176
  221.8 7.4 %all-to-all-done = f32[8,64,384]{2,1,0:T(8,128)S(1)} async-done(((f32[8,64,384]{2,1,0:T(8,128)}), f32[8,64,384]{2,1,0:T(8,128)S(1)}, u32[]{:S(2)}, u32[]{:S(2)}) %all-to-all-start) | async-done | bytes 786464 | tf_op jit(solution)/shard_map/all_to_all | solution.py:150
  229.2 3.6 %all-to-all-start.3 = ((f32[8,6,384]{2,1,0:T(8,128)}), f32[8,6,384]{2,1,0:T(8,128)S(1)}, u32[]{:S(2)}, u32[]{:S(2)}) async-start(f32[8,6,384]{2,1,0:T(8,128)} %copy.84), calls=%async_computation.3 | async-start | bytes 196608 | tf_op jit(solution)/shard_map/all_to_all | solution.py:177
  233.9 5.4 %all-to-all-done.3 = f32[8,6,384]{2,1,0:T(8,128)S(1)} async-done(((f32[8,6,384]{2,1,0:T(8,128)}), f32[8,6,384]{2,1,0:T(8,128)S(1)}, u32[]{:S(2)}, u32[]{:S(2)}) %all-to-all-start.3) | async-done | bytes 73760 | tf_op jit(solution)/shard_map/all_to_all | solution.py:177
  240.2 3.5 %all-to-all-start.1 = ((f32[8,64,384]{2,1,0:T(8,128)}), f32[8,64,384]{2,1,0:T(8,128)S(1)}, u32[]{:S(2)}, u32[]{:S(2)}) async-start(f32[8,64,384]{2,1,0:T(8,128)} %broadcast_in_dim.121), calls=%async_computation.1 | async-start | bytes 1572864 | tf_op jit(solution)/shard_map/all_to_all | solution.py:163
  246.0 9.0 %all-to-all-done.1 = f32[8,64,384]{2,1,0:T(8,128)S(1)} async-done(((f32[8,64,384]{2,1,0:T(8,128)}), f32[8,64,384]{2,1,0:T(8,128)S(1)}, u32[]{:S(2)}, u32[]{:S(2)}) %all-to-all-start.1) | async-done | bytes 786464 | tf_op jit(solution)/shard_map/all_to_all | solution.py:163
  (140 shorter events, 53.7 us)
Async XLA Ops:
  0.6 18.0 %copy-start.5 = (f32[512,384]{1,0:T(8,128)S(1)}, f32[512,384]{1,0:T(8,128)}, u32[]{:S(2)}) copy-start(f32[512,384]{1,0:T(8,128)} %param.18) | copy-start | bytes 2359300
  8.1 10.5 %collective-permute-start = (f32[2,4,512,384]{3,2,1,0:T(8,128)}, f32[2,4,512,384]{3,2,1,0:T(8,128)}, u32[]{:S(2)}, u32[]{:S(2)}) collective-permute-start(f32[2,4,512,384]{3,2,1,0:T(8,128)} %fusion), channel_id=1, source_target_pairs={{0,1},{1,0},{2,3},{3,2},{4,5},{5,4},{6,7},{7,6},{8,9},{9,8},{10,11... | collective-permute-start | bytes 18874376 | tf_op jit(solution)/shard_map/ppermute | solution.py:64
  28.3 21.1 %collective-permute-start.4 = (f32[2,256,384]{2,1,0:T(8,128)}, f32[2,256,384]{2,1,0:T(8,128)}, u32[]{:S(2)}, u32[]{:S(2)}) collective-permute-start(f32[2,256,384]{2,1,0:T(8,128)} %dynamic-slice_bitcast_fusion), channel_id=1, source_target_pairs={{0,6},{1,7},{2,0},{3,1},{4,2},{5,3},{6,4},{7,5},{8,14},{9,15},{10,... | collective-permute-start | bytes 2359304 | tf_op jit(solution)/shard_map/ppermute | solution.py:47
  30.1 21.7 %collective-permute-start.1 = (f32[2,256,384]{2,1,0:T(8,128)}, f32[2,256,384]{2,1,0:T(8,128)}, u32[]{:S(2)}, u32[]{:S(2)}) collective-permute-start(f32[2,256,384]{2,1,0:T(8,128)} %dynamic-slice_bitcast_fusion.1), channel_id=1, source_target_pairs={{0,2},{1,3},{2,4},{3,5},{4,6},{5,7},{6,0},{7,1},{8,10},{9,11},{10,... | collective-permute-start | bytes 2359304 | tf_op jit(solution)/shard_map/ppermute | solution.py:47
  51.8 20.3 %collective-permute-start.5 = (f32[2,256,384]{2,1,0:T(8,128)}, f32[2,256,384]{2,1,0:T(8,128)}, u32[]{:S(2)}, u32[]{:S(2)}) collective-permute-start(f32[2,256,384]{2,1,0:T(8,128)} %bitcast_add_fusion.2), channel_id=1, source_target_pairs={{0,6},{1,7},{2,0},{3,1},{4,2},{5,3},{6,4},{7,5},{8,14},{9,15},{10,... | collective-permute-start | bytes 2359304 | tf_op jit(solution)/shard_map/ppermute | solution.py:47
  53.9 20.5 %collective-permute-start.2 = (f32[2,256,384]{2,1,0:T(8,128)}, f32[2,256,384]{2,1,0:T(8,128)}, u32[]{:S(2)}, u32[]{:S(2)}) collective-permute-start(f32[2,256,384]{2,1,0:T(8,128)} %bitcast_add_fusion.5), channel_id=1, source_target_pairs={{0,2},{1,3},{2,4},{3,5},{4,6},{5,7},{6,0},{7,1},{8,10},{9,11},{10,... | collective-permute-start | bytes 2359304 | tf_op jit(solution)/shard_map/ppermute | solution.py:47
  74.4 19.4 %collective-permute-start.6 = (f32[2,256,384]{2,1,0:T(8,128)}, f32[2,256,384]{2,1,0:T(8,128)}, u32[]{:S(2)}, u32[]{:S(2)}) collective-permute-start(f32[2,256,384]{2,1,0:T(8,128)} %bitcast_add_fusion.1), channel_id=1, source_target_pairs={{0,6},{1,7},{2,0},{3,1},{4,2},{5,3},{6,4},{7,5},{8,14},{9,15},{10,... | collective-permute-start | bytes 2359304 | tf_op jit(solution)/shard_map/ppermute | solution.py:47
  76.5 18.8 %collective-permute-start.3 = (f32[2,256,384]{2,1,0:T(8,128)}, f32[2,256,384]{2,1,0:T(8,128)}, u32[]{:S(2)}, u32[]{:S(2)}) collective-permute-start(f32[2,256,384]{2,1,0:T(8,128)} %bitcast_add_fusion.4), channel_id=1, source_target_pairs={{0,2},{1,3},{2,4},{3,5},{4,6},{5,7},{6,0},{7,1},{8,10},{9,11},{10,... | collective-permute-start | bytes 2359304 | tf_op jit(solution)/shard_map/ppermute | solution.py:47
  79.7 21.1 %copy-start.15 = (f32[512]{0:T(512)S(1)}, f32[512]{0:T(512)}, u32[]{:S(2)}) copy-start(f32[512]{0:T(512)} %param.20) | copy-start | bytes 6148
  97.6 18.5 %collective-permute-start.7 = (f32[512,384]{1,0:T(8,128)S(1)}, f32[512,384]{1,0:T(8,128)S(1)}, u32[]{:S(2)}, u32[]{:S(2)}) collective-permute-start(f32[512,384]{1,0:T(8,128)S(1)} %fusion.12), channel_id=1, source_target_pairs={{0,8},{1,9},{2,10},{3,11},{4,12},{5,13},{6,14},{7,15},{8,0},{9,1},... | collective-permute-start | bytes 2359304 | tf_op jit(solution)/shard_map/ppermute | solution.py:69
  116.2 38.4 %copy-start.12 = (s32[1024,3]{0,1:T(4,128)S(1)}, s32[1024,3]{0,1:T(4,128)}, u32[]{:S(2)}) copy-start(s32[1024,3]{0,1:T(4,128)} %param.27) | copy-start | bytes 36868
  118.6 36.4 %copy-start.11 = (bf16[8,1536]{1,0:T(8,128)(2,1)S(1)}, bf16[8,1536]{1,0:T(8,128)(2,1)}, u32[]{:S(2)}) copy-start(bf16[8,1536]{1,0:T(8,128)(2,1)} %param.29) | copy-start | bytes 73732
  118.6 9.3 %collective-permute-start.8 = (bf16[512,384]{1,0:T(8,128)(2,1)S(1)}, bf16[512,384]{1,0:T(8,128)(2,1)S(1)}, u32[]{:S(2)}, u32[]{:S(2)}) collective-permute-start(bf16[512,384]{1,0:T(8,128)(2,1)S(1)} %get-tuple-element.7), channel_id=1, source_target_pairs={{0,8},{1,9},{2,10},{3,11},{4,12},{5,13},{6,14},{7,15},{8,0},{9,1},... | collective-permute-start | bytes 1179656 | tf_op jit(solution)/shard_map/ppermute | solution.py:74
  128.2 10.4 %collective-permute-start.9 = (bf16[2,256,384]{2,1,0:T(8,128)(2,1)S(1)}, bf16[2,256,384]{2,1,0:T(8,128)(2,1)S(1)}, u32[]{:S(2)}, u32[]{:S(2)}) collective-permute-start(bf16[2,256,384]{2,1,0:T(8,128)(2,1)S(1)} %get-tuple-element.18), channel_id=1, source_target_pairs={{0,2},{1,3},{2,4},{3,5},{4,6},{5,7},{6,0},{7,1},{8,10},{9,11},{10,... | collective-permute-start | bytes 1179656 | tf_op jit(solution)/shard_map/ppermute | solution.py:56
  131.3 11.6 %collective-permute-start.12 = (bf16[2,256,384]{2,1,0:T(8,128)(2,1)S(1)}, bf16[2,256,384]{2,1,0:T(8,128)(2,1)S(1)}, u32[]{:S(2)}, u32[]{:S(2)}) collective-permute-start(bf16[2,256,384]{2,1,0:T(8,128)(2,1)S(1)} %get-tuple-element.17), channel_id=1, source_target_pairs={{0,6},{1,7},{2,0},{3,1},{4,2},{5,3},{6,4},{7,5},{8,14},{9,15},{10,... | collective-permute-start | bytes 1179656 | tf_op jit(solution)/shard_map/ppermute | solution.py:56
  138.6 12.2 %collective-permute-start.10 = (bf16[2,256,384]{2,1,0:T(8,128)(2,1)S(1)}, bf16[2,256,384]{2,1,0:T(8,128)(2,1)S(1)}, u32[]{:S(2)}, u32[]{:S(2)}) collective-permute-start(bf16[2,256,384]{2,1,0:T(8,128)(2,1)S(1)} %collective-permute-done.9), channel_id=1, source_target_pairs={{0,2},{1,3},{2,4},{3,5},{4,6},{5,7},{6,0},{7,1},{8,10},{9,11},{10,... | collective-permute-start | bytes 1179656 | tf_op jit(solution)/shard_map/ppermute | solution.py:56
  142.9 16.9 %copy-start.6 = (bf16[2,256,384]{2,1,0:T(8,128)(2,1)}, bf16[2,256,384]{2,1,0:T(8,128)(2,1)S(1)}, u32[]{:S(2)}) copy-start(bf16[2,256,384]{2,1,0:T(8,128)(2,1)S(1)} %collective-permute-done.12) | copy-start | bytes 1179652
  142.9 13.6 %collective-permute-start.13 = (bf16[2,256,384]{2,1,0:T(8,128)(2,1)S(1)}, bf16[2,256,384]{2,1,0:T(8,128)(2,1)}, u32[]{:S(2)}, u32[]{:S(2)}) collective-permute-start(bf16[2,256,384]{2,1,0:T(8,128)(2,1)S(1)} %collective-permute-done.12), channel_id=1, source_target_pairs={{0,6},{1,7},{2,0},{3,1},{4,2},{5,3},{6,4},{7,5},{8,14},{9,15},{10,... | collective-permute-start | bytes 1179656 | tf_op jit(solution)/shard_map/ppermute | solution.py:56
  150.8 9.0 %collective-permute-start.11 = (bf16[2,256,384]{2,1,0:T(8,128)(2,1)S(1)}, bf16[2,256,384]{2,1,0:T(8,128)(2,1)S(1)}, u32[]{:S(2)}, u32[]{:S(2)}) collective-permute-start(bf16[2,256,384]{2,1,0:T(8,128)(2,1)S(1)} %collective-permute-done.10), channel_id=1, source_target_pairs={{0,2},{1,3},{2,4},{3,5},{4,6},{5,7},{6,0},{7,1},{8,10},{9,11},{10,... | collective-permute-start | bytes 1179656 | tf_op jit(solution)/shard_map/ppermute | solution.py:56
  156.4 15.5 %copy-start.17 = (s32[24]{0:T(128)}, s32[24]{0:T(128)S(1)}, u32[]{:S(2)}) copy-start(s32[24]{0:T(128)S(1)} %convert_reduce_fusion.1) | copy-start | bytes 292
  156.4 9.4 %collective-permute-start.14 = (bf16[2,256,384]{2,1,0:T(8,128)(2,1)}, bf16[2,256,384]{2,1,0:T(8,128)(2,1)}, u32[]{:S(2)}, u32[]{:S(2)}) collective-permute-start(bf16[2,256,384]{2,1,0:T(8,128)(2,1)} %collective-permute-done.13), channel_id=1, source_target_pairs={{0,6},{1,7},{2,0},{3,1},{4,2},{5,3},{6,4},{7,5},{8,14},{9,15},{10,... | collective-permute-start | bytes 1179656 | tf_op jit(solution)/shard_map/ppermute | solution.py:56
  169.5 15.3 %copy-start.8 = (f32[64,1024]{1,0:T(8,128)S(1)}, f32[64,1024]{1,0:T(8,128)}, u32[]{:S(2)}) copy-start(f32[64,1024]{1,0:T(8,128)} %param.24) | copy-start | bytes 786436
  169.5 18.7 %copy-start.14 = (s32[384]{0:T(512)S(1)}, s32[384]{0:T(512)}, u32[]{:S(2)}) copy-start(s32[384]{0:T(512)} %param.26) | copy-start | bytes 4612
  172.0 21.2 %collective-permute-start.15 = (bf16[2,4,512,384]{3,2,0,1:T(8,128)(2,1)}, bf16[2,4,512,384]{3,2,0,1:T(8,128)(2,1)}, u32[]{:S(2)}, u32[]{:S(2)}) collective-permute-start(bf16[2,4,512,384]{3,2,0,1:T(8,128)(2,1)} %get-tuple-element.14), channel_id=1, source_target_pairs={{0,1},{1,0},{2,3},{3,2},{4,5},{5,4},{6,7},{7,6},{8,9},{9,8},{10,11... | collective-permute-start | bytes 9437192 | tf_op jit(solution)/shard_map/ppermute | solution.py:80
  172.8 20.3 %all-to-all-start.2 = ((bf16[8,6,512]{2,1,0:T(8,128)(2,1)}), bf16[8,6,512]{2,1,0:T(8,128)(2,1)S(1)}, u32[]{:S(2)}, u32[]{:S(2)}) async-start(bf16[8,6,512]{2,1,0:T(8,128)(2,1)} %copy.82), calls=%async_computation.2 | async-start | bytes 131072 | tf_op jit(solution)/shard_map/all_to_all | solution.py:131
  193.2 13.7 %slice-start = ((s8[8388608]{0:T(1024)(128)(4,1)}), s8[4194304]{0:T(1024)(128)(4,1)S(1)}, s32[]{:S(2)}) async-start(s8[8388608]{0:T(1024)(128)(4,1)} %bitcast.98), calls=%async_computation.4 | async-start | bytes 8388608
  211.4 17.8 %all-to-all-start = ((f32[8,64,384]{2,1,0:T(8,128)}), f32[8,64,384]{2,1,0:T(8,128)S(1)}, u32[]{:S(2)}, u32[]{:S(2)}) async-start(f32[8,64,384]{2,1,0:T(8,128)} %bitcast.32), calls=%async_computation | async-start | bytes 1572864 | tf_op jit(solution)/shard_map/all_to_all | solution.py:150
  217.3 15.6 %copy-start.19 = (f32[64]{0:T(128)S(1)}, f32[64]{0:T(128)}, u32[]{:S(2)}) copy-start(f32[64]{0:T(128)} %dynamic-slice_negate_fusion) | copy-start | bytes 772
  221.1 22.6 %copy-start.18 = (s32[24]{0:T(128)S(1)}, s32[24]{0:T(128)}, u32[]{:S(2)}) copy-start(s32[24]{0:T(128)} %copy-done.17) | copy-start | bytes 292
  221.1 22.7 %copy-start.16 = (s32[24]{0:T(128)S(1)}, s32[24]{0:T(128)}, u32[]{:S(2)}) copy-start(s32[24]{0:T(128)} %get-tuple-element.19) | copy-start | bytes 292
  229.2 10.1 %all-to-all-start.3 = ((f32[8,6,384]{2,1,0:T(8,128)}), f32[8,6,384]{2,1,0:T(8,128)S(1)}, u32[]{:S(2)}, u32[]{:S(2)}) async-start(f32[8,6,384]{2,1,0:T(8,128)} %copy.84), calls=%async_computation.3 | async-start | bytes 196608 | tf_op jit(solution)/shard_map/all_to_all | solution.py:177
  240.2 14.8 %all-to-all-start.1 = ((f32[8,64,384]{2,1,0:T(8,128)}), f32[8,64,384]{2,1,0:T(8,128)S(1)}, u32[]{:S(2)}, u32[]{:S(2)}) async-start(f32[8,64,384]{2,1,0:T(8,128)} %broadcast_in_dim.121), calls=%async_computation.1 | async-start | bytes 1572864 | tf_op jit(solution)/shard_map/all_to_all | solution.py:163
  (11 other events, 39.9 us)

commit v3 on v2

--- a/solution.py
+++ b/solution.py
@@ -77,9 +77,7 @@
     cw = ring_gather(pair[:, :half], xi, True)
     ccw = ring_gather(pair[:, half:], xi, False)
     quad = jnp.moveaxis(jnp.concatenate([cw, ccw], axis=2), 0, 1)
-    mate = lax.ppermute(quad, "bus", CORE_SWAP)
-    full = jnp.where(c == 0, jnp.stack([quad, mate], axis=2), jnp.stack([mate, quad], axis=2))
-    return full.reshape(-1, p.shape[1])
+    return quad, lax.ppermute(quad, "bus", CORE_SWAP)
 
 
 def slots_of(slabs):
@@ -130,25 +128,21 @@
     ).astype(jnp.bfloat16)
     arrived_w = lax.all_to_all(outgoing_w, "br", 0, 0, tiled=True)
 
-    inject_half = injections.astype(jnp.bfloat16)
+    sources = slab_range * bus_axis + column_index
+    src_slab = jnp.take(slab_by_device, sources, axis=0)
+    src_block = jnp.take(block_by_device, sources, axis=0)
+    src_slot = slots_of(src_slab)
+    pick_in = (src_slab[:, None, :] == slab_index) & (src_slot[:, None, :] == slot_range[None, :, None])
+    block_choice = jnp.sum(jnp.where(pick_in, src_block[:, None, :], 0), axis=2)
+    block_hot = block_choice[:, :, None] == jnp.arange(blocks_per_slab, dtype=jnp.int32)[None, None, :]
+    masked = jnp.where(block_hot[:, :, :, None], arrived_w[:, :, None, :], jnp.zeros((), jnp.bfloat16))
     yh, xi, core = bus_place()
-    by_place = shift_factors.reshape(YHI, XR, CORES, -1, shift_factors.shape[1])
-    flow_send = jnp.dot(pick(by_place, 1 - core, 2), inject_half, preferred_element_type=jnp.float32)
-    flow_keep = jnp.dot(pick(by_place, core, 2), inject_half, preferred_element_type=jnp.float32)
-    flow = bus_reduce_scatter(flow_send, flow_keep)
-    moved = prices + step_dual * flow
-    bound = step_dual * limits[:, None]
-    new_prices = moved - jnp.clip(moved, -bound, bound)
-    price_half = new_prices.astype(jnp.bfloat16)
-    slab_prices = bus_all_gather(price_half)
-    partial_grad = lax.dot_general(
-        shift_factors, slab_prices, (((0,), (0,)), ((), ())), preferred_element_type=jnp.float32
-    )
-
-    bus_rows = partial_grad.shape[0]
+    masked = masked.reshape(slab_axis * CAP, YHI, XR, CORES, -1)
+    masked_keep = pick(masked, core, 3)
+    masked_send = pick(masked, 1 - core, 3)
+
+    bus_rows = injections.shape[0]
     share_rows = bus_rows // slab_axis
-    gathered = lax.all_to_all(partial_grad.reshape(slab_axis, share_rows, scenarios), "br", 0, 0, tiled=True)
-    gradient = jnp.sum(gathered, axis=0)
     start = slab_index * share_rows
     my_inj = lax.dynamic_slice_in_dim(injections, start, share_rows, 0)
     my_cost = lax.dynamic_slice_in_dim(unit_cost, start, share_rows, 0)
@@ -158,23 +152,43 @@
     by_group = jnp.take(irradiance_profile, my_group, axis=1)
     share = jnp.take(by_group, scenario_profile, axis=0).T
     upper = my_cap[:, None] * share
-    trial = my_inj - step_primal * (my_cost[:, None] + gradient)
-    my_new = jnp.minimum(jnp.maximum(trial, -my_load[:, None]), upper)
+    lower = -my_load[:, None]
+    base = my_inj - step_primal * my_cost[:, None]
+
+    inject_half = injections.astype(jnp.bfloat16)
+    by_place = shift_factors.reshape(YHI, XR, CORES, -1, shift_factors.shape[1])
+    sf_keep = pick(by_place, core, 2)
+    sf_send = pick(by_place, 1 - core, 2)
+    flow_send = jnp.dot(sf_send, inject_half, preferred_element_type=jnp.float32)
+    flow_keep = jnp.dot(sf_keep, inject_half, preferred_element_type=jnp.float32)
+    flow_keep, masked_keep, masked_send, upper, lower, base = lax.optimization_barrier(
+        (flow_keep, masked_keep, masked_send, upper, lower, base)
+    )
+    flow = bus_reduce_scatter(flow_send, flow_keep)
+    moved = prices + step_dual * flow
+    bound = step_dual * limits[:, None]
+    new_prices = moved - jnp.clip(moved, -bound, bound)
+    price_half = new_prices.astype(jnp.bfloat16)
+    prices_keep, prices_send = bus_all_gather(price_half)
+    contract = (((0, 1, 2), (0, 1, 2)), ((), ()))
+    partial_grad = lax.dot_general(sf_keep, prices_keep, contract, preferred_element_type=jnp.float32)
+    partial_grad = partial_grad + lax.dot_general(sf_send, prices_send, contract, preferred_element_type=jnp.float32)
+    contract_w = (((1, 2, 3), (0, 1, 2)), ((), ()))
+    partial_rent = lax.dot_general(masked_keep, prices_keep, contract_w, preferred_element_type=jnp.float32)
+    partial_rent = partial_rent + lax.dot_general(masked_send, prices_send, contract_w, preferred_element_type=jnp.float32)
+
+    outgoing = jnp.concatenate(
+        [partial_grad.reshape(slab_axis, share_rows, scenarios), partial_rent.reshape(slab_axis, CAP, scenarios)], axis=1
+    )
+    gathered = lax.all_to_all(outgoing, "br", 0, 0, tiled=True)
+    gradient = jnp.sum(gathered[:, :share_rows], axis=0)
+    returned = gathered[:, share_rows:]
+    trial = base - step_primal * gradient
+    my_new = jnp.minimum(jnp.maximum(trial, lower), upper)
     new_injections = lax.all_to_all(
         jnp.broadcast_to(my_new[None], (slab_axis, share_rows, scenarios)), "br", 0, 0, tiled=True
     ).reshape(bus_rows, scenarios)
 
-    sources = slab_range * bus_axis + column_index
-    src_slab = jnp.take(slab_by_device, sources, axis=0)
-    src_block = jnp.take(block_by_device, sources, axis=0)
-    src_slot = slots_of(src_slab)
-    pick_in = (src_slab[:, None, :] == slab_index) & (src_slot[:, None, :] == slot_range[None, :, None])
-    block_choice = jnp.sum(jnp.where(pick_in, src_block[:, None, :], 0), axis=2)
-    block_hot = block_choice[:, :, None] == jnp.arange(blocks_per_slab, dtype=jnp.int32)[None, None, :]
-    masked = jnp.where(block_hot[:, :, :, None], arrived_w[:, :, None, :], jnp.zeros((), jnp.bfloat16))
-    masked = masked.reshape(slab_axis * CAP, slab_rows)
-    partial_rent = jnp.dot(masked, slab_prices, preferred_element_type=jnp.float32)
-    returned = lax.all_to_all(partial_rent.reshape(slab_axis, CAP, scenarios), "br", 0, 0, tiled=True)
     lookup = own_slab * CAP + own_slot
     fetched = jnp.take(returned.reshape(slab_axis * CAP, scenarios), lookup, axis=0)
     group_rent = jnp.sum(fetched.reshape(GDEV, list_len, scenarios), axis=1)

time: 257 us -> 235 us (0.914)
  blocking collectives: 0 us -> 19.3 us
  waiting for transfers between devices: 121 us -> 102 us
  starting transfers between devices: 45.8 us -> 32.7 us
  local copies, waits for them, and re-layouts: 31.4 us -> 20.5 us
  matrix products: 21.5 us -> 26.1 us
    all_to_all x0 -> x1, blocking collectives: none -> 19.3 us  [per_device(): gathered = lax.all_to_all(outgoing, 'br', 0, 0, tiled=True)]
    all_to_all x2 -> x0, waiting for transfers between devices: 12.8 us -> none  [the longest x1 7.41 us: per_device(): lax.all_to_all(partial_grad.reshape(slab_axis, share_rows, scenarios), 'b...]
    ppermute x1, waiting for transfers between devices: 10.5 us -> 0.01 us  [bus_reduce_scatter(): y = keep + lax.ppermute(send, 'bus', CORE_SWAP)]
    all_to_all x2 -> x0, starting transfers between devices: 9.33 us -> none  [the longest x1 5.7 us: per_device(): lax.all_to_all(partial_grad.reshape(slab_axis, share_rows, scenarios), 'b...]
    select_n x1 -> x0, other arithmetic: 7.33 us -> none  [bus_all_gather(): jnp.where(c == 0, jnp.stack([quad, mate], axis=2), jnp.stack([mate, quad]...]
    add x0 -> x1, other arithmetic: none -> 5.23 us  [bus_reduce_scatter(): y = keep + lax.ppermute(send, 'bus', CORE_SWAP)]
    dot_general x4 -> x6, matrix products: 21.4 us -> 26 us  [the longest x1 7.46 us: per_device(): jnp.dot(sf_send, inject_half, preferred_element_type=jnp.float32)]
    ppermute x6, waiting for transfers between devices: 45.9 us -> 49.7 us  [ring_scatter(): lax.ppermute(acc, 'bus', perm) + pick(parts, (xi - step * (k + 2)) % XR, 0)]
  transfers between devices with their start and end apart: 20 -> 18, of which waited for: 13 -> 10; matrix products, arithmetic and copies ran while one was open for 15% -> 18% of each run, Pallas kernels for 0% -> 0%
where the time goes in v3:
time: 235 us; the launch traced here: 234 us
  waiting for transfers between devices  102 us (43%)
  starting transfers between devices  32.7 us (14%)
  other arithmetic  32.4 us (14%)
  matrix products  26.1 us (11%)
  local copies, waits for them, and re-layouts  20.5 us (9%)
  blocking collectives  19.3 us (8%)
    ppermute x6, waiting for transfers between devices, ring_scatter(): lax.ppermute(acc, 'bus', perm) + pick(parts, (xi - step * (k + 2)) % XR, 0)  49.7 us
    ppermute x6, waiting for transfers between devices, ring_gather(): got.append(lax.ppermute(got[-1], 'bus', perm))  21.5 us
    all_to_all x1, blocking collectives, per_device(): gathered = lax.all_to_all(outgoing, 'br', 0, 0, tiled=True)  19.3 us
    ppermute x1, waiting for transfers between devices, bus_reduce_scatter(): return pick(z, yh, 0) + lax.ppermute(pick(z, 1 - yh, 0), 'bus', Y_SWAP)  15.4 us
    add x6, other arithmetic, ring_scatter(): lax.ppermute(acc, 'bus', perm) + pick(parts, (xi - step * (k + 2)) % XR, 0)  11.5 us
    ppermute x6, starting transfers between devices, ring_gather(): got.append(lax.ppermute(got[-1], 'bus', perm))  9.98 us
    all_to_all x1, waiting for transfers between devices, per_device(): lax.all_to_all(jnp.broadcast_to(my_new[None], (slab_axis, share_rows, sce...  8.97 us
    dot_general x1, matrix products, per_device(): jnp.dot(sf_send, inject_half, preferred_element_type=jnp.float32)  7.46 us
  transfers between devices with their start and end apart: 18, of which 10 were waited for; matrix products, arithmetic and copies ran while one was open for 18% of the time, Pallas kernels for 0%

profile of v3, /device:TPU:6, one launch (start us, length us, event | category | flops | bytes accessed | tf_op | source)
XLA Modules:
  0.0 234.2 jit_solution(12644367175618422795)
XLA Ops:
  0.7 7.5 %fusion.2 = f32[2,4,512,384]{3,2,1,0:T(8,128)} fusion(bf16[2,4,2,512,512]{4,3,2,1,0:T(8,128)(2,1)} %bitcast.121, s32[]{:T(128)S(6)} %select_n.195, f32[512,384]{1,0:T(8,128)} %param.18), kind=kOutput, calls=%fused_computation.9 | convolution fusion | flops 1610809344 | bytes 11272196 | tf_op jit(solution)/shard_map/dot_general | solution.py:162
  9.7 6.3 %all-to-all-start = ((bf16[8,6,512]{2,1,0:T(8,128)(2,1)}), bf16[8,6,512]{2,1,0:T(8,128)(2,1)S(1)}, u32[]{:S(2)}, u32[]{:S(2)}) async-start(bf16[8,6,512]{2,1,0:T(8,128)(2,1)} %copy.57), calls=%async_computation | async-start | bytes 131072 | tf_op jit(solution)/shard_map/all_to_all | solution.py:129
  24.5 7.1 %fusion.6 = f32[2,4,512,384]{3,2,1,0:T(8,128)} fusion(bf16[2,4,2,512,512]{4,3,2,1,0:T(8,128)(2,1)} %bitcast.122, s32[]{:T(128)S(6)} %select_n.191, f32[512,384]{1,0:T(8,128)S(1)} %copy-done.3), kind=kOutput, calls=%fused_computation.13 | convolution fusion | flops 1610809344 | bytes 11272196 | tf_op jit(solution)/shard_map/dot_general | solution.py:163
  34.1 5.2 %add.216 = f32[2,4,512,384]{3,2,1,0:T(8,128)S(1)} add(f32[2,4,512,384]{3,2,1,0:T(8,128)} %fusion.6, f32[2,4,512,384]{3,2,1,0:T(8,128)} %collective-permute-done) | non-fusion elementwise | flops 1572864 | bytes 18874368 | tf_op jit(solution)/shard_map/add | solution.py:64
  45.3 17.0 %collective-permute-done.1 = f32[2,256,384]{2,1,0:T(8,128)} collective-permute-done((f32[2,256,384]{2,1,0:T(8,128)}, f32[2,256,384]{2,1,0:T(8,128)}, u32[]{:S(2)}, u32[]{:S(2)}) %collective-permute-start.1) | collective-permute-done | bytes 786464 | tf_op jit(solution)/shard_map/ppermute | solution.py:47
  62.3 2.3 bitcast_add_fusion.5
  66.3 2.1 bitcast_add_fusion.2
  68.8 15.0 %collective-permute-done.2 = f32[2,256,384]{2,1,0:T(8,128)} collective-permute-done((f32[2,256,384]{2,1,0:T(8,128)}, f32[2,256,384]{2,1,0:T(8,128)}, u32[]{:S(2)}, u32[]{:S(2)}) %collective-permute-start.2) | collective-permute-done | bytes 786464 | tf_op jit(solution)/shard_map/ppermute | solution.py:47
  83.7 2.3 bitcast_add_fusion.4
  86.1 2.9 %collective-permute-start.3 = (f32[2,256,384]{2,1,0:T(8,128)}, f32[2,256,384]{2,1,0:T(8,128)}, u32[]{:S(2)}, u32[]{:S(2)}) collective-permute-start(f32[2,256,384]{2,1,0:T(8,128)} %bitcast_add_fusion.4), channel_id=1, source_target_pairs={{0,2},{1,3},{2,4},{3,5},{4,6},{5,7},{6,0},{7,1},{8,10},{9,11},{10,... | collective-permute-start | bytes 2359304 | tf_op jit(solution)/shard_map/ppermute | solution.py:47
  89.0 2.1 bitcast_add_fusion.1
  91.1 13.7 %collective-permute-done.3 = f32[2,256,384]{2,1,0:T(8,128)} collective-permute-done((f32[2,256,384]{2,1,0:T(8,128)}, f32[2,256,384]{2,1,0:T(8,128)}, u32[]{:S(2)}, u32[]{:S(2)}) %collective-permute-start.3) | collective-permute-done | bytes 786464 | tf_op jit(solution)/shard_map/ppermute | solution.py:47
  106.2 4.0 %collective-permute-done.6 = f32[2,256,384]{2,1,0:T(8,128)} collective-permute-done((f32[2,256,384]{2,1,0:T(8,128)}, f32[2,256,384]{2,1,0:T(8,128)}, u32[]{:S(2)}, u32[]{:S(2)}) %collective-permute-start.6) | collective-permute-done | bytes 786464 | tf_op jit(solution)/shard_map/ppermute | solution.py:47
  112.4 2.9 %collective-permute-start.7 = (f32[512,384]{1,0:T(8,128)S(1)}, f32[512,384]{1,0:T(8,128)S(1)}, u32[]{:S(2)}, u32[]{:S(2)}) collective-permute-start(f32[512,384]{1,0:T(8,128)S(1)} %fusion.23), channel_id=1, source_target_pairs={{0,8},{1,9},{2,10},{3,11},{4,12},{5,13},{6,14},{7,15},{8,0},{9,1},... | collective-permute-start | bytes 2359304 | tf_op jit(solution)/shard_map/ppermute | solution.py:69
  115.3 15.4 %collective-permute-done.7 = f32[512,384]{1,0:T(8,128)S(1)} collective-permute-done((f32[512,384]{1,0:T(8,128)S(1)}, f32[512,384]{1,0:T(8,128)S(1)}, u32[]{:S(2)}, u32[]{:S(2)}) %collective-permute-start.7) | collective-permute-done | bytes 786464 | tf_op jit(solution)/shard_map/ppermute | solution.py:69
  130.7 2.5 %fusion.46 = (bf16[512,384]{1,0:T(8,128)(2,1)S(1)}, f32[512,384]{1,0:T(8,128)}) fusion(f32[512]{0:T(512)S(1)} %get-tuple-element.34, f32[512]{0:T(512)S(1)} %get-tuple-element.33, f32[512,384]{1,0:T(8,128)} %param.19, f32[512,384]{1,0:T(8,128)S(1)} %collective-permute-done.7, s32[]{:T(128)S(6)} %select_n.221, f32[2,256,384]{2,1,0:T(8,128)} %copy-done.2, ...), kind=kLoop, calls=%fused_computation.126 | loop fusion | flops 1572864 | bytes 4329476 | tf_op jit(solution)/shard_map/convert_element_type | solution.py:171
  133.1 2.9 %collective-permute-start.8 = (bf16[512,384]{1,0:T(8,128)(2,1)S(1)}, bf16[512,384]{1,0:T(8,128)(2,1)S(1)}, u32[]{:S(2)}, u32[]{:S(2)}) collective-permute-start(bf16[512,384]{1,0:T(8,128)(2,1)S(1)} %get-tuple-element.17), channel_id=1, source_target_pairs={{0,8},{1,9},{2,10},{3,11},{4,12},{5,13},{6,14},{7,15},{8,0},{9,1},... | collective-permute-start | bytes 1179656 | tf_op jit(solution)/shard_map/ppermute | solution.py:74
  136.0 6.4 %collective-permute-done.8 = bf16[512,384]{1,0:T(8,128)(2,1)S(1)} collective-permute-done((bf16[512,384]{1,0:T(8,128)(2,1)S(1)}, bf16[512,384]{1,0:T(8,128)(2,1)S(1)}, u32[]{:S(2)}, u32[]{:S(2)}) %collective-permute-start.8) | collective-permute-done | bytes 393248 | tf_op jit(solution)/shard_map/ppermute | solution.py:74
  142.8 3.2 %collective-permute-start.9 = (bf16[2,256,384]{2,1,0:T(8,128)(2,1)S(1)}, bf16[2,256,384]{2,1,0:T(8,128)(2,1)S(1)}, u32[]{:S(2)}, u32[]{:S(2)}) collective-permute-start(bf16[2,256,384]{2,1,0:T(8,128)(2,1)S(1)} %get-tuple-element.28), channel_id=1, source_target_pairs={{0,2},{1,3},{2,4},{3,5},{4,6},{5,7},{6,0},{7,1},{8,10},{9,11},{10,... | collective-permute-start | bytes 1179656 | tf_op jit(solution)/shard_map/ppermute | solution.py:56
  146.0 7.7 %collective-permute-done.12 = bf16[2,256,384]{2,1,0:T(8,128)(2,1)S(1)} collective-permute-done((bf16[2,256,384]{2,1,0:T(8,128)(2,1)S(1)}, bf16[2,256,384]{2,1,0:T(8,128)(2,1)S(1)}, u32[]{:S(2)}, u32[]{:S(2)}) %collective-permute-start.12) | collective-permute-done | bytes 393248 | tf_op jit(solution)/shard_map/ppermute | solution.py:56
  153.8 3.4 %collective-permute-start.10 = (bf16[2,256,384]{2,1,0:T(8,128)(2,1)S(1)}, bf16[2,256,384]{2,1,0:T(8,128)(2,1)}, u32[]{:S(2)}, u32[]{:S(2)}) collective-permute-start(bf16[2,256,384]{2,1,0:T(8,128)(2,1)S(1)} %collective-permute-done.9), channel_id=1, source_target_pairs={{0,2},{1,3},{2,4},{3,5},{4,6},{5,7},{6,0},{7,1},{8,10},{9,11},{10,... | collective-permute-start | bytes 1179656 | tf_op jit(solution)/shard_map/ppermute | solution.py:56
  157.2 8.7 %collective-permute-done.13 = bf16[2,256,384]{2,1,0:T(8,128)(2,1)S(1)} collective-permute-done((bf16[2,256,384]{2,1,0:T(8,128)(2,1)S(1)}, bf16[2,256,384]{2,1,0:T(8,128)(2,1)S(1)}, u32[]{:S(2)}, u32[]{:S(2)}) %collective-permute-start.13) | collective-permute-done | bytes 393248 | tf_op jit(solution)/shard_map/ppermute | solution.py:56
  166.5 3.3 %collective-permute-start.11 = (bf16[2,256,384]{2,1,0:T(8,128)(2,1)}, bf16[2,256,384]{2,1,0:T(8,128)(2,1)}, u32[]{:S(2)}, u32[]{:S(2)}) collective-permute-start(bf16[2,256,384]{2,1,0:T(8,128)(2,1)} %collective-permute-done.10), channel_id=1, source_target_pairs={{0,2},{1,3},{2,4},{3,5},{4,6},{5,7},{6,0},{7,1},{8,10},{9,11},{10,... | collective-permute-start | bytes 1179656 | tf_op jit(solution)/shard_map/ppermute | solution.py:56
  169.8 5.1 %collective-permute-done.14 = bf16[2,256,384]{2,1,0:T(8,128)(2,1)S(1)} collective-permute-done((bf16[2,256,384]{2,1,0:T(8,128)(2,1)S(1)}, bf16[2,256,384]{2,1,0:T(8,128)(2,1)S(1)}, u32[]{:S(2)}, u32[]{:S(2)}) %collective-permute-start.14) | collective-permute-done | bytes 393248 | tf_op jit(solution)/shard_map/ppermute | solution.py:56
  175.1 2.0 gather_fusion.6
  177.1 1.7 copy_select_fusion
  180.2 2.0 gather_fusion.5
  185.4 4.6 %fusion.12 = f32[512,384]{1,0:T(8,128)S(1)} fusion(bf16[2,4,2,512,512]{4,3,2,1,0:T(8,128)(2,1)} %bitcast.123, s32[]{:T(128)S(6)} %select_n.191, bf16[4,2,256,384]{3,2,0,1:T(8,128)(2,1)S(1)} %copy_select_fusion, bf16[4,2,256,384]{3,2,0,1:T(8,128)(2,1)S(1)} %copy_select_fusion.1), kind=kOutput, calls=%fused_computation.28 | convolution fusion | flops 1616904192 | bytes 8126468 | tf_op jit(solution)/shard_map/dot_general | solution.py:174
  192.3 5.6 %fusion.18 = f32[512,384]{1,0:T(8,128)S(1)} fusion(f32[512,384]{1,0:T(8,128)S(1)} %fusion.12, bf16[2,4,512,384]{3,2,1,0:T(8,128)(2,1)} %copy-done.4, bf16[2,4,2,512,512]{4,3,2,1,0:T(8,128)(2,1)} %bitcast.124, s32[]{:T(128)S(6)} %select_n.195), kind=kOutput, calls=%fused_computation.30 | convolution fusion | flops 1610809344 | bytes 8912900 | tf_op jit(solution)/shard_map/dot_general | solution.py:175
  198.0 19.3 %all_to_all.15 = f32[8,70,384]{2,1,0:T(8,128)S(1)} all-to-all(f32[8,70,384]{2,1,0:T(8,128)S(1)} %pad_maximum_fusion.2), channel_id=1, replica_groups=mesh['br'=8,'bus'=16] {'br'}, dimensions={0} | all-to-all | bytes 1720320 | tf_op jit(solution)/shard_map/all_to_all | solution.py:183
  218.6 3.5 %all-to-all-start.2 = ((f32[8,64,384]{2,1,0:T(8,128)}), f32[8,64,384]{2,1,0:T(8,128)S(1)}, u32[]{:S(2)}, u32[]{:S(2)}) async-start(f32[8,64,384]{2,1,0:T(8,128)} %broadcast_in_dim.129), calls=%async_computation.2 | async-start | bytes 1572864 | tf_op jit(solution)/shard_map/all_to_all | solution.py:188
  224.4 9.0 %all-to-all-done.2 = f32[8,64,384]{2,1,0:T(8,128)S(1)} async-done(((f32[8,64,384]{2,1,0:T(8,128)}), f32[8,64,384]{2,1,0:T(8,128)S(1)}, u32[]{:S(2)}, u32[]{:S(2)}) %all-to-all-start.2) | async-done | bytes 786464 | tf_op jit(solution)/shard_map/all_to_all | solution.py:188
  (141 shorter events, 36.3 us)
Async XLA Ops:
  0.7 7.5 %copy-start.13 = (bf16[8,1536]{1,0:T(8,128)(2,1)S(1)}, bf16[8,1536]{1,0:T(8,128)(2,1)}, u32[]{:S(2)}) copy-start(bf16[8,1536]{1,0:T(8,128)(2,1)} %param.29) | copy-start | bytes 73732
  0.7 7.6 %copy-start.14 = (s32[1024,3]{0,1:T(4,128)S(1)}, s32[1024,3]{0,1:T(4,128)}, u32[]{:S(2)}) copy-start(s32[1024,3]{0,1:T(4,128)} %param.27) | copy-start | bytes 36868
  0.7 16.1 %copy-start.3 = (f32[512,384]{1,0:T(8,128)S(1)}, f32[512,384]{1,0:T(8,128)}, u32[]{:S(2)}) copy-start(f32[512,384]{1,0:T(8,128)} %param.18) | copy-start | bytes 2359300
  0.7 16.2 %copy-start.11 = (f32[64,1024]{1,0:T(8,128)S(1)}, f32[64,1024]{1,0:T(8,128)}, u32[]{:S(2)}) copy-start(f32[64,1024]{1,0:T(8,128)} %param.24) | copy-start | bytes 786436
  8.2 11.1 %copy-start.15 = (s32[1024,3]{0,1:T(4,128)S(1)}, s32[1024,3]{0,1:T(4,128)}, u32[]{:S(2)}) copy-start(s32[1024,3]{0,1:T(4,128)} %param.28) | copy-start | bytes 36868
  8.2 12.9 %copy-start.16 = (s32[384]{0:T(512)S(1)}, s32[384]{0:T(512)}, u32[]{:S(2)}) copy-start(s32[384]{0:T(512)} %param.26) | copy-start | bytes 4612
  8.2 26.0 %collective-permute-start = (f32[2,4,512,384]{3,2,1,0:T(8,128)}, f32[2,4,512,384]{3,2,1,0:T(8,128)}, u32[]{:S(2)}, u32[]{:S(2)}) collective-permute-start(f32[2,4,512,384]{3,2,1,0:T(8,128)} %fusion.2), channel_id=1, source_target_pairs={{0,1},{1,0},{2,3},{3,2},{4,5},{5,4},{6,7},{7,6},{8,9},{9,8},{10,11... | collective-permute-start | bytes 18874376 | tf_op jit(solution)/shard_map/ppermute | solution.py:64
  8.6 23.0 %copy-start.12 = (s32[128,24]{1,0:T(8,128)}, s32[128,24]{1,0:T(8,128)S(1)}, u32[]{:S(2)}) copy-start(s32[128,24]{1,0:T(8,128)S(1)} %reshape.198) | copy-start | bytes 36868
  9.7 23.3 %all-to-all-start = ((bf16[8,6,512]{2,1,0:T(8,128)(2,1)}), bf16[8,6,512]{2,1,0:T(8,128)(2,1)S(1)}, u32[]{:S(2)}, u32[]{:S(2)}) async-start(bf16[8,6,512]{2,1,0:T(8,128)(2,1)} %copy.57), calls=%async_computation | async-start | bytes 131072 | tf_op jit(solution)/shard_map/all_to_all | solution.py:129
  42.3 20.0 %collective-permute-start.1 = (f32[2,256,384]{2,1,0:T(8,128)}, f32[2,256,384]{2,1,0:T(8,128)}, u32[]{:S(2)}, u32[]{:S(2)}) collective-permute-start(f32[2,256,384]{2,1,0:T(8,128)} %dynamic-slice_bitcast_fusion.1), channel_id=1, source_target_pairs={{0,2},{1,3},{2,4},{3,5},{4,6},{5,7},{6,0},{7,1},{8,10},{9,11},{10,... | collective-permute-start | bytes 2359304 | tf_op jit(solution)/shard_map/ppermute | solution.py:47
  43.7 22.6 %collective-permute-start.4 = (f32[2,256,384]{2,1,0:T(8,128)}, f32[2,256,384]{2,1,0:T(8,128)}, u32[]{:S(2)}, u32[]{:S(2)}) collective-permute-start(f32[2,256,384]{2,1,0:T(8,128)} %dynamic-slice_bitcast_fusion), channel_id=1, source_target_pairs={{0,6},{1,7},{2,0},{3,1},{4,2},{5,3},{6,4},{7,5},{8,14},{9,15},{10,... | collective-permute-start | bytes 2359304 | tf_op jit(solution)/shard_map/ppermute | solution.py:47
  64.6 19.1 %collective-permute-start.2 = (f32[2,256,384]{2,1,0:T(8,128)}, f32[2,256,384]{2,1,0:T(8,128)}, u32[]{:S(2)}, u32[]{:S(2)}) collective-permute-start(f32[2,256,384]{2,1,0:T(8,128)} %bitcast_add_fusion.5), channel_id=1, source_target_pairs={{0,2},{1,3},{2,4},{3,5},{4,6},{5,7},{6,0},{7,1},{8,10},{9,11},{10,... | collective-permute-start | bytes 2359304 | tf_op jit(solution)/shard_map/ppermute | solution.py:47
  68.4 20.6 %collective-permute-start.5 = (f32[2,256,384]{2,1,0:T(8,128)}, f32[2,256,384]{2,1,0:T(8,128)}, u32[]{:S(2)}, u32[]{:S(2)}) collective-permute-start(f32[2,256,384]{2,1,0:T(8,128)} %bitcast_add_fusion.2), channel_id=1, source_target_pairs={{0,6},{1,7},{2,0},{3,1},{4,2},{5,3},{6,4},{7,5},{8,14},{9,15},{10,... | collective-permute-start | bytes 2359304 | tf_op jit(solution)/shard_map/ppermute | solution.py:47
  86.1 18.7 %collective-permute-start.3 = (f32[2,256,384]{2,1,0:T(8,128)}, f32[2,256,384]{2,1,0:T(8,128)}, u32[]{:S(2)}, u32[]{:S(2)}) collective-permute-start(f32[2,256,384]{2,1,0:T(8,128)} %bitcast_add_fusion.4), channel_id=1, source_target_pairs={{0,2},{1,3},{2,4},{3,5},{4,6},{5,7},{6,0},{7,1},{8,10},{9,11},{10,... | collective-permute-start | bytes 2359304 | tf_op jit(solution)/shard_map/ppermute | solution.py:47
  91.1 19.2 %collective-permute-start.6 = (f32[2,256,384]{2,1,0:T(8,128)}, f32[2,256,384]{2,1,0:T(8,128)}, u32[]{:S(2)}, u32[]{:S(2)}) collective-permute-start(f32[2,256,384]{2,1,0:T(8,128)} %bitcast_add_fusion.1), channel_id=1, source_target_pairs={{0,6},{1,7},{2,0},{3,1},{4,2},{5,3},{6,4},{7,5},{8,14},{9,15},{10,... | collective-permute-start | bytes 2359304 | tf_op jit(solution)/shard_map/ppermute | solution.py:47
  91.1 24.2 %copy-start.17 = (f32[512]{0:T(512)S(1)}, f32[512]{0:T(512)}, u32[]{:S(2)}) copy-start(f32[512]{0:T(512)} %param.20) | copy-start | bytes 6148
  106.2 5.3 %copy-start.1 = (f32[2,256,384]{2,1,0:T(8,128)}, f32[2,256,384]{2,1,0:T(8,128)S(1)}, u32[]{:S(2)}) copy-start(f32[2,256,384]{2,1,0:T(8,128)S(1)} %bitcast_add_fusion.3) | copy-start | bytes 2359300
  112.4 18.3 %collective-permute-start.7 = (f32[512,384]{1,0:T(8,128)S(1)}, f32[512,384]{1,0:T(8,128)S(1)}, u32[]{:S(2)}, u32[]{:S(2)}) collective-permute-start(f32[512,384]{1,0:T(8,128)S(1)} %fusion.23), channel_id=1, source_target_pairs={{0,8},{1,9},{2,10},{3,11},{4,12},{5,13},{6,14},{7,15},{8,0},{9,1},... | collective-permute-start | bytes 2359304 | tf_op jit(solution)/shard_map/ppermute | solution.py:69
  133.1 9.3 %collective-permute-start.8 = (bf16[512,384]{1,0:T(8,128)(2,1)S(1)}, bf16[512,384]{1,0:T(8,128)(2,1)S(1)}, u32[]{:S(2)}, u32[]{:S(2)}) collective-permute-start(bf16[512,384]{1,0:T(8,128)(2,1)S(1)} %get-tuple-element.17), channel_id=1, source_target_pairs={{0,8},{1,9},{2,10},{3,11},{4,12},{5,13},{6,14},{7,15},{8,0},{9,1},... | collective-permute-start | bytes 1179656 | tf_op jit(solution)/shard_map/ppermute | solution.py:74
  142.7 11.0 %collective-permute-start.12 = (bf16[2,256,384]{2,1,0:T(8,128)(2,1)S(1)}, bf16[2,256,384]{2,1,0:T(8,128)(2,1)S(1)}, u32[]{:S(2)}, u32[]{:S(2)}) collective-permute-start(bf16[2,256,384]{2,1,0:T(8,128)(2,1)S(1)} %get-tuple-element.27), channel_id=1, source_target_pairs={{0,6},{1,7},{2,0},{3,1},{4,2},{5,3},{6,4},{7,5},{8,14},{9,15},{10,... | collective-permute-start | bytes 1179656 | tf_op jit(solution)/shard_map/ppermute | solution.py:56
  142.8 11.0 %collective-permute-start.9 = (bf16[2,256,384]{2,1,0:T(8,128)(2,1)S(1)}, bf16[2,256,384]{2,1,0:T(8,128)(2,1)S(1)}, u32[]{:S(2)}, u32[]{:S(2)}) collective-permute-start(bf16[2,256,384]{2,1,0:T(8,128)(2,1)S(1)} %get-tuple-element.28), channel_id=1, source_target_pairs={{0,2},{1,3},{2,4},{3,5},{4,6},{5,7},{6,0},{7,1},{8,10},{9,11},{10,... | collective-permute-start | bytes 1179656 | tf_op jit(solution)/shard_map/ppermute | solution.py:56
  153.7 12.1 %collective-permute-start.13 = (bf16[2,256,384]{2,1,0:T(8,128)(2,1)S(1)}, bf16[2,256,384]{2,1,0:T(8,128)(2,1)S(1)}, u32[]{:S(2)}, u32[]{:S(2)}) collective-permute-start(bf16[2,256,384]{2,1,0:T(8,128)(2,1)S(1)} %collective-permute-done.12), channel_id=1, source_target_pairs={{0,6},{1,7},{2,0},{3,1},{4,2},{5,3},{6,4},{7,5},{8,14},{9,15},{10,... | collective-permute-start | bytes 1179656 | tf_op jit(solution)/shard_map/ppermute | solution.py:56
  153.8 23.3 %copy-start.8 = (bf16[2,256,384]{2,1,0:T(8,128)(2,1)}, bf16[2,256,384]{2,1,0:T(8,128)(2,1)S(1)}, u32[]{:S(2)}) copy-start(bf16[2,256,384]{2,1,0:T(8,128)(2,1)S(1)} %collective-permute-done.9) | copy-start | bytes 1179652
  153.8 12.7 %collective-permute-start.10 = (bf16[2,256,384]{2,1,0:T(8,128)(2,1)S(1)}, bf16[2,256,384]{2,1,0:T(8,128)(2,1)}, u32[]{:S(2)}, u32[]{:S(2)}) collective-permute-start(bf16[2,256,384]{2,1,0:T(8,128)(2,1)S(1)} %collective-permute-done.9), channel_id=1, source_target_pairs={{0,2},{1,3},{2,4},{3,5},{4,6},{5,7},{6,0},{7,1},{8,10},{9,11},{10,... | collective-permute-start | bytes 1179656 | tf_op jit(solution)/shard_map/ppermute | solution.py:56
  165.9 9.0 %collective-permute-start.14 = (bf16[2,256,384]{2,1,0:T(8,128)(2,1)S(1)}, bf16[2,256,384]{2,1,0:T(8,128)(2,1)S(1)}, u32[]{:S(2)}, u32[]{:S(2)}) collective-permute-start(bf16[2,256,384]{2,1,0:T(8,128)(2,1)S(1)} %collective-permute-done.13), channel_id=1, source_target_pairs={{0,6},{1,7},{2,0},{3,1},{4,2},{5,3},{6,4},{7,5},{8,14},{9,15},{10,... | collective-permute-start | bytes 1179656 | tf_op jit(solution)/shard_map/ppermute | solution.py:56
  166.5 12.3 %collective-permute-start.11 = (bf16[2,256,384]{2,1,0:T(8,128)(2,1)}, bf16[2,256,384]{2,1,0:T(8,128)(2,1)}, u32[]{:S(2)}, u32[]{:S(2)}) collective-permute-start(bf16[2,256,384]{2,1,0:T(8,128)(2,1)} %collective-permute-done.10), channel_id=1, source_target_pairs={{0,2},{1,3},{2,4},{3,5},{4,6},{5,7},{6,0},{7,1},{8,10},{9,11},{10,... | collective-permute-start | bytes 1179656 | tf_op jit(solution)/shard_map/ppermute | solution.py:56
  184.2 5.9 %collective-permute-start.15 = (bf16[2,4,512,384]{3,2,1,0:T(8,128)(2,1)S(1)}, bf16[2,4,512,384]{3,2,1,0:T(8,128)(2,1)S(1)}, u32[]{:S(2)}, u32[]{:S(2)}) collective-permute-start(bf16[2,4,512,384]{3,2,1,0:T(8,128)(2,1)S(1)} %maximum_bitcast_fusion), channel_id=1, source_target_pairs={{0,1},{1,0},{2,3},{3,2},{4,5},{5,4},{6,7},{7,6},{8,9},{9,8},{10,11... | collective-permute-start | bytes 9437192 | tf_op jit(solution)/shard_map/ppermute | solution.py:80
  185.4 6.3 %copy-start.5 = (bf16[48,2,4,512]{3,0,2,1:T(8,128)(2,1)S(1)}, bf16[48,2,4,512]{3,0,2,1:T(8,128)(2,1)}, u32[]{:S(2)}) copy-start(bf16[48,2,4,512]{3,0,2,1:T(8,128)(2,1)} %get-tuple-element.14) | copy-start | bytes 1179652
  197.9 19.5 %copy-start.6 = (f32[64,384]{0,1:T(8,128)S(1)}, f32[64,384]{0,1:T(8,128)}, u32[]{:S(2)}) copy-start(f32[64,384]{0,1:T(8,128)} %broadcast_subtract_fusion) | copy-start | bytes 294916
  197.9 19.5 %copy-start.7 = (f32[64,384]{0,1:T(8,128)S(1)}, f32[64,384]{0,1:T(8,128)}, u32[]{:S(2)}) copy-start(f32[64,384]{0,1:T(8,128)} %multiply_bitcast_fusion) | copy-start | bytes 294916
  197.9 19.5 %copy-start.18 = (f32[64,1]{0,1:T(1,128)S(1)}, f32[64,1]{0,1:T(1,128)}, u32[]{:S(2)}) copy-start(f32[64,1]{0,1:T(1,128)} %negate_bitcast_fusion) | copy-start | bytes 772
  218.6 14.8 %all-to-all-start.2 = ((f32[8,64,384]{2,1,0:T(8,128)}), f32[8,64,384]{2,1,0:T(8,128)S(1)}, u32[]{:S(2)}, u32[]{:S(2)}) async-start(f32[8,64,384]{2,1,0:T(8,128)} %broadcast_in_dim.129), calls=%async_computation.2 | async-start | bytes 1572864 | tf_op jit(solution)/shard_map/all_to_all | solution.py:188
  (6 other events, 10.2 us)

commit v4 on v3

--- a/solution.py
+++ b/solution.py
@@ -39,12 +39,11 @@
     return lax.dynamic_index_in_dim(a, i, axis, keepdims=False)
 
 
-def ring_scatter(parts, xi, up):
-    step = 1 if up else -1
+def ring_scatter(contribs, up):
     perm = X_UP if up else X_DOWN
-    acc = pick(parts, (xi - step) % XR, 0)
-    for k in range(XR - 1):
-        acc = lax.ppermute(acc, "bus", perm) + pick(parts, (xi - step * (k + 2)) % XR, 0)
+    acc = contribs[0]
+    for more in contribs[1:]:
+        acc = lax.ppermute(acc, "bus", perm) + more
     return acc
 
 
@@ -59,13 +58,25 @@
     return jnp.take(stacked, order, axis=0)
 
 
-def bus_reduce_scatter(send, keep):
+def bus_reduce_scatter(flow_part):
     yh, xi, c = bus_place()
-    y = keep + lax.ppermute(send, "bus", CORE_SWAP)
-    half = y.shape[2] // 2
-    cw = ring_scatter(jnp.moveaxis(y[:, :, :half], 1, 0), xi, True)
-    ccw = ring_scatter(jnp.moveaxis(y[:, :, half:], 1, 0), xi, False)
+    first = [(xi - 1) % XR, (xi + 1) % XR]
+    second = [(xi + 2) % XR, xi]
+    summed = []
+    for group in (first, second):
+        send = jnp.stack([flow_part(x, False) for x in group])
+        keep = jnp.stack([flow_part(x, True) for x in group])
+        summed.append(keep + lax.ppermute(send, "bus", CORE_SWAP))
+    a, b = summed
+    half = a.shape[2] // 2
+    cw = ring_scatter([a[0, :, :half], b[0, :, :half], a[1, :, :half], b[1, :, :half]], True)
+    ccw = ring_scatter([a[1, :, half:], b[0, :, half:], a[0, :, half:], b[1, :, half:]], False)
     z = jnp.concatenate([cw, ccw], axis=1)
+    return z
+
+
+def bus_pair_sum(z):
+    yh, xi, c = bus_place()
     return pick(z, yh, 0) + lax.ppermute(pick(z, 1 - yh, 0), "bus", Y_SWAP)
 
 
@@ -119,20 +130,15 @@
     own_slot = slots_of(own_slab)
     slab_range = jnp.arange(slab_axis, dtype=jnp.int32)
     slot_range = jnp.arange(CAP, dtype=jnp.int32)
-    pick_out = (own_slab[None, None, :] == slab_range[:, None, None]) & (
-        own_slot[None, None, :] == slot_range[None, :, None]
-    )
-    weight_rows = rent_weight.reshape(entries, BLOCK)
-    outgoing_w = jnp.einsum(
-        "sce,er->scr", pick_out.astype(jnp.bfloat16), weight_rows, preferred_element_type=jnp.float32
-    ).astype(jnp.bfloat16)
-    arrived_w = lax.all_to_all(outgoing_w, "br", 0, 0, tiled=True)
-
+    column_weights = lax.all_gather(rent_weight.reshape(entries, BLOCK), "br", axis=0, tiled=False)
     sources = slab_range * bus_axis + column_index
     src_slab = jnp.take(slab_by_device, sources, axis=0)
     src_block = jnp.take(block_by_device, sources, axis=0)
     src_slot = slots_of(src_slab)
     pick_in = (src_slab[:, None, :] == slab_index) & (src_slot[:, None, :] == slot_range[None, :, None])
+    arrived_w = jnp.einsum(
+        "ice,ier->icr", pick_in.astype(jnp.bfloat16), column_weights, preferred_element_type=jnp.float32
+    ).astype(jnp.bfloat16)
     block_choice = jnp.sum(jnp.where(pick_in, src_block[:, None, :], 0), axis=2)
     block_hot = block_choice[:, :, None] == jnp.arange(blocks_per_slab, dtype=jnp.int32)[None, None, :]
     masked = jnp.where(block_hot[:, :, :, None], arrived_w[:, :, None, :], jnp.zeros((), jnp.bfloat16))
@@ -159,12 +165,16 @@
     by_place = shift_factors.reshape(YHI, XR, CORES, -1, shift_factors.shape[1])
     sf_keep = pick(by_place, core, 2)
     sf_send = pick(by_place, 1 - core, 2)
-    flow_send = jnp.dot(sf_send, inject_half, preferred_element_type=jnp.float32)
-    flow_keep = jnp.dot(sf_keep, inject_half, preferred_element_type=jnp.float32)
-    flow_keep, masked_keep, masked_send, upper, lower, base = lax.optimization_barrier(
-        (flow_keep, masked_keep, masked_send, upper, lower, base)
-    )
-    flow = bus_reduce_scatter(flow_send, flow_keep)
+
+    def flow_part(x, mine):
+        rows = pick(sf_keep if mine else sf_send, x, 1)
+        return jnp.dot(rows, inject_half, preferred_element_type=jnp.float32)
+
+    ring_out = bus_reduce_scatter(flow_part)
+    ring_out, masked_keep, masked_send, upper, lower, base = lax.optimization_barrier(
+        (ring_out, masked_keep, masked_send, upper, lower, base)
+    )
+    flow = bus_pair_sum(ring_out)
     moved = prices + step_dual * flow
     bound = step_dual * limits[:, None]
     new_prices = moved - jnp.clip(moved, -bound, bound)

time: 235 us -> 239 us (1.017)
  blocking collectives: 19.3 us -> 29.9 us
  local copies, waits for them, and re-layouts: 20.5 us -> 30.3 us
  other arithmetic: 32.4 us -> 24.5 us
  starting transfers between devices: 32.7 us -> 26.3 us
  waiting for transfers between devices: 102 us -> 96.4 us
    all_gather x0 -> x1, blocking collectives: none -> 29.9 us  [per_device(): lax.all_gather(rent_weight.reshape(entries, BLOCK), 'br', axis=0, tiled=F...]
    all_to_all x1 -> x0, blocking collectives: 19.3 us -> none  [per_device(): gathered = lax.all_to_all(outgoing, 'br', 0, 0, tiled=True)]
    ppermute x8 -> x9, waiting for transfers between devices: 65.1 us -> 45.9 us  [the longest x6 31 us: ring_scatter(): acc = lax.ppermute(acc, 'bus', perm) + more]
    all_to_all x1, waiting for transfers between devices: 0.01 us -> 12.6 us  [per_device(): gathered = lax.all_to_all(outgoing, 'br', 0, 0, tiled=True)]
    add x7 -> x5, other arithmetic: 16.7 us -> 4.96 us  [the longest x2 4.4 us: bus_reduce_scatter(): summed.append(keep + lax.ppermute(send, 'bus', CORE_SWAP))]
    ppermute x6, starting transfers between devices: 9.98 us -> 6.28 us  [ring_gather(): got.append(lax.ppermute(got[-1], 'bus', perm))]
    unnamed x45 -> x39, local copies, waits for them, and re-layouts: 6.33 us -> 9.65 us
    all_to_all x1, starting transfers between devices: 6.33 us -> 3.64 us  [per_device(): gathered = lax.all_to_all(outgoing, 'br', 0, 0, tiled=True)]
  transfers between devices with their start and end apart: 18 -> 19, of which waited for: 10 -> 14; matrix products, arithmetic and copies ran while one was open for 18% -> 23% of each run, Pallas kernels for 0% -> 0%
where the time goes in v4:
time: 239 us; the launch traced here: 236 us
  waiting for transfers between devices  96.4 us (40%)
  local copies, waits for them, and re-layouts  30.3 us (13%)
  blocking collectives  29.9 us (13%)
  matrix products  27.6 us (12%)
  starting transfers between devices  26.3 us (11%)
  other arithmetic  24.5 us (10%)
    ppermute x6, waiting for transfers between devices, ring_scatter(): acc = lax.ppermute(acc, 'bus', perm) + more  31 us
    all_gather x1, blocking collectives, per_device(): lax.all_gather(rent_weight.reshape(entries, BLOCK), 'br', axis=0, tiled=F...  29.9 us
    ppermute x6, waiting for transfers between devices, ring_gather(): got.append(lax.ppermute(got[-1], 'bus', perm))  21.8 us
    dot_general x8, matrix products, flow_part(): return jnp.dot(rows, inject_half, preferred_element_type=jnp.float32)  15.5 us
    ppermute x1, waiting for transfers between devices, bus_pair_sum(): return pick(z, yh, 0) + lax.ppermute(pick(z, 1 - yh, 0), 'bus', Y_SWAP)  14.9 us
    all_to_all x1, waiting for transfers between devices, per_device(): gathered = lax.all_to_all(outgoing, 'br', 0, 0, tiled=True)  12.6 us
    all_to_all x1, waiting for transfers between devices, per_device(): lax.all_to_all(jnp.broadcast_to(my_new[None], (slab_axis, share_rows, sce...  9.75 us
    unnamed x39, local copies, waits for them, and re-layouts  9.65 us
  transfers between devices with their start and end apart: 19, of which 14 were waited for; matrix products, arithmetic and copies ran while one was open for 23% of the time, Pallas kernels for 0%

profile of v4, /device:TPU:6, one launch (start us, length us, event | category | flops | bytes accessed | tf_op | source)
XLA Modules:
  0.0 236.3 jit_solution(15435948520035864374)
XLA Ops:
  1.9 1.9 convolution_bitcast_fusion.5
  3.8 1.9 convolution_bitcast_fusion.4
  6.1 1.9 convolution_bitcast_fusion.1
  8.1 1.9 convolution_bitcast_fusion
  23.0 1.9 copy.79
  25.7 2.2 gather_fusion
  27.9 29.9 %all_gather.3 = bf16[8,24,512]{2,1,0:T(8,128)(2,1)S(1)} all-gather(bf16[1,24,512]{2,1,0:T(8,128)(2,1)} %all_gather_reshape.3), channel_id=1, replica_groups=mesh['br'=8,'bus'=16] {'br'}, dimensions={0}, use_global_device_ids=true | all-gather | bytes 221184 | tf_op jit(solution)/shard_map/all_gather | solution.py:133
  62.0 1.9 convolution_bitcast_fusion.6
  65.4 2.2 maximum_add_fusion
  74.6 1.9 convolution_bitcast_fusion.3
  78.4 2.2 maximum_add_fusion.1
  80.6 6.4 %collective-permute-done.1 = f32[2,256,384]{2,1,0:T(8,128)S(1)} collective-permute-done((f32[2,256,384]{2,1,0:T(8,128)}, f32[2,256,384]{2,1,0:T(8,128)S(1)}, u32[]{:S(2)}, u32[]{:S(2)}) %collective-permute-start.1) | collective-permute-done | bytes 786464 | tf_op jit(solution)/shard_map/ppermute | solution.py:46
  92.0 13.2 %collective-permute-done.3 = f32[2,256,384]{2,1,0:T(8,128)S(1)} collective-permute-done((f32[2,256,384]{2,1,0:T(8,128)S(1)}, f32[2,256,384]{2,1,0:T(8,128)S(1)}, u32[]{:S(2)}, u32[]{:S(2)}) %collective-permute-start.3) | collective-permute-done | bytes 786464 | tf_op jit(solution)/shard_map/ppermute | solution.py:46
  110.3 7.7 %collective-permute-done.4 = f32[2,256,384]{2,1,0:T(8,128)S(1)} collective-permute-done((f32[2,256,384]{2,1,0:T(8,128)S(1)}, f32[2,256,384]{2,1,0:T(8,128)S(1)}, u32[]{:S(2)}, u32[]{:S(2)}) %collective-permute-start.4) | collective-permute-done | bytes 786464 | tf_op jit(solution)/shard_map/ppermute | solution.py:46
  118.0 2.3 collective-permute-done.7
  120.8 3.0 %collective-permute-start.8 = (f32[512,384]{1,0:T(8,128)S(1)}, f32[512,384]{1,0:T(8,128)}, u32[]{:S(2)}, u32[]{:S(2)}) collective-permute-start(f32[512,384]{1,0:T(8,128)S(1)} %dynamic-slice_bitcast_fusion), channel_id=1, source_target_pairs={{0,8},{1,9},{2,10},{3,11},{4,12},{5,13},{6,14},{7,15},{8,0},{9,1},... | collective-permute-start | bytes 2359304 | tf_op jit(solution)/shard_map/ppermute | solution.py:80
  123.8 14.9 %collective-permute-done.8 = f32[512,384]{1,0:T(8,128)} collective-permute-done((f32[512,384]{1,0:T(8,128)S(1)}, f32[512,384]{1,0:T(8,128)}, u32[]{:S(2)}, u32[]{:S(2)}) %collective-permute-start.8) | collective-permute-done | bytes 786464 | tf_op jit(solution)/shard_map/ppermute | solution.py:80
  138.7 2.2 fusion.67
  141.0 2.9 %collective-permute-start.9 = (bf16[512,384]{1,0:T(8,128)(2,1)S(1)}, bf16[512,384]{1,0:T(8,128)(2,1)S(1)}, u32[]{:S(2)}, u32[]{:S(2)}) collective-permute-start(bf16[512,384]{1,0:T(8,128)(2,1)S(1)} %get-tuple-element.17), channel_id=1, source_target_pairs={{0,8},{1,9},{2,10},{3,11},{4,12},{5,13},{6,14},{7,15},{8,0},{9,1},... | collective-permute-start | bytes 1179656 | tf_op jit(solution)/shard_map/ppermute | solution.py:85
  143.9 6.4 %collective-permute-done.9 = bf16[512,384]{1,0:T(8,128)(2,1)S(1)} collective-permute-done((bf16[512,384]{1,0:T(8,128)(2,1)S(1)}, bf16[512,384]{1,0:T(8,128)(2,1)S(1)}, u32[]{:S(2)}, u32[]{:S(2)}) %collective-permute-start.9) | collective-permute-done | bytes 393248 | tf_op jit(solution)/shard_map/ppermute | solution.py:85
  150.6 2.0 collective-permute-start.13
  152.6 9.8 %collective-permute-done.10 = bf16[2,256,384]{2,1,0:T(8,128)(2,1)S(1)} collective-permute-done((bf16[2,256,384]{2,1,0:T(8,128)(2,1)S(1)}, bf16[2,256,384]{2,1,0:T(8,128)(2,1)S(1)}, u32[]{:S(2)}, u32[]{:S(2)}) %collective-permute-start.10) | collective-permute-done | bytes 393248 | tf_op jit(solution)/shard_map/ppermute | solution.py:55
  162.4 2.1 collective-permute-start.14
  164.5 5.6 %collective-permute-done.11 = bf16[2,256,384]{2,1,0:T(8,128)(2,1)S(1)} collective-permute-done((bf16[2,256,384]{2,1,0:T(8,128)(2,1)S(1)}, bf16[2,256,384]{2,1,0:T(8,128)(2,1)S(1)}, u32[]{:S(2)}, u32[]{:S(2)}) %collective-permute-start.11) | collective-permute-done | bytes 393248 | tf_op jit(solution)/shard_map/ppermute | solution.py:55
  172.8 5.1 %collective-permute-done.12 = bf16[2,256,384]{2,1,0:T(8,128)(2,1)S(1)} collective-permute-done((bf16[2,256,384]{2,1,0:T(8,128)(2,1)S(1)}, bf16[2,256,384]{2,1,0:T(8,128)(2,1)S(1)}, u32[]{:S(2)}, u32[]{:S(2)}) %collective-permute-start.12) | collective-permute-done | bytes 393248 | tf_op jit(solution)/shard_map/ppermute | solution.py:55
  182.7 2.0 gather_fusion.6
  187.9 4.6 %fusion.6 = f32[512,384]{1,0:T(8,128)S(1)} fusion(bf16[2,4,2,512,512]{4,3,2,1,0:T(8,128)(2,1)} %bitcast.199, s32[]{:T(128)S(6)} %select_n.180, bf16[4,2,256,384]{3,2,0,1:T(8,128)(2,1)S(1)} %copy_select_fusion, bf16[4,2,256,384]{3,2,0,1:T(8,128)(2,1)S(1)} %copy_select_fusion.1), kind=kOutput, calls=%fused_computation.31 | convolution fusion | flops 1616904192 | bytes 8126468 | tf_op jit(solution)/shard_map/dot_general | solution.py:184
  194.8 5.6 %fusion.12 = f32[512,384]{1,0:T(8,128)S(1)} fusion(f32[512,384]{1,0:T(8,128)S(1)} %fusion.6, bf16[2,4,512,384]{3,2,1,0:T(8,128)(2,1)} %copy-done.2, bf16[2,4,2,512,512]{4,3,2,1,0:T(8,128)(2,1)} %bitcast.200, s32[]{:T(128)S(6)} %select_n.185), kind=kOutput, calls=%fused_computation.33 | convolution fusion | flops 1610809344 | bytes 8912900 | tf_op jit(solution)/shard_map/dot_general | solution.py:185
  201.4 3.6 %all-to-all-start = ((f32[8,70,384]{2,1,0:T(8,128)}), f32[8,70,384]{2,1,0:T(8,128)S(1)}, u32[]{:S(2)}, u32[]{:S(2)}) async-start(f32[8,70,384]{2,1,0:T(8,128)} %pad_maximum_fusion.5), calls=%async_computation | async-start | bytes 1769472 | tf_op jit(solution)/shard_map/all_to_all | solution.py:193
  205.7 12.6 %all-to-all-done = f32[8,70,384]{2,1,0:T(8,128)S(1)} async-done(((f32[8,70,384]{2,1,0:T(8,128)}), f32[8,70,384]{2,1,0:T(8,128)S(1)}, u32[]{:S(2)}, u32[]{:S(2)}) %all-to-all-start) | async-done | bytes 860192 | tf_op jit(solution)/shard_map/all_to_all | solution.py:193
  219.6 3.6 %all-to-all-start.1 = ((f32[8,64,384]{2,1,0:T(8,128)}), f32[8,64,384]{2,1,0:T(8,128)S(1)}, u32[]{:S(2)}, u32[]{:S(2)}) async-start(f32[8,64,384]{2,1,0:T(8,128)} %broadcast_in_dim.125), calls=%async_computation.1 | async-start | bytes 1572864 | tf_op jit(solution)/shard_map/all_to_all | solution.py:198
  225.7 9.8 %all-to-all-done.1 = f32[8,64,384]{2,1,0:T(8,128)S(1)} async-done(((f32[8,64,384]{2,1,0:T(8,128)}), f32[8,64,384]{2,1,0:T(8,128)S(1)}, u32[]{:S(2)}, u32[]{:S(2)}) %all-to-all-start.1) | async-done | bytes 786464 | tf_op jit(solution)/shard_map/all_to_all | solution.py:198
  (139 shorter events, 59.5 us)
Async XLA Ops:
  6.0 59.4 %collective-permute-start = (f32[2,2,512,384]{3,2,1,0:T(8,128)S(1)}, f32[2,2,512,384]{3,2,1,0:T(8,128)}, u32[]{:S(2)}, u32[]{:S(2)}) collective-permute-start(f32[2,2,512,384]{3,2,1,0:T(8,128)S(1)} %pad_maximum_fusion), channel_id=1, source_target_pairs={{0,1},{1,0},{2,3},{3,2},{4,5},{5,4},{6,7},{7,6},{8,9},{9,8},{10,11... | collective-permute-start | bytes 9437192 | tf_op jit(solution)/shard_map/ppermute | solution.py:69
  10.0 2.3 copy-start.14
  11.9 66.6 %collective-permute-start.2 = (f32[2,2,512,384]{3,2,1,0:T(8,128)}, f32[2,2,512,384]{3,2,1,0:T(8,128)}, u32[]{:S(2)}, u32[]{:S(2)}) collective-permute-start(f32[2,2,512,384]{3,2,1,0:T(8,128)} %pad_maximum_fusion.1), channel_id=1, source_target_pairs={{0,1},{1,0},{2,3},{3,2},{4,5},{5,4},{6,7},{7,6},{8,9},{9,8},{10,11... | collective-permute-start | bytes 9437192 | tf_op jit(solution)/shard_map/ppermute | solution.py:69
  57.8 6.1 %copy-start.15 = (s32[384]{0:T(512)S(1)}, s32[384]{0:T(512)}, u32[]{:S(2)}) copy-start(s32[384]{0:T(512)} %param.26) | copy-start | bytes 4612
  57.8 6.1 %copy-start.12 = (f32[64,64]{1,0:T(8,128)S(1)}, f32[64,64]{1,0:T(8,128)}, u32[]{:S(2)}) copy-start(f32[64,64]{1,0:T(8,128)} %gather_fusion) | copy-start | bytes 49156
  69.3 3.1 %copy-start.11 = (bf16[8,6,512]{2,1,0:T(8,128)(2,1)S(1)}, bf16[8,6,512]{2,1,0:T(8,128)(2,1)}, u32[]{:S(2)}) copy-start(bf16[8,6,512]{2,1,0:T(8,128)(2,1)} %convolution_convert_fusion) | copy-start | bytes 147460
  69.3 3.1 %copy-start.13 = (f32[64,64]{0,1:T(8,128)S(1)}, f32[64,64]{0,1:T(8,128)}, u32[]{:S(2)}) copy-start(f32[64,64]{0,1:T(8,128)} %select_bitcast_fusion) | copy-start | bytes 49156
  69.3 4.0 %copy-start.9 = (f32[64,384]{1,0:T(8,128)S(1)}, f32[64,384]{1,0:T(8,128)}, u32[]{:S(2)}) copy-start(f32[64,384]{1,0:T(8,128)} %constant_dynamic-slice_fusion.1) | copy-start | bytes 294916
  70.3 16.8 %collective-permute-start.1 = (f32[2,256,384]{2,1,0:T(8,128)}, f32[2,256,384]{2,1,0:T(8,128)S(1)}, u32[]{:S(2)}, u32[]{:S(2)}) collective-permute-start(f32[2,256,384]{2,1,0:T(8,128)} %get-tuple-element.29), channel_id=1, source_target_pairs={{0,2},{1,3},{2,4},{3,5},{4,6},{5,7},{6,0},{7,1},{8,10},{9,11},{10,... | collective-permute-start | bytes 2359304 | tf_op jit(solution)/shard_map/ppermute | solution.py:46
  70.8 17.0 %collective-permute-start.5 = (f32[2,256,384]{2,1,0:T(8,128)S(1)}, f32[2,256,384]{2,1,0:T(8,128)S(1)}, u32[]{:S(2)}, u32[]{:S(2)}) collective-permute-start(f32[2,256,384]{2,1,0:T(8,128)S(1)} %get-tuple-element.30), channel_id=1, source_target_pairs={{0,6},{1,7},{2,0},{3,1},{4,2},{5,3},{6,4},{7,5},{8,14},{9,15},{10,... | collective-permute-start | bytes 2359304 | tf_op jit(solution)/shard_map/ppermute | solution.py:46
  80.6 25.2 %copy-start.1 = (f32[2,2,512,384]{3,2,1,0:T(8,128)S(1)}, f32[2,2,512,384]{3,2,1,0:T(8,128)}, u32[]{:S(2)}) copy-start(f32[2,2,512,384]{3,2,1,0:T(8,128)} %copy-done) | copy-start | bytes 9437188
  87.9 17.3 %collective-permute-start.3 = (f32[2,256,384]{2,1,0:T(8,128)S(1)}, f32[2,256,384]{2,1,0:T(8,128)S(1)}, u32[]{:S(2)}, u32[]{:S(2)}) collective-permute-start(f32[2,256,384]{2,1,0:T(8,128)S(1)} %get-tuple-element.27), channel_id=1, source_target_pairs={{0,2},{1,3},{2,4},{3,5},{4,6},{5,7},{6,0},{7,1},{8,10},{9,11},{10,... | collective-permute-start | bytes 2359304 | tf_op jit(solution)/shard_map/ppermute | solution.py:46
  88.7 17.1 %collective-permute-start.6 = (f32[2,256,384]{2,1,0:T(8,128)S(1)}, f32[2,256,384]{2,1,0:T(8,128)S(1)}, u32[]{:S(2)}, u32[]{:S(2)}) collective-permute-start(f32[2,256,384]{2,1,0:T(8,128)S(1)} %get-tuple-element.28), channel_id=1, source_target_pairs={{0,6},{1,7},{2,0},{3,1},{4,2},{5,3},{6,4},{7,5},{8,14},{9,15},{10,... | collective-permute-start | bytes 2359304 | tf_op jit(solution)/shard_map/ppermute | solution.py:46
  106.0 12.1 %collective-permute-start.4 = (f32[2,256,384]{2,1,0:T(8,128)S(1)}, f32[2,256,384]{2,1,0:T(8,128)S(1)}, u32[]{:S(2)}, u32[]{:S(2)}) collective-permute-start(f32[2,256,384]{2,1,0:T(8,128)S(1)} %get-tuple-element.25), channel_id=1, source_target_pairs={{0,2},{1,3},{2,4},{3,5},{4,6},{5,7},{6,0},{7,1},{8,10},{9,11},{10,... | collective-permute-start | bytes 2359304 | tf_op jit(solution)/shard_map/ppermute | solution.py:46
  107.2 13.2 %collective-permute-start.7 = (f32[2,256,384]{2,1,0:T(8,128)S(1)}, f32[2,256,384]{2,1,0:T(8,128)S(1)}, u32[]{:S(2)}, u32[]{:S(2)}) collective-permute-start(f32[2,256,384]{2,1,0:T(8,128)S(1)} %get-tuple-element.26), channel_id=1, source_target_pairs={{0,6},{1,7},{2,0},{3,1},{4,2},{5,3},{6,4},{7,5},{8,14},{9,15},{10,... | collective-permute-start | bytes 2359304 | tf_op jit(solution)/shard_map/ppermute | solution.py:46
  120.6 3.2 %copy-start.16 = (f32[512]{0:T(512)S(1)}, f32[512]{0:T(512)}, u32[]{:S(2)}) copy-start(f32[512]{0:T(512)} %param.20) | copy-start | bytes 6148
  120.6 18.1 %copy-start.6 = (f32[512,384]{1,0:T(8,128)S(1)}, f32[512,384]{1,0:T(8,128)}, u32[]{:S(2)}) copy-start(f32[512,384]{1,0:T(8,128)} %param.19) | copy-start | bytes 2359300
  120.8 17.9 %collective-permute-start.8 = (f32[512,384]{1,0:T(8,128)S(1)}, f32[512,384]{1,0:T(8,128)}, u32[]{:S(2)}, u32[]{:S(2)}) collective-permute-start(f32[512,384]{1,0:T(8,128)S(1)} %dynamic-slice_bitcast_fusion), channel_id=1, source_target_pairs={{0,8},{1,9},{2,10},{3,11},{4,12},{5,13},{6,14},{7,15},{8,0},{9,1},... | collective-permute-start | bytes 2359304 | tf_op jit(solution)/shard_map/ppermute | solution.py:80
  141.0 9.3 %collective-permute-start.9 = (bf16[512,384]{1,0:T(8,128)(2,1)S(1)}, bf16[512,384]{1,0:T(8,128)(2,1)S(1)}, u32[]{:S(2)}, u32[]{:S(2)}) collective-permute-start(bf16[512,384]{1,0:T(8,128)(2,1)S(1)} %get-tuple-element.17), channel_id=1, source_target_pairs={{0,8},{1,9},{2,10},{3,11},{4,12},{5,13},{6,14},{7,15},{8,0},{9,1},... | collective-permute-start | bytes 1179656 | tf_op jit(solution)/shard_map/ppermute | solution.py:85
  150.5 11.9 %collective-permute-start.10 = (bf16[2,256,384]{2,1,0:T(8,128)(2,1)S(1)}, bf16[2,256,384]{2,1,0:T(8,128)(2,1)S(1)}, u32[]{:S(2)}, u32[]{:S(2)}) collective-permute-start(bf16[2,256,384]{2,1,0:T(8,128)(2,1)S(1)} %get-tuple-element.34), channel_id=1, source_target_pairs={{0,2},{1,3},{2,4},{3,5},{4,6},{5,7},{6,0},{7,1},{8,10},{9,11},{10,... | collective-permute-start | bytes 1179656 | tf_op jit(solution)/shard_map/ppermute | solution.py:55
  150.6 11.8 %collective-permute-start.13 = (bf16[2,256,384]{2,1,0:T(8,128)(2,1)S(1)}, bf16[2,256,384]{2,1,0:T(8,128)(2,1)S(1)}, u32[]{:S(2)}, u32[]{:S(2)}) collective-permute-start(bf16[2,256,384]{2,1,0:T(8,128)(2,1)S(1)} %get-tuple-element.33), channel_id=1, source_target_pairs={{0,6},{1,7},{2,0},{3,1},{4,2},{5,3},{6,4},{7,5},{8,14},{9,15},{10,... | collective-permute-start | bytes 1179656 | tf_op jit(solution)/shard_map/ppermute | solution.py:55
  162.4 7.8 %collective-permute-start.11 = (bf16[2,256,384]{2,1,0:T(8,128)(2,1)S(1)}, bf16[2,256,384]{2,1,0:T(8,128)(2,1)S(1)}, u32[]{:S(2)}, u32[]{:S(2)}) collective-permute-start(bf16[2,256,384]{2,1,0:T(8,128)(2,1)S(1)} %collective-permute-done.10), channel_id=1, source_target_pairs={{0,2},{1,3},{2,4},{3,5},{4,6},{5,7},{6,0},{7,1},{8,10},{9,11},{10,... | collective-permute-start | bytes 1179656 | tf_op jit(solution)/shard_map/ppermute | solution.py:55
  162.4 15.5 %copy-start.7 = (bf16[2,256,384]{2,1,0:T(8,128)(2,1)}, bf16[2,256,384]{2,1,0:T(8,128)(2,1)S(1)}, u32[]{:S(2)}) copy-start(bf16[2,256,384]{2,1,0:T(8,128)(2,1)S(1)} %collective-permute-done.13) | copy-start | bytes 1179652
  162.4 9.5 %collective-permute-start.14 = (bf16[2,256,384]{2,1,0:T(8,128)(2,1)S(1)}, bf16[2,256,384]{2,1,0:T(8,128)(2,1)}, u32[]{:S(2)}, u32[]{:S(2)}) collective-permute-start(bf16[2,256,384]{2,1,0:T(8,128)(2,1)S(1)} %collective-permute-done.13), channel_id=1, source_target_pairs={{0,6},{1,7},{2,0},{3,1},{4,2},{5,3},{6,4},{7,5},{8,14},{9,15},{10,... | collective-permute-start | bytes 1179656 | tf_op jit(solution)/shard_map/ppermute | solution.py:55
  170.2 7.8 %collective-permute-start.12 = (bf16[2,256,384]{2,1,0:T(8,128)(2,1)S(1)}, bf16[2,256,384]{2,1,0:T(8,128)(2,1)S(1)}, u32[]{:S(2)}, u32[]{:S(2)}) collective-permute-start(bf16[2,256,384]{2,1,0:T(8,128)(2,1)S(1)} %collective-permute-done.11), channel_id=1, source_target_pairs={{0,2},{1,3},{2,4},{3,5},{4,6},{5,7},{6,0},{7,1},{8,10},{9,11},{10,... | collective-permute-start | bytes 1179656 | tf_op jit(solution)/shard_map/ppermute | solution.py:55
  171.9 9.4 %collective-permute-start.15 = (bf16[2,256,384]{2,1,0:T(8,128)(2,1)}, bf16[2,256,384]{2,1,0:T(8,128)(2,1)}, u32[]{:S(2)}, u32[]{:S(2)}) collective-permute-start(bf16[2,256,384]{2,1,0:T(8,128)(2,1)} %collective-permute-done.14), channel_id=1, source_target_pairs={{0,6},{1,7},{2,0},{3,1},{4,2},{5,3},{6,4},{7,5},{8,14},{9,15},{10,... | collective-permute-start | bytes 1179656 | tf_op jit(solution)/shard_map/ppermute | solution.py:55
  186.6 5.9 %collective-permute-start.16 = (bf16[2,4,512,384]{3,2,1,0:T(8,128)(2,1)S(1)}, bf16[2,4,512,384]{3,2,1,0:T(8,128)(2,1)S(1)}, u32[]{:S(2)}, u32[]{:S(2)}) collective-permute-start(bf16[2,4,512,384]{3,2,1,0:T(8,128)(2,1)S(1)} %maximum_bitcast_fusion), channel_id=1, source_target_pairs={{0,1},{1,0},{2,3},{3,2},{4,5},{5,4},{6,7},{7,6},{8,9},{9,8},{10,11... | collective-permute-start | bytes 9437192 | tf_op jit(solution)/shard_map/ppermute | solution.py:91
  187.9 6.3 %copy-start.3 = (bf16[48,2,4,512]{3,0,2,1:T(8,128)(2,1)S(1)}, bf16[48,2,4,512]{3,0,2,1:T(8,128)(2,1)}, u32[]{:S(2)}) copy-start(bf16[48,2,4,512]{3,0,2,1:T(8,128)(2,1)} %get-tuple-element.14) | copy-start | bytes 1179652
  200.4 18.2 %copy-start.4 = (f32[64,384]{0,1:T(8,128)S(1)}, f32[64,384]{0,1:T(8,128)}, u32[]{:S(2)}) copy-start(f32[64,384]{0,1:T(8,128)} %broadcast_subtract_fusion) | copy-start | bytes 294916
  200.4 18.2 %copy-start.5 = (f32[64,384]{0,1:T(8,128)S(1)}, f32[64,384]{0,1:T(8,128)}, u32[]{:S(2)}) copy-start(f32[64,384]{0,1:T(8,128)} %multiply_bitcast_fusion) | copy-start | bytes 294916
  201.4 17.0 %all-to-all-start = ((f32[8,70,384]{2,1,0:T(8,128)}), f32[8,70,384]{2,1,0:T(8,128)S(1)}, u32[]{:S(2)}, u32[]{:S(2)}) async-start(f32[8,70,384]{2,1,0:T(8,128)} %pad_maximum_fusion.5), calls=%async_computation | async-start | bytes 1769472 | tf_op jit(solution)/shard_map/all_to_all | solution.py:193
  219.6 15.8 %all-to-all-start.1 = ((f32[8,64,384]{2,1,0:T(8,128)}), f32[8,64,384]{2,1,0:T(8,128)S(1)}, u32[]{:S(2)}, u32[]{:S(2)}) async-start(f32[8,64,384]{2,1,0:T(8,128)} %broadcast_in_dim.125), calls=%async_computation.1 | async-start | bytes 1572864 | tf_op jit(solution)/shard_map/all_to_all | solution.py:198
  (4 other events, 6.6 us)

commit v5 on v4

--- a/solution.py
+++ b/solution.py
@@ -50,12 +50,13 @@
 def ring_gather(own, xi, up):
     step = 1 if up else -1
     perm = X_UP if up else X_DOWN
-    got = [own]
-    for _ in range(XR - 1):
-        got.append(lax.ppermute(got[-1], "bus", perm))
-    stacked = jnp.stack(got)
-    order = (step * (xi - jnp.arange(XR, dtype=jnp.int32))) % XR
-    return jnp.take(stacked, order, axis=0)
+    out = jnp.zeros((XR,) + own.shape, own.dtype)
+    cur = own
+    for m in range(XR):
+        if m:
+            cur = lax.ppermute(cur, "bus", perm)
+        out = lax.dynamic_update_index_in_dim(out, cur, (xi - step * m) % XR, 0)
+    return out
 
 
 def bus_reduce_scatter(flow_part):
@@ -64,13 +65,14 @@
     second = [(xi + 2) % XR, xi]
     summed = []
     for group in (first, second):
-        send = jnp.stack([flow_part(x, False) for x in group])
-        keep = jnp.stack([flow_part(x, True) for x in group])
-        summed.append(keep + lax.ppermute(send, "bus", CORE_SWAP))
-    a, b = summed
-    half = a.shape[2] // 2
-    cw = ring_scatter([a[0, :, :half], b[0, :, :half], a[1, :, :half], b[1, :, :half]], True)
-    ccw = ring_scatter([a[1, :, half:], b[0, :, half:], a[0, :, half:], b[1, :, half:]], False)
+        send = tuple(flow_part(x, False) for x in group)
+        keep = tuple(flow_part(x, True) for x in group)
+        came = lax.ppermute(send, "bus", CORE_SWAP)
+        summed.append([k + r for k, r in zip(keep, came)])
+    (a0, a1), (b0, b1) = summed
+    half = a0.shape[1] // 2
+    cw = ring_scatter([a0[:, :half], b0[:, :half], a1[:, :half], b1[:, :half]], True)
+    ccw = ring_scatter([a1[:, half:], b0[:, half:], a0[:, half:], b1[:, half:]], False)
     z = jnp.concatenate([cw, ccw], axis=1)
     return z
 
@@ -123,6 +125,21 @@
     slab_rows = shift_factors.shape[0]
     blocks_per_slab = slab_rows // BLOCK
 
+    yh, xi, core = bus_place()
+    inject_half = injections.astype(jnp.bfloat16)
+    by_place = shift_factors.reshape(YHI, XR, CORES, -1, shift_factors.shape[1])
+    sf_keep = pick(by_place, core, 2)
+    sf_send = pick(by_place, 1 - core, 2)
+
+    def flow_part(x, mine):
+        rows = pick(sf_keep if mine else sf_send, x, 1)
+        return jnp.dot(rows, inject_half, preferred_element_type=jnp.float32)
+
+    ring_out = bus_reduce_scatter(flow_part)
+    inputs_after = (listed_slab, listed_block, rent_weight, irradiance_profile, plant_group, scenario_profile)
+    ring_out, inputs_after = lax.optimization_barrier((ring_out, inputs_after))
+    listed_slab, listed_block, rent_weight, irradiance_profile, plant_group, scenario_profile = inputs_after
+
     slab_by_device = listed_slab.reshape(-1, entries)
     block_by_device = listed_block.reshape(-1, entries)
     self_device = slab_index * bus_axis + column_index
@@ -130,19 +147,23 @@
     own_slot = slots_of(own_slab)
     slab_range = jnp.arange(slab_axis, dtype=jnp.int32)
     slot_range = jnp.arange(CAP, dtype=jnp.int32)
-    column_weights = lax.all_gather(rent_weight.reshape(entries, BLOCK), "br", axis=0, tiled=False)
+    pick_out = (own_slab[None, None, :] == slab_range[:, None, None]) & (
+        own_slot[None, None, :] == slot_range[None, :, None]
+    )
+    weight_rows = rent_weight.reshape(entries, BLOCK)
+    outgoing_w = jnp.einsum(
+        "sce,er->scr", pick_out.astype(jnp.bfloat16), weight_rows, preferred_element_type=jnp.float32
+    ).astype(jnp.bfloat16)
+    arrived_w = lax.all_to_all(outgoing_w, "br", 0, 0, tiled=True)
+
     sources = slab_range * bus_axis + column_index
     src_slab = jnp.take(slab_by_device, sources, axis=0)
     src_block = jnp.take(block_by_device, sources, axis=0)
     src_slot = slots_of(src_slab)
     pick_in = (src_slab[:, None, :] == slab_index) & (src_slot[:, None, :] == slot_range[None, :, None])
-    arrived_w = jnp.einsum(
-        "ice,ier->icr", pick_in.astype(jnp.bfloat16), column_weights, preferred_element_type=jnp.float32
-    ).astype(jnp.bfloat16)
     block_choice = jnp.sum(jnp.where(pick_in, src_block[:, None, :], 0), axis=2)
     block_hot = block_choice[:, :, None] == jnp.arange(blocks_per_slab, dtype=jnp.int32)[None, None, :]
     masked = jnp.where(block_hot[:, :, :, None], arrived_w[:, :, None, :], jnp.zeros((), jnp.bfloat16))
-    yh, xi, core = bus_place()
     masked = masked.reshape(slab_axis * CAP, YHI, XR, CORES, -1)
     masked_keep = pick(masked, core, 3)
     masked_send = pick(masked, 1 - core, 3)
@@ -161,19 +182,6 @@
     lower = -my_load[:, None]
     base = my_inj - step_primal * my_cost[:, None]
 
-    inject_half = injections.astype(jnp.bfloat16)
-    by_place = shift_factors.reshape(YHI, XR, CORES, -1, shift_factors.shape[1])
-    sf_keep = pick(by_place, core, 2)
-    sf_send = pick(by_place, 1 - core, 2)
-
-    def flow_part(x, mine):
-        rows = pick(sf_keep if mine else sf_send, x, 1)
-        return jnp.dot(rows, inject_half, preferred_element_type=jnp.float32)
-
-    ring_out = bus_reduce_scatter(flow_part)
-    ring_out, masked_keep, masked_send, upper, lower, base = lax.optimization_barrier(
-        (ring_out, masked_keep, masked_send, upper, lower, base)
-    )
     flow = bus_pair_sum(ring_out)
     moved = prices + step_dual * flow
     bound = step_dual * limits[:, None]

time: 239 us -> 261 us (1.092)
  waiting for transfers between devices: 96.4 us -> 149 us
  blocking collectives: 29.9 us -> 0 us
  local copies, waits for them, and re-layouts: 30.3 us -> 17.7 us
  starting transfers between devices: 26.3 us -> 34.9 us
  matrix products: 27.6 us -> 34.7 us
    ppermute x6, waiting for transfers between devices: 31 us -> 78.6 us  [ring_scatter(): acc = lax.ppermute(acc, 'bus', perm) + more]
    all_gather x1 -> x0, blocking collectives: 29.9 us -> none  [per_device(): lax.all_gather(rent_weight.reshape(entries, BLOCK), 'br', axis=0, tiled=F...]
    unnamed x39 -> x27, local copies, waits for them, and re-layouts: 9.65 us -> 0.95 us
    all_to_all x0 -> x1, starting transfers between devices: none -> 6.36 us  [per_device(): arrived_w = lax.all_to_all(outgoing_w, 'br', 0, 0, tiled=True)]
    ppermute x8 -> x10, waiting for transfers between devices: 21.8 us -> 27.7 us  [the longest x6 27.7 us: ring_gather(): cur = lax.ppermute(cur, 'bus', perm)]
    dot_general x8, matrix products: 15.5 us -> 20.6 us  [flow_part(): return jnp.dot(rows, inject_half, preferred_element_type=jnp.float32)]
    add x2 -> x0, other arithmetic: 4.4 us -> none  [bus_reduce_scatter(): summed.append(keep + lax.ppermute(send, 'bus', CORE_SWAP))]
    another operation x4 -> x0, other arithmetic: 3.64 us -> none  [the longest x2 2.04 us: bus_reduce_scatter(): send = jnp.stack([flow_part(x, False) for x in group])]
  transfers between devices with their start and end apart: 19 -> 22, of which waited for: 14 -> 15; matrix products, arithmetic and copies ran while one was open for 23% -> 18% of each run, Pallas kernels for 0% -> 0%
where the time goes in v5:
time: 261 us; the launch traced here: 259 us
  waiting for transfers between devices  149 us (57%)
  starting transfers between devices  34.9 us (13%)
  matrix products  34.7 us (13%)
  other arithmetic  22.1 us (8%)
  local copies, waits for them, and re-layouts  17.7 us (7%)
    ppermute x6, waiting for transfers between devices, ring_scatter(): acc = lax.ppermute(acc, 'bus', perm) + more  78.6 us
    ppermute x6, waiting for transfers between devices, ring_gather(): cur = lax.ppermute(cur, 'bus', perm)  27.7 us
    dot_general x8, matrix products, flow_part(): return jnp.dot(rows, inject_half, preferred_element_type=jnp.float32)  20.6 us
    ppermute x1, waiting for transfers between devices, bus_pair_sum(): return pick(z, yh, 0) + lax.ppermute(pick(z, 1 - yh, 0), 'bus', Y_SWAP)  14 us
    all_to_all x1, waiting for transfers between devices, per_device(): gathered = lax.all_to_all(outgoing, 'br', 0, 0, tiled=True)  11.6 us
    all_to_all x1, waiting for transfers between devices, per_device(): lax.all_to_all(jnp.broadcast_to(my_new[None], (slab_axis, share_rows, sce...  10.6 us
    all_to_all x1, starting transfers between devices, per_device(): arrived_w = lax.all_to_all(outgoing_w, 'br', 0, 0, tiled=True)  6.36 us
    ppermute x6, starting transfers between devices, ring_scatter(): acc = lax.ppermute(acc, 'bus', perm) + more  6.22 us
  transfers between devices with their start and end apart: 22, of which 15 were waited for; matrix products, arithmetic and copies ran while one was open for 18% of the time, Pallas kernels for 0%

profile of v5, /device:TPU:6, one launch (start us, length us, event | category | flops | bytes accessed | tf_op | source)
XLA Modules:
  0.0 259.3 jit_solution(14398259670318490712)
XLA Ops:
  3.9 3.1 %fusion.22 = f32[2,512,384]{2,1,0:T(8,128)} fusion(bf16[2,4,2,512,512]{4,3,2,1,0:T(8,128)(2,1)} %bitcast.165, s32[]{:T(128)S(6)} %select_n.213, s32[]{:T(128)S(6)} %select_n.210, bf16[512,384]{1,0:T(8,128)(2,1)S(1)} %convert_element_type.16), kind=kOutput, calls=%fused_computation.30 | convolution fusion | flops 402653184 | bytes 3014664 | tf_op jit(solution)/shard_map/dot_general | solution.py:136
  7.5 3.1 %fusion.19 = f32[2,512,384]{2,1,0:T(8,128)} fusion(bf16[2,4,2,512,512]{4,3,2,1,0:T(8,128)(2,1)} %bitcast.166, s32[]{:T(128)S(6)} %select_n.216, s32[]{:T(128)S(6)} %select_n.210, bf16[512,384]{1,0:T(8,128)(2,1)S(1)} %convert_element_type.16), kind=kOutput, calls=%fused_computation.27 | convolution fusion | flops 402653184 | bytes 3014664 | tf_op jit(solution)/shard_map/dot_general | solution.py:136
  13.1 2.4 convolution_add_fusion.2
  15.6 17.1 %collective-permute-done.1 = f32[2,256,384]{2,1,0:T(8,128)S(1)} collective-permute-done((f32[2,256,384]{2,1,0:T(8,128)S(1)}, f32[2,256,384]{2,1,0:T(8,128)S(1)}, u32[]{:S(2)}, u32[]{:S(2)}) %collective-permute-start.1) | collective-permute-done | bytes 786464 | tf_op jit(solution)/shard_map/ppermute | solution.py:46
  34.4 2.5 convolution_add_fusion.1
  36.9 15.0 %collective-permute-done.3 = f32[2,256,384]{2,1,0:T(8,128)S(1)} collective-permute-done((f32[2,256,384]{2,1,0:T(8,128)S(1)}, f32[2,256,384]{2,1,0:T(8,128)S(1)}, u32[]{:S(2)}, u32[]{:S(2)}) %collective-permute-start.3) | collective-permute-done | bytes 786464 | tf_op jit(solution)/shard_map/ppermute | solution.py:46
  54.0 3.1 %fusion.16 = f32[2,512,384]{2,1,0:T(8,128)} fusion(bf16[2,4,2,512,512]{4,3,2,1,0:T(8,128)(2,1)} %bitcast.170, s32[]{:T(128)S(6)} %select_n.218, s32[]{:T(128)S(6)} %select_n.210, bf16[512,384]{1,0:T(8,128)(2,1)S(1)} %convert_element_type.16), kind=kOutput, calls=%fused_computation.24 | convolution fusion | flops 402653184 | bytes 3014664 | tf_op jit(solution)/shard_map/dot_general | solution.py:136
  57.1 15.8 %collective-permute-done.7 = f32[2,256,384]{2,1,0:T(8,128)} collective-permute-done((f32[2,256,384]{2,1,0:T(8,128)}, f32[2,256,384]{2,1,0:T(8,128)}, u32[]{:S(2)}, u32[]{:S(2)}) %collective-permute-start.7) | collective-permute-done | bytes 786464 | tf_op jit(solution)/shard_map/ppermute | solution.py:46
  74.1 3.2 %collective-permute-start.5 = (f32[2,256,384]{2,1,0:T(8,128)}, f32[2,256,384]{2,1,0:T(8,128)S(1)}, u32[]{:S(2)}, u32[]{:S(2)}) collective-permute-start(f32[2,256,384]{2,1,0:T(8,128)} %get-tuple-element.26), channel_id=1, source_target_pairs={{0,2},{1,3},{2,4},{3,5},{4,6},{5,7},{6,0},{7,1},{8,10},{9,11},{10,... | collective-permute-start | bytes 2359304 | tf_op jit(solution)/shard_map/ppermute | solution.py:46
  77.4 15.3 %collective-permute-done.8 = f32[2,256,384]{2,1,0:T(8,128)S(1)} collective-permute-done((f32[2,256,384]{2,1,0:T(8,128)S(1)}, f32[2,256,384]{2,1,0:T(8,128)S(1)}, u32[]{:S(2)}, u32[]{:S(2)}) %collective-permute-start.8) | collective-permute-done | bytes 786464 | tf_op jit(solution)/shard_map/ppermute | solution.py:46
  93.6 2.5 convolution_add_fusion
  96.1 15.4 %collective-permute-done.9 = f32[2,256,384]{2,1,0:T(8,128)S(1)} collective-permute-done((f32[2,256,384]{2,1,0:T(8,128)}, f32[2,256,384]{2,1,0:T(8,128)S(1)}, u32[]{:S(2)}, u32[]{:S(2)}) %collective-permute-start.9) | collective-permute-done | bytes 786464 | tf_op jit(solution)/shard_map/ppermute | solution.py:46
  111.9 3.3 %collective-permute-start.10 = (f32[512,384]{1,0:T(8,128)S(1)}, f32[512,384]{1,0:T(8,128)}, u32[]{:S(2)}, u32[]{:S(2)}) collective-permute-start(f32[512,384]{1,0:T(8,128)S(1)} %dynamic-slice_bitcast_fusion), channel_id=1, source_target_pairs={{0,8},{1,9},{2,10},{3,11},{4,12},{5,13},{6,14},{7,15},{8,0},{9,1},... | collective-permute-start | bytes 2359304 | tf_op jit(solution)/shard_map/ppermute | solution.py:82
  115.2 14.0 %collective-permute-done.10 = f32[512,384]{1,0:T(8,128)} collective-permute-done((f32[512,384]{1,0:T(8,128)S(1)}, f32[512,384]{1,0:T(8,128)}, u32[]{:S(2)}, u32[]{:S(2)}) %collective-permute-start.10) | collective-permute-done | bytes 786464 | tf_op jit(solution)/shard_map/ppermute | solution.py:82
  129.2 2.2 fusion.69
  131.5 3.2 %collective-permute-start.11 = (bf16[512,384]{1,0:T(8,128)(2,1)S(1)}, bf16[512,384]{1,0:T(8,128)(2,1)S(1)}, u32[]{:S(2)}, u32[]{:S(2)}) collective-permute-start(bf16[512,384]{1,0:T(8,128)(2,1)S(1)} %get-tuple-element.20), channel_id=1, source_target_pairs={{0,8},{1,9},{2,10},{3,11},{4,12},{5,13},{6,14},{7,15},{8,0},{9,1},... | collective-permute-start | bytes 1179656 | tf_op jit(solution)/shard_map/ppermute | solution.py:87
  134.7 6.1 %collective-permute-done.11 = bf16[512,384]{1,0:T(8,128)(2,1)S(1)} collective-permute-done((bf16[512,384]{1,0:T(8,128)(2,1)S(1)}, bf16[512,384]{1,0:T(8,128)(2,1)S(1)}, u32[]{:S(2)}, u32[]{:S(2)}) %collective-permute-start.11) | collective-permute-done | bytes 393248 | tf_op jit(solution)/shard_map/ppermute | solution.py:87
  141.1 2.0 collective-permute-start.15
  143.5 9.3 %collective-permute-done.12 = bf16[2,256,384]{2,1,0:T(8,128)(2,1)S(1)} collective-permute-done((bf16[2,256,384]{2,1,0:T(8,128)(2,1)S(1)}, bf16[2,256,384]{2,1,0:T(8,128)(2,1)S(1)}, u32[]{:S(2)}, u32[]{:S(2)}) %collective-permute-start.12) | collective-permute-done | bytes 393248 | tf_op jit(solution)/shard_map/ppermute | solution.py:57
  155.1 8.8 %collective-permute-done.13 = bf16[2,256,384]{2,1,0:T(8,128)(2,1)S(1)} collective-permute-done((bf16[2,256,384]{2,1,0:T(8,128)(2,1)S(1)}, bf16[2,256,384]{2,1,0:T(8,128)(2,1)S(1)}, u32[]{:S(2)}, u32[]{:S(2)}) %collective-permute-start.13) | collective-permute-done | bytes 393248 | tf_op jit(solution)/shard_map/ppermute | solution.py:57
  163.8 2.2 collective-permute-start.14
  166.5 5.1 %collective-permute-done.14 = bf16[2,256,384]{2,1,0:T(8,128)(2,1)S(1)} collective-permute-done((bf16[2,256,384]{2,1,0:T(8,128)(2,1)S(1)}, bf16[2,256,384]{2,1,0:T(8,128)(2,1)S(1)}, u32[]{:S(2)}, u32[]{:S(2)}) %collective-permute-start.14) | collective-permute-done | bytes 393248 | tf_op jit(solution)/shard_map/ppermute | solution.py:57
  171.7 3.7 %collective-permute-done.17 = bf16[2,256,384]{2,1,0:T(8,128)(2,1)S(1)} collective-permute-done((bf16[2,256,384]{2,1,0:T(8,128)(2,1)S(1)}, bf16[2,256,384]{2,1,0:T(8,128)(2,1)S(1)}, u32[]{:S(2)}, u32[]{:S(2)}) %collective-permute-start.17) | collective-permute-done | bytes 393248 | tf_op jit(solution)/shard_map/ppermute | solution.py:57
  186.4 6.4 %all-to-all-start = ((bf16[8,6,512]{2,1,0:T(8,128)(2,1)}), bf16[8,6,512]{2,1,0:T(8,128)(2,1)S(1)}, u32[]{:S(2)}, u32[]{:S(2)}) async-start(bf16[8,6,512]{2,1,0:T(8,128)(2,1)} %copy.134), calls=%async_computation | async-start | bytes 131072 | tf_op jit(solution)/shard_map/all_to_all | solution.py:157
  205.6 5.5 %fusion.9 = f32[512,384]{1,0:T(8,128)S(1)} fusion(bf16[2,4,512,384]{3,2,1,0:T(8,128)(2,1)} %collective-permute-done.18, bf16[2,4,2,512,512]{4,3,2,1,0:T(8,128)(2,1)} %bitcast.172, s32[]{:T(128)S(6)} %select_n.209), kind=kOutput, calls=%fused_computation.18 | convolution fusion | flops 1610612736 | bytes 8126468 | tf_op jit(solution)/shard_map/dot_general | solution.py:193
  211.1 5.5 %fusion.12 = f32[512,384]{1,0:T(8,128)} fusion(f32[512,384]{1,0:T(8,128)S(1)} %fusion.9, bf16[2,4,2,512,512]{4,3,2,1,0:T(8,128)(2,1)} %bitcast.173, s32[]{:T(128)S(6)} %select_n.200, bf16[4,2,256,384]{3,2,0,1:T(8,128)(2,1)S(1)} %bitcast_dynamic-update-slice_fusion.7, bf16[4,2,256,384]{3,2,0,1:T(8,128)(2,1)S(1)} %bitcast_dynamic-update-slice_fusion.3), kind=kOutput, calls=%fused_computation.19 | convolution fusion | flops 1617100800 | bytes 8912900 | tf_op jit(solution)/shard_map/dot_general | solution.py:192
  216.6 2.5 convolution_bitcast_fusion
  219.7 2.1 pad_maximum_fusion.1
  221.8 5.7 %all-to-all-start.1 = ((f32[8,70,384]{2,1,0:T(8,128)}), f32[8,70,384]{2,1,0:T(8,128)S(1)}, u32[]{:S(2)}, u32[]{:S(2)}) async-start(f32[8,70,384]{2,1,0:T(8,128)} %pad_maximum_fusion.1), calls=%async_computation.1 | async-start | bytes 1769472 | tf_op jit(solution)/shard_map/all_to_all | solution.py:201
  229.0 11.6 %all-to-all-done.1 = f32[8,70,384]{2,1,0:T(8,128)S(1)} async-done(((f32[8,70,384]{2,1,0:T(8,128)}), f32[8,70,384]{2,1,0:T(8,128)S(1)}, u32[]{:S(2)}, u32[]{:S(2)}) %all-to-all-start.1) | async-done | bytes 860192 | tf_op jit(solution)/shard_map/all_to_all | solution.py:201
  242.6 3.6 %all-to-all-start.2 = ((f32[8,64,384]{2,1,0:T(8,128)}), f32[8,64,384]{2,1,0:T(8,128)S(1)}, u32[]{:S(2)}, u32[]{:S(2)}) async-start(f32[8,64,384]{2,1,0:T(8,128)} %broadcast_in_dim.153), calls=%async_computation.2 | async-start | bytes 1572864 | tf_op jit(solution)/shard_map/all_to_all | solution.py:206
  247.8 10.6 %all-to-all-done.2 = f32[8,64,384]{2,1,0:T(8,128)S(1)} async-done(((f32[8,64,384]{2,1,0:T(8,128)}), f32[8,64,384]{2,1,0:T(8,128)S(1)}, u32[]{:S(2)}, u32[]{:S(2)}) %all-to-all-start.2) | async-done | bytes 786464 | tf_op jit(solution)/shard_map/all_to_all | solution.py:206
  (130 shorter events, 46.2 us)
Async XLA Ops:
  3.8 6.9 %collective-permute-start = (f32[2,512,384]{2,1,0:T(8,128)S(1)}, f32[2,512,384]{2,1,0:T(8,128)S(1)}, u32[]{:S(2)}, u32[]{:S(2)}) collective-permute-start(f32[2,512,384]{2,1,0:T(8,128)S(1)} %fusion.25), channel_id=1, source_target_pairs={{0,1},{1,0},{2,3},{3,2},{4,5},{5,4},{6,7},{7,6},{8,9},{9,8},{10,11... | collective-permute-start | bytes 4718600 | tf_op jit(solution)/shard_map/ppermute | solution.py:70
  7.1 6.1 %collective-permute-start.2 = (f32[2,512,384]{2,1,0:T(8,128)}, f32[2,512,384]{2,1,0:T(8,128)}, u32[]{:S(2)}, u32[]{:S(2)}) collective-permute-start(f32[2,512,384]{2,1,0:T(8,128)} %fusion.22), channel_id=1, source_target_pairs={{0,1},{1,0},{2,3},{3,2},{4,5},{5,4},{6,7},{7,6},{8,9},{9,8},{10,11... | collective-permute-start | bytes 4718600 | tf_op jit(solution)/shard_map/ppermute | solution.py:70
  10.6 23.8 %collective-permute-start.4 = (f32[2,512,384]{2,1,0:T(8,128)}, f32[2,512,384]{2,1,0:T(8,128)}, u32[]{:S(2)}, u32[]{:S(2)}) collective-permute-start(f32[2,512,384]{2,1,0:T(8,128)} %fusion.19), channel_id=1, source_target_pairs={{0,1},{1,0},{2,3},{3,2},{4,5},{5,4},{6,7},{7,6},{8,9},{9,8},{10,11... | collective-permute-start | bytes 4718600 | tf_op jit(solution)/shard_map/ppermute | solution.py:70
  12.7 20.0 %collective-permute-start.1 = (f32[2,256,384]{2,1,0:T(8,128)S(1)}, f32[2,256,384]{2,1,0:T(8,128)S(1)}, u32[]{:S(2)}, u32[]{:S(2)}) collective-permute-start(f32[2,256,384]{2,1,0:T(8,128)S(1)} %slice.58), channel_id=1, source_target_pairs={{0,2},{1,3},{2,4},{3,5},{4,6},{5,7},{6,0},{7,1},{8,10},{9,11},{10,... | collective-permute-start | bytes 2359304 | tf_op jit(solution)/shard_map/ppermute | solution.py:46
  32.7 19.1 %collective-permute-start.3 = (f32[2,256,384]{2,1,0:T(8,128)S(1)}, f32[2,256,384]{2,1,0:T(8,128)S(1)}, u32[]{:S(2)}, u32[]{:S(2)}) collective-permute-start(f32[2,256,384]{2,1,0:T(8,128)S(1)} %slice_add_fusion.5), channel_id=1, source_target_pairs={{0,2},{1,3},{2,4},{3,5},{4,6},{5,7},{6,0},{7,1},{8,10},{9,11},{10,... | collective-permute-start | bytes 2359304 | tf_op jit(solution)/shard_map/ppermute | solution.py:46
  53.1 19.7 %collective-permute-start.7 = (f32[2,256,384]{2,1,0:T(8,128)}, f32[2,256,384]{2,1,0:T(8,128)}, u32[]{:S(2)}, u32[]{:S(2)}) collective-permute-start(f32[2,256,384]{2,1,0:T(8,128)} %get-tuple-element.27), channel_id=1, source_target_pairs={{0,6},{1,7},{2,0},{3,1},{4,2},{5,3},{6,4},{7,5},{8,14},{9,15},{10,... | collective-permute-start | bytes 2359304 | tf_op jit(solution)/shard_map/ppermute | solution.py:46
  57.1 36.6 %collective-permute-start.6 = (f32[2,512,384]{2,1,0:T(8,128)}, f32[2,512,384]{2,1,0:T(8,128)}, u32[]{:S(2)}, u32[]{:S(2)}) collective-permute-start(f32[2,512,384]{2,1,0:T(8,128)} %fusion.16), channel_id=1, source_target_pairs={{0,1},{1,0},{2,3},{3,2},{4,5},{5,4},{6,7},{7,6},{8,9},{9,8},{10,11... | collective-permute-start | bytes 4718600 | tf_op jit(solution)/shard_map/ppermute | solution.py:70
  74.0 18.6 %collective-permute-start.8 = (f32[2,256,384]{2,1,0:T(8,128)S(1)}, f32[2,256,384]{2,1,0:T(8,128)S(1)}, u32[]{:S(2)}, u32[]{:S(2)}) collective-permute-start(f32[2,256,384]{2,1,0:T(8,128)S(1)} %slice_add_fusion.2), channel_id=1, source_target_pairs={{0,6},{1,7},{2,0},{3,1},{4,2},{5,3},{6,4},{7,5},{8,14},{9,15},{10,... | collective-permute-start | bytes 2359304 | tf_op jit(solution)/shard_map/ppermute | solution.py:46
  74.1 22.0 %collective-permute-start.5 = (f32[2,256,384]{2,1,0:T(8,128)}, f32[2,256,384]{2,1,0:T(8,128)S(1)}, u32[]{:S(2)}, u32[]{:S(2)}) collective-permute-start(f32[2,256,384]{2,1,0:T(8,128)} %get-tuple-element.26), channel_id=1, source_target_pairs={{0,2},{1,3},{2,4},{3,5},{4,6},{5,7},{6,0},{7,1},{8,10},{9,11},{10,... | collective-permute-start | bytes 2359304 | tf_op jit(solution)/shard_map/ppermute | solution.py:46
  93.6 17.9 %collective-permute-start.9 = (f32[2,256,384]{2,1,0:T(8,128)}, f32[2,256,384]{2,1,0:T(8,128)S(1)}, u32[]{:S(2)}, u32[]{:S(2)}) collective-permute-start(f32[2,256,384]{2,1,0:T(8,128)} %slice_add_fusion.1), channel_id=1, source_target_pairs={{0,6},{1,7},{2,0},{3,1},{4,2},{5,3},{6,4},{7,5},{8,14},{9,15},{10,... | collective-permute-start | bytes 2359304 | tf_op jit(solution)/shard_map/ppermute | solution.py:46
  111.9 17.4 %copy-start = (f32[512,384]{1,0:T(8,128)S(1)}, f32[512,384]{1,0:T(8,128)}, u32[]{:S(2)}) copy-start(f32[512,384]{1,0:T(8,128)} %param.17) | copy-start | bytes 2359300
  111.9 17.3 %collective-permute-start.10 = (f32[512,384]{1,0:T(8,128)S(1)}, f32[512,384]{1,0:T(8,128)}, u32[]{:S(2)}, u32[]{:S(2)}) collective-permute-start(f32[512,384]{1,0:T(8,128)S(1)} %dynamic-slice_bitcast_fusion), channel_id=1, source_target_pairs={{0,8},{1,9},{2,10},{3,11},{4,12},{5,13},{6,14},{7,15},{8,0},{9,1},... | collective-permute-start | bytes 2359304 | tf_op jit(solution)/shard_map/ppermute | solution.py:82
  131.5 9.3 %collective-permute-start.11 = (bf16[512,384]{1,0:T(8,128)(2,1)S(1)}, bf16[512,384]{1,0:T(8,128)(2,1)S(1)}, u32[]{:S(2)}, u32[]{:S(2)}) collective-permute-start(bf16[512,384]{1,0:T(8,128)(2,1)S(1)} %get-tuple-element.20), channel_id=1, source_target_pairs={{0,8},{1,9},{2,10},{3,11},{4,12},{5,13},{6,14},{7,15},{8,0},{9,1},... | collective-permute-start | bytes 1179656 | tf_op jit(solution)/shard_map/ppermute | solution.py:87
  141.0 11.9 %collective-permute-start.12 = (bf16[2,256,384]{2,1,0:T(8,128)(2,1)S(1)}, bf16[2,256,384]{2,1,0:T(8,128)(2,1)S(1)}, u32[]{:S(2)}, u32[]{:S(2)}) collective-permute-start(bf16[2,256,384]{2,1,0:T(8,128)(2,1)S(1)} %get-tuple-element.28), channel_id=1, source_target_pairs={{0,2},{1,3},{2,4},{3,5},{4,6},{5,7},{6,0},{7,1},{8,10},{9,11},{10,... | collective-permute-start | bytes 1179656 | tf_op jit(solution)/shard_map/ppermute | solution.py:57
  141.1 12.2 %collective-permute-start.15 = (bf16[2,256,384]{2,1,0:T(8,128)(2,1)S(1)}, bf16[2,256,384]{2,1,0:T(8,128)(2,1)S(1)}, u32[]{:S(2)}, u32[]{:S(2)}) collective-permute-start(bf16[2,256,384]{2,1,0:T(8,128)(2,1)S(1)} %get-tuple-element.29), channel_id=1, source_target_pairs={{0,6},{1,7},{2,0},{3,1},{4,2},{5,3},{6,4},{7,5},{8,14},{9,15},{10,... | collective-permute-start | bytes 1179656 | tf_op jit(solution)/shard_map/ppermute | solution.py:57
  152.9 11.0 %collective-permute-start.13 = (bf16[2,256,384]{2,1,0:T(8,128)(2,1)S(1)}, bf16[2,256,384]{2,1,0:T(8,128)(2,1)S(1)}, u32[]{:S(2)}, u32[]{:S(2)}) collective-permute-start(bf16[2,256,384]{2,1,0:T(8,128)(2,1)S(1)} %collective-permute-done.12), channel_id=1, source_target_pairs={{0,2},{1,3},{2,4},{3,5},{4,6},{5,7},{6,0},{7,1},{8,10},{9,11},{10,... | collective-permute-start | bytes 1179656 | tf_op jit(solution)/shard_map/ppermute | solution.py:57
  153.3 13.1 %collective-permute-start.16 = (bf16[2,256,384]{2,1,0:T(8,128)(2,1)S(1)}, bf16[2,256,384]{2,1,0:T(8,128)(2,1)S(1)}, u32[]{:S(2)}, u32[]{:S(2)}) collective-permute-start(bf16[2,256,384]{2,1,0:T(8,128)(2,1)S(1)} %collective-permute-done.15), channel_id=1, source_target_pairs={{0,6},{1,7},{2,0},{3,1},{4,2},{5,3},{6,4},{7,5},{8,14},{9,15},{10,... | collective-permute-start | bytes 1179656 | tf_op jit(solution)/shard_map/ppermute | solution.py:57
  163.8 7.8 %collective-permute-start.14 = (bf16[2,256,384]{2,1,0:T(8,128)(2,1)S(1)}, bf16[2,256,384]{2,1,0:T(8,128)(2,1)S(1)}, u32[]{:S(2)}, u32[]{:S(2)}) collective-permute-start(bf16[2,256,384]{2,1,0:T(8,128)(2,1)S(1)} %collective-permute-done.13), channel_id=1, source_target_pairs={{0,2},{1,3},{2,4},{3,5},{4,6},{5,7},{6,0},{7,1},{8,10},{9,11},{10,... | collective-permute-start | bytes 1179656 | tf_op jit(solution)/shard_map/ppermute | solution.py:57
  166.4 9.0 %collective-permute-start.17 = (bf16[2,256,384]{2,1,0:T(8,128)(2,1)S(1)}, bf16[2,256,384]{2,1,0:T(8,128)(2,1)S(1)}, u32[]{:S(2)}, u32[]{:S(2)}) collective-permute-start(bf16[2,256,384]{2,1,0:T(8,128)(2,1)S(1)} %collective-permute-done.16), channel_id=1, source_target_pairs={{0,6},{1,7},{2,0},{3,1},{4,2},{5,3},{6,4},{7,5},{8,14},{9,15},{10,... | collective-permute-start | bytes 1179656 | tf_op jit(solution)/shard_map/ppermute | solution.py:57
  175.5 7.1 %copy-start.3 = (s32[1024,3]{0,1:T(4,128)S(1)}, s32[1024,3]{0,1:T(4,128)}, u32[]{:S(2)}) copy-start(s32[1024,3]{0,1:T(4,128)} %param.25) | copy-start | bytes 36868
  175.5 9.3 %copy-start.2 = (bf16[8,1536]{1,0:T(8,128)(2,1)S(1)}, bf16[8,1536]{1,0:T(8,128)(2,1)}, u32[]{:S(2)}) copy-start(bf16[8,1536]{1,0:T(8,128)(2,1)} %param.27) | copy-start | bytes 73732
  177.5 16.5 %copy-start.4 = (s32[1024,3]{0,1:T(4,128)S(1)}, s32[1024,3]{0,1:T(4,128)}, u32[]{:S(2)}) copy-start(s32[1024,3]{0,1:T(4,128)} %param.26) | copy-start | bytes 36868
  177.5 25.2 %copy-start.1 = (f32[64,1024]{1,0:T(8,128)S(1)}, f32[64,1024]{1,0:T(8,128)}, u32[]{:S(2)}) copy-start(f32[64,1024]{1,0:T(8,128)} %param.22) | copy-start | bytes 786436
  177.5 28.1 %collective-permute-start.18 = (bf16[2,4,512,384]{3,2,1,0:T(8,128)(2,1)}, bf16[2,4,512,384]{3,2,1,0:T(8,128)(2,1)}, u32[]{:S(2)}, u32[]{:S(2)}) collective-permute-start(bf16[2,4,512,384]{3,2,1,0:T(8,128)(2,1)} %maximum_bitcast_fusion), channel_id=1, source_target_pairs={{0,1},{1,0},{2,3},{3,2},{4,5},{5,4},{6,7},{7,6},{8,9},{9,8},{10,11... | collective-permute-start | bytes 9437192 | tf_op jit(solution)/shard_map/ppermute | solution.py:93
  186.4 19.0 %all-to-all-start = ((bf16[8,6,512]{2,1,0:T(8,128)(2,1)}), bf16[8,6,512]{2,1,0:T(8,128)(2,1)S(1)}, u32[]{:S(2)}, u32[]{:S(2)}) async-start(bf16[8,6,512]{2,1,0:T(8,128)(2,1)} %copy.134), calls=%async_computation | async-start | bytes 131072 | tf_op jit(solution)/shard_map/all_to_all | solution.py:157
  219.6 8.0 %copy-start.5 = (s32[384]{0:T(512)S(1)}, s32[384]{0:T(512)}, u32[]{:S(2)}) copy-start(s32[384]{0:T(512)} %param.24) | copy-start | bytes 4612
  221.8 18.8 %all-to-all-start.1 = ((f32[8,70,384]{2,1,0:T(8,128)}), f32[8,70,384]{2,1,0:T(8,128)S(1)}, u32[]{:S(2)}, u32[]{:S(2)}) async-start(f32[8,70,384]{2,1,0:T(8,128)} %pad_maximum_fusion.1), calls=%async_computation.1 | async-start | bytes 1769472 | tf_op jit(solution)/shard_map/all_to_all | solution.py:201
  227.5 13.2 %copy-start.6 = (f32[64]{0:T(128)S(1)}, f32[64]{0:T(128)}, u32[]{:S(2)}) copy-start(f32[64]{0:T(128)} %get-tuple-element.34) | copy-start | bytes 772
  227.5 13.2 %copy-start.7 = (f32[64]{0:T(128)S(1)}, f32[64]{0:T(128)}, u32[]{:S(2)}) copy-start(f32[64]{0:T(128)} %get-tuple-element.35) | copy-start | bytes 772
  227.5 13.2 %copy-start.12 = (f32[64]{0:T(128)S(1)}, f32[64]{0:T(128)}, u32[]{:S(2)}) copy-start(f32[64]{0:T(128)} %dynamic_slice.83) | copy-start | bytes 772
  240.7 5.7 %copy-start.11 = (s32[24]{0:T(128)S(1)}, s32[24]{0:T(128)}, u32[]{:S(2)}) copy-start(s32[24]{0:T(128)} %get-tuple-element.30) | copy-start | bytes 292
  242.6 15.8 %all-to-all-start.2 = ((f32[8,64,384]{2,1,0:T(8,128)}), f32[8,64,384]{2,1,0:T(8,128)S(1)}, u32[]{:S(2)}, u32[]{:S(2)}) async-start(f32[8,64,384]{2,1,0:T(8,128)} %broadcast_in_dim.153), calls=%async_computation.2 | async-start | bytes 1572864 | tf_op jit(solution)/shard_map/all_to_all | solution.py:206
  (3 other events, 9.8 us)

commit v6 on v4

--- a/solution.py
+++ b/solution.py
@@ -50,12 +50,13 @@
 def ring_gather(own, xi, up):
     step = 1 if up else -1
     perm = X_UP if up else X_DOWN
-    got = [own]
-    for _ in range(XR - 1):
-        got.append(lax.ppermute(got[-1], "bus", perm))
-    stacked = jnp.stack(got)
-    order = (step * (xi - jnp.arange(XR, dtype=jnp.int32))) % XR
-    return jnp.take(stacked, order, axis=0)
+    out = jnp.zeros((XR,) + own.shape, own.dtype)
+    cur = own
+    for m in range(XR):
+        if m:
+            cur = lax.ppermute(cur, "bus", perm)
+        out = lax.dynamic_update_index_in_dim(out, cur, (xi - step * m) % XR, 0)
+    return out
 
 
 def bus_reduce_scatter(flow_part):
@@ -130,15 +131,19 @@
     own_slot = slots_of(own_slab)
     slab_range = jnp.arange(slab_axis, dtype=jnp.int32)
     slot_range = jnp.arange(CAP, dtype=jnp.int32)
-    column_weights = lax.all_gather(rent_weight.reshape(entries, BLOCK), "br", axis=0, tiled=False)
+    pick_out = (own_slab[None, None, :] == slab_range[:, None, None]) & (
+        own_slot[None, None, :] == slot_range[None, :, None]
+    )
+    weight_rows = rent_weight.reshape(entries, BLOCK)
+    outgoing_w = jnp.einsum(
+        "sce,er->scr", pick_out.astype(jnp.bfloat16), weight_rows, preferred_element_type=jnp.float32
+    ).astype(jnp.bfloat16)
+    arrived_w = lax.all_to_all(outgoing_w, "br", 0, 0, tiled=True)
     sources = slab_range * bus_axis + column_index
     src_slab = jnp.take(slab_by_device, sources, axis=0)
     src_block = jnp.take(block_by_device, sources, axis=0)
     src_slot = slots_of(src_slab)
     pick_in = (src_slab[:, None, :] == slab_index) & (src_slot[:, None, :] == slot_range[None, :, None])
-    arrived_w = jnp.einsum(
-        "ice,ier->icr", pick_in.astype(jnp.bfloat16), column_weights, preferred_element_type=jnp.float32
-    ).astype(jnp.bfloat16)
     block_choice = jnp.sum(jnp.where(pick_in, src_block[:, None, :], 0), axis=2)
     block_hot = block_choice[:, :, None] == jnp.arange(blocks_per_slab, dtype=jnp.int32)[None, None, :]
     masked = jnp.where(block_hot[:, :, :, None], arrived_w[:, :, None, :], jnp.zeros((), jnp.bfloat16))

time: 239 us -> 215 us (0.90)
  local copies, waits for them, and re-layouts: 30.3 us -> 13.3 us
  blocking collectives: 29.9 us -> 19.3 us
  waiting for transfers between devices: 96.4 us -> 107 us
  matrix products: 27.6 us -> 22.7 us
    all_gather x1 -> x0, blocking collectives: 29.9 us -> none  [per_device(): lax.all_gather(rent_weight.reshape(entries, BLOCK), 'br', axis=0, tiled=F...]
    all_to_all x0 -> x1, blocking collectives: none -> 19.3 us  [per_device(): gathered = lax.all_to_all(outgoing, 'br', 0, 0, tiled=True)]
    all_to_all x1, waiting for transfers between devices: 12.6 us -> 0.01 us  [per_device(): arrived_w = lax.all_to_all(outgoing_w, 'br', 0, 0, tiled=True)]
    ppermute x6, waiting for transfers between devices: 31 us -> 43.4 us  [ring_scatter(): acc = lax.ppermute(acc, 'bus', perm) + more]
    unnamed x39 -> x35, local copies, waits for them, and re-layouts: 9.65 us -> 2.48 us
    ppermute x1, waiting for transfers between devices: 0.01 us -> 5.65 us  [bus_all_gather(): return (quad, lax.ppermute(quad, 'bus', CORE_SWAP))]
    ppermute x6, waiting for transfers between devices: 21.8 us -> 27 us  [ring_gather(): cur = lax.ppermute(cur, 'bus', perm)]
    add x3, other arithmetic: 0.56 us -> 4.35 us  [ring_scatter(): acc = lax.ppermute(acc, 'bus', perm) + more]
  transfers between devices with their start and end apart: 19 -> 19, of which waited for: 14 -> 16; matrix products, arithmetic and copies ran while one was open for 23% -> 18% of each run, Pallas kernels for 0% -> 0%
where the time goes in v6:
time: 215 us; the launch traced here: 214 us
  waiting for transfers between devices  107 us (50%)
  starting transfers between devices  27.5 us (13%)
  other arithmetic  23.5 us (11%)
  matrix products  22.7 us (11%)
  blocking collectives  19.3 us (9%)
  local copies, waits for them, and re-layouts  13.3 us (6%)
    ppermute x6, waiting for transfers between devices, ring_scatter(): acc = lax.ppermute(acc, 'bus', perm) + more  43.4 us
    ppermute x6, waiting for transfers between devices, ring_gather(): cur = lax.ppermute(cur, 'bus', perm)  27 us
    all_to_all x1, blocking collectives, per_device(): gathered = lax.all_to_all(outgoing, 'br', 0, 0, tiled=True)  19.3 us
    dot_general x8, matrix products, flow_part(): return jnp.dot(rows, inject_half, preferred_element_type=jnp.float32)  16.6 us
    ppermute x1, waiting for transfers between devices, bus_pair_sum(): return pick(z, yh, 0) + lax.ppermute(pick(z, 1 - yh, 0), 'bus', Y_SWAP)  15.3 us
    all_to_all x1, waiting for transfers between devices, per_device(): lax.all_to_all(jnp.broadcast_to(my_new[None], (slab_axis, share_rows, sce...  8.98 us
    ppermute x1, waiting for transfers between devices, bus_all_gather(): other = lax.ppermute(p, 'bus', Y_SWAP)  6.39 us
    all_to_all x1, starting transfers between devices, per_device(): arrived_w = lax.all_to_all(outgoing_w, 'br', 0, 0, tiled=True)  6.33 us
  transfers between devices with their start and end apart: 19, of which 16 were waited for; matrix products, arithmetic and copies ran while one was open for 18% of the time, Pallas kernels for 0%

profile of v6, /device:TPU:6, one launch (start us, length us, event | category | flops | bytes accessed | tf_op | source)
XLA Modules:
  0.0 214.3 jit_solution(12648061427583364524)
XLA Ops:
  1.9 1.9 convolution_bitcast_fusion.5
  3.9 1.9 convolution_bitcast_fusion.4
  5.8 1.9 pad_maximum_fusion
  7.7 1.9 convolution_bitcast_fusion.1
  9.6 1.9 convolution_bitcast_fusion
  15.5 6.3 %all-to-all-start = ((bf16[8,6,512]{2,1,0:T(8,128)(2,1)}), bf16[8,6,512]{2,1,0:T(8,128)(2,1)S(1)}, u32[]{:S(2)}, u32[]{:S(2)}) async-start(bf16[8,6,512]{2,1,0:T(8,128)(2,1)} %copy.99), calls=%async_computation | async-start | bytes 131072 | tf_op jit(solution)/shard_map/all_to_all | solution.py:141
  26.7 3.1 %convolution_bitcast_fusion.3 = f32[1,2,512,384]{3,2,1,0:T(8,128)} fusion(bf16[2,4,2,512,512]{4,3,2,1,0:T(8,128)(2,1)} %bitcast.215, s32[]{:T(128)S(6)} %select_n.213, s32[]{:T(128)S(6)} %select_n.205, bf16[512,384]{1,0:T(8,128)(2,1)S(1)} %convert_element_type.16), kind=kOutput, calls=%fused_computation.20 | convolution fusion | flops 402653184 | bytes 3014664 | tf_op jit(solution)/shard_map/dot_general | solution.py:176
  29.8 1.9 convolution_bitcast_fusion.7
  31.7 1.9 convolution_bitcast_fusion.6
  33.7 2.2 %maximum_add_fusion = f32[2,2,512,384]{3,2,1,0:T(8,128)S(1)} fusion(f32[2,2,512,384]{3,2,1,0:T(8,128)} %collective-permute-done, f32[1,2,512,384]{3,2,1,0:T(8,128)S(1)} %convolution_bitcast_fusion.6, f32[1,2,512,384]{3,2,1,0:T(8,128)S(1)} %convolution_bitcast_fusion.7), kind=kLoop, calls=%fused_computation.11 | loop fusion | flops 1572864 | bytes 9437184 | tf_op jit(solution)/shard_map/add | solution.py:70
  40.3 1.9 convolution_bitcast_fusion.2
  42.2 2.7 %maximum_add_fusion.1 = f32[2,2,512,384]{3,2,1,0:T(8,128)S(1)} fusion(f32[2,2,512,384]{3,2,1,0:T(8,128)} %collective-permute-done.2, f32[1,2,512,384]{3,2,1,0:T(8,128)S(1)} %convolution_bitcast_fusion.2, f32[1,2,512,384]{3,2,1,0:T(8,128)} %convolution_bitcast_fusion.3), kind=kLoop, calls=%fused_computation.13 | loop fusion | flops 1572864 | bytes 9437184 | tf_op jit(solution)/shard_map/add | solution.py:70
  44.9 11.8 %collective-permute-done.1 = f32[2,256,384]{2,1,0:T(8,128)} collective-permute-done((f32[2,256,384]{2,1,0:T(8,128)}, f32[2,256,384]{2,1,0:T(8,128)}, u32[]{:S(2)}, u32[]{:S(2)}) %collective-permute-start.1) | collective-permute-done | bytes 786464 | tf_op jit(solution)/shard_map/ppermute | solution.py:46
  56.8 2.0 collective-permute-done.5
  60.4 2.0 collective-permute-start.6
  63.9 14.8 %collective-permute-done.3 = f32[2,256,384]{2,1,0:T(8,128)S(1)} collective-permute-done((f32[2,256,384]{2,1,0:T(8,128)S(1)}, f32[2,256,384]{2,1,0:T(8,128)S(1)}, u32[]{:S(2)}, u32[]{:S(2)}) %collective-permute-start.3) | collective-permute-done | bytes 786464 | tf_op jit(solution)/shard_map/ppermute | solution.py:46
  87.1 12.0 %collective-permute-done.4 = f32[2,256,384]{2,1,0:T(8,128)} collective-permute-done((f32[2,256,384]{2,1,0:T(8,128)}, f32[2,256,384]{2,1,0:T(8,128)}, u32[]{:S(2)}, u32[]{:S(2)}) %collective-permute-start.4) | collective-permute-done | bytes 786464 | tf_op jit(solution)/shard_map/ppermute | solution.py:46
  102.2 3.0 %collective-permute-start.8 = (f32[512,384]{1,0:T(8,128)S(1)}, f32[512,384]{1,0:T(8,128)}, u32[]{:S(2)}, u32[]{:S(2)}) collective-permute-start(f32[512,384]{1,0:T(8,128)S(1)} %dynamic-slice_bitcast_fusion), channel_id=1, source_target_pairs={{0,8},{1,9},{2,10},{3,11},{4,12},{5,13},{6,14},{7,15},{8,0},{9,1},... | collective-permute-start | bytes 2359304 | tf_op jit(solution)/shard_map/ppermute | solution.py:81
  105.2 15.3 %collective-permute-done.8 = f32[512,384]{1,0:T(8,128)} collective-permute-done((f32[512,384]{1,0:T(8,128)S(1)}, f32[512,384]{1,0:T(8,128)}, u32[]{:S(2)}, u32[]{:S(2)}) %collective-permute-start.8) | collective-permute-done | bytes 786464 | tf_op jit(solution)/shard_map/ppermute | solution.py:81
  120.5 2.2 %fusion.65 = (bf16[512,384]{1,0:T(8,128)(2,1)S(1)}, f32[512,384]{1,0:T(8,128)}) fusion(f32[512]{0:T(512)S(1)} %get-tuple-element.37, f32[512]{0:T(512)S(1)} %get-tuple-element.36, f32[512,384]{1,0:T(8,128)S(1)} %copy-done.4, f32[512,384]{1,0:T(8,128)} %collective-permute-done.8, f32[2,512,384]{2,1,0:T(8,128)S(1)} %pad_maximum_fusion.2, s32[]{:T(128)S(6)} %select_n.226), kind=kLoop, calls=%fused_computation.143 | loop fusion | flops 1376256 | bytes 3543044 | tf_op jit(solution)/shard_map/convert_element_type | solution.py:186
  122.8 2.9 %collective-permute-start.9 = (bf16[512,384]{1,0:T(8,128)(2,1)S(1)}, bf16[512,384]{1,0:T(8,128)(2,1)S(1)}, u32[]{:S(2)}, u32[]{:S(2)}) collective-permute-start(bf16[512,384]{1,0:T(8,128)(2,1)S(1)} %get-tuple-element.16), channel_id=1, source_target_pairs={{0,8},{1,9},{2,10},{3,11},{4,12},{5,13},{6,14},{7,15},{8,0},{9,1},... | collective-permute-start | bytes 1179656 | tf_op jit(solution)/shard_map/ppermute | solution.py:86
  125.6 6.4 %collective-permute-done.9 = bf16[512,384]{1,0:T(8,128)(2,1)S(1)} collective-permute-done((bf16[512,384]{1,0:T(8,128)(2,1)S(1)}, bf16[512,384]{1,0:T(8,128)(2,1)S(1)}, u32[]{:S(2)}, u32[]{:S(2)}) %collective-permute-start.9) | collective-permute-done | bytes 393248 | tf_op jit(solution)/shard_map/ppermute | solution.py:86
  134.8 8.7 %collective-permute-done.10 = bf16[2,256,384]{2,1,0:T(8,128)(2,1)S(1)} collective-permute-done((bf16[2,256,384]{2,1,0:T(8,128)(2,1)S(1)}, bf16[2,256,384]{2,1,0:T(8,128)(2,1)S(1)}, u32[]{:S(2)}, u32[]{:S(2)}) %collective-permute-start.10) | collective-permute-done | bytes 393248 | tf_op jit(solution)/shard_map/ppermute | solution.py:57
  145.7 9.5 %collective-permute-done.11 = bf16[2,256,384]{2,1,0:T(8,128)(2,1)S(1)} collective-permute-done((bf16[2,256,384]{2,1,0:T(8,128)(2,1)S(1)}, bf16[2,256,384]{2,1,0:T(8,128)(2,1)S(1)}, u32[]{:S(2)}, u32[]{:S(2)}) %collective-permute-start.11) | collective-permute-done | bytes 393248 | tf_op jit(solution)/shard_map/ppermute | solution.py:57
  157.4 5.6 %collective-permute-done.12 = bf16[2,256,384]{2,1,0:T(8,128)(2,1)S(1)} collective-permute-done((bf16[2,256,384]{2,1,0:T(8,128)(2,1)S(1)}, bf16[2,256,384]{2,1,0:T(8,128)(2,1)S(1)}, u32[]{:S(2)}, u32[]{:S(2)}) %collective-permute-start.12) | collective-permute-done | bytes 393248 | tf_op jit(solution)/shard_map/ppermute | solution.py:57
  163.1 2.3 %collective-permute-done.15 = bf16[2,256,384]{2,1,0:T(8,128)(2,1)S(1)} collective-permute-done((bf16[2,256,384]{2,1,0:T(8,128)(2,1)S(1)}, bf16[2,256,384]{2,1,0:T(8,128)(2,1)S(1)}, u32[]{:S(2)}, u32[]{:S(2)}) %collective-permute-start.15) | collective-permute-done | bytes 393248 | tf_op jit(solution)/shard_map/ppermute | solution.py:57
  165.9 5.6 %collective-permute-done.16 = bf16[2,4,512,384]{3,2,1,0:T(8,128)(2,1)S(1)} collective-permute-done((bf16[2,4,512,384]{3,2,1,0:T(8,128)(2,1)S(1)}, bf16[2,4,512,384]{3,2,1,0:T(8,128)(2,1)S(1)}, u32[]{:S(2)}, u32[]{:S(2)}) %collective-permute-start.16) | collective-permute-done | bytes 3145760 | tf_op jit(solution)/shard_map/ppermute | solution.py:92
  171.5 2.4 %fusion.9 = f32[512,384]{1,0:T(8,128)S(1)} fusion(bf16[2,4,512,384]{3,2,1,0:T(8,128)(2,1)S(1)} %collective-permute-done.16, bf16[2,4,2,512,512]{4,3,2,1,0:T(8,128)(2,1)S(1)} %bitcast.221, s32[]{:T(128)S(6)} %select_n.209), kind=kOutput, calls=%fused_computation.26 | convolution fusion | flops 1610612736 | bytes 8126468 | tf_op jit(solution)/shard_map/dot_general | solution.py:190
  173.9 2.4 %fusion.12 = f32[512,384]{1,0:T(8,128)S(1)} fusion(f32[512,384]{1,0:T(8,128)S(1)} %fusion.9, bf16[2,4,2,512,512]{4,3,2,1,0:T(8,128)(2,1)S(1)} %bitcast.222, s32[]{:T(128)S(6)} %select_n.204, bf16[4,2,256,384]{3,2,0,1:T(8,128)(2,1)S(1)} %bitcast_dynamic-update-slice_fusion.7, bf16[4,2,256,384]{3,2,0,1:T(8,128)(2,1)S(1)} %bitcast_dynamic-update-slice_fusion.3), kind=kOutput, calls=%fused_computation.27 | convolution fusion | flops 1617100800 | bytes 8912900 | tf_op jit(solution)/shard_map/dot_general | solution.py:189
  178.0 19.3 %all_to_all.15 = f32[8,70,384]{2,1,0:T(8,128)S(1)} all-to-all(f32[8,70,384]{2,1,0:T(8,128)S(1)} %pad_maximum_fusion.3), channel_id=1, replica_groups=mesh['br'=8,'bus'=16] {'br'}, dimensions={0} | all-to-all | bytes 1720320 | tf_op jit(solution)/shard_map/all_to_all | solution.py:198
  198.7 3.5 %all-to-all-start.2 = ((f32[8,64,384]{2,1,0:T(8,128)}), f32[8,64,384]{2,1,0:T(8,128)S(1)}, u32[]{:S(2)}, u32[]{:S(2)}) async-start(f32[8,64,384]{2,1,0:T(8,128)} %broadcast_in_dim.153), calls=%async_computation.2 | async-start | bytes 1572864 | tf_op jit(solution)/shard_map/all_to_all | solution.py:203
  204.5 9.0 %all-to-all-done.2 = f32[8,64,384]{2,1,0:T(8,128)S(1)} async-done(((f32[8,64,384]{2,1,0:T(8,128)}), f32[8,64,384]{2,1,0:T(8,128)S(1)}, u32[]{:S(2)}, u32[]{:S(2)}) %all-to-all-start.2) | async-done | bytes 786464 | tf_op jit(solution)/shard_map/all_to_all | solution.py:203
  (139 shorter events, 42.3 us)
Async XLA Ops:
  7.7 26.0 %collective-permute-start = (f32[2,2,512,384]{3,2,1,0:T(8,128)}, f32[2,2,512,384]{3,2,1,0:T(8,128)}, u32[]{:S(2)}, u32[]{:S(2)}) collective-permute-start(f32[2,2,512,384]{3,2,1,0:T(8,128)} %pad_maximum_fusion), channel_id=1, source_target_pairs={{0,1},{1,0},{2,3},{3,2},{4,5},{5,4},{6,7},{7,6},{8,9},{9,8},{10,11... | collective-permute-start | bytes 9437192 | tf_op jit(solution)/shard_map/ppermute | solution.py:70
  11.6 2.4 %copy-start.9 = (s32[1024,3]{0,1:T(4,128)S(1)}, s32[1024,3]{0,1:T(4,128)}, u32[]{:S(2)}) copy-start(s32[1024,3]{0,1:T(4,128)} %param.25) | copy-start | bytes 36868
  11.6 2.8 %copy-start.8 = (bf16[8,1536]{1,0:T(8,128)(2,1)S(1)}, bf16[8,1536]{1,0:T(8,128)(2,1)}, u32[]{:S(2)}) copy-start(bf16[8,1536]{1,0:T(8,128)(2,1)} %param.27) | copy-start | bytes 73732
  11.6 10.8 %copy-start.10 = (s32[1024,3]{0,1:T(4,128)S(1)}, s32[1024,3]{0,1:T(4,128)}, u32[]{:S(2)}) copy-start(s32[1024,3]{0,1:T(4,128)} %param.26) | copy-start | bytes 36868
  11.6 12.6 %copy-start.6 = (f32[64,1024]{1,0:T(8,128)S(1)}, f32[64,1024]{1,0:T(8,128)}, u32[]{:S(2)}) copy-start(f32[64,1024]{1,0:T(8,128)} %param.22) | copy-start | bytes 786436
  13.5 28.8 %collective-permute-start.2 = (f32[2,2,512,384]{3,2,1,0:T(8,128)}, f32[2,2,512,384]{3,2,1,0:T(8,128)}, u32[]{:S(2)}, u32[]{:S(2)}) collective-permute-start(f32[2,2,512,384]{3,2,1,0:T(8,128)} %pad_maximum_fusion.1), channel_id=1, source_target_pairs={{0,1},{1,0},{2,3},{3,2},{4,5},{5,4},{6,7},{7,6},{8,9},{9,8},{10,11... | collective-permute-start | bytes 9437192 | tf_op jit(solution)/shard_map/ppermute | solution.py:70
  14.4 17.3 %copy-start.7 = (s32[128,24]{1,0:T(8,128)}, s32[128,24]{1,0:T(8,128)S(1)}, u32[]{:S(2)}) copy-start(s32[128,24]{1,0:T(8,128)S(1)} %reshape.193) | copy-start | bytes 36868
  15.5 70.6 %all-to-all-start = ((bf16[8,6,512]{2,1,0:T(8,128)(2,1)}), bf16[8,6,512]{2,1,0:T(8,128)(2,1)S(1)}, u32[]{:S(2)}, u32[]{:S(2)}) async-start(bf16[8,6,512]{2,1,0:T(8,128)(2,1)} %copy.99), calls=%async_computation | async-start | bytes 131072 | tf_op jit(solution)/shard_map/all_to_all | solution.py:141
  35.9 6.3 %copy-start.11 = (s32[384]{0:T(512)S(1)}, s32[384]{0:T(512)}, u32[]{:S(2)}) copy-start(s32[384]{0:T(512)} %param.24) | copy-start | bytes 4612
  37.3 19.5 %collective-permute-start.1 = (f32[2,256,384]{2,1,0:T(8,128)}, f32[2,256,384]{2,1,0:T(8,128)}, u32[]{:S(2)}, u32[]{:S(2)}) collective-permute-start(f32[2,256,384]{2,1,0:T(8,128)} %get-tuple-element.28), channel_id=1, source_target_pairs={{0,2},{1,3},{2,4},{3,5},{4,6},{5,7},{6,0},{7,1},{8,10},{9,11},{10,... | collective-permute-start | bytes 2359304 | tf_op jit(solution)/shard_map/ppermute | solution.py:46
  38.1 20.7 %collective-permute-start.5 = (f32[2,256,384]{2,1,0:T(8,128)}, f32[2,256,384]{2,1,0:T(8,128)}, u32[]{:S(2)}, u32[]{:S(2)}) collective-permute-start(f32[2,256,384]{2,1,0:T(8,128)} %get-tuple-element.29), channel_id=1, source_target_pairs={{0,6},{1,7},{2,0},{3,1},{4,2},{5,3},{6,4},{7,5},{8,14},{9,15},{10,... | collective-permute-start | bytes 2359304 | tf_op jit(solution)/shard_map/ppermute | solution.py:46
  44.9 35.1 %copy-start.1 = (f32[2,2,512,384]{3,2,1,0:T(8,128)S(1)}, f32[2,2,512,384]{3,2,1,0:T(8,128)}, u32[]{:S(2)}) copy-start(f32[2,2,512,384]{3,2,1,0:T(8,128)} %copy-done) | copy-start | bytes 9437188
  60.3 18.4 %collective-permute-start.3 = (f32[2,256,384]{2,1,0:T(8,128)S(1)}, f32[2,256,384]{2,1,0:T(8,128)S(1)}, u32[]{:S(2)}, u32[]{:S(2)}) collective-permute-start(f32[2,256,384]{2,1,0:T(8,128)S(1)} %get-tuple-element.26), channel_id=1, source_target_pairs={{0,2},{1,3},{2,4},{3,5},{4,6},{5,7},{6,0},{7,1},{8,10},{9,11},{10,... | collective-permute-start | bytes 2359304 | tf_op jit(solution)/shard_map/ppermute | solution.py:46
  60.4 19.6 %collective-permute-start.6 = (f32[2,256,384]{2,1,0:T(8,128)S(1)}, f32[2,256,384]{2,1,0:T(8,128)S(1)}, u32[]{:S(2)}, u32[]{:S(2)}) collective-permute-start(f32[2,256,384]{2,1,0:T(8,128)S(1)} %get-tuple-element.27), channel_id=1, source_target_pairs={{0,6},{1,7},{2,0},{3,1},{4,2},{5,3},{6,4},{7,5},{8,14},{9,15},{10,... | collective-permute-start | bytes 2359304 | tf_op jit(solution)/shard_map/ppermute | solution.py:46
  81.3 17.8 %collective-permute-start.4 = (f32[2,256,384]{2,1,0:T(8,128)}, f32[2,256,384]{2,1,0:T(8,128)}, u32[]{:S(2)}, u32[]{:S(2)}) collective-permute-start(f32[2,256,384]{2,1,0:T(8,128)} %get-tuple-element.24), channel_id=1, source_target_pairs={{0,2},{1,3},{2,4},{3,5},{4,6},{5,7},{6,0},{7,1},{8,10},{9,11},{10,... | collective-permute-start | bytes 2359304 | tf_op jit(solution)/shard_map/ppermute | solution.py:46
  81.5 19.0 %collective-permute-start.7 = (f32[2,256,384]{2,1,0:T(8,128)}, f32[2,256,384]{2,1,0:T(8,128)}, u32[]{:S(2)}, u32[]{:S(2)}) collective-permute-start(f32[2,256,384]{2,1,0:T(8,128)} %get-tuple-element.25), channel_id=1, source_target_pairs={{0,6},{1,7},{2,0},{3,1},{4,2},{5,3},{6,4},{7,5},{8,14},{9,15},{10,... | collective-permute-start | bytes 2359304 | tf_op jit(solution)/shard_map/ppermute | solution.py:46
  102.0 3.2 %copy-start.12 = (f32[512]{0:T(512)S(1)}, f32[512]{0:T(512)}, u32[]{:S(2)}) copy-start(f32[512]{0:T(512)} %param.18) | copy-start | bytes 6148
  102.0 18.5 %copy-start.4 = (f32[512,384]{1,0:T(8,128)S(1)}, f32[512,384]{1,0:T(8,128)}, u32[]{:S(2)}) copy-start(f32[512,384]{1,0:T(8,128)} %param.17) | copy-start | bytes 2359300
  102.2 18.3 %collective-permute-start.8 = (f32[512,384]{1,0:T(8,128)S(1)}, f32[512,384]{1,0:T(8,128)}, u32[]{:S(2)}, u32[]{:S(2)}) collective-permute-start(f32[512,384]{1,0:T(8,128)S(1)} %dynamic-slice_bitcast_fusion), channel_id=1, source_target_pairs={{0,8},{1,9},{2,10},{3,11},{4,12},{5,13},{6,14},{7,15},{8,0},{9,1},... | collective-permute-start | bytes 2359304 | tf_op jit(solution)/shard_map/ppermute | solution.py:81
  122.8 9.3 %collective-permute-start.9 = (bf16[512,384]{1,0:T(8,128)(2,1)S(1)}, bf16[512,384]{1,0:T(8,128)(2,1)S(1)}, u32[]{:S(2)}, u32[]{:S(2)}) collective-permute-start(bf16[512,384]{1,0:T(8,128)(2,1)S(1)} %get-tuple-element.16), channel_id=1, source_target_pairs={{0,8},{1,9},{2,10},{3,11},{4,12},{5,13},{6,14},{7,15},{8,0},{9,1},... | collective-permute-start | bytes 1179656 | tf_op jit(solution)/shard_map/ppermute | solution.py:86
  132.3 11.3 %collective-permute-start.10 = (bf16[2,256,384]{2,1,0:T(8,128)(2,1)S(1)}, bf16[2,256,384]{2,1,0:T(8,128)(2,1)S(1)}, u32[]{:S(2)}, u32[]{:S(2)}) collective-permute-start(bf16[2,256,384]{2,1,0:T(8,128)(2,1)S(1)} %get-tuple-element.30), channel_id=1, source_target_pairs={{0,2},{1,3},{2,4},{3,5},{4,6},{5,7},{6,0},{7,1},{8,10},{9,11},{10,... | collective-permute-start | bytes 1179656 | tf_op jit(solution)/shard_map/ppermute | solution.py:57
  132.9 11.2 %collective-permute-start.13 = (bf16[2,256,384]{2,1,0:T(8,128)(2,1)S(1)}, bf16[2,256,384]{2,1,0:T(8,128)(2,1)S(1)}, u32[]{:S(2)}, u32[]{:S(2)}) collective-permute-start(bf16[2,256,384]{2,1,0:T(8,128)(2,1)S(1)} %get-tuple-element.31), channel_id=1, source_target_pairs={{0,6},{1,7},{2,0},{3,1},{4,2},{5,3},{6,4},{7,5},{8,14},{9,15},{10,... | collective-permute-start | bytes 1179656 | tf_op jit(solution)/shard_map/ppermute | solution.py:57
  134.4 37.2 %slice-start = ((s8[8388608]{0:T(1024)(128)(4,1)}), s8[4194304]{0:T(1024)(128)(4,1)S(1)}, s32[]{:S(2)}) async-start(s8[8388608]{0:T(1024)(128)(4,1)} %bitcast.219), calls=%async_computation.3 | async-start | bytes 8388608
  143.5 11.7 %collective-permute-start.11 = (bf16[2,256,384]{2,1,0:T(8,128)(2,1)S(1)}, bf16[2,256,384]{2,1,0:T(8,128)(2,1)S(1)}, u32[]{:S(2)}, u32[]{:S(2)}) collective-permute-start(bf16[2,256,384]{2,1,0:T(8,128)(2,1)S(1)} %collective-permute-done.10), channel_id=1, source_target_pairs={{0,2},{1,3},{2,4},{3,5},{4,6},{5,7},{6,0},{7,1},{8,10},{9,11},{10,... | collective-permute-start | bytes 1179656 | tf_op jit(solution)/shard_map/ppermute | solution.py:57
  144.1 12.3 %collective-permute-start.14 = (bf16[2,256,384]{2,1,0:T(8,128)(2,1)S(1)}, bf16[2,256,384]{2,1,0:T(8,128)(2,1)S(1)}, u32[]{:S(2)}, u32[]{:S(2)}) collective-permute-start(bf16[2,256,384]{2,1,0:T(8,128)(2,1)S(1)} %collective-permute-done.13), channel_id=1, source_target_pairs={{0,6},{1,7},{2,0},{3,1},{4,2},{5,3},{6,4},{7,5},{8,14},{9,15},{10,... | collective-permute-start | bytes 1179656 | tf_op jit(solution)/shard_map/ppermute | solution.py:57
  155.2 7.8 %collective-permute-start.12 = (bf16[2,256,384]{2,1,0:T(8,128)(2,1)S(1)}, bf16[2,256,384]{2,1,0:T(8,128)(2,1)S(1)}, u32[]{:S(2)}, u32[]{:S(2)}) collective-permute-start(bf16[2,256,384]{2,1,0:T(8,128)(2,1)S(1)} %collective-permute-done.11), channel_id=1, source_target_pairs={{0,2},{1,3},{2,4},{3,5},{4,6},{5,7},{6,0},{7,1},{8,10},{9,11},{10,... | collective-permute-start | bytes 1179656 | tf_op jit(solution)/shard_map/ppermute | solution.py:57
  156.4 9.0 %collective-permute-start.15 = (bf16[2,256,384]{2,1,0:T(8,128)(2,1)S(1)}, bf16[2,256,384]{2,1,0:T(8,128)(2,1)S(1)}, u32[]{:S(2)}, u32[]{:S(2)}) collective-permute-start(bf16[2,256,384]{2,1,0:T(8,128)(2,1)S(1)} %collective-permute-done.14), channel_id=1, source_target_pairs={{0,6},{1,7},{2,0},{3,1},{4,2},{5,3},{6,4},{7,5},{8,14},{9,15},{10,... | collective-permute-start | bytes 1179656 | tf_op jit(solution)/shard_map/ppermute | solution.py:57
  157.3 14.2 %slice-start.1 = ((s8[8388608]{0:T(1024)(128)(4,1)}), s8[4194304]{0:T(1024)(128)(4,1)S(1)}, s32[]{:S(2)}) async-start(s8[8388608]{0:T(1024)(128)(4,1)} %bitcast.219), calls=%async_computation.4 | async-start | bytes 8388608
  165.8 5.7 %collective-permute-start.16 = (bf16[2,4,512,384]{3,2,1,0:T(8,128)(2,1)S(1)}, bf16[2,4,512,384]{3,2,1,0:T(8,128)(2,1)S(1)}, u32[]{:S(2)}, u32[]{:S(2)}) collective-permute-start(bf16[2,4,512,384]{3,2,1,0:T(8,128)(2,1)S(1)} %maximum_bitcast_fusion), channel_id=1, source_target_pairs={{0,1},{1,0},{2,3},{3,2},{4,5},{5,4},{6,7},{7,6},{8,9},{9,8},{10,11... | collective-permute-start | bytes 9437192 | tf_op jit(solution)/shard_map/ppermute | solution.py:92
  177.9 19.6 %copy-start.2 = (f32[64,384]{0,1:T(8,128)S(1)}, f32[64,384]{0,1:T(8,128)}, u32[]{:S(2)}) copy-start(f32[64,384]{0,1:T(8,128)} %broadcast_subtract_fusion) | copy-start | bytes 294916
  177.9 19.6 %copy-start.3 = (f32[64,384]{0,1:T(8,128)S(1)}, f32[64,384]{0,1:T(8,128)}, u32[]{:S(2)}) copy-start(f32[64,384]{0,1:T(8,128)} %multiply_bitcast_fusion) | copy-start | bytes 294916
  198.7 14.8 %all-to-all-start.2 = ((f32[8,64,384]{2,1,0:T(8,128)}), f32[8,64,384]{2,1,0:T(8,128)S(1)}, u32[]{:S(2)}, u32[]{:S(2)}) async-start(f32[8,64,384]{2,1,0:T(8,128)} %broadcast_in_dim.153), calls=%async_computation.2 | async-start | bytes 1572864 | tf_op jit(solution)/shard_map/all_to_all | solution.py:203
  (2 other events, 3.2 us)

commit v7 on v6

--- a/solution.py
+++ b/solution.py
@@ -39,12 +39,14 @@
     return lax.dynamic_index_in_dim(a, i, axis, keepdims=False)
 
 
-def ring_scatter(contribs, up):
+def ring_scatter(contribs, up, rider=None):
     perm = X_UP if up else X_DOWN
     acc = contribs[0]
-    for more in contribs[1:]:
+    for k, more in enumerate(contribs[1:]):
         acc = lax.ppermute(acc, "bus", perm) + more
-    return acc
+        if k == 0 and rider is not None:
+            acc, rider = lax.optimization_barrier((acc, rider))
+    return acc, rider
 
 
 def ring_gather(own, xi, up):
@@ -59,7 +61,7 @@
     return out
 
 
-def bus_reduce_scatter(flow_part):
+def bus_reduce_scatter(flow_part, rider):
     yh, xi, c = bus_place()
     first = [(xi - 1) % XR, (xi + 1) % XR]
     second = [(xi + 2) % XR, xi]
@@ -70,10 +72,10 @@
         summed.append(keep + lax.ppermute(send, "bus", CORE_SWAP))
     a, b = summed
     half = a.shape[2] // 2
-    cw = ring_scatter([a[0, :, :half], b[0, :, :half], a[1, :, :half], b[1, :, :half]], True)
-    ccw = ring_scatter([a[1, :, half:], b[0, :, half:], a[0, :, half:], b[1, :, half:]], False)
+    cw, rider = ring_scatter([a[0, :, :half], b[0, :, :half], a[1, :, :half], b[1, :, :half]], True, rider)
+    ccw, _ = ring_scatter([a[1, :, half:], b[0, :, half:], a[0, :, half:], b[1, :, half:]], False)
     z = jnp.concatenate([cw, ccw], axis=1)
-    return z
+    return z, rider
 
 
 def bus_pair_sum(z):
@@ -138,7 +140,6 @@
     outgoing_w = jnp.einsum(
         "sce,er->scr", pick_out.astype(jnp.bfloat16), weight_rows, preferred_element_type=jnp.float32
     ).astype(jnp.bfloat16)
-    arrived_w = lax.all_to_all(outgoing_w, "br", 0, 0, tiled=True)
     sources = slab_range * bus_axis + column_index
     src_slab = jnp.take(slab_by_device, sources, axis=0)
     src_block = jnp.take(block_by_device, sources, axis=0)
@@ -146,11 +147,7 @@
     pick_in = (src_slab[:, None, :] == slab_index) & (src_slot[:, None, :] == slot_range[None, :, None])
     block_choice = jnp.sum(jnp.where(pick_in, src_block[:, None, :], 0), axis=2)
     block_hot = block_choice[:, :, None] == jnp.arange(blocks_per_slab, dtype=jnp.int32)[None, None, :]
-    masked = jnp.where(block_hot[:, :, :, None], arrived_w[:, :, None, :], jnp.zeros((), jnp.bfloat16))
     yh, xi, core = bus_place()
-    masked = masked.reshape(slab_axis * CAP, YHI, XR, CORES, -1)
-    masked_keep = pick(masked, core, 3)
-    masked_send = pick(masked, 1 - core, 3)
 
     bus_rows = injections.shape[0]
     share_rows = bus_rows // slab_axis
@@ -175,7 +172,12 @@
         rows = pick(sf_keep if mine else sf_send, x, 1)
         return jnp.dot(rows, inject_half, preferred_element_type=jnp.float32)
 
-    ring_out = bus_reduce_scatter(flow_part)
+    ring_out, outgoing_w = bus_reduce_scatter(flow_part, outgoing_w)
+    arrived_w = lax.all_to_all(outgoing_w, "br", 0, 0, tiled=True)
+    masked = jnp.where(block_hot[:, :, :, None], arrived_w[:, :, None, :], jnp.zeros((), jnp.bfloat16))
+    masked = masked.reshape(slab_axis * CAP, YHI, XR, CORES, -1)
+    masked_keep = pick(masked, core, 3)
+    masked_send = pick(masked, 1 - core, 3)
     ring_out, masked_keep, masked_send, upper, lower, base = lax.optimization_barrier(
         (ring_out, masked_keep, masked_send, upper, lower, base)
     )
@@ -192,12 +194,9 @@
     partial_rent = lax.dot_general(masked_keep, prices_keep, contract_w, preferred_element_type=jnp.float32)
     partial_rent = partial_rent + lax.dot_general(masked_send, prices_send, contract_w, preferred_element_type=jnp.float32)
 
-    outgoing = jnp.concatenate(
-        [partial_grad.reshape(slab_axis, share_rows, scenarios), partial_rent.reshape(slab_axis, CAP, scenarios)], axis=1
-    )
-    gathered = lax.all_to_all(outgoing, "br", 0, 0, tiled=True)
-    gradient = jnp.sum(gathered[:, :share_rows], axis=0)
-    returned = gathered[:, share_rows:]
+    gathered = lax.all_to_all(partial_grad.reshape(slab_axis, share_rows, scenarios), "br", 0, 0, tiled=True)
+    returned = lax.all_to_all(partial_rent.reshape(slab_axis, CAP, scenarios), "br", 0, 0, tiled=True)
+    gradient = jnp.sum(gathered, axis=0)
     trial = base - step_primal * gradient
     my_new = jnp.minimum(jnp.maximum(trial, lower), upper)
     new_injections = lax.all_to_all(

time: 215 us -> 215 us (level)
  blocking collectives: 19.3 us -> 0 us
  starting transfers between devices: 27.5 us -> 38.8 us
  waiting for transfers between devices: 107 us -> 112 us
  matrix products: 22.7 us -> 25.1 us
    all_to_all x1 -> x0, blocking collectives: 19.3 us -> none  [per_device(): gathered = lax.all_to_all(outgoing, 'br', 0, 0, tiled=True)]
    all_to_all x0 -> x2, waiting for transfers between devices: none -> 12 us  [the longest x1 7.06 us: per_device(): lax.all_to_all(partial_grad.reshape(slab_axis, share_rows, scenarios), 'b...]
    ppermute x6, waiting for transfers between devices: 43.4 us -> 31.4 us  [ring_scatter(): acc = lax.ppermute(acc, 'bus', perm) + more]
    all_to_all x0 -> x2, starting transfers between devices: none -> 9.98 us  [the longest x1 6.35 us: per_device(): lax.all_to_all(partial_grad.reshape(slab_axis, share_rows, scenarios), 'b...]
    all_to_all x1, waiting for transfers between devices: 0.01 us -> 5.59 us  [per_device(): arrived_w = lax.all_to_all(outgoing_w, 'br', 0, 0, tiled=True)]
  transfers between devices with their start and end apart: 19 -> 21, of which waited for: 16 -> 18; matrix products, arithmetic and copies ran while one was open for 18% -> 19% of each run, Pallas kernels for 0% -> 0%
where the time goes in v7:
time: 215 us; the launch traced here: 214 us
  waiting for transfers between devices  112 us (52%)
  starting transfers between devices  38.8 us (18%)
  matrix products  25.1 us (12%)
  other arithmetic  22.9 us (11%)
  local copies, waits for them, and re-layouts  14.5 us (7%)
    ppermute x6, waiting for transfers between devices, ring_scatter(): acc = lax.ppermute(acc, 'bus', perm) + more  31.4 us
    ppermute x6, waiting for transfers between devices, ring_gather(): cur = lax.ppermute(cur, 'bus', perm)  27 us
    dot_general x8, matrix products, flow_part(): return jnp.dot(rows, inject_half, preferred_element_type=jnp.float32)  15.4 us
    ppermute x1, waiting for transfers between devices, bus_pair_sum(): return pick(z, yh, 0) + lax.ppermute(pick(z, 1 - yh, 0), 'bus', Y_SWAP)  15 us
    all_to_all x1, waiting for transfers between devices, per_device(): lax.all_to_all(jnp.broadcast_to(my_new[None], (slab_axis, share_rows, sce...  8.98 us
    all_to_all x1, waiting for transfers between devices, per_device(): lax.all_to_all(partial_grad.reshape(slab_axis, share_rows, scenarios), 'b...  7.06 us
    all_to_all x1, starting transfers between devices, per_device(): arrived_w = lax.all_to_all(outgoing_w, 'br', 0, 0, tiled=True)  6.42 us
    all_to_all x1, starting transfers between devices, per_device(): lax.all_to_all(partial_grad.reshape(slab_axis, share_rows, scenarios), 'b...  6.35 us
  transfers between devices with their start and end apart: 21, of which 18 were waited for; matrix products, arithmetic and copies ran while one was open for 19% of the time, Pallas kernels for 0%

profile of v7, /device:TPU:6, one launch (start us, length us, event | category | flops | bytes accessed | tf_op | source)
XLA Modules:
  0.0 214.2 jit_solution(7540800337780669845)
XLA Ops:
  1.9 1.9 convolution_bitcast_fusion.5
  3.9 1.9 convolution_bitcast_fusion.4
  9.6 1.9 convolution_bitcast_fusion
  11.6 1.9 pad_maximum_fusion.1
  20.6 1.9 convolution_bitcast_fusion.3
  22.6 1.9 convolution_bitcast_fusion.7
  24.5 1.9 convolution_bitcast_fusion.6
  26.5 2.2 %maximum_add_fusion = f32[2,2,512,384]{3,2,1,0:T(8,128)S(1)} fusion(f32[2,2,512,384]{3,2,1,0:T(8,128)} %collective-permute-done, f32[1,2,512,384]{3,2,1,0:T(8,128)S(1)} %convolution_bitcast_fusion.6, f32[1,2,512,384]{3,2,1,0:T(8,128)S(1)} %convolution_bitcast_fusion.7), kind=kLoop, calls=%fused_computation.11 | loop fusion | flops 1572864 | bytes 9437184 | tf_op jit(solution)/shard_map/add | solution.py:72
  33.0 2.2 %maximum_add_fusion.1 = f32[2,2,512,384]{3,2,1,0:T(8,128)S(1)} fusion(f32[2,2,512,384]{3,2,1,0:T(8,128)} %collective-permute-done.2, f32[1,2,512,384]{3,2,1,0:T(8,128)S(1)} %convolution_bitcast_fusion.2, f32[1,2,512,384]{3,2,1,0:T(8,128)S(1)} %convolution_bitcast_fusion.3), kind=kLoop, calls=%fused_computation.13 | loop fusion | flops 1572864 | bytes 9437184 | tf_op jit(solution)/shard_map/add | solution.py:72
  35.2 13.2 %collective-permute-done.1 = f32[2,256,384]{2,1,0:T(8,128)S(1)} collective-permute-done((f32[2,256,384]{2,1,0:T(8,128)S(1)}, f32[2,256,384]{2,1,0:T(8,128)S(1)}, u32[]{:S(2)}, u32[]{:S(2)}) %collective-permute-start.1) | collective-permute-done | bytes 786464 | tf_op jit(solution)/shard_map/ppermute | solution.py:46
  53.5 14.7 %collective-permute-done.3 = f32[2,256,384]{2,1,0:T(8,128)S(1)} collective-permute-done((f32[2,256,384]{2,1,0:T(8,128)S(1)}, f32[2,256,384]{2,1,0:T(8,128)S(1)}, u32[]{:S(2)}, u32[]{:S(2)}) %collective-permute-start.3) | collective-permute-done | bytes 786464 | tf_op jit(solution)/shard_map/ppermute | solution.py:46
  75.7 6.4 %all-to-all-start = ((bf16[8,6,512]{2,1,0:T(8,128)(2,1)}), bf16[8,6,512]{2,1,0:T(8,128)(2,1)S(1)}, u32[]{:S(2)}, u32[]{:S(2)}) async-start(bf16[8,6,512]{2,1,0:T(8,128)(2,1)} %copy.99), calls=%async_computation | async-start | bytes 131072 | tf_op jit(solution)/shard_map/all_to_all | solution.py:176
  82.9 5.6 %all-to-all-done = bf16[8,6,512]{2,1,0:T(8,128)(2,1)S(1)} async-done(((bf16[8,6,512]{2,1,0:T(8,128)(2,1)}), bf16[8,6,512]{2,1,0:T(8,128)(2,1)S(1)}, u32[]{:S(2)}, u32[]{:S(2)}) %all-to-all-start) | async-done | bytes 49184 | tf_op jit(solution)/shard_map/all_to_all | solution.py:176
  92.0 3.5 %collective-permute-start.8 = (f32[512,384]{1,0:T(8,128)S(1)}, f32[512,384]{1,0:T(8,128)}, u32[]{:S(2)}, u32[]{:S(2)}) collective-permute-start(f32[512,384]{1,0:T(8,128)S(1)} %dynamic-slice_bitcast_fusion), channel_id=1, source_target_pairs={{0,8},{1,9},{2,10},{3,11},{4,12},{5,13},{6,14},{7,15},{8,0},{9,1},... | collective-permute-start | bytes 2359304 | tf_op jit(solution)/shard_map/ppermute | solution.py:83
  95.5 15.0 %collective-permute-done.8 = f32[512,384]{1,0:T(8,128)} collective-permute-done((f32[512,384]{1,0:T(8,128)S(1)}, f32[512,384]{1,0:T(8,128)}, u32[]{:S(2)}, u32[]{:S(2)}) %collective-permute-start.8) | collective-permute-done | bytes 786464 | tf_op jit(solution)/shard_map/ppermute | solution.py:83
  110.5 2.2 %fusion.65 = (bf16[512,384]{1,0:T(8,128)(2,1)S(1)}, f32[512,384]{1,0:T(8,128)}) fusion(f32[512]{0:T(512)S(1)} %get-tuple-element.41, f32[512]{0:T(512)S(1)} %get-tuple-element.40, f32[512,384]{1,0:T(8,128)S(1)} %copy-done.3, f32[512,384]{1,0:T(8,128)} %collective-permute-done.8, f32[2,512,384]{2,1,0:T(8,128)S(1)} %pad_maximum_fusion.2, s32[]{:T(128)S(6)} %select_n.226), kind=kLoop, calls=%fused_computation.141 | loop fusion | flops 1376256 | bytes 3543044 | tf_op jit(solution)/shard_map/convert_element_type | solution.py:188
  112.7 3.2 %collective-permute-start.9 = (bf16[512,384]{1,0:T(8,128)(2,1)S(1)}, bf16[512,384]{1,0:T(8,128)(2,1)S(1)}, u32[]{:S(2)}, u32[]{:S(2)}) collective-permute-start(bf16[512,384]{1,0:T(8,128)(2,1)S(1)} %get-tuple-element.20), channel_id=1, source_target_pairs={{0,8},{1,9},{2,10},{3,11},{4,12},{5,13},{6,14},{7,15},{8,0},{9,1},... | collective-permute-start | bytes 1179656 | tf_op jit(solution)/shard_map/ppermute | solution.py:88
  116.0 6.0 %collective-permute-done.9 = bf16[512,384]{1,0:T(8,128)(2,1)S(1)} collective-permute-done((bf16[512,384]{1,0:T(8,128)(2,1)S(1)}, bf16[512,384]{1,0:T(8,128)(2,1)S(1)}, u32[]{:S(2)}, u32[]{:S(2)}) %collective-permute-start.9) | collective-permute-done | bytes 393248 | tf_op jit(solution)/shard_map/ppermute | solution.py:88
  124.8 8.5 %collective-permute-done.10 = bf16[2,256,384]{2,1,0:T(8,128)(2,1)S(1)} collective-permute-done((bf16[2,256,384]{2,1,0:T(8,128)(2,1)S(1)}, bf16[2,256,384]{2,1,0:T(8,128)(2,1)S(1)}, u32[]{:S(2)}, u32[]{:S(2)}) %collective-permute-start.10) | collective-permute-done | bytes 393248 | tf_op jit(solution)/shard_map/ppermute | solution.py:59
  135.4 9.7 %collective-permute-done.11 = bf16[2,256,384]{2,1,0:T(8,128)(2,1)S(1)} collective-permute-done((bf16[2,256,384]{2,1,0:T(8,128)(2,1)S(1)}, bf16[2,256,384]{2,1,0:T(8,128)(2,1)S(1)}, u32[]{:S(2)}, u32[]{:S(2)}) %collective-permute-start.11) | collective-permute-done | bytes 393248 | tf_op jit(solution)/shard_map/ppermute | solution.py:59
  147.3 5.6 %collective-permute-done.12 = bf16[2,256,384]{2,1,0:T(8,128)(2,1)S(1)} collective-permute-done((bf16[2,256,384]{2,1,0:T(8,128)(2,1)S(1)}, bf16[2,256,384]{2,1,0:T(8,128)(2,1)S(1)}, u32[]{:S(2)}, u32[]{:S(2)}) %collective-permute-start.12) | collective-permute-done | bytes 393248 | tf_op jit(solution)/shard_map/ppermute | solution.py:59
  153.0 2.3 %collective-permute-done.15 = bf16[2,256,384]{2,1,0:T(8,128)(2,1)S(1)} collective-permute-done((bf16[2,256,384]{2,1,0:T(8,128)(2,1)S(1)}, bf16[2,256,384]{2,1,0:T(8,128)(2,1)S(1)}, u32[]{:S(2)}, u32[]{:S(2)}) %collective-permute-start.15) | collective-permute-done | bytes 393248 | tf_op jit(solution)/shard_map/ppermute | solution.py:59
  155.8 5.6 %collective-permute-done.16 = bf16[2,4,512,384]{3,2,1,0:T(8,128)(2,1)S(1)} collective-permute-done((bf16[2,4,512,384]{3,2,1,0:T(8,128)(2,1)S(1)}, bf16[2,4,512,384]{3,2,1,0:T(8,128)(2,1)S(1)}, u32[]{:S(2)}, u32[]{:S(2)}) %collective-permute-start.16) | collective-permute-done | bytes 3145760 | tf_op jit(solution)/shard_map/ppermute | solution.py:94
  163.1 2.4 %fusion.9 = f32[512,384]{1,0:T(8,128)S(1)} fusion(bf16[2,4,512,384]{3,2,1,0:T(8,128)(2,1)S(1)} %collective-permute-done.16, bf16[2,4,2,512,512]{4,3,2,1,0:T(8,128)(2,1)S(1)} %bitcast.221, s32[]{:T(128)S(6)} %select_n.209), kind=kOutput, calls=%fused_computation.26 | convolution fusion | flops 1610612736 | bytes 8126468 | tf_op jit(solution)/shard_map/dot_general | solution.py:192
  165.5 3.4 %fusion.12 = f32[512,384]{1,0:T(8,128)} fusion(f32[512,384]{1,0:T(8,128)S(1)} %fusion.9, bf16[2,4,2,512,512]{4,3,2,1,0:T(8,128)(2,1)S(1)} %bitcast.222, s32[]{:T(128)S(6)} %select_n.204, bf16[4,2,256,384]{3,2,0,1:T(8,128)(2,1)S(1)} %bitcast_dynamic-update-slice_fusion.7, bf16[4,2,256,384]{3,2,0,1:T(8,128)(2,1)S(1)} %bitcast_dynamic-update-slice_fusion.3), kind=kOutput, calls=%fused_computation.27 | convolution fusion | flops 1617100800 | bytes 8912900 | tf_op jit(solution)/shard_map/dot_general | solution.py:191
  168.8 6.3 %all-to-all-start.1 = ((f32[8,64,384]{2,1,0:T(8,128)}), f32[8,64,384]{2,1,0:T(8,128)}, u32[]{:S(2)}, u32[]{:S(2)}) async-start(f32[8,64,384]{2,1,0:T(8,128)} %bitcast.225), calls=%async_computation.1 | async-start | bytes 1572864 | tf_op jit(solution)/shard_map/all_to_all | solution.py:197
  175.2 2.5 %convolution_bitcast_fusion.8 = f32[48,384]{1,0:T(8,128)S(1)} fusion(bf16[48,2,4,512]{3,0,2,1:T(8,128)(2,1)S(1)} %get-tuple-element.19, bf16[2,4,512,384]{3,2,1,0:T(8,128)(2,1)} %copy-done), kind=kOutput, calls=%fused_computation.28 | convolution fusion | flops 150994944 | bytes 3612672 | tf_op jit(solution)/shard_map/dot_general | solution.py:195
  180.5 7.1 %all-to-all-done.1 = f32[8,64,384]{2,1,0:T(8,128)} async-done(((f32[8,64,384]{2,1,0:T(8,128)}), f32[8,64,384]{2,1,0:T(8,128)}, u32[]{:S(2)}, u32[]{:S(2)}) %all-to-all-start.1) | async-done | bytes 786464 | tf_op jit(solution)/shard_map/all_to_all | solution.py:197
  187.6 3.6 %all-to-all-start.3 = ((f32[8,6,384]{2,1,0:T(8,128)}), f32[8,6,384]{2,1,0:T(8,128)S(1)}, u32[]{:S(2)}, u32[]{:S(2)}) async-start(f32[8,6,384]{2,1,0:T(8,128)} %reshape.201), calls=%async_computation.3 | async-start | bytes 196608 | tf_op jit(solution)/shard_map/all_to_all | solution.py:198
  192.7 4.9 %all-to-all-done.3 = f32[8,6,384]{2,1,0:T(8,128)S(1)} async-done(((f32[8,6,384]{2,1,0:T(8,128)}), f32[8,6,384]{2,1,0:T(8,128)S(1)}, u32[]{:S(2)}, u32[]{:S(2)}) %all-to-all-start.3) | async-done | bytes 73760 | tf_op jit(solution)/shard_map/all_to_all | solution.py:198
  198.6 3.5 %all-to-all-start.2 = ((f32[8,64,384]{2,1,0:T(8,128)}), f32[8,64,384]{2,1,0:T(8,128)S(1)}, u32[]{:S(2)}, u32[]{:S(2)}) async-start(f32[8,64,384]{2,1,0:T(8,128)} %broadcast_in_dim.153), calls=%async_computation.2 | async-start | bytes 1572864 | tf_op jit(solution)/shard_map/all_to_all | solution.py:202
  204.4 9.0 %all-to-all-done.2 = f32[8,64,384]{2,1,0:T(8,128)S(1)} async-done(((f32[8,64,384]{2,1,0:T(8,128)}), f32[8,64,384]{2,1,0:T(8,128)S(1)}, u32[]{:S(2)}, u32[]{:S(2)}) %all-to-all-start.2) | async-done | bytes 786464 | tf_op jit(solution)/shard_map/all_to_all | solution.py:202
  (138 shorter events, 50.6 us)
Async XLA Ops:
  7.6 18.9 %collective-permute-start = (f32[2,2,512,384]{3,2,1,0:T(8,128)}, f32[2,2,512,384]{3,2,1,0:T(8,128)}, u32[]{:S(2)}, u32[]{:S(2)}) collective-permute-start(f32[2,2,512,384]{3,2,1,0:T(8,128)} %pad_maximum_fusion), channel_id=1, source_target_pairs={{0,1},{1,0},{2,3},{3,2},{4,5},{5,4},{6,7},{7,6},{8,9},{9,8},{10,11... | collective-permute-start | bytes 9437192 | tf_op jit(solution)/shard_map/ppermute | solution.py:72
  11.5 2.9 %copy-start.7 = (bf16[8,1536]{1,0:T(8,128)(2,1)S(1)}, bf16[8,1536]{1,0:T(8,128)(2,1)}, u32[]{:S(2)}) copy-start(bf16[8,1536]{1,0:T(8,128)(2,1)} %param.27) | copy-start | bytes 73732
  11.5 2.9 %copy-start.9 = (s32[1024,3]{0,1:T(4,128)S(1)}, s32[1024,3]{0,1:T(4,128)}, u32[]{:S(2)}) copy-start(s32[1024,3]{0,1:T(4,128)} %param.26) | copy-start | bytes 36868
  11.5 5.3 %copy-start.5 = (f32[64,1024]{1,0:T(8,128)S(1)}, f32[64,1024]{1,0:T(8,128)}, u32[]{:S(2)}) copy-start(f32[64,1024]{1,0:T(8,128)} %param.22) | copy-start | bytes 786436
  13.5 19.5 %collective-permute-start.2 = (f32[2,2,512,384]{3,2,1,0:T(8,128)}, f32[2,2,512,384]{3,2,1,0:T(8,128)}, u32[]{:S(2)}, u32[]{:S(2)}) collective-permute-start(f32[2,2,512,384]{3,2,1,0:T(8,128)} %pad_maximum_fusion.1), channel_id=1, source_target_pairs={{0,1},{1,0},{2,3},{3,2},{4,5},{5,4},{6,7},{7,6},{8,9},{9,8},{10,11... | collective-permute-start | bytes 9437192 | tf_op jit(solution)/shard_map/ppermute | solution.py:72
  14.4 10.1 %copy-start.6 = (s32[128,24]{1,0:T(8,128)}, s32[128,24]{1,0:T(8,128)S(1)}, u32[]{:S(2)}) copy-start(s32[128,24]{1,0:T(8,128)S(1)} %reshape.196) | copy-start | bytes 36868
  22.5 3.9 %copy-start.10 = (s32[384]{0:T(512)S(1)}, s32[384]{0:T(512)}, u32[]{:S(2)}) copy-start(s32[384]{0:T(512)} %param.24) | copy-start | bytes 4612
  28.8 19.5 %collective-permute-start.1 = (f32[2,256,384]{2,1,0:T(8,128)S(1)}, f32[2,256,384]{2,1,0:T(8,128)S(1)}, u32[]{:S(2)}, u32[]{:S(2)}) collective-permute-start(f32[2,256,384]{2,1,0:T(8,128)S(1)} %get-tuple-element.32), channel_id=1, source_target_pairs={{0,2},{1,3},{2,4},{3,5},{4,6},{5,7},{6,0},{7,1},{8,10},{9,11},{10,... | collective-permute-start | bytes 2359304 | tf_op jit(solution)/shard_map/ppermute | solution.py:46
  29.3 20.4 %collective-permute-start.5 = (f32[2,256,384]{2,1,0:T(8,128)S(1)}, f32[2,256,384]{2,1,0:T(8,128)S(1)}, u32[]{:S(2)}, u32[]{:S(2)}) collective-permute-start(f32[2,256,384]{2,1,0:T(8,128)S(1)} %get-tuple-element.33), channel_id=1, source_target_pairs={{0,6},{1,7},{2,0},{3,1},{4,2},{5,3},{6,4},{7,5},{8,14},{9,15},{10,... | collective-permute-start | bytes 2359304 | tf_op jit(solution)/shard_map/ppermute | solution.py:46
  49.8 18.4 %collective-permute-start.3 = (f32[2,256,384]{2,1,0:T(8,128)S(1)}, f32[2,256,384]{2,1,0:T(8,128)S(1)}, u32[]{:S(2)}, u32[]{:S(2)}) collective-permute-start(f32[2,256,384]{2,1,0:T(8,128)S(1)} %get-tuple-element.12), channel_id=1, source_target_pairs={{0,2},{1,3},{2,4},{3,5},{4,6},{5,7},{6,0},{7,1},{8,10},{9,11},{10,... | collective-permute-start | bytes 2359304 | tf_op jit(solution)/shard_map/ppermute | solution.py:46
  50.3 19.4 %collective-permute-start.6 = (f32[2,256,384]{2,1,0:T(8,128)S(1)}, f32[2,256,384]{2,1,0:T(8,128)S(1)}, u32[]{:S(2)}, u32[]{:S(2)}) collective-permute-start(f32[2,256,384]{2,1,0:T(8,128)S(1)} %get-tuple-element.31), channel_id=1, source_target_pairs={{0,6},{1,7},{2,0},{3,1},{4,2},{5,3},{6,4},{7,5},{8,14},{9,15},{10,... | collective-permute-start | bytes 2359304 | tf_op jit(solution)/shard_map/ppermute | solution.py:46
  71.1 18.4 %collective-permute-start.4 = (f32[2,256,384]{2,1,0:T(8,128)}, f32[2,256,384]{2,1,0:T(8,128)}, u32[]{:S(2)}, u32[]{:S(2)}) collective-permute-start(f32[2,256,384]{2,1,0:T(8,128)} %get-tuple-element.28), channel_id=1, source_target_pairs={{0,2},{1,3},{2,4},{3,5},{4,6},{5,7},{6,0},{7,1},{8,10},{9,11},{10,... | collective-permute-start | bytes 2359304 | tf_op jit(solution)/shard_map/ppermute | solution.py:46
  71.4 18.9 %collective-permute-start.7 = (f32[2,256,384]{2,1,0:T(8,128)}, f32[2,256,384]{2,1,0:T(8,128)}, u32[]{:S(2)}, u32[]{:S(2)}) collective-permute-start(f32[2,256,384]{2,1,0:T(8,128)} %get-tuple-element.29), channel_id=1, source_target_pairs={{0,6},{1,7},{2,0},{3,1},{4,2},{5,3},{6,4},{7,5},{8,14},{9,15},{10,... | collective-permute-start | bytes 2359304 | tf_op jit(solution)/shard_map/ppermute | solution.py:46
  75.7 12.8 %all-to-all-start = ((bf16[8,6,512]{2,1,0:T(8,128)(2,1)}), bf16[8,6,512]{2,1,0:T(8,128)(2,1)S(1)}, u32[]{:S(2)}, u32[]{:S(2)}) async-start(bf16[8,6,512]{2,1,0:T(8,128)(2,1)} %copy.99), calls=%async_computation | async-start | bytes 131072 | tf_op jit(solution)/shard_map/all_to_all | solution.py:176
  91.8 3.7 %copy-start.11 = (f32[512]{0:T(512)S(1)}, f32[512]{0:T(512)}, u32[]{:S(2)}) copy-start(f32[512]{0:T(512)} %param.18) | copy-start | bytes 6148
  91.8 18.7 %copy-start.3 = (f32[512,384]{1,0:T(8,128)S(1)}, f32[512,384]{1,0:T(8,128)}, u32[]{:S(2)}) copy-start(f32[512,384]{1,0:T(8,128)} %param.17) | copy-start | bytes 2359300
  92.0 18.5 %collective-permute-start.8 = (f32[512,384]{1,0:T(8,128)S(1)}, f32[512,384]{1,0:T(8,128)}, u32[]{:S(2)}, u32[]{:S(2)}) collective-permute-start(f32[512,384]{1,0:T(8,128)S(1)} %dynamic-slice_bitcast_fusion), channel_id=1, source_target_pairs={{0,8},{1,9},{2,10},{3,11},{4,12},{5,13},{6,14},{7,15},{8,0},{9,1},... | collective-permute-start | bytes 2359304 | tf_op jit(solution)/shard_map/ppermute | solution.py:83
  112.7 9.3 %collective-permute-start.9 = (bf16[512,384]{1,0:T(8,128)(2,1)S(1)}, bf16[512,384]{1,0:T(8,128)(2,1)S(1)}, u32[]{:S(2)}, u32[]{:S(2)}) collective-permute-start(bf16[512,384]{1,0:T(8,128)(2,1)S(1)} %get-tuple-element.20), channel_id=1, source_target_pairs={{0,8},{1,9},{2,10},{3,11},{4,12},{5,13},{6,14},{7,15},{8,0},{9,1},... | collective-permute-start | bytes 1179656 | tf_op jit(solution)/shard_map/ppermute | solution.py:88
  122.2 11.0 %collective-permute-start.10 = (bf16[2,256,384]{2,1,0:T(8,128)(2,1)S(1)}, bf16[2,256,384]{2,1,0:T(8,128)(2,1)S(1)}, u32[]{:S(2)}, u32[]{:S(2)}) collective-permute-start(bf16[2,256,384]{2,1,0:T(8,128)(2,1)S(1)} %get-tuple-element.34), channel_id=1, source_target_pairs={{0,2},{1,3},{2,4},{3,5},{4,6},{5,7},{6,0},{7,1},{8,10},{9,11},{10,... | collective-permute-start | bytes 1179656 | tf_op jit(solution)/shard_map/ppermute | solution.py:59
  122.9 11.2 %collective-permute-start.13 = (bf16[2,256,384]{2,1,0:T(8,128)(2,1)S(1)}, bf16[2,256,384]{2,1,0:T(8,128)(2,1)S(1)}, u32[]{:S(2)}, u32[]{:S(2)}) collective-permute-start(bf16[2,256,384]{2,1,0:T(8,128)(2,1)S(1)} %get-tuple-element.35), channel_id=1, source_target_pairs={{0,6},{1,7},{2,0},{3,1},{4,2},{5,3},{6,4},{7,5},{8,14},{9,15},{10,... | collective-permute-start | bytes 1179656 | tf_op jit(solution)/shard_map/ppermute | solution.py:59
  124.3 38.8 %slice-start = ((s8[8388608]{0:T(1024)(128)(4,1)}), s8[4194304]{0:T(1024)(128)(4,1)S(1)}, s32[]{:S(2)}) async-start(s8[8388608]{0:T(1024)(128)(4,1)} %bitcast.219), calls=%async_computation.4 | async-start | bytes 8388608
  133.3 11.9 %collective-permute-start.11 = (bf16[2,256,384]{2,1,0:T(8,128)(2,1)S(1)}, bf16[2,256,384]{2,1,0:T(8,128)(2,1)S(1)}, u32[]{:S(2)}, u32[]{:S(2)}) collective-permute-start(bf16[2,256,384]{2,1,0:T(8,128)(2,1)S(1)} %collective-permute-done.10), channel_id=1, source_target_pairs={{0,2},{1,3},{2,4},{3,5},{4,6},{5,7},{6,0},{7,1},{8,10},{9,11},{10,... | collective-permute-start | bytes 1179656 | tf_op jit(solution)/shard_map/ppermute | solution.py:59
  134.0 12.3 %collective-permute-start.14 = (bf16[2,256,384]{2,1,0:T(8,128)(2,1)S(1)}, bf16[2,256,384]{2,1,0:T(8,128)(2,1)S(1)}, u32[]{:S(2)}, u32[]{:S(2)}) collective-permute-start(bf16[2,256,384]{2,1,0:T(8,128)(2,1)S(1)} %collective-permute-done.13), channel_id=1, source_target_pairs={{0,6},{1,7},{2,0},{3,1},{4,2},{5,3},{6,4},{7,5},{8,14},{9,15},{10,... | collective-permute-start | bytes 1179656 | tf_op jit(solution)/shard_map/ppermute | solution.py:59
  145.2 7.8 %collective-permute-start.12 = (bf16[2,256,384]{2,1,0:T(8,128)(2,1)S(1)}, bf16[2,256,384]{2,1,0:T(8,128)(2,1)S(1)}, u32[]{:S(2)}, u32[]{:S(2)}) collective-permute-start(bf16[2,256,384]{2,1,0:T(8,128)(2,1)S(1)} %collective-permute-done.11), channel_id=1, source_target_pairs={{0,2},{1,3},{2,4},{3,5},{4,6},{5,7},{6,0},{7,1},{8,10},{9,11},{10,... | collective-permute-start | bytes 1179656 | tf_op jit(solution)/shard_map/ppermute | solution.py:59
  146.3 9.0 %collective-permute-start.15 = (bf16[2,256,384]{2,1,0:T(8,128)(2,1)S(1)}, bf16[2,256,384]{2,1,0:T(8,128)(2,1)S(1)}, u32[]{:S(2)}, u32[]{:S(2)}) collective-permute-start(bf16[2,256,384]{2,1,0:T(8,128)(2,1)S(1)} %collective-permute-done.14), channel_id=1, source_target_pairs={{0,6},{1,7},{2,0},{3,1},{4,2},{5,3},{6,4},{7,5},{8,14},{9,15},{10,... | collective-permute-start | bytes 1179656 | tf_op jit(solution)/shard_map/ppermute | solution.py:59
  147.3 15.9 %slice-start.1 = ((s8[8388608]{0:T(1024)(128)(4,1)}), s8[4194304]{0:T(1024)(128)(4,1)S(1)}, s32[]{:S(2)}) async-start(s8[8388608]{0:T(1024)(128)(4,1)} %bitcast.219), calls=%async_computation.5 | async-start | bytes 8388608
  155.7 5.7 %collective-permute-start.16 = (bf16[2,4,512,384]{3,2,1,0:T(8,128)(2,1)S(1)}, bf16[2,4,512,384]{3,2,1,0:T(8,128)(2,1)S(1)}, u32[]{:S(2)}, u32[]{:S(2)}) collective-permute-start(bf16[2,4,512,384]{3,2,1,0:T(8,128)(2,1)S(1)} %maximum_bitcast_fusion), channel_id=1, source_target_pairs={{0,1},{1,0},{2,3},{3,2},{4,5},{5,4},{6,7},{7,6},{8,9},{9,8},{10,11... | collective-permute-start | bytes 9437192 | tf_op jit(solution)/shard_map/ppermute | solution.py:94
  168.8 18.7 %all-to-all-start.1 = ((f32[8,64,384]{2,1,0:T(8,128)}), f32[8,64,384]{2,1,0:T(8,128)}, u32[]{:S(2)}, u32[]{:S(2)}) async-start(f32[8,64,384]{2,1,0:T(8,128)} %bitcast.225), calls=%async_computation.1 | async-start | bytes 1572864 | tf_op jit(solution)/shard_map/all_to_all | solution.py:197
  177.7 14.8 %copy-start.1 = (f32[64,384]{0,1:T(8,128)S(1)}, f32[64,384]{0,1:T(8,128)}, u32[]{:S(2)}) copy-start(f32[64,384]{0,1:T(8,128)} %broadcast_subtract_fusion) | copy-start | bytes 294916
  177.7 14.8 %copy-start.2 = (f32[64,384]{0,1:T(8,128)S(1)}, f32[64,384]{0,1:T(8,128)}, u32[]{:S(2)}) copy-start(f32[64,384]{0,1:T(8,128)} %multiply_bitcast_fusion) | copy-start | bytes 294916
  187.6 10.1 %all-to-all-start.3 = ((f32[8,6,384]{2,1,0:T(8,128)}), f32[8,6,384]{2,1,0:T(8,128)S(1)}, u32[]{:S(2)}, u32[]{:S(2)}) async-start(f32[8,6,384]{2,1,0:T(8,128)} %reshape.201), calls=%async_computation.3 | async-start | bytes 196608 | tf_op jit(solution)/shard_map/all_to_all | solution.py:198
  198.6 14.8 %all-to-all-start.2 = ((f32[8,64,384]{2,1,0:T(8,128)}), f32[8,64,384]{2,1,0:T(8,128)S(1)}, u32[]{:S(2)}, u32[]{:S(2)}) async-start(f32[8,64,384]{2,1,0:T(8,128)} %broadcast_in_dim.153), calls=%async_computation.2 | async-start | bytes 1572864 | tf_op jit(solution)/shard_map/all_to_all | solution.py:202
  (3 other events, 6.7 us)

commit v8 on v7

--- a/solution.py
+++ b/solution.py
@@ -194,9 +194,12 @@
     partial_rent = lax.dot_general(masked_keep, prices_keep, contract_w, preferred_element_type=jnp.float32)
     partial_rent = partial_rent + lax.dot_general(masked_send, prices_send, contract_w, preferred_element_type=jnp.float32)
 
-    gathered = lax.all_to_all(partial_grad.reshape(slab_axis, share_rows, scenarios), "br", 0, 0, tiled=True)
-    returned = lax.all_to_all(partial_rent.reshape(slab_axis, CAP, scenarios), "br", 0, 0, tiled=True)
-    gradient = jnp.sum(gathered, axis=0)
+    outgoing = jnp.concatenate(
+        [partial_grad.reshape(slab_axis, share_rows, scenarios), partial_rent.reshape(slab_axis, CAP, scenarios)], axis=1
+    )
+    gathered = lax.all_to_all(outgoing, "br", 0, 0, tiled=True)
+    gradient = jnp.sum(gathered[:, :share_rows], axis=0)
+    returned = gathered[:, share_rows:]
     trial = base - step_primal * gradient
     my_new = jnp.minimum(jnp.maximum(trial, lower), upper)
     new_injections = lax.all_to_all(

time: 215 us -> 206 us (0.958)
  blocking collectives: 0 us -> 20.6 us
  waiting for transfers between devices: 112 us -> 99.6 us
  starting transfers between devices: 38.8 us -> 28.9 us
  matrix products: 25.1 us -> 21.6 us
  local copies, waits for them, and re-layouts: 14.5 us -> 11.8 us
    all_to_all x0 -> x1, blocking collectives: none -> 20.6 us  [per_device(): gathered = lax.all_to_all(outgoing, 'br', 0, 0, tiled=True)]
    all_to_all x2 -> x0, waiting for transfers between devices: 12 us -> none  [the longest x1 7.06 us: per_device(): lax.all_to_all(partial_grad.reshape(slab_axis, share_rows, scenarios), 'b...]
    all_to_all x2 -> x0, starting transfers between devices: 9.98 us -> none  [the longest x1 6.35 us: per_device(): lax.all_to_all(partial_grad.reshape(slab_axis, share_rows, scenarios), 'b...]
  transfers between devices with their start and end apart: 21 -> 19, of which waited for: 18 -> 16; matrix products, arithmetic and copies ran while one was open for 19% -> 16% of each run, Pallas kernels for 0% -> 0%
where the time goes in v8:
time: 206 us; the launch traced here: 205 us
  waiting for transfers between devices  99.6 us (48%)
  starting transfers between devices  28.9 us (14%)
  other arithmetic  21.7 us (11%)
  matrix products  21.6 us (10%)
  blocking collectives  20.6 us (10%)
  local copies, waits for them, and re-layouts  11.8 us (6%)
    ppermute x6, waiting for transfers between devices, ring_scatter(): acc = lax.ppermute(acc, 'bus', perm) + more  31.4 us
    ppermute x6, waiting for transfers between devices, ring_gather(): cur = lax.ppermute(cur, 'bus', perm)  27 us
    all_to_all x1, blocking collectives, per_device(): gathered = lax.all_to_all(outgoing, 'br', 0, 0, tiled=True)  20.6 us
    dot_general x8, matrix products, flow_part(): return jnp.dot(rows, inject_half, preferred_element_type=jnp.float32)  15.5 us
    ppermute x1, waiting for transfers between devices, bus_pair_sum(): return pick(z, yh, 0) + lax.ppermute(pick(z, 1 - yh, 0), 'bus', Y_SWAP)  15 us
    all_to_all x1, waiting for transfers between devices, per_device(): lax.all_to_all(jnp.broadcast_to(my_new[None], (slab_axis, share_rows, sce...  8.98 us
    all_to_all x1, starting transfers between devices, per_device(): arrived_w = lax.all_to_all(outgoing_w, 'br', 0, 0, tiled=True)  6.45 us
    ppermute x6, starting transfers between devices, ring_scatter(): acc = lax.ppermute(acc, 'bus', perm) + more  6.22 us
  transfers between devices with their start and end apart: 19, of which 16 were waited for; matrix products, arithmetic and copies ran while one was open for 16% of the time, Pallas kernels for 0%

profile of v8, /device:TPU:6, one launch (start us, length us, event | category | flops | bytes accessed | tf_op | source)
XLA Modules:
  0.0 205.5 jit_solution(15788526696653787070)
XLA Ops:
  1.9 1.9 convolution_bitcast_fusion.5
  3.9 1.9 convolution_bitcast_fusion.4
  5.8 1.8 pad_maximum_fusion
  7.6 1.9 convolution_bitcast_fusion.1
  9.6 1.9 convolution_bitcast_fusion
  11.6 1.9 pad_maximum_fusion.1
  20.6 1.9 convolution_bitcast_fusion.3
  22.5 1.9 convolution_bitcast_fusion.7
  24.5 1.9 convolution_bitcast_fusion.6
  26.5 2.2 %maximum_add_fusion = f32[2,2,512,384]{3,2,1,0:T(8,128)S(1)} fusion(f32[2,2,512,384]{3,2,1,0:T(8,128)} %collective-permute-done, f32[1,2,512,384]{3,2,1,0:T(8,128)S(1)} %convolution_bitcast_fusion.6, f32[1,2,512,384]{3,2,1,0:T(8,128)S(1)} %convolution_bitcast_fusion.7), kind=kLoop, calls=%fused_computation.11 | loop fusion | flops 1572864 | bytes 9437184 | tf_op jit(solution)/shard_map/add | solution.py:72
  30.9 1.9 convolution_bitcast_fusion.2
  33.0 2.2 %maximum_add_fusion.1 = f32[2,2,512,384]{3,2,1,0:T(8,128)S(1)} fusion(f32[2,2,512,384]{3,2,1,0:T(8,128)} %collective-permute-done.2, f32[1,2,512,384]{3,2,1,0:T(8,128)S(1)} %convolution_bitcast_fusion.2, f32[1,2,512,384]{3,2,1,0:T(8,128)S(1)} %convolution_bitcast_fusion.3), kind=kLoop, calls=%fused_computation.13 | loop fusion | flops 1572864 | bytes 9437184 | tf_op jit(solution)/shard_map/add | solution.py:72
  35.2 13.2 %collective-permute-done.1 = f32[2,256,384]{2,1,0:T(8,128)S(1)} collective-permute-done((f32[2,256,384]{2,1,0:T(8,128)S(1)}, f32[2,256,384]{2,1,0:T(8,128)S(1)}, u32[]{:S(2)}, u32[]{:S(2)}) %collective-permute-start.1) | collective-permute-done | bytes 786464 | tf_op jit(solution)/shard_map/ppermute | solution.py:46
  53.4 14.8 %collective-permute-done.3 = f32[2,256,384]{2,1,0:T(8,128)S(1)} collective-permute-done((f32[2,256,384]{2,1,0:T(8,128)S(1)}, f32[2,256,384]{2,1,0:T(8,128)S(1)}, u32[]{:S(2)}, u32[]{:S(2)}) %collective-permute-start.3) | collective-permute-done | bytes 786464 | tf_op jit(solution)/shard_map/ppermute | solution.py:46
  71.3 1.7 collective-permute-start.7
  75.6 6.5 %all-to-all-start = ((bf16[8,6,512]{2,1,0:T(8,128)(2,1)}), bf16[8,6,512]{2,1,0:T(8,128)(2,1)S(1)}, u32[]{:S(2)}, u32[]{:S(2)}) async-start(bf16[8,6,512]{2,1,0:T(8,128)(2,1)} %copy.99), calls=%async_computation | async-start | bytes 131072 | tf_op jit(solution)/shard_map/all_to_all | solution.py:176
  82.8 5.6 %all-to-all-done = bf16[8,6,512]{2,1,0:T(8,128)(2,1)S(1)} async-done(((bf16[8,6,512]{2,1,0:T(8,128)(2,1)}), bf16[8,6,512]{2,1,0:T(8,128)(2,1)S(1)}, u32[]{:S(2)}, u32[]{:S(2)}) %all-to-all-start) | async-done | bytes 49184 | tf_op jit(solution)/shard_map/all_to_all | solution.py:176
  91.9 3.5 %collective-permute-start.8 = (f32[512,384]{1,0:T(8,128)S(1)}, f32[512,384]{1,0:T(8,128)}, u32[]{:S(2)}, u32[]{:S(2)}) collective-permute-start(f32[512,384]{1,0:T(8,128)S(1)} %dynamic-slice_bitcast_fusion), channel_id=1, source_target_pairs={{0,8},{1,9},{2,10},{3,11},{4,12},{5,13},{6,14},{7,15},{8,0},{9,1},... | collective-permute-start | bytes 2359304 | tf_op jit(solution)/shard_map/ppermute | solution.py:83
  95.4 15.0 %collective-permute-done.8 = f32[512,384]{1,0:T(8,128)} collective-permute-done((f32[512,384]{1,0:T(8,128)S(1)}, f32[512,384]{1,0:T(8,128)}, u32[]{:S(2)}, u32[]{:S(2)}) %collective-permute-start.8) | collective-permute-done | bytes 786464 | tf_op jit(solution)/shard_map/ppermute | solution.py:83
  110.4 2.2 %fusion.65 = (bf16[512,384]{1,0:T(8,128)(2,1)S(1)}, f32[512,384]{1,0:T(8,128)}) fusion(f32[512]{0:T(512)S(1)} %get-tuple-element.41, f32[512]{0:T(512)S(1)} %get-tuple-element.40, f32[512,384]{1,0:T(8,128)S(1)} %copy-done.2, f32[512,384]{1,0:T(8,128)} %collective-permute-done.8, f32[2,512,384]{2,1,0:T(8,128)S(1)} %pad_maximum_fusion.2, s32[]{:T(128)S(6)} %select_n.226), kind=kLoop, calls=%fused_computation.143 | loop fusion | flops 1376256 | bytes 3543044 | tf_op jit(solution)/shard_map/convert_element_type | solution.py:188
  112.6 3.2 %collective-permute-start.9 = (bf16[512,384]{1,0:T(8,128)(2,1)S(1)}, bf16[512,384]{1,0:T(8,128)(2,1)S(1)}, u32[]{:S(2)}, u32[]{:S(2)}) collective-permute-start(bf16[512,384]{1,0:T(8,128)(2,1)S(1)} %get-tuple-element.20), channel_id=1, source_target_pairs={{0,8},{1,9},{2,10},{3,11},{4,12},{5,13},{6,14},{7,15},{8,0},{9,1},... | collective-permute-start | bytes 1179656 | tf_op jit(solution)/shard_map/ppermute | solution.py:88
  115.9 6.0 %collective-permute-done.9 = bf16[512,384]{1,0:T(8,128)(2,1)S(1)} collective-permute-done((bf16[512,384]{1,0:T(8,128)(2,1)S(1)}, bf16[512,384]{1,0:T(8,128)(2,1)S(1)}, u32[]{:S(2)}, u32[]{:S(2)}) %collective-permute-start.9) | collective-permute-done | bytes 393248 | tf_op jit(solution)/shard_map/ppermute | solution.py:88
  124.7 8.5 %collective-permute-done.10 = bf16[2,256,384]{2,1,0:T(8,128)(2,1)S(1)} collective-permute-done((bf16[2,256,384]{2,1,0:T(8,128)(2,1)S(1)}, bf16[2,256,384]{2,1,0:T(8,128)(2,1)S(1)}, u32[]{:S(2)}, u32[]{:S(2)}) %collective-permute-start.10) | collective-permute-done | bytes 393248 | tf_op jit(solution)/shard_map/ppermute | solution.py:59
  135.4 9.7 %collective-permute-done.11 = bf16[2,256,384]{2,1,0:T(8,128)(2,1)S(1)} collective-permute-done((bf16[2,256,384]{2,1,0:T(8,128)(2,1)S(1)}, bf16[2,256,384]{2,1,0:T(8,128)(2,1)S(1)}, u32[]{:S(2)}, u32[]{:S(2)}) %collective-permute-start.11) | collective-permute-done | bytes 393248 | tf_op jit(solution)/shard_map/ppermute | solution.py:59
  147.3 5.6 %collective-permute-done.12 = bf16[2,256,384]{2,1,0:T(8,128)(2,1)S(1)} collective-permute-done((bf16[2,256,384]{2,1,0:T(8,128)(2,1)S(1)}, bf16[2,256,384]{2,1,0:T(8,128)(2,1)S(1)}, u32[]{:S(2)}, u32[]{:S(2)}) %collective-permute-start.12) | collective-permute-done | bytes 393248 | tf_op jit(solution)/shard_map/ppermute | solution.py:59
  153.0 2.3 %collective-permute-done.15 = bf16[2,256,384]{2,1,0:T(8,128)(2,1)S(1)} collective-permute-done((bf16[2,256,384]{2,1,0:T(8,128)(2,1)S(1)}, bf16[2,256,384]{2,1,0:T(8,128)(2,1)S(1)}, u32[]{:S(2)}, u32[]{:S(2)}) %collective-permute-start.15) | collective-permute-done | bytes 393248 | tf_op jit(solution)/shard_map/ppermute | solution.py:59
  155.8 5.6 %collective-permute-done.16 = bf16[2,4,512,384]{3,2,1,0:T(8,128)(2,1)S(1)} collective-permute-done((bf16[2,4,512,384]{3,2,1,0:T(8,128)(2,1)S(1)}, bf16[2,4,512,384]{3,2,1,0:T(8,128)(2,1)S(1)}, u32[]{:S(2)}, u32[]{:S(2)}) %collective-permute-start.16) | collective-permute-done | bytes 3145760 | tf_op jit(solution)/shard_map/ppermute | solution.py:94
  161.4 2.4 %fusion.9 = f32[512,384]{1,0:T(8,128)S(1)} fusion(bf16[2,4,512,384]{3,2,1,0:T(8,128)(2,1)S(1)} %collective-permute-done.16, bf16[2,4,2,512,512]{4,3,2,1,0:T(8,128)(2,1)S(1)} %bitcast.221, s32[]{:T(128)S(6)} %select_n.209), kind=kOutput, calls=%fused_computation.26 | convolution fusion | flops 1610612736 | bytes 8126468 | tf_op jit(solution)/shard_map/dot_general | solution.py:192
  163.8 2.4 %fusion.12 = f32[512,384]{1,0:T(8,128)S(1)} fusion(f32[512,384]{1,0:T(8,128)S(1)} %fusion.9, bf16[2,4,2,512,512]{4,3,2,1,0:T(8,128)(2,1)S(1)} %bitcast.222, s32[]{:T(128)S(6)} %select_n.204, bf16[4,2,256,384]{3,2,0,1:T(8,128)(2,1)S(1)} %bitcast_dynamic-update-slice_fusion.7, bf16[4,2,256,384]{3,2,0,1:T(8,128)(2,1)S(1)} %bitcast_dynamic-update-slice_fusion.3), kind=kOutput, calls=%fused_computation.27 | convolution fusion | flops 1617100800 | bytes 8912900 | tf_op jit(solution)/shard_map/dot_general | solution.py:191
  167.9 20.6 %all_to_all.15 = f32[8,70,384]{2,1,0:T(8,128)S(1)} all-to-all(f32[8,70,384]{2,1,0:T(8,128)S(1)} %pad_maximum_fusion.3), channel_id=1, replica_groups=mesh['br'=8,'bus'=16] {'br'}, dimensions={0} | all-to-all | bytes 1720320 | tf_op jit(solution)/shard_map/all_to_all | solution.py:200
  189.8 3.5 %all-to-all-start.2 = ((f32[8,64,384]{2,1,0:T(8,128)}), f32[8,64,384]{2,1,0:T(8,128)S(1)}, u32[]{:S(2)}, u32[]{:S(2)}) async-start(f32[8,64,384]{2,1,0:T(8,128)} %broadcast_in_dim.153), calls=%async_computation.2 | async-start | bytes 1572864 | tf_op jit(solution)/shard_map/all_to_all | solution.py:205
  195.6 9.0 %all-to-all-done.2 = f32[8,64,384]{2,1,0:T(8,128)S(1)} async-done(((f32[8,64,384]{2,1,0:T(8,128)}), f32[8,64,384]{2,1,0:T(8,128)S(1)}, u32[]{:S(2)}, u32[]{:S(2)}) %all-to-all-start.2) | async-done | bytes 786464 | tf_op jit(solution)/shard_map/all_to_all | solution.py:205
  (135 shorter events, 39.1 us)
Async XLA Ops:
  7.6 18.9 %collective-permute-start = (f32[2,2,512,384]{3,2,1,0:T(8,128)}, f32[2,2,512,384]{3,2,1,0:T(8,128)}, u32[]{:S(2)}, u32[]{:S(2)}) collective-permute-start(f32[2,2,512,384]{3,2,1,0:T(8,128)} %pad_maximum_fusion), channel_id=1, source_target_pairs={{0,1},{1,0},{2,3},{3,2},{4,5},{5,4},{6,7},{7,6},{8,9},{9,8},{10,11... | collective-permute-start | bytes 9437192 | tf_op jit(solution)/shard_map/ppermute | solution.py:72
  11.5 2.5 %copy-start.7 = (s32[1024,3]{0,1:T(4,128)S(1)}, s32[1024,3]{0,1:T(4,128)}, u32[]{:S(2)}) copy-start(s32[1024,3]{0,1:T(4,128)} %param.25) | copy-start | bytes 36868
  11.5 2.9 %copy-start.6 = (bf16[8,1536]{1,0:T(8,128)(2,1)S(1)}, bf16[8,1536]{1,0:T(8,128)(2,1)}, u32[]{:S(2)}) copy-start(bf16[8,1536]{1,0:T(8,128)(2,1)} %param.27) | copy-start | bytes 73732
  11.5 2.9 %copy-start.8 = (s32[1024,3]{0,1:T(4,128)S(1)}, s32[1024,3]{0,1:T(4,128)}, u32[]{:S(2)}) copy-start(s32[1024,3]{0,1:T(4,128)} %param.26) | copy-start | bytes 36868
  11.5 5.3 %copy-start.4 = (f32[64,1024]{1,0:T(8,128)S(1)}, f32[64,1024]{1,0:T(8,128)}, u32[]{:S(2)}) copy-start(f32[64,1024]{1,0:T(8,128)} %param.22) | copy-start | bytes 786436
  13.5 19.5 %collective-permute-start.2 = (f32[2,2,512,384]{3,2,1,0:T(8,128)}, f32[2,2,512,384]{3,2,1,0:T(8,128)}, u32[]{:S(2)}, u32[]{:S(2)}) collective-permute-start(f32[2,2,512,384]{3,2,1,0:T(8,128)} %pad_maximum_fusion.1), channel_id=1, source_target_pairs={{0,1},{1,0},{2,3},{3,2},{4,5},{5,4},{6,7},{7,6},{8,9},{9,8},{10,11... | collective-permute-start | bytes 9437192 | tf_op jit(solution)/shard_map/ppermute | solution.py:72
  14.4 10.1 %copy-start.5 = (s32[128,24]{1,0:T(8,128)}, s32[128,24]{1,0:T(8,128)S(1)}, u32[]{:S(2)}) copy-start(s32[128,24]{1,0:T(8,128)S(1)} %reshape.196) | copy-start | bytes 36868
  22.5 3.9 %copy-start.9 = (s32[384]{0:T(512)S(1)}, s32[384]{0:T(512)}, u32[]{:S(2)}) copy-start(s32[384]{0:T(512)} %param.24) | copy-start | bytes 4612
  28.8 19.5 %collective-permute-start.1 = (f32[2,256,384]{2,1,0:T(8,128)S(1)}, f32[2,256,384]{2,1,0:T(8,128)S(1)}, u32[]{:S(2)}, u32[]{:S(2)}) collective-permute-start(f32[2,256,384]{2,1,0:T(8,128)S(1)} %get-tuple-element.32), channel_id=1, source_target_pairs={{0,2},{1,3},{2,4},{3,5},{4,6},{5,7},{6,0},{7,1},{8,10},{9,11},{10,... | collective-permute-start | bytes 2359304 | tf_op jit(solution)/shard_map/ppermute | solution.py:46
  29.3 20.4 %collective-permute-start.5 = (f32[2,256,384]{2,1,0:T(8,128)S(1)}, f32[2,256,384]{2,1,0:T(8,128)S(1)}, u32[]{:S(2)}, u32[]{:S(2)}) collective-permute-start(f32[2,256,384]{2,1,0:T(8,128)S(1)} %get-tuple-element.33), channel_id=1, source_target_pairs={{0,6},{1,7},{2,0},{3,1},{4,2},{5,3},{6,4},{7,5},{8,14},{9,15},{10,... | collective-permute-start | bytes 2359304 | tf_op jit(solution)/shard_map/ppermute | solution.py:46
  49.8 18.4 %collective-permute-start.3 = (f32[2,256,384]{2,1,0:T(8,128)S(1)}, f32[2,256,384]{2,1,0:T(8,128)S(1)}, u32[]{:S(2)}, u32[]{:S(2)}) collective-permute-start(f32[2,256,384]{2,1,0:T(8,128)S(1)} %get-tuple-element.12), channel_id=1, source_target_pairs={{0,2},{1,3},{2,4},{3,5},{4,6},{5,7},{6,0},{7,1},{8,10},{9,11},{10,... | collective-permute-start | bytes 2359304 | tf_op jit(solution)/shard_map/ppermute | solution.py:46
  50.3 19.4 %collective-permute-start.6 = (f32[2,256,384]{2,1,0:T(8,128)S(1)}, f32[2,256,384]{2,1,0:T(8,128)S(1)}, u32[]{:S(2)}, u32[]{:S(2)}) collective-permute-start(f32[2,256,384]{2,1,0:T(8,128)S(1)} %get-tuple-element.31), channel_id=1, source_target_pairs={{0,6},{1,7},{2,0},{3,1},{4,2},{5,3},{6,4},{7,5},{8,14},{9,15},{10,... | collective-permute-start | bytes 2359304 | tf_op jit(solution)/shard_map/ppermute | solution.py:46
  71.1 18.4 %collective-permute-start.4 = (f32[2,256,384]{2,1,0:T(8,128)}, f32[2,256,384]{2,1,0:T(8,128)}, u32[]{:S(2)}, u32[]{:S(2)}) collective-permute-start(f32[2,256,384]{2,1,0:T(8,128)} %get-tuple-element.28), channel_id=1, source_target_pairs={{0,2},{1,3},{2,4},{3,5},{4,6},{5,7},{6,0},{7,1},{8,10},{9,11},{10,... | collective-permute-start | bytes 2359304 | tf_op jit(solution)/shard_map/ppermute | solution.py:46
  71.3 18.9 %collective-permute-start.7 = (f32[2,256,384]{2,1,0:T(8,128)}, f32[2,256,384]{2,1,0:T(8,128)}, u32[]{:S(2)}, u32[]{:S(2)}) collective-permute-start(f32[2,256,384]{2,1,0:T(8,128)} %get-tuple-element.29), channel_id=1, source_target_pairs={{0,6},{1,7},{2,0},{3,1},{4,2},{5,3},{6,4},{7,5},{8,14},{9,15},{10,... | collective-permute-start | bytes 2359304 | tf_op jit(solution)/shard_map/ppermute | solution.py:46
  75.6 12.8 %all-to-all-start = ((bf16[8,6,512]{2,1,0:T(8,128)(2,1)}), bf16[8,6,512]{2,1,0:T(8,128)(2,1)S(1)}, u32[]{:S(2)}, u32[]{:S(2)}) async-start(bf16[8,6,512]{2,1,0:T(8,128)(2,1)} %copy.99), calls=%async_computation | async-start | bytes 131072 | tf_op jit(solution)/shard_map/all_to_all | solution.py:176
  91.7 3.7 %copy-start.10 = (f32[512]{0:T(512)S(1)}, f32[512]{0:T(512)}, u32[]{:S(2)}) copy-start(f32[512]{0:T(512)} %param.18) | copy-start | bytes 6148
  91.8 18.7 %copy-start.2 = (f32[512,384]{1,0:T(8,128)S(1)}, f32[512,384]{1,0:T(8,128)}, u32[]{:S(2)}) copy-start(f32[512,384]{1,0:T(8,128)} %param.17) | copy-start | bytes 2359300
  91.9 18.5 %collective-permute-start.8 = (f32[512,384]{1,0:T(8,128)S(1)}, f32[512,384]{1,0:T(8,128)}, u32[]{:S(2)}, u32[]{:S(2)}) collective-permute-start(f32[512,384]{1,0:T(8,128)S(1)} %dynamic-slice_bitcast_fusion), channel_id=1, source_target_pairs={{0,8},{1,9},{2,10},{3,11},{4,12},{5,13},{6,14},{7,15},{8,0},{9,1},... | collective-permute-start | bytes 2359304 | tf_op jit(solution)/shard_map/ppermute | solution.py:83
  112.6 9.3 %collective-permute-start.9 = (bf16[512,384]{1,0:T(8,128)(2,1)S(1)}, bf16[512,384]{1,0:T(8,128)(2,1)S(1)}, u32[]{:S(2)}, u32[]{:S(2)}) collective-permute-start(bf16[512,384]{1,0:T(8,128)(2,1)S(1)} %get-tuple-element.20), channel_id=1, source_target_pairs={{0,8},{1,9},{2,10},{3,11},{4,12},{5,13},{6,14},{7,15},{8,0},{9,1},... | collective-permute-start | bytes 1179656 | tf_op jit(solution)/shard_map/ppermute | solution.py:88
  122.2 11.1 %collective-permute-start.10 = (bf16[2,256,384]{2,1,0:T(8,128)(2,1)S(1)}, bf16[2,256,384]{2,1,0:T(8,128)(2,1)S(1)}, u32[]{:S(2)}, u32[]{:S(2)}) collective-permute-start(bf16[2,256,384]{2,1,0:T(8,128)(2,1)S(1)} %get-tuple-element.34), channel_id=1, source_target_pairs={{0,2},{1,3},{2,4},{3,5},{4,6},{5,7},{6,0},{7,1},{8,10},{9,11},{10,... | collective-permute-start | bytes 1179656 | tf_op jit(solution)/shard_map/ppermute | solution.py:59
  122.8 11.2 %collective-permute-start.13 = (bf16[2,256,384]{2,1,0:T(8,128)(2,1)S(1)}, bf16[2,256,384]{2,1,0:T(8,128)(2,1)S(1)}, u32[]{:S(2)}, u32[]{:S(2)}) collective-permute-start(bf16[2,256,384]{2,1,0:T(8,128)(2,1)S(1)} %get-tuple-element.35), channel_id=1, source_target_pairs={{0,6},{1,7},{2,0},{3,1},{4,2},{5,3},{6,4},{7,5},{8,14},{9,15},{10,... | collective-permute-start | bytes 1179656 | tf_op jit(solution)/shard_map/ppermute | solution.py:59
  124.3 37.2 %slice-start = ((s8[8388608]{0:T(1024)(128)(4,1)}), s8[4194304]{0:T(1024)(128)(4,1)S(1)}, s32[]{:S(2)}) async-start(s8[8388608]{0:T(1024)(128)(4,1)} %bitcast.219), calls=%async_computation.3 | async-start | bytes 8388608
  133.2 11.9 %collective-permute-start.11 = (bf16[2,256,384]{2,1,0:T(8,128)(2,1)S(1)}, bf16[2,256,384]{2,1,0:T(8,128)(2,1)S(1)}, u32[]{:S(2)}, u32[]{:S(2)}) collective-permute-start(bf16[2,256,384]{2,1,0:T(8,128)(2,1)S(1)} %collective-permute-done.10), channel_id=1, source_target_pairs={{0,2},{1,3},{2,4},{3,5},{4,6},{5,7},{6,0},{7,1},{8,10},{9,11},{10,... | collective-permute-start | bytes 1179656 | tf_op jit(solution)/shard_map/ppermute | solution.py:59
  134.0 12.3 %collective-permute-start.14 = (bf16[2,256,384]{2,1,0:T(8,128)(2,1)S(1)}, bf16[2,256,384]{2,1,0:T(8,128)(2,1)S(1)}, u32[]{:S(2)}, u32[]{:S(2)}) collective-permute-start(bf16[2,256,384]{2,1,0:T(8,128)(2,1)S(1)} %collective-permute-done.13), channel_id=1, source_target_pairs={{0,6},{1,7},{2,0},{3,1},{4,2},{5,3},{6,4},{7,5},{8,14},{9,15},{10,... | collective-permute-start | bytes 1179656 | tf_op jit(solution)/shard_map/ppermute | solution.py:59
  145.1 7.8 %collective-permute-start.12 = (bf16[2,256,384]{2,1,0:T(8,128)(2,1)S(1)}, bf16[2,256,384]{2,1,0:T(8,128)(2,1)S(1)}, u32[]{:S(2)}, u32[]{:S(2)}) collective-permute-start(bf16[2,256,384]{2,1,0:T(8,128)(2,1)S(1)} %collective-permute-done.11), channel_id=1, source_target_pairs={{0,2},{1,3},{2,4},{3,5},{4,6},{5,7},{6,0},{7,1},{8,10},{9,11},{10,... | collective-permute-start | bytes 1179656 | tf_op jit(solution)/shard_map/ppermute | solution.py:59
  146.3 9.0 %collective-permute-start.15 = (bf16[2,256,384]{2,1,0:T(8,128)(2,1)S(1)}, bf16[2,256,384]{2,1,0:T(8,128)(2,1)S(1)}, u32[]{:S(2)}, u32[]{:S(2)}) collective-permute-start(bf16[2,256,384]{2,1,0:T(8,128)(2,1)S(1)} %collective-permute-done.14), channel_id=1, source_target_pairs={{0,6},{1,7},{2,0},{3,1},{4,2},{5,3},{6,4},{7,5},{8,14},{9,15},{10,... | collective-permute-start | bytes 1179656 | tf_op jit(solution)/shard_map/ppermute | solution.py:59
  147.2 14.2 %slice-start.1 = ((s8[8388608]{0:T(1024)(128)(4,1)}), s8[4194304]{0:T(1024)(128)(4,1)S(1)}, s32[]{:S(2)}) async-start(s8[8388608]{0:T(1024)(128)(4,1)} %bitcast.219), calls=%async_computation.4 | async-start | bytes 8388608
  155.7 5.7 %collective-permute-start.16 = (bf16[2,4,512,384]{3,2,1,0:T(8,128)(2,1)S(1)}, bf16[2,4,512,384]{3,2,1,0:T(8,128)(2,1)S(1)}, u32[]{:S(2)}, u32[]{:S(2)}) collective-permute-start(bf16[2,4,512,384]{3,2,1,0:T(8,128)(2,1)S(1)} %maximum_bitcast_fusion), channel_id=1, source_target_pairs={{0,1},{1,0},{2,3},{3,2},{4,5},{5,4},{6,7},{7,6},{8,9},{9,8},{10,11... | collective-permute-start | bytes 9437192 | tf_op jit(solution)/shard_map/ppermute | solution.py:94
  166.2 1.0 copy-start.3
  167.8 20.9 %copy-start = (f32[64,384]{0,1:T(8,128)S(1)}, f32[64,384]{0,1:T(8,128)}, u32[]{:S(2)}) copy-start(f32[64,384]{0,1:T(8,128)} %broadcast_subtract_fusion) | copy-start | bytes 294916
  167.8 20.9 %copy-start.1 = (f32[64,384]{0,1:T(8,128)S(1)}, f32[64,384]{0,1:T(8,128)}, u32[]{:S(2)}) copy-start(f32[64,384]{0,1:T(8,128)} %multiply_bitcast_fusion) | copy-start | bytes 294916
  189.8 14.8 %all-to-all-start.2 = ((f32[8,64,384]{2,1,0:T(8,128)}), f32[8,64,384]{2,1,0:T(8,128)S(1)}, u32[]{:S(2)}, u32[]{:S(2)}) async-start(f32[8,64,384]{2,1,0:T(8,128)} %broadcast_in_dim.153), calls=%async_computation.2 | async-start | bytes 1572864 | tf_op jit(solution)/shard_map/all_to_all | solution.py:205

commit v9 on v8

--- a/solution.py
+++ b/solution.py
@@ -61,19 +61,27 @@
     return out
 
 
-def bus_reduce_scatter(flow_part, rider):
+def bus_reduce_scatter(flow_rows, inj, rider):
     yh, xi, c = bus_place()
-    first = [(xi - 1) % XR, (xi + 1) % XR]
-    second = [(xi + 2) % XR, xi]
-    summed = []
-    for group in (first, second):
-        send = jnp.stack([flow_part(x, False) for x in group])
-        keep = jnp.stack([flow_part(x, True) for x in group])
-        summed.append(keep + lax.ppermute(send, "bus", CORE_SWAP))
-    a, b = summed
-    half = a.shape[2] // 2
-    cw, rider = ring_scatter([a[0, :, :half], b[0, :, :half], a[1, :, :half], b[1, :, :half]], True, rider)
-    ccw, _ = ring_scatter([a[1, :, half:], b[0, :, half:], a[0, :, half:], b[1, :, half:]], False)
+    up, down, across = (xi + 1) % XR, (xi - 1) % XR, (xi + 2) % XR
+
+    def exchanged(pieces, inj):
+        return flow_rows(pieces, True, inj) + lax.ppermute(flow_rows(pieces, False, inj), "bus", CORE_SWAP)
+
+    half = BLOCK // 2
+    lead = [(down, 0, half), (up, half, half)]
+    lead_send = flow_rows(lead, False, inj)
+    lead_send, inj_second = lax.optimization_barrier((lead_send, inj))
+    first = flow_rows(lead, True, inj) + lax.ppermute(lead_send, "bus", CORE_SWAP)
+    second = exchanged([(across, 0, BLOCK)], inj_second)
+    first, inj_rest = lax.optimization_barrier((first, inj))
+    rest = exchanged([(up, 0, half), (down, half, half), (xi, 0, BLOCK)], inj_rest)
+    cw, rider = ring_scatter(
+        [first[:, :half], second[:, :half], rest[:, :half], rest[:, 2 * half:3 * half]], True, rider
+    )
+    ccw, _ = ring_scatter(
+        [first[:, half:], second[:, half:], rest[:, half:2 * half], rest[:, 3 * half:]], False
+    )
     z = jnp.concatenate([cw, ccw], axis=1)
     return z, rider
 
@@ -168,11 +176,13 @@
     sf_keep = pick(by_place, core, 2)
     sf_send = pick(by_place, 1 - core, 2)
 
-    def flow_part(x, mine):
-        rows = pick(sf_keep if mine else sf_send, x, 1)
-        return jnp.dot(rows, inject_half, preferred_element_type=jnp.float32)
-
-    ring_out, outgoing_w = bus_reduce_scatter(flow_part, outgoing_w)
+    def flow_rows(pieces, mine, inj):
+        own = sf_keep if mine else sf_send
+        rows = [lax.dynamic_slice_in_dim(pick(own, x, 1), r0, n, 1) for x, r0, n in pieces]
+        rows = rows[0] if len(rows) == 1 else jnp.concatenate(rows, axis=1)
+        return jnp.dot(rows, inj, preferred_element_type=jnp.float32)
+
+    ring_out, outgoing_w = bus_reduce_scatter(flow_rows, inject_half, outgoing_w)
     arrived_w = lax.all_to_all(outgoing_w, "br", 0, 0, tiled=True)
     masked = jnp.where(block_hot[:, :, :, None], arrived_w[:, :, None, :], jnp.zeros((), jnp.bfloat16))
     masked = masked.reshape(slab_axis * CAP, YHI, XR, CORES, -1)

time: 206 us -> 214 us (1.039)
  local copies, waits for them, and re-layouts: 11.8 us -> 24.4 us
  waiting for transfers between devices: 99.6 us -> 93.3 us
    ppermute x6, waiting for transfers between devices: 31.4 us -> 25.9 us  [ring_scatter(): acc = lax.ppermute(acc, 'bus', perm) + more]
    squeeze x2 -> x3, local copies, waits for them, and re-layouts: 0.92 us -> 5.65 us  [pick(): return lax.dynamic_index_in_dim(a, i, axis, keepdims=False)]
    add x2 -> x0, other arithmetic: 4.4 us -> none  [bus_reduce_scatter(): summed.append(keep + lax.ppermute(send, 'bus', CORE_SWAP))]
    another operation x2 -> x0, other arithmetic: 3.76 us -> none  [bus_reduce_scatter(): send = jnp.stack([flow_part(x, False) for x in group])]
    add x3, other arithmetic: 3.06 us -> 5.54 us  [ring_scatter(): acc = lax.ppermute(acc, 'bus', perm) + more]
    dot_general x8 -> x6, matrix products: 15.5 us -> 16.6 us  [flow_rows(): return jnp.dot(rows, inj, preferred_element_type=jnp.float32)]
  transfers between devices with their start and end apart: 19 -> 20, of which waited for: 16 -> 16; matrix products, arithmetic and copies ran while one was open for 16% -> 21% of each run, Pallas kernels for 0% -> 0%
where the time goes in v9:
time: 214 us; the launch traced here: 213 us
  waiting for transfers between devices  93.3 us (44%)
  starting transfers between devices  28.8 us (13%)
  local copies, waits for them, and re-layouts  24.4 us (11%)
  matrix products  23.4 us (11%)
  other arithmetic  20.8 us (10%)
  blocking collectives  20.6 us (10%)
    ppermute x6, waiting for transfers between devices, ring_scatter(): acc = lax.ppermute(acc, 'bus', perm) + more  25.9 us
    ppermute x6, waiting for transfers between devices, ring_gather(): cur = lax.ppermute(cur, 'bus', perm)  25.6 us
    all_to_all x1, blocking collectives, per_device(): gathered = lax.all_to_all(outgoing, 'br', 0, 0, tiled=True)  20.6 us
    dot_general x6, matrix products, flow_rows(): return jnp.dot(rows, inj, preferred_element_type=jnp.float32)  16.6 us
    ppermute x1, waiting for transfers between devices, bus_pair_sum(): return pick(z, yh, 0) + lax.ppermute(pick(z, 1 - yh, 0), 'bus', Y_SWAP)  15.4 us
    all_to_all x1, waiting for transfers between devices, per_device(): lax.all_to_all(jnp.broadcast_to(my_new[None], (slab_axis, share_rows, sce...  8.96 us
    all_to_all x1, starting transfers between devices, per_device(): arrived_w = lax.all_to_all(outgoing_w, 'br', 0, 0, tiled=True)  6.45 us
    ppermute x1, waiting for transfers between devices, bus_all_gather(): other = lax.ppermute(p, 'bus', Y_SWAP)  6.11 us
  transfers between devices with their start and end apart: 20, of which 16 were waited for; matrix products, arithmetic and copies ran while one was open for 21% of the time, Pallas kernels for 0%

profile of v9, /device:TPU:6, one launch (start us, length us, event | category | flops | bytes accessed | tf_op | source)
XLA Modules:
  0.0 212.5 jit_solution(7714426950663362638)
XLA Ops:
  1.9 4.8 %dynamic-slice_bitcast_fusion.1 = (bf16[2,512,512]{2,1,0:T(8,128)(2,1)}, bf16[2,512,512]{2,1,0:T(8,128)(2,1)}, bf16[2,512,512]{2,1,0:T(8,128)(2,1)S(1)}, bf16[2,...) fusion(bf16[2,4,2,512,512]{4,3,2,1,0:T(8,128)(2,1)} %bitcast.159, ...), kind=kLoop, calls=%fused_computation.46 | loop fusion | bytes 12582932 | tf_op jit(solution)/shard_map/jit(dynamic_index_in_dim)/squeeze | solution.py:39
  7.6 1.9 fusion.34
  9.5 3.1 %fusion.38 = f32[2,512,384]{2,1,0:T(8,128)} fusion(bf16[2,4,2,512,512]{4,3,2,1,0:T(8,128)(2,1)} %bitcast.160, s32[]{:T(128)S(6)} %select_n.217, s32[]{:T(128)S(6)} %select_n.214, bf16[512,384]{1,0:T(8,128)(2,1)S(1)} %convert_element_type.16), kind=kOutput, calls=%fused_computation.42 | convolution fusion | flops 402653184 | bytes 3014664 | tf_op jit(solution)/shard_map/dot_general | solution.py:183
  23.2 2.2 %convolution_add_fusion.1 = f32[2,512,384]{2,1,0:T(8,128)S(1)} fusion(f32[2,512,384]{2,1,0:T(8,128)} %collective-permute-done, bf16[2,256,512]{2,1,0:T(8,128)(2,1)S(1)} %get-tuple-element.49, bf16[2,256,512]{2,1,0:T(8,128)(2,1)S(1)} %get-tuple-element.64, bf16[512,384]{1,0:T(8,128)(2,1)S(1)} %convert_element_type.16), kind=kOutput, calls=%fused_computation.27 | convolution fusion | flops 405143552 | bytes 4587520 | tf_op jit(solution)/shard_map/dot_general | solution.py:183
  25.4 2.9 %fusion.12 = f32[2,1024,384]{2,1,0:T(8,128)} fusion(bf16[2,512,512]{2,1,0:T(8,128)(2,1)S(1)} %copy-done.1, bf16[2,256,512]{2,1,0:T(8,128)(2,1)S(1)} %copy-done.5, bf16[2,256,512]{2,1,0:T(8,128)(2,1)S(1)} %get-tuple-element.52, bf16[512,384]{1,0:T(8,128)(2,1)S(1)} %convert_element_type.16), kind=kOutput, calls=%fused_computation.18 | convolution fusion | flops 811597824 | bytes 5636096 | tf_op jit(solution)/shard_map/dot_general | solution.py:183
  32.5 1.7 collective-permute-start.6
  37.9 2.5 %convolution_add_fusion = f32[2,512,384]{2,1,0:T(8,128)S(1)} fusion(f32[2,512,384]{2,1,0:T(8,128)} %collective-permute-done.2, bf16[2,4,2,512,512]{4,3,2,1,0:T(8,128)(2,1)} %bitcast.161, s32[]{:T(128)S(6)} %select_n.217, s32[]{:T(128)S(6)} %select_n.209, bf16[512,384]{1,0:T(8,128)(2,1)S(1)} %convert_element_type.16), kind=kOutput, calls=%fused_computation.26 | convolution fusion | flops 403046400 | bytes 4587528 | tf_op jit(solution)/shard_map/dot_general | solution.py:183
  40.4 11.9 %collective-permute-done.1 = f32[2,256,384]{2,1,0:T(8,128)S(1)} collective-permute-done((f32[2,256,384]{2,1,0:T(8,128)}, f32[2,256,384]{2,1,0:T(8,128)S(1)}, u32[]{:S(2)}, u32[]{:S(2)}) %collective-permute-start.1) | collective-permute-done | bytes 786464 | tf_op jit(solution)/shard_map/ppermute | solution.py:46
  55.2 1.5 collective-permute-start.7
  60.1 3.9 %fusion.18 = f32[2,1024,384]{2,1,0:T(8,128)S(1)} fusion(f32[2,1024,384]{2,1,0:T(8,128)} %collective-permute-done.4, bf16[2,512,512]{2,1,0:T(8,128)(2,1)} %get-tuple-element.34, bf16[2,256,512]{2,1,0:T(8,128)(2,1)} %get-tuple-element.65, bf16[2,256,512]{2,1,0:T(8,128)(2,1)} %get-tuple-element.48, bf16[512,384]{1,0:T(8,128)(2,1)} %copy-done), kind=kOutput, calls=%fused_computation.24 | convolution fusion | flops 812384256 | bytes 8781824 | tf_op jit(solution)/shard_map/dot_general | solution.py:183
  64.0 9.8 %collective-permute-done.3 = f32[2,256,384]{2,1,0:T(8,128)} collective-permute-done((f32[2,256,384]{2,1,0:T(8,128)}, f32[2,256,384]{2,1,0:T(8,128)}, u32[]{:S(2)}, u32[]{:S(2)}) %collective-permute-start.3) | collective-permute-done | bytes 786464 | tf_op jit(solution)/shard_map/ppermute | solution.py:46
  73.8 1.7 collective-permute-done.7
  75.5 2.7 %slice_add_fusion.4 = (f32[2,256,384]{2,1,0:T(8,128)}, f32[2,256,384]{2,1,0:T(8,128)}) fusion(f32[2,256,384]{2,1,0:T(8,128)} %collective-permute-done.3, f32[2,1024,384]{2,1,0:T(8,128)S(1)} %fusion.18, f32[2,256,384]{2,1,0:T(8,128)} %collective-permute-done.7), kind=kLoop, calls=%fused_computation.59 | loop fusion | flops 393216 | bytes 4718592 | tf_op jit(solution)/shard_map/add | solution.py:46
  78.5 1.7 collective-permute-start.8
  82.8 6.4 %all-to-all-start = ((bf16[8,6,512]{2,1,0:T(8,128)(2,1)}), bf16[8,6,512]{2,1,0:T(8,128)(2,1)S(1)}, u32[]{:S(2)}, u32[]{:S(2)}) async-start(bf16[8,6,512]{2,1,0:T(8,128)(2,1)} %copy.99), calls=%async_computation | async-start | bytes 131072 | tf_op jit(solution)/shard_map/all_to_all | solution.py:186
  90.0 5.6 %all-to-all-done = bf16[8,6,512]{2,1,0:T(8,128)(2,1)S(1)} async-done(((bf16[8,6,512]{2,1,0:T(8,128)(2,1)}), bf16[8,6,512]{2,1,0:T(8,128)(2,1)S(1)}, u32[]{:S(2)}, u32[]{:S(2)}) %all-to-all-start) | async-done | bytes 49184 | tf_op jit(solution)/shard_map/all_to_all | solution.py:186
  98.0 1.5 slice_add_fusion.3
  99.7 3.5 %collective-permute-start.9 = (f32[512,384]{1,0:T(8,128)S(1)}, f32[512,384]{1,0:T(8,128)}, u32[]{:S(2)}, u32[]{:S(2)}) collective-permute-start(f32[512,384]{1,0:T(8,128)S(1)} %dynamic-slice_bitcast_fusion.6), channel_id=1, source_target_pairs={{0,8},{1,9},{2,10},{3,11},{4,12},{5,13},{6,14},{7,15},{8,0},{9,1},... | collective-permute-start | bytes 2359304 | tf_op jit(solution)/shard_map/ppermute | solution.py:91
  103.2 15.4 %collective-permute-done.9 = f32[512,384]{1,0:T(8,128)} collective-permute-done((f32[512,384]{1,0:T(8,128)S(1)}, f32[512,384]{1,0:T(8,128)}, u32[]{:S(2)}, u32[]{:S(2)}) %collective-permute-start.9) | collective-permute-done | bytes 786464 | tf_op jit(solution)/shard_map/ppermute | solution.py:91
  118.7 2.2 %fusion.66 = (bf16[512,384]{1,0:T(8,128)(2,1)S(1)}, f32[512,384]{1,0:T(8,128)}) fusion(f32[512]{0:T(512)S(1)} %get-tuple-element.63, f32[512]{0:T(512)S(1)} %get-tuple-element.62, f32[512,384]{1,0:T(8,128)S(1)} %copy-done.4, f32[512,384]{1,0:T(8,128)} %collective-permute-done.9, f32[2,512,384]{2,1,0:T(8,128)S(1)} %pad_maximum_fusion, s32[]{:T(128)S(6)} %select_n.230), kind=kLoop, calls=%fused_computation.136 | loop fusion | flops 1376256 | bytes 3543044 | tf_op jit(solution)/shard_map/convert_element_type | solution.py:198
  120.9 3.2 %collective-permute-start.10 = (bf16[512,384]{1,0:T(8,128)(2,1)S(1)}, bf16[512,384]{1,0:T(8,128)(2,1)S(1)}, u32[]{:S(2)}, u32[]{:S(2)}) collective-permute-start(bf16[512,384]{1,0:T(8,128)(2,1)S(1)} %get-tuple-element.28), channel_id=1, source_target_pairs={{0,8},{1,9},{2,10},{3,11},{4,12},{5,13},{6,14},{7,15},{8,0},{9,1},... | collective-permute-start | bytes 1179656 | tf_op jit(solution)/shard_map/ppermute | solution.py:96
  124.2 6.1 %collective-permute-done.10 = bf16[512,384]{1,0:T(8,128)(2,1)S(1)} collective-permute-done((bf16[512,384]{1,0:T(8,128)(2,1)S(1)}, bf16[512,384]{1,0:T(8,128)(2,1)S(1)}, u32[]{:S(2)}, u32[]{:S(2)}) %collective-permute-start.10) | collective-permute-done | bytes 393248 | tf_op jit(solution)/shard_map/ppermute | solution.py:96
  133.1 7.9 %collective-permute-done.11 = bf16[2,256,384]{2,1,0:T(8,128)(2,1)S(1)} collective-permute-done((bf16[2,256,384]{2,1,0:T(8,128)(2,1)S(1)}, bf16[2,256,384]{2,1,0:T(8,128)(2,1)S(1)}, u32[]{:S(2)}, u32[]{:S(2)}) %collective-permute-start.11) | collective-permute-done | bytes 393248 | tf_op jit(solution)/shard_map/ppermute | solution.py:59
  143.1 9.3 %collective-permute-done.12 = bf16[2,256,384]{2,1,0:T(8,128)(2,1)S(1)} collective-permute-done((bf16[2,256,384]{2,1,0:T(8,128)(2,1)S(1)}, bf16[2,256,384]{2,1,0:T(8,128)(2,1)S(1)}, u32[]{:S(2)}, u32[]{:S(2)}) %collective-permute-start.12) | collective-permute-done | bytes 393248 | tf_op jit(solution)/shard_map/ppermute | solution.py:59
  154.6 5.6 %collective-permute-done.13 = bf16[2,256,384]{2,1,0:T(8,128)(2,1)S(1)} collective-permute-done((bf16[2,256,384]{2,1,0:T(8,128)(2,1)S(1)}, bf16[2,256,384]{2,1,0:T(8,128)(2,1)S(1)}, u32[]{:S(2)}, u32[]{:S(2)}) %collective-permute-start.13) | collective-permute-done | bytes 393248 | tf_op jit(solution)/shard_map/ppermute | solution.py:59
  160.3 2.0 collective-permute-done.16
  162.8 5.6 %collective-permute-done.17 = bf16[2,4,512,384]{3,2,1,0:T(8,128)(2,1)S(1)} collective-permute-done((bf16[2,4,512,384]{3,2,1,0:T(8,128)(2,1)S(1)}, bf16[2,4,512,384]{3,2,1,0:T(8,128)(2,1)S(1)}, u32[]{:S(2)}, u32[]{:S(2)}) %collective-permute-start.17) | collective-permute-done | bytes 3145760 | tf_op jit(solution)/shard_map/ppermute | solution.py:102
  168.4 2.4 %fusion.24 = f32[512,384]{1,0:T(8,128)S(1)} fusion(bf16[2,4,512,384]{3,2,1,0:T(8,128)(2,1)S(1)} %collective-permute-done.17, bf16[2,4,2,512,512]{4,3,2,1,0:T(8,128)(2,1)S(1)} %bitcast.164, s32[]{:T(128)S(6)} %select_n.213), kind=kOutput, calls=%fused_computation.29 | convolution fusion | flops 1610612736 | bytes 8126468 | tf_op jit(solution)/shard_map/dot_general | solution.py:202
  170.8 2.4 %fusion.27 = f32[512,384]{1,0:T(8,128)S(1)} fusion(f32[512,384]{1,0:T(8,128)S(1)} %fusion.24, bf16[2,4,2,512,512]{4,3,2,1,0:T(8,128)(2,1)S(1)} %bitcast.165, s32[]{:T(128)S(6)} %select_n.208, bf16[4,2,256,384]{3,2,0,1:T(8,128)(2,1)S(1)} %bitcast_dynamic-update-slice_fusion.7, bf16[4,2,256,384]{3,2,0,1:T(8,128)(2,1)S(1)} %bitcast_dynamic-update-slice_fusion.3), kind=kOutput, calls=%fused_computation.30 | convolution fusion | flops 1617100800 | bytes 8912900 | tf_op jit(solution)/shard_map/dot_general | solution.py:201
  174.9 20.6 %all_to_all.15 = f32[8,70,384]{2,1,0:T(8,128)S(1)} all-to-all(f32[8,70,384]{2,1,0:T(8,128)S(1)} %pad_maximum_fusion.1), channel_id=1, replica_groups=mesh['br'=8,'bus'=16] {'br'}, dimensions={0} | all-to-all | bytes 1720320 | tf_op jit(solution)/shard_map/all_to_all | solution.py:210
  196.9 3.5 %all-to-all-start.2 = ((f32[8,64,384]{2,1,0:T(8,128)}), f32[8,64,384]{2,1,0:T(8,128)S(1)}, u32[]{:S(2)}, u32[]{:S(2)}) async-start(f32[8,64,384]{2,1,0:T(8,128)} %broadcast_in_dim.153), calls=%async_computation.2 | async-start | bytes 1572864 | tf_op jit(solution)/shard_map/all_to_all | solution.py:215
  202.7 9.0 %all-to-all-done.2 = f32[8,64,384]{2,1,0:T(8,128)S(1)} async-done(((f32[8,64,384]{2,1,0:T(8,128)}), f32[8,64,384]{2,1,0:T(8,128)S(1)}, u32[]{:S(2)}, u32[]{:S(2)}) %all-to-all-start.2) | async-done | bytes 786464 | tf_op jit(solution)/shard_map/all_to_all | solution.py:215
  (142 shorter events, 46.4 us)
Async XLA Ops:
  1.9 36.0 %copy-start = (bf16[512,384]{1,0:T(8,128)(2,1)}, bf16[512,384]{1,0:T(8,128)(2,1)S(1)}, u32[]{:S(2)}) copy-start(bf16[512,384]{1,0:T(8,128)(2,1)S(1)} %convert_element_type.16) | copy-start | bytes 1179652
  9.5 4.1 %copy-start.8 = (s32[1024,3]{0,1:T(4,128)S(1)}, s32[1024,3]{0,1:T(4,128)}, u32[]{:S(2)}) copy-start(s32[1024,3]{0,1:T(4,128)} %param.25) | copy-start | bytes 36868
  9.5 13.6 %collective-permute-start = (f32[2,512,384]{2,1,0:T(8,128)}, f32[2,512,384]{2,1,0:T(8,128)}, u32[]{:S(2)}, u32[]{:S(2)}) collective-permute-start(f32[2,512,384]{2,1,0:T(8,128)} %fusion.34), channel_id=1, source_target_pairs={{0,1},{1,0},{2,3},{3,2},{4,5},{5,4},{6,7},{7,6},{8,9},{9,8},{10,11... | collective-permute-start | bytes 4718600 | tf_op jit(solution)/shard_map/ppermute | solution.py:75
  12.6 25.3 %collective-permute-start.2 = (f32[2,512,384]{2,1,0:T(8,128)}, f32[2,512,384]{2,1,0:T(8,128)}, u32[]{:S(2)}, u32[]{:S(2)}) collective-permute-start(f32[2,512,384]{2,1,0:T(8,128)} %fusion.38), channel_id=1, source_target_pairs={{0,1},{1,0},{2,3},{3,2},{4,5},{5,4},{6,7},{7,6},{8,9},{9,8},{10,11... | collective-permute-start | bytes 4718600 | tf_op jit(solution)/shard_map/ppermute | solution.py:69
  22.0 7.0 %copy-start.12 = (s32[24]{0:T(128)}, s32[24]{0:T(128)S(1)}, u32[]{:S(2)}) copy-start(s32[24]{0:T(128)S(1)} %convert_reduce_fusion.1) | copy-start | bytes 292
  25.4 5.6 %copy-start.9 = (s32[384]{0:T(512)S(1)}, s32[384]{0:T(512)}, u32[]{:S(2)}) copy-start(s32[384]{0:T(512)} %param.24) | copy-start | bytes 4612
  28.4 7.1 %copy-start.7 = (f32[64,1024]{1,0:T(8,128)S(1)}, f32[64,1024]{1,0:T(8,128)}, u32[]{:S(2)}) copy-start(f32[64,1024]{1,0:T(8,128)} %param.22) | copy-start | bytes 786436
  28.4 31.7 %collective-permute-start.4 = (f32[2,1024,384]{2,1,0:T(8,128)}, f32[2,1024,384]{2,1,0:T(8,128)}, u32[]{:S(2)}, u32[]{:S(2)}) collective-permute-start(f32[2,1024,384]{2,1,0:T(8,128)} %fusion.12), channel_id=1, source_target_pairs={{0,1},{1,0},{2,3},{3,2},{4,5},{5,4},{6,7},{7,6},{8,9},{9,8},{10,11... | collective-permute-start | bytes 9437192 | tf_op jit(solution)/shard_map/ppermute | solution.py:69
  32.1 20.2 %collective-permute-start.1 = (f32[2,256,384]{2,1,0:T(8,128)}, f32[2,256,384]{2,1,0:T(8,128)S(1)}, u32[]{:S(2)}, u32[]{:S(2)}) collective-permute-start(f32[2,256,384]{2,1,0:T(8,128)} %get-tuple-element.46), channel_id=1, source_target_pairs={{0,2},{1,3},{2,4},{3,5},{4,6},{5,7},{6,0},{7,1},{8,10},{9,11},{10,... | collective-permute-start | bytes 2359304 | tf_op jit(solution)/shard_map/ppermute | solution.py:46
  32.5 20.9 %collective-permute-start.6 = (f32[2,256,384]{2,1,0:T(8,128)S(1)}, f32[2,256,384]{2,1,0:T(8,128)S(1)}, u32[]{:S(2)}, u32[]{:S(2)}) collective-permute-start(f32[2,256,384]{2,1,0:T(8,128)S(1)} %get-tuple-element.47), channel_id=1, source_target_pairs={{0,6},{1,7},{2,0},{3,1},{4,2},{5,3},{6,4},{7,5},{8,14},{9,15},{10,... | collective-permute-start | bytes 2359304 | tf_op jit(solution)/shard_map/ppermute | solution.py:46
  54.7 19.1 %collective-permute-start.3 = (f32[2,256,384]{2,1,0:T(8,128)}, f32[2,256,384]{2,1,0:T(8,128)}, u32[]{:S(2)}, u32[]{:S(2)}) collective-permute-start(f32[2,256,384]{2,1,0:T(8,128)} %get-tuple-element.19), channel_id=1, source_target_pairs={{0,2},{1,3},{2,4},{3,5},{4,6},{5,7},{6,0},{7,1},{8,10},{9,11},{10,... | collective-permute-start | bytes 2359304 | tf_op jit(solution)/shard_map/ppermute | solution.py:46
  55.2 20.3 %collective-permute-start.7 = (f32[2,256,384]{2,1,0:T(8,128)}, f32[2,256,384]{2,1,0:T(8,128)}, u32[]{:S(2)}, u32[]{:S(2)}) collective-permute-start(f32[2,256,384]{2,1,0:T(8,128)} %get-tuple-element.45), channel_id=1, source_target_pairs={{0,6},{1,7},{2,0},{3,1},{4,2},{5,3},{6,4},{7,5},{8,14},{9,15},{10,... | collective-permute-start | bytes 2359304 | tf_op jit(solution)/shard_map/ppermute | solution.py:46
  78.2 18.4 %collective-permute-start.5 = (f32[2,256,384]{2,1,0:T(8,128)}, f32[2,256,384]{2,1,0:T(8,128)}, u32[]{:S(2)}, u32[]{:S(2)}) collective-permute-start(f32[2,256,384]{2,1,0:T(8,128)} %get-tuple-element.42), channel_id=1, source_target_pairs={{0,2},{1,3},{2,4},{3,5},{4,6},{5,7},{6,0},{7,1},{8,10},{9,11},{10,... | collective-permute-start | bytes 2359304 | tf_op jit(solution)/shard_map/ppermute | solution.py:46
  78.5 19.5 %collective-permute-start.8 = (f32[2,256,384]{2,1,0:T(8,128)}, f32[2,256,384]{2,1,0:T(8,128)}, u32[]{:S(2)}, u32[]{:S(2)}) collective-permute-start(f32[2,256,384]{2,1,0:T(8,128)} %get-tuple-element.43), channel_id=1, source_target_pairs={{0,6},{1,7},{2,0},{3,1},{4,2},{5,3},{6,4},{7,5},{8,14},{9,15},{10,... | collective-permute-start | bytes 2359304 | tf_op jit(solution)/shard_map/ppermute | solution.py:46
  82.8 12.8 %all-to-all-start = ((bf16[8,6,512]{2,1,0:T(8,128)(2,1)}), bf16[8,6,512]{2,1,0:T(8,128)(2,1)S(1)}, u32[]{:S(2)}, u32[]{:S(2)}) async-start(bf16[8,6,512]{2,1,0:T(8,128)(2,1)} %copy.99), calls=%async_computation | async-start | bytes 131072 | tf_op jit(solution)/shard_map/all_to_all | solution.py:186
  99.5 19.2 %copy-start.4 = (f32[512,384]{1,0:T(8,128)S(1)}, f32[512,384]{1,0:T(8,128)}, u32[]{:S(2)}) copy-start(f32[512,384]{1,0:T(8,128)} %param.17) | copy-start | bytes 2359300
  99.7 19.0 %collective-permute-start.9 = (f32[512,384]{1,0:T(8,128)S(1)}, f32[512,384]{1,0:T(8,128)}, u32[]{:S(2)}, u32[]{:S(2)}) collective-permute-start(f32[512,384]{1,0:T(8,128)S(1)} %dynamic-slice_bitcast_fusion.6), channel_id=1, source_target_pairs={{0,8},{1,9},{2,10},{3,11},{4,12},{5,13},{6,14},{7,15},{8,0},{9,1},... | collective-permute-start | bytes 2359304 | tf_op jit(solution)/shard_map/ppermute | solution.py:91
  120.9 9.4 %collective-permute-start.10 = (bf16[512,384]{1,0:T(8,128)(2,1)S(1)}, bf16[512,384]{1,0:T(8,128)(2,1)S(1)}, u32[]{:S(2)}, u32[]{:S(2)}) collective-permute-start(bf16[512,384]{1,0:T(8,128)(2,1)S(1)} %get-tuple-element.28), channel_id=1, source_target_pairs={{0,8},{1,9},{2,10},{3,11},{4,12},{5,13},{6,14},{7,15},{8,0},{9,1},... | collective-permute-start | bytes 1179656 | tf_op jit(solution)/shard_map/ppermute | solution.py:96
  130.5 10.4 %collective-permute-start.11 = (bf16[2,256,384]{2,1,0:T(8,128)(2,1)S(1)}, bf16[2,256,384]{2,1,0:T(8,128)(2,1)S(1)}, u32[]{:S(2)}, u32[]{:S(2)}) collective-permute-start(bf16[2,256,384]{2,1,0:T(8,128)(2,1)S(1)} %get-tuple-element.56), channel_id=1, source_target_pairs={{0,2},{1,3},{2,4},{3,5},{4,6},{5,7},{6,0},{7,1},{8,10},{9,11},{10,... | collective-permute-start | bytes 1179656 | tf_op jit(solution)/shard_map/ppermute | solution.py:59
  131.4 10.4 %collective-permute-start.14 = (bf16[2,256,384]{2,1,0:T(8,128)(2,1)S(1)}, bf16[2,256,384]{2,1,0:T(8,128)(2,1)S(1)}, u32[]{:S(2)}, u32[]{:S(2)}) collective-permute-start(bf16[2,256,384]{2,1,0:T(8,128)(2,1)S(1)} %get-tuple-element.57), channel_id=1, source_target_pairs={{0,6},{1,7},{2,0},{3,1},{4,2},{5,3},{6,4},{7,5},{8,14},{9,15},{10,... | collective-permute-start | bytes 1179656 | tf_op jit(solution)/shard_map/ppermute | solution.py:59
  132.6 35.8 %slice-start = ((s8[8388608]{0:T(1024)(128)(4,1)}), s8[4194304]{0:T(1024)(128)(4,1)S(1)}, s32[]{:S(2)}) async-start(s8[8388608]{0:T(1024)(128)(4,1)} %bitcast.162), calls=%async_computation.3 | async-start | bytes 8388608
  140.9 11.5 %collective-permute-start.12 = (bf16[2,256,384]{2,1,0:T(8,128)(2,1)S(1)}, bf16[2,256,384]{2,1,0:T(8,128)(2,1)S(1)}, u32[]{:S(2)}, u32[]{:S(2)}) collective-permute-start(bf16[2,256,384]{2,1,0:T(8,128)(2,1)S(1)} %collective-permute-done.11), channel_id=1, source_target_pairs={{0,2},{1,3},{2,4},{3,5},{4,6},{5,7},{6,0},{7,1},{8,10},{9,11},{10,... | collective-permute-start | bytes 1179656 | tf_op jit(solution)/shard_map/ppermute | solution.py:59
  141.8 11.5 %collective-permute-start.15 = (bf16[2,256,384]{2,1,0:T(8,128)(2,1)S(1)}, bf16[2,256,384]{2,1,0:T(8,128)(2,1)S(1)}, u32[]{:S(2)}, u32[]{:S(2)}) collective-permute-start(bf16[2,256,384]{2,1,0:T(8,128)(2,1)S(1)} %collective-permute-done.14), channel_id=1, source_target_pairs={{0,6},{1,7},{2,0},{3,1},{4,2},{5,3},{6,4},{7,5},{8,14},{9,15},{10,... | collective-permute-start | bytes 1179656 | tf_op jit(solution)/shard_map/ppermute | solution.py:59
  152.4 7.8 %collective-permute-start.13 = (bf16[2,256,384]{2,1,0:T(8,128)(2,1)S(1)}, bf16[2,256,384]{2,1,0:T(8,128)(2,1)S(1)}, u32[]{:S(2)}, u32[]{:S(2)}) collective-permute-start(bf16[2,256,384]{2,1,0:T(8,128)(2,1)S(1)} %collective-permute-done.12), channel_id=1, source_target_pairs={{0,2},{1,3},{2,4},{3,5},{4,6},{5,7},{6,0},{7,1},{8,10},{9,11},{10,... | collective-permute-start | bytes 1179656 | tf_op jit(solution)/shard_map/ppermute | solution.py:59
  153.3 9.0 %collective-permute-start.16 = (bf16[2,256,384]{2,1,0:T(8,128)(2,1)S(1)}, bf16[2,256,384]{2,1,0:T(8,128)(2,1)S(1)}, u32[]{:S(2)}, u32[]{:S(2)}) collective-permute-start(bf16[2,256,384]{2,1,0:T(8,128)(2,1)S(1)} %collective-permute-done.15), channel_id=1, source_target_pairs={{0,6},{1,7},{2,0},{3,1},{4,2},{5,3},{6,4},{7,5},{8,14},{9,15},{10,... | collective-permute-start | bytes 1179656 | tf_op jit(solution)/shard_map/ppermute | solution.py:59
  154.5 13.9 %slice-start.1 = ((s8[8388608]{0:T(1024)(128)(4,1)}), s8[4194304]{0:T(1024)(128)(4,1)S(1)}, s32[]{:S(2)}) async-start(s8[8388608]{0:T(1024)(128)(4,1)} %bitcast.162), calls=%async_computation.4 | async-start | bytes 8388608
  162.7 5.7 %collective-permute-start.17 = (bf16[2,4,512,384]{3,2,1,0:T(8,128)(2,1)S(1)}, bf16[2,4,512,384]{3,2,1,0:T(8,128)(2,1)S(1)}, u32[]{:S(2)}, u32[]{:S(2)}) collective-permute-start(bf16[2,4,512,384]{3,2,1,0:T(8,128)(2,1)S(1)} %maximum_bitcast_fusion), channel_id=1, source_target_pairs={{0,1},{1,0},{2,3},{3,2},{4,5},{5,4},{6,7},{7,6},{8,9},{9,8},{10,11... | collective-permute-start | bytes 9437192 | tf_op jit(solution)/shard_map/ppermute | solution.py:102
  174.8 20.9 %copy-start.2 = (f32[64,384]{0,1:T(8,128)S(1)}, f32[64,384]{0,1:T(8,128)}, u32[]{:S(2)}) copy-start(f32[64,384]{0,1:T(8,128)} %broadcast_subtract_fusion) | copy-start | bytes 294916
  174.9 20.9 %copy-start.3 = (f32[64,384]{0,1:T(8,128)S(1)}, f32[64,384]{0,1:T(8,128)}, u32[]{:S(2)}) copy-start(f32[64,384]{0,1:T(8,128)} %multiply_bitcast_fusion) | copy-start | bytes 294916
  195.6 4.8 %copy-start.13 = (s32[24]{0:T(128)S(1)}, s32[24]{0:T(128)}, u32[]{:S(2)}) copy-start(s32[24]{0:T(128)} %copy-done.12) | copy-start | bytes 292
  195.6 4.9 %copy-start.11 = (s32[24]{0:T(128)S(1)}, s32[24]{0:T(128)}, u32[]{:S(2)}) copy-start(s32[24]{0:T(128)} %get-tuple-element.60) | copy-start | bytes 292
  196.9 14.8 %all-to-all-start.2 = ((f32[8,64,384]{2,1,0:T(8,128)}), f32[8,64,384]{2,1,0:T(8,128)S(1)}, u32[]{:S(2)}, u32[]{:S(2)}) async-start(f32[8,64,384]{2,1,0:T(8,128)} %broadcast_in_dim.153), calls=%async_computation.2 | async-start | bytes 1572864 | tf_op jit(solution)/shard_map/all_to_all | solution.py:215
  (5 other events, 12.4 us)

commit v10 on v8

--- a/solution.py
+++ b/solution.py
@@ -67,8 +67,8 @@
     second = [(xi + 2) % XR, xi]
     summed = []
     for group in (first, second):
-        send = jnp.stack([flow_part(x, False) for x in group])
-        keep = jnp.stack([flow_part(x, True) for x in group])
+        send = flow_part(group, False)
+        keep = flow_part(group, True)
         summed.append(keep + lax.ppermute(send, "bus", CORE_SWAP))
     a, b = summed
     half = a.shape[2] // 2
@@ -140,6 +140,25 @@
     outgoing_w = jnp.einsum(
         "sce,er->scr", pick_out.astype(jnp.bfloat16), weight_rows, preferred_element_type=jnp.float32
     ).astype(jnp.bfloat16)
+    yh, xi, core = bus_place()
+
+    bus_rows = injections.shape[0]
+    share_rows = bus_rows // slab_axis
+    start = slab_index * share_rows
+    inject_half = injections.astype(jnp.bfloat16)
+    by_place = shift_factors.reshape(YHI, XR, CORES, -1, shift_factors.shape[1])
+    sf_keep = pick(by_place, core, 2)
+    sf_send = pick(by_place, 1 - core, 2)
+
+    def flow_part(group, mine):
+        rows = jnp.stack([pick(sf_keep if mine else sf_send, x, 1) for x in group])
+        return jnp.dot(rows, inject_half, preferred_element_type=jnp.float32)
+
+    rider = (outgoing_w, slab_by_device, block_by_device, irradiance_profile, plant_group, scenario_profile,
+             unit_cost, bus_load, bus_capacity)
+    ring_out, rider = bus_reduce_scatter(flow_part, rider)
+    (outgoing_w, slab_by_device, block_by_device, irradiance_profile, plant_group, scenario_profile,
+     unit_cost, bus_load, bus_capacity) = rider
     sources = slab_range * bus_axis + column_index
     src_slab = jnp.take(slab_by_device, sources, axis=0)
     src_block = jnp.take(block_by_device, sources, axis=0)
@@ -147,11 +166,6 @@
     pick_in = (src_slab[:, None, :] == slab_index) & (src_slot[:, None, :] == slot_range[None, :, None])
     block_choice = jnp.sum(jnp.where(pick_in, src_block[:, None, :], 0), axis=2)
     block_hot = block_choice[:, :, None] == jnp.arange(blocks_per_slab, dtype=jnp.int32)[None, None, :]
-    yh, xi, core = bus_place()
-
-    bus_rows = injections.shape[0]
-    share_rows = bus_rows // slab_axis
-    start = slab_index * share_rows
     my_inj = lax.dynamic_slice_in_dim(injections, start, share_rows, 0)
     my_cost = lax.dynamic_slice_in_dim(unit_cost, start, share_rows, 0)
     my_load = lax.dynamic_slice_in_dim(bus_load, start, share_rows, 0)
@@ -163,16 +177,6 @@
     lower = -my_load[:, None]
     base = my_inj - step_primal * my_cost[:, None]
 
-    inject_half = injections.astype(jnp.bfloat16)
-    by_place = shift_factors.reshape(YHI, XR, CORES, -1, shift_factors.shape[1])
-    sf_keep = pick(by_place, core, 2)
-    sf_send = pick(by_place, 1 - core, 2)
-
-    def flow_part(x, mine):
-        rows = pick(sf_keep if mine else sf_send, x, 1)
-        return jnp.dot(rows, inject_half, preferred_element_type=jnp.float32)
-
-    ring_out, outgoing_w = bus_reduce_scatter(flow_part, outgoing_w)
     arrived_w = lax.all_to_all(outgoing_w, "br", 0, 0, tiled=True)
     masked = jnp.where(block_hot[:, :, :, None], arrived_w[:, :, None, :], jnp.zeros((), jnp.bfloat16))
     masked = masked.reshape(slab_axis * CAP, YHI, XR, CORES, -1)

time: 206 us -> 232 us (1.13)
  local copies, waits for them, and re-layouts: 11.8 us -> 34.3 us
  other arithmetic: 21.7 us -> 29.1 us
    another operation x2 -> x3, local copies, waits for them, and re-layouts: 0.28 us -> 6.28 us  [the longest x1 6.01 us: flow_part(): rows = jnp.stack([pick(sf_keep if mine else sf_send, x, 1) for x in group])]
    all_to_all x1, waiting for transfers between devices: 5.59 us -> 0.01 us  [per_device(): arrived_w = lax.all_to_all(outgoing_w, 'br', 0, 0, tiled=True)]
    unnamed x31 -> x46, local copies, waits for them, and re-layouts: 2.11 us -> 6.88 us
    add x2 -> x0, other arithmetic: 4.4 us -> none  [bus_reduce_scatter(): summed.append(keep + lax.ppermute(send, 'bus', CORE_SWAP))]
    another operation x2 -> x0, other arithmetic: 3.76 us -> none  [bus_reduce_scatter(): send = jnp.stack([flow_part(x, False) for x in group])]
    add x3, other arithmetic: 3.06 us -> 5.64 us  [ring_scatter(): acc = lax.ppermute(acc, 'bus', perm) + more]
    ppermute x6, waiting for transfers between devices: 31.4 us -> 33.9 us  [ring_scatter(): acc = lax.ppermute(acc, 'bus', perm) + more]
    dot_general x8 -> x4, matrix products: 15.5 us -> 13.5 us  [flow_part(): return jnp.dot(rows, inject_half, preferred_element_type=jnp.float32)]
  transfers between devices with their start and end apart: 19 -> 19, of which waited for: 16 -> 16; matrix products, arithmetic and copies ran while one was open for 16% -> 18% of each run, Pallas kernels for 0% -> 0%
where the time goes in v10:
time: 232 us; the launch traced here: 231 us
  waiting for transfers between devices  97.4 us (42%)
  local copies, waits for them, and re-layouts  34.3 us (15%)
  other arithmetic  29.1 us (13%)
  starting transfers between devices  28 us (12%)
  matrix products  21 us (9%)
  blocking collectives  19.6 us (8%)
    ppermute x6, waiting for transfers between devices, ring_scatter(): acc = lax.ppermute(acc, 'bus', perm) + more  33.9 us
    ppermute x6, waiting for transfers between devices, ring_gather(): cur = lax.ppermute(cur, 'bus', perm)  27.5 us
    all_to_all x1, blocking collectives, per_device(): gathered = lax.all_to_all(outgoing, 'br', 0, 0, tiled=True)  19.6 us
    ppermute x1, waiting for transfers between devices, bus_pair_sum(): return pick(z, yh, 0) + lax.ppermute(pick(z, 1 - yh, 0), 'bus', Y_SWAP)  15 us
    dot_general x4, matrix products, flow_part(): return jnp.dot(rows, inject_half, preferred_element_type=jnp.float32)  13.5 us
    all_to_all x1, waiting for transfers between devices, per_device(): lax.all_to_all(jnp.broadcast_to(my_new[None], (slab_axis, share_rows, sce...  8.96 us
    unnamed x46, local copies, waits for them, and re-layouts  6.88 us
    all_to_all x1, starting transfers between devices, per_device(): arrived_w = lax.all_to_all(outgoing_w, 'br', 0, 0, tiled=True)  6.42 us
  transfers between devices with their start and end apart: 19, of which 16 were waited for; matrix products, arithmetic and copies ran while one was open for 18% of the time, Pallas kernels for 0%

profile of v10, /device:TPU:6, one launch (start us, length us, event | category | flops | bytes accessed | tf_op | source)
XLA Modules:
  0.0 230.7 jit_solution(10628446539786474088)
XLA Ops:
  1.9 6.0 %dynamic-slice_bitcast_fusion.3 = (bf16[1,2,512,512]{3,2,1,0:T(8,128)(2,1)}, bf16[1,2,512,512]{3,2,1,0:T(8,128)(2,1)S(1)}, bf16[1,2,512,512]{3,2,1,0:T(8,128)(2,...) fusion(bf16[2,4,2,512,512]{4,3,2,1,0:T(8,128)(2,1)} %bitcast.18, ...), kind=kLoop, calls=%fused_computation.41 | loop fusion | bytes 16777240 | tf_op jit(solution)/shard_map/stack | solution.py:154
  8.0 3.0 %fusion.10 = f32[2,2,512,384]{3,2,1,0:T(8,128)} fusion(bf16[1,2,512,512]{3,2,1,0:T(8,128)(2,1)S(1)} %get-tuple-element.46, bf16[1,2,512,512]{3,2,1,0:T(8,128)(2,1)S(1)} %get-tuple-element.47, bf16[512,384]{1,0:T(8,128)(2,1)S(1)} %convert_element_type.16), kind=kOutput, calls=%fused_computation.16 | convolution fusion | flops 806354944 | bytes 5636096 | tf_op jit(solution)/shard_map/dot_general | solution.py:155
  10.9 3.0 %fusion.18 = f32[2,2,512,384]{3,2,1,0:T(8,128)} fusion(bf16[1,2,512,512]{3,2,1,0:T(8,128)(2,1)S(1)} %get-tuple-element.43, bf16[1,2,512,512]{3,2,1,0:T(8,128)(2,1)S(1)} %get-tuple-element.44, bf16[512,384]{1,0:T(8,128)(2,1)S(1)} %convert_element_type.16), kind=kOutput, calls=%fused_computation.24 | convolution fusion | flops 806354944 | bytes 5636096 | tf_op jit(solution)/shard_map/dot_general | solution.py:155
  15.4 1.9 reshape.204
  24.9 3.8 %fusion.25 = f32[2,2,512,384]{3,2,1,0:T(8,128)S(1)} fusion(f32[2,2,512,384]{3,2,1,0:T(8,128)} %copy-done.2, bf16[1,2,512,512]{3,2,1,0:T(8,128)(2,1)} %get-tuple-element.48, bf16[1,2,512,512]{3,2,1,0:T(8,128)(2,1)} %get-tuple-element.49, bf16[512,384]{1,0:T(8,128)(2,1)S(1)} %convert_element_type.16), kind=kOutput, calls=%fused_computation.29 | convolution fusion | flops 807141376 | bytes 8781824 | tf_op jit(solution)/shard_map/dot_general | solution.py:155
  35.0 1.9 reshape.206
  36.8 1.7 copy.127
  41.3 3.8 %fusion.22 = f32[2,2,512,384]{3,2,1,0:T(8,128)S(1)} fusion(f32[2,2,512,384]{3,2,1,0:T(8,128)} %collective-permute-done.2, bf16[1,2,512,512]{3,2,1,0:T(8,128)(2,1)} %get-tuple-element.45, bf16[1,2,512,512]{3,2,1,0:T(8,128)(2,1)} %get-tuple-element.42, bf16[512,384]{1,0:T(8,128)(2,1)S(1)} %convert_element_type.16), kind=kOutput, calls=%fused_computation.28 | convolution fusion | flops 807141376 | bytes 8781824 | tf_op jit(solution)/shard_map/dot_general | solution.py:155
  45.2 4.5 %collective-permute-done.1 = f32[2,256,384]{2,1,0:T(8,128)} collective-permute-done((f32[2,256,384]{2,1,0:T(8,128)}, f32[2,256,384]{2,1,0:T(8,128)}, u32[]{:S(2)}, u32[]{:S(2)}) %collective-permute-start.1) | collective-permute-done | bytes 786464 | tf_op jit(solution)/shard_map/ppermute | solution.py:46
  51.0 2.7 %fusion.43 = (f32[2,256,384]{2,1,0:T(8,128)}, f32[2,256,384]{2,1,0:T(8,128)}) fusion(f32[2,256,384]{2,1,0:T(8,128)} %collective-permute-done.1, f32[2,2,512,384]{3,2,1,0:T(8,128)S(1)} %fusion.22, f32[2,256,384]{2,1,0:T(8,128)} %collective-permute-done.5), kind=kLoop, calls=%fused_computation.60 | loop fusion | flops 393216 | bytes 4718592 | tf_op jit(solution)/shard_map/add | solution.py:46
  53.8 1.9 copy.100
  57.7 1.8 gather_fusion
  69.6 6.4 %all-to-all-start = ((bf16[8,6,512]{2,1,0:T(8,128)(2,1)}), bf16[8,6,512]{2,1,0:T(8,128)(2,1)S(1)}, u32[]{:S(2)}, u32[]{:S(2)}) async-start(bf16[8,6,512]{2,1,0:T(8,128)(2,1)} %copy.99), calls=%async_computation | async-start | bytes 131072 | tf_op jit(solution)/shard_map/all_to_all | solution.py:180
  76.3 1.7 collective-permute-start.6
  81.0 13.3 %collective-permute-done.3 = f32[2,256,384]{2,1,0:T(8,128)S(1)} collective-permute-done((f32[2,256,384]{2,1,0:T(8,128)}, f32[2,256,384]{2,1,0:T(8,128)S(1)}, u32[]{:S(2)}, u32[]{:S(2)}) %collective-permute-start.3) | collective-permute-done | bytes 786464 | tf_op jit(solution)/shard_map/ppermute | solution.py:46
  97.4 1.7 collective-permute-start.7
  102.9 11.7 %collective-permute-done.4 = f32[2,256,384]{2,1,0:T(8,128)} collective-permute-done((f32[2,256,384]{2,1,0:T(8,128)}, f32[2,256,384]{2,1,0:T(8,128)}, u32[]{:S(2)}, u32[]{:S(2)}) %collective-permute-start.4) | collective-permute-done | bytes 786464 | tf_op jit(solution)/shard_map/ppermute | solution.py:46
  117.9 3.1 %collective-permute-start.8 = (f32[512,384]{1,0:T(8,128)S(1)}, f32[512,384]{1,0:T(8,128)}, u32[]{:S(2)}, u32[]{:S(2)}) collective-permute-start(f32[512,384]{1,0:T(8,128)S(1)} %dynamic-slice_bitcast_fusion.8), channel_id=1, source_target_pairs={{0,8},{1,9},{2,10},{3,11},{4,12},{5,13},{6,14},{7,15},{8,0},{9,1},... | collective-permute-start | bytes 2359304 | tf_op jit(solution)/shard_map/ppermute | solution.py:83
  121.0 15.0 %collective-permute-done.8 = f32[512,384]{1,0:T(8,128)} collective-permute-done((f32[512,384]{1,0:T(8,128)S(1)}, f32[512,384]{1,0:T(8,128)}, u32[]{:S(2)}, u32[]{:S(2)}) %collective-permute-start.8) | collective-permute-done | bytes 786464 | tf_op jit(solution)/shard_map/ppermute | solution.py:83
  136.1 2.2 fusion.63
  138.3 2.9 %collective-permute-start.9 = (bf16[512,384]{1,0:T(8,128)(2,1)S(1)}, bf16[512,384]{1,0:T(8,128)(2,1)S(1)}, u32[]{:S(2)}, u32[]{:S(2)}) collective-permute-start(bf16[512,384]{1,0:T(8,128)(2,1)S(1)} %get-tuple-element.36), channel_id=1, source_target_pairs={{0,8},{1,9},{2,10},{3,11},{4,12},{5,13},{6,14},{7,15},{8,0},{9,1},... | collective-permute-start | bytes 1179656 | tf_op jit(solution)/shard_map/ppermute | solution.py:88
  141.2 6.4 %collective-permute-done.9 = bf16[512,384]{1,0:T(8,128)(2,1)S(1)} collective-permute-done((bf16[512,384]{1,0:T(8,128)(2,1)S(1)}, bf16[512,384]{1,0:T(8,128)(2,1)S(1)}, u32[]{:S(2)}, u32[]{:S(2)}) %collective-permute-start.9) | collective-permute-done | bytes 393248 | tf_op jit(solution)/shard_map/ppermute | solution.py:88
  150.4 9.0 %collective-permute-done.10 = bf16[2,256,384]{2,1,0:T(8,128)(2,1)S(1)} collective-permute-done((bf16[2,256,384]{2,1,0:T(8,128)(2,1)S(1)}, bf16[2,256,384]{2,1,0:T(8,128)(2,1)S(1)}, u32[]{:S(2)}, u32[]{:S(2)}) %collective-permute-start.10) | collective-permute-done | bytes 393248 | tf_op jit(solution)/shard_map/ppermute | solution.py:59
  161.5 9.5 %collective-permute-done.11 = bf16[2,256,384]{2,1,0:T(8,128)(2,1)S(1)} collective-permute-done((bf16[2,256,384]{2,1,0:T(8,128)(2,1)S(1)}, bf16[2,256,384]{2,1,0:T(8,128)(2,1)S(1)}, u32[]{:S(2)}, u32[]{:S(2)}) %collective-permute-start.11) | collective-permute-done | bytes 393248 | tf_op jit(solution)/shard_map/ppermute | solution.py:59
  173.2 5.6 %collective-permute-done.12 = bf16[2,256,384]{2,1,0:T(8,128)(2,1)S(1)} collective-permute-done((bf16[2,256,384]{2,1,0:T(8,128)(2,1)S(1)}, bf16[2,256,384]{2,1,0:T(8,128)(2,1)S(1)}, u32[]{:S(2)}, u32[]{:S(2)}) %collective-permute-start.12) | collective-permute-done | bytes 393248 | tf_op jit(solution)/shard_map/ppermute | solution.py:59
  178.9 2.6 %collective-permute-done.15 = bf16[2,256,384]{2,1,0:T(8,128)(2,1)S(1)} collective-permute-done((bf16[2,256,384]{2,1,0:T(8,128)(2,1)S(1)}, bf16[2,256,384]{2,1,0:T(8,128)(2,1)S(1)}, u32[]{:S(2)}, u32[]{:S(2)}) %collective-permute-start.15) | collective-permute-done | bytes 393248 | tf_op jit(solution)/shard_map/ppermute | solution.py:59
  182.0 5.6 %collective-permute-done.16 = bf16[2,4,512,384]{3,2,1,0:T(8,128)(2,1)S(1)} collective-permute-done((bf16[2,4,512,384]{3,2,1,0:T(8,128)(2,1)S(1)}, bf16[2,4,512,384]{3,2,1,0:T(8,128)(2,1)S(1)}, u32[]{:S(2)}, u32[]{:S(2)}) %collective-permute-start.16) | collective-permute-done | bytes 3145760 | tf_op jit(solution)/shard_map/ppermute | solution.py:94
  187.6 2.4 %fusion.31 = f32[512,384]{1,0:T(8,128)S(1)} fusion(bf16[2,4,512,384]{3,2,1,0:T(8,128)(2,1)S(1)} %collective-permute-done.16, bf16[2,4,2,512,512]{4,3,2,1,0:T(8,128)(2,1)S(1)} %bitcast.184, s32[]{:T(128)S(6)} %select_n.209), kind=kOutput, calls=%fused_computation.32 | convolution fusion | flops 1610612736 | bytes 8126468 | tf_op jit(solution)/shard_map/dot_general | solution.py:196
  190.0 2.4 %fusion.34 = f32[512,384]{1,0:T(8,128)S(1)} fusion(f32[512,384]{1,0:T(8,128)S(1)} %fusion.31, bf16[2,4,2,512,512]{4,3,2,1,0:T(8,128)(2,1)S(1)} %bitcast.185, s32[]{:T(128)S(6)} %select_n.204, bf16[4,2,256,384]{3,2,0,1:T(8,128)(2,1)S(1)} %bitcast_dynamic-update-slice_fusion.7, bf16[4,2,256,384]{3,2,0,1:T(8,128)(2,1)S(1)} %bitcast_dynamic-update-slice_fusion.3), kind=kOutput, calls=%fused_computation.33 | convolution fusion | flops 1617100800 | bytes 8912900 | tf_op jit(solution)/shard_map/dot_general | solution.py:195
  194.2 19.6 %all_to_all.15 = f32[8,70,384]{2,1,0:T(8,128)S(1)} all-to-all(f32[8,70,384]{2,1,0:T(8,128)S(1)} %pad_maximum_fusion.1), channel_id=1, replica_groups=mesh['br'=8,'bus'=16] {'br'}, dimensions={0} | all-to-all | bytes 1720320 | tf_op jit(solution)/shard_map/all_to_all | solution.py:204
  215.1 3.5 %all-to-all-start.2 = ((f32[8,64,384]{2,1,0:T(8,128)}), f32[8,64,384]{2,1,0:T(8,128)S(1)}, u32[]{:S(2)}, u32[]{:S(2)}) async-start(f32[8,64,384]{2,1,0:T(8,128)} %broadcast_in_dim.153), calls=%async_computation.2 | async-start | bytes 1572864 | tf_op jit(solution)/shard_map/all_to_all | solution.py:209
  220.9 9.0 %all-to-all-done.2 = f32[8,64,384]{2,1,0:T(8,128)S(1)} async-done(((f32[8,64,384]{2,1,0:T(8,128)}), f32[8,64,384]{2,1,0:T(8,128)S(1)}, u32[]{:S(2)}, u32[]{:S(2)}) %all-to-all-start.2) | async-done | bytes 786464 | tf_op jit(solution)/shard_map/all_to_all | solution.py:209
  (144 shorter events, 59.6 us)
Async XLA Ops:
  10.9 12.3 %collective-permute-start = (f32[2,2,512,384]{3,2,1,0:T(8,128)}, f32[2,2,512,384]{3,2,1,0:T(8,128)S(1)}, u32[]{:S(2)}, u32[]{:S(2)}) collective-permute-start(f32[2,2,512,384]{3,2,1,0:T(8,128)} %fusion.10), channel_id=1, source_target_pairs={{0,1},{1,0},{2,3},{3,2},{4,5},{5,4},{6,7},{7,6},{8,9},{9,8},{10,11... | collective-permute-start | bytes 9437192 | tf_op jit(solution)/shard_map/ppermute | solution.py:72
  13.9 27.4 %collective-permute-start.2 = (f32[2,2,512,384]{3,2,1,0:T(8,128)}, f32[2,2,512,384]{3,2,1,0:T(8,128)}, u32[]{:S(2)}, u32[]{:S(2)}) collective-permute-start(f32[2,2,512,384]{3,2,1,0:T(8,128)} %fusion.18), channel_id=1, source_target_pairs={{0,1},{1,0},{2,3},{3,2},{4,5},{5,4},{6,7},{7,6},{8,9},{9,8},{10,11... | collective-permute-start | bytes 9437192 | tf_op jit(solution)/shard_map/ppermute | solution.py:72
  30.0 19.8 %collective-permute-start.1 = (f32[2,256,384]{2,1,0:T(8,128)}, f32[2,256,384]{2,1,0:T(8,128)}, u32[]{:S(2)}, u32[]{:S(2)}) collective-permute-start(f32[2,256,384]{2,1,0:T(8,128)} %get-tuple-element.56), channel_id=1, source_target_pairs={{0,2},{1,3},{2,4},{3,5},{4,6},{5,7},{6,0},{7,1},{8,10},{9,11},{10,... | collective-permute-start | bytes 2359304 | tf_op jit(solution)/shard_map/ppermute | solution.py:46
  30.4 20.7 %collective-permute-start.5 = (f32[2,256,384]{2,1,0:T(8,128)}, f32[2,256,384]{2,1,0:T(8,128)}, u32[]{:S(2)}, u32[]{:S(2)}) collective-permute-start(f32[2,256,384]{2,1,0:T(8,128)} %get-tuple-element.57), channel_id=1, source_target_pairs={{0,6},{1,7},{2,0},{3,1},{4,2},{5,3},{6,4},{7,5},{8,14},{9,15},{10,... | collective-permute-start | bytes 2359304 | tf_op jit(solution)/shard_map/ppermute | solution.py:46
  45.2 8.6 %copy-start = (f32[2,2,512,384]{3,2,1,0:T(8,128)}, f32[2,2,512,384]{3,2,1,0:T(8,128)S(1)}, u32[]{:S(2)}) copy-start(f32[2,2,512,384]{3,2,1,0:T(8,128)S(1)} %fusion.22) | copy-start | bytes 9437188
  45.2 19.0 %copy-start.9 = (s32[128,24]{1,0:T(8,128)S(1)}, s32[128,24]{1,0:T(8,128)}, u32[]{:S(2)}) copy-start(s32[128,24]{1,0:T(8,128)} %reshape.204) | copy-start | bytes 36868
  45.2 20.3 %copy-start.10 = (s32[128,24]{1,0:T(8,128)S(1)}, s32[128,24]{1,0:T(8,128)}, u32[]{:S(2)}) copy-start(s32[128,24]{1,0:T(8,128)} %reshape.206) | copy-start | bytes 36868
  45.2 23.8 %copy-start.8 = (bf16[8,6,512]{2,0,1:T(8,128)(2,1)S(1)}, bf16[8,6,512]{2,0,1:T(8,128)(2,1)}, u32[]{:S(2)}) copy-start(bf16[8,6,512]{2,0,1:T(8,128)(2,1)} %convolution_convert_fusion) | copy-start | bytes 147460
  45.2 35.0 %copy-start.3 = (f32[64,384]{0,1:T(8,128)S(1)}, f32[64,384]{0,1:T(8,128)}, u32[]{:S(2)}) copy-start(f32[64,384]{0,1:T(8,128)} %copy.127) | copy-start | bytes 294916
  69.6 32.3 %all-to-all-start = ((bf16[8,6,512]{2,1,0:T(8,128)(2,1)}), bf16[8,6,512]{2,1,0:T(8,128)(2,1)S(1)}, u32[]{:S(2)}, u32[]{:S(2)}) async-start(bf16[8,6,512]{2,1,0:T(8,128)(2,1)} %copy.99), calls=%async_computation | async-start | bytes 131072 | tf_op jit(solution)/shard_map/all_to_all | solution.py:180
  76.0 18.2 %collective-permute-start.3 = (f32[2,256,384]{2,1,0:T(8,128)}, f32[2,256,384]{2,1,0:T(8,128)S(1)}, u32[]{:S(2)}, u32[]{:S(2)}) collective-permute-start(f32[2,256,384]{2,1,0:T(8,128)} %get-tuple-element.20), channel_id=1, source_target_pairs={{0,2},{1,3},{2,4},{3,5},{4,6},{5,7},{6,0},{7,1},{8,10},{9,11},{10,... | collective-permute-start | bytes 2359304 | tf_op jit(solution)/shard_map/ppermute | solution.py:46
  76.3 19.5 %collective-permute-start.6 = (f32[2,256,384]{2,1,0:T(8,128)}, f32[2,256,384]{2,1,0:T(8,128)S(1)}, u32[]{:S(2)}, u32[]{:S(2)}) collective-permute-start(f32[2,256,384]{2,1,0:T(8,128)} %get-tuple-element.55), channel_id=1, source_target_pairs={{0,6},{1,7},{2,0},{3,1},{4,2},{5,3},{6,4},{7,5},{8,14},{9,15},{10,... | collective-permute-start | bytes 2359304 | tf_op jit(solution)/shard_map/ppermute | solution.py:46
  81.0 19.4 %copy-start.13 = (pred[384]{0:T(512)(128)(4,1)S(1)}, pred[384]{0:T(512)(128)(4,1)}, u32[]{:S(2)}) copy-start(pred[384]{0:T(512)(128)(4,1)} %compare_and_fusion.3) | copy-start | bytes 1156
  81.0 19.4 %copy-start.18 = (f32[64]{0:T(128)S(1)}, f32[64]{0:T(128)}, u32[]{:S(2)}) copy-start(f32[64]{0:T(128)} %dynamic_slice.76) | copy-start | bytes 772
  97.2 17.5 %collective-permute-start.4 = (f32[2,256,384]{2,1,0:T(8,128)}, f32[2,256,384]{2,1,0:T(8,128)}, u32[]{:S(2)}, u32[]{:S(2)}) collective-permute-start(f32[2,256,384]{2,1,0:T(8,128)} %get-tuple-element.52), channel_id=1, source_target_pairs={{0,2},{1,3},{2,4},{3,5},{4,6},{5,7},{6,0},{7,1},{8,10},{9,11},{10,... | collective-permute-start | bytes 2359304 | tf_op jit(solution)/shard_map/ppermute | solution.py:46
  97.4 18.7 %collective-permute-start.7 = (f32[2,256,384]{2,1,0:T(8,128)}, f32[2,256,384]{2,1,0:T(8,128)}, u32[]{:S(2)}, u32[]{:S(2)}) collective-permute-start(f32[2,256,384]{2,1,0:T(8,128)} %get-tuple-element.53), channel_id=1, source_target_pairs={{0,6},{1,7},{2,0},{3,1},{4,2},{5,3},{6,4},{7,5},{8,14},{9,15},{10,... | collective-permute-start | bytes 2359304 | tf_op jit(solution)/shard_map/ppermute | solution.py:46
  99.2 17.0 %copy-start.1 = (f32[2,2,512,384]{3,2,1,0:T(8,128)S(1)}, f32[2,2,512,384]{3,2,1,0:T(8,128)}, u32[]{:S(2)}) copy-start(f32[2,2,512,384]{3,2,1,0:T(8,128)} %copy-done) | copy-start | bytes 9437188
  117.7 18.4 %copy-start.6 = (f32[512,384]{1,0:T(8,128)S(1)}, f32[512,384]{1,0:T(8,128)}, u32[]{:S(2)}) copy-start(f32[512,384]{1,0:T(8,128)} %param.17) | copy-start | bytes 2359300
  117.9 18.2 %collective-permute-start.8 = (f32[512,384]{1,0:T(8,128)S(1)}, f32[512,384]{1,0:T(8,128)}, u32[]{:S(2)}, u32[]{:S(2)}) collective-permute-start(f32[512,384]{1,0:T(8,128)S(1)} %dynamic-slice_bitcast_fusion.8), channel_id=1, source_target_pairs={{0,8},{1,9},{2,10},{3,11},{4,12},{5,13},{6,14},{7,15},{8,0},{9,1},... | collective-permute-start | bytes 2359304 | tf_op jit(solution)/shard_map/ppermute | solution.py:83
  138.3 9.3 %collective-permute-start.9 = (bf16[512,384]{1,0:T(8,128)(2,1)S(1)}, bf16[512,384]{1,0:T(8,128)(2,1)S(1)}, u32[]{:S(2)}, u32[]{:S(2)}) collective-permute-start(bf16[512,384]{1,0:T(8,128)(2,1)S(1)} %get-tuple-element.36), channel_id=1, source_target_pairs={{0,8},{1,9},{2,10},{3,11},{4,12},{5,13},{6,14},{7,15},{8,0},{9,1},... | collective-permute-start | bytes 1179656 | tf_op jit(solution)/shard_map/ppermute | solution.py:88
  147.8 11.5 %collective-permute-start.10 = (bf16[2,256,384]{2,1,0:T(8,128)(2,1)S(1)}, bf16[2,256,384]{2,1,0:T(8,128)(2,1)S(1)}, u32[]{:S(2)}, u32[]{:S(2)}) collective-permute-start(bf16[2,256,384]{2,1,0:T(8,128)(2,1)S(1)} %get-tuple-element.58), channel_id=1, source_target_pairs={{0,2},{1,3},{2,4},{3,5},{4,6},{5,7},{6,0},{7,1},{8,10},{9,11},{10,... | collective-permute-start | bytes 1179656 | tf_op jit(solution)/shard_map/ppermute | solution.py:59
  148.5 11.5 %collective-permute-start.13 = (bf16[2,256,384]{2,1,0:T(8,128)(2,1)S(1)}, bf16[2,256,384]{2,1,0:T(8,128)(2,1)S(1)}, u32[]{:S(2)}, u32[]{:S(2)}) collective-permute-start(bf16[2,256,384]{2,1,0:T(8,128)(2,1)S(1)} %get-tuple-element.59), channel_id=1, source_target_pairs={{0,6},{1,7},{2,0},{3,1},{4,2},{5,3},{6,4},{7,5},{8,14},{9,15},{10,... | collective-permute-start | bytes 1179656 | tf_op jit(solution)/shard_map/ppermute | solution.py:59
  149.9 37.7 %slice-start = ((s8[8388608]{0:T(1024)(128)(4,1)}), s8[4194304]{0:T(1024)(128)(4,1)S(1)}, s32[]{:S(2)}) async-start(s8[8388608]{0:T(1024)(128)(4,1)} %bitcast.182), calls=%async_computation.3 | async-start | bytes 8388608
  159.4 11.7 %collective-permute-start.11 = (bf16[2,256,384]{2,1,0:T(8,128)(2,1)S(1)}, bf16[2,256,384]{2,1,0:T(8,128)(2,1)S(1)}, u32[]{:S(2)}, u32[]{:S(2)}) collective-permute-start(bf16[2,256,384]{2,1,0:T(8,128)(2,1)S(1)} %collective-permute-done.10), channel_id=1, source_target_pairs={{0,2},{1,3},{2,4},{3,5},{4,6},{5,7},{6,0},{7,1},{8,10},{9,11},{10,... | collective-permute-start | bytes 1179656 | tf_op jit(solution)/shard_map/ppermute | solution.py:59
  159.9 12.6 %collective-permute-start.14 = (bf16[2,256,384]{2,1,0:T(8,128)(2,1)S(1)}, bf16[2,256,384]{2,1,0:T(8,128)(2,1)S(1)}, u32[]{:S(2)}, u32[]{:S(2)}) collective-permute-start(bf16[2,256,384]{2,1,0:T(8,128)(2,1)S(1)} %collective-permute-done.13), channel_id=1, source_target_pairs={{0,6},{1,7},{2,0},{3,1},{4,2},{5,3},{6,4},{7,5},{8,14},{9,15},{10,... | collective-permute-start | bytes 1179656 | tf_op jit(solution)/shard_map/ppermute | solution.py:59
  171.0 7.8 %collective-permute-start.12 = (bf16[2,256,384]{2,1,0:T(8,128)(2,1)S(1)}, bf16[2,256,384]{2,1,0:T(8,128)(2,1)S(1)}, u32[]{:S(2)}, u32[]{:S(2)}) collective-permute-start(bf16[2,256,384]{2,1,0:T(8,128)(2,1)S(1)} %collective-permute-done.11), channel_id=1, source_target_pairs={{0,2},{1,3},{2,4},{3,5},{4,6},{5,7},{6,0},{7,1},{8,10},{9,11},{10,... | collective-permute-start | bytes 1179656 | tf_op jit(solution)/shard_map/ppermute | solution.py:59
  172.5 9.0 %collective-permute-start.15 = (bf16[2,256,384]{2,1,0:T(8,128)(2,1)S(1)}, bf16[2,256,384]{2,1,0:T(8,128)(2,1)S(1)}, u32[]{:S(2)}, u32[]{:S(2)}) collective-permute-start(bf16[2,256,384]{2,1,0:T(8,128)(2,1)S(1)} %collective-permute-done.14), channel_id=1, source_target_pairs={{0,6},{1,7},{2,0},{3,1},{4,2},{5,3},{6,4},{7,5},{8,14},{9,15},{10,... | collective-permute-start | bytes 1179656 | tf_op jit(solution)/shard_map/ppermute | solution.py:59
  173.1 14.5 %slice-start.1 = ((s8[8388608]{0:T(1024)(128)(4,1)}), s8[4194304]{0:T(1024)(128)(4,1)S(1)}, s32[]{:S(2)}) async-start(s8[8388608]{0:T(1024)(128)(4,1)} %bitcast.182), calls=%async_computation.4 | async-start | bytes 8388608
  181.9 5.7 %collective-permute-start.16 = (bf16[2,4,512,384]{3,2,1,0:T(8,128)(2,1)S(1)}, bf16[2,4,512,384]{3,2,1,0:T(8,128)(2,1)S(1)}, u32[]{:S(2)}, u32[]{:S(2)}) collective-permute-start(bf16[2,4,512,384]{3,2,1,0:T(8,128)(2,1)S(1)} %maximum_bitcast_fusion), channel_id=1, source_target_pairs={{0,1},{1,0},{2,3},{3,2},{4,5},{5,4},{6,7},{7,6},{8,9},{9,8},{10,11... | collective-permute-start | bytes 9437192 | tf_op jit(solution)/shard_map/ppermute | solution.py:94
  194.1 19.9 %copy-start.4 = (f32[64,384]{0,1:T(8,128)S(1)}, f32[64,384]{0,1:T(8,128)}, u32[]{:S(2)}) copy-start(f32[64,384]{0,1:T(8,128)} %broadcast_subtract_fusion) | copy-start | bytes 294916
  194.1 19.9 %copy-start.5 = (f32[64,384]{0,1:T(8,128)S(1)}, f32[64,384]{0,1:T(8,128)}, u32[]{:S(2)}) copy-start(f32[64,384]{0,1:T(8,128)} %multiply_bitcast_fusion) | copy-start | bytes 294916
  215.1 14.8 %all-to-all-start.2 = ((f32[8,64,384]{2,1,0:T(8,128)}), f32[8,64,384]{2,1,0:T(8,128)S(1)}, u32[]{:S(2)}, u32[]{:S(2)}) async-start(f32[8,64,384]{2,1,0:T(8,128)} %broadcast_in_dim.153), calls=%async_computation.2 | async-start | bytes 1572864 | tf_op jit(solution)/shard_map/all_to_all | solution.py:209
  (8 other events, 27.2 us)

commit v11 on v8

--- a/solution.py
+++ b/solution.py
@@ -178,10 +178,9 @@
     masked = masked.reshape(slab_axis * CAP, YHI, XR, CORES, -1)
     masked_keep = pick(masked, core, 3)
     masked_send = pick(masked, 1 - core, 3)
-    ring_out, masked_keep, masked_send, upper, lower, base = lax.optimization_barrier(
-        (ring_out, masked_keep, masked_send, upper, lower, base)
-    )
+    ring_out, upper, lower, base = lax.optimization_barrier((ring_out, upper, lower, base))
     flow = bus_pair_sum(ring_out)
+    flow, masked_keep, masked_send = lax.optimization_barrier((flow, masked_keep, masked_send))
     moved = prices + step_dual * flow
     bound = step_dual * limits[:, None]
     new_prices = moved - jnp.clip(moved, -bound, bound)

time: 206 us -> 209 us (1.015)
  waiting for transfers between devices: 99.6 us -> 106 us
  blocking collectives: 20.6 us -> 17.3 us
  starting transfers between devices: 28.9 us -> 26.7 us
    ppermute x1, waiting for transfers between devices: 15 us -> 0.01 us  [bus_pair_sum(): return pick(z, yh, 0) + lax.ppermute(pick(z, 1 - yh, 0), 'bus', Y_SWAP)]
    ppermute x6, waiting for transfers between devices: 31.4 us -> 42.9 us  [ring_scatter(): acc = lax.ppermute(acc, 'bus', perm) + more]
    all_to_all x1, waiting for transfers between devices: 5.59 us -> 13.2 us  [per_device(): arrived_w = lax.all_to_all(outgoing_w, 'br', 0, 0, tiled=True)]
    all_to_all x1, blocking collectives: 20.6 us -> 17.3 us  [per_device(): gathered = lax.all_to_all(outgoing, 'br', 0, 0, tiled=True)]
  transfers between devices with their start and end apart: 19 -> 19, of which waited for: 16 -> 16; matrix products, arithmetic and copies ran while one was open for 16% -> 17% of each run, Pallas kernels for 0% -> 0%
where the time goes in v11:
time: 209 us; the launch traced here: 208 us
  waiting for transfers between devices  106 us (51%)
  starting transfers between devices  26.7 us (13%)
  other arithmetic  22.2 us (11%)
  matrix products  22.2 us (11%)
  blocking collectives  17.3 us (8%)
  local copies, waits for them, and re-layouts  12.3 us (6%)
    ppermute x6, waiting for transfers between devices, ring_scatter(): acc = lax.ppermute(acc, 'bus', perm) + more  42.9 us
    ppermute x6, waiting for transfers between devices, ring_gather(): cur = lax.ppermute(cur, 'bus', perm)  27.7 us
    all_to_all x1, blocking collectives, per_device(): gathered = lax.all_to_all(outgoing, 'br', 0, 0, tiled=True)  17.3 us
    dot_general x8, matrix products, flow_part(): return jnp.dot(rows, inject_half, preferred_element_type=jnp.float32)  15.5 us
    all_to_all x1, waiting for transfers between devices, per_device(): arrived_w = lax.all_to_all(outgoing_w, 'br', 0, 0, tiled=True)  13.2 us
    all_to_all x1, waiting for transfers between devices, per_device(): lax.all_to_all(jnp.broadcast_to(my_new[None], (slab_axis, share_rows, sce...  8.95 us
    ppermute x1, waiting for transfers between devices, bus_all_gather(): other = lax.ppermute(p, 'bus', Y_SWAP)  7.41 us
    ppermute x6, starting transfers between devices, ring_scatter(): acc = lax.ppermute(acc, 'bus', perm) + more  6.22 us
  transfers between devices with their start and end apart: 19, of which 16 were waited for; matrix products, arithmetic and copies ran while one was open for 17% of the time, Pallas kernels for 0%

profile of v11, /device:TPU:6, one launch (start us, length us, event | category | flops | bytes accessed | tf_op | source)
XLA Modules:
  0.0 207.9 jit_solution(17163805722432165310)
XLA Ops:
  1.9 1.9 convolution_bitcast_fusion.5
  3.9 1.9 convolution_bitcast_fusion.4
  5.8 1.9 pad_maximum_fusion
  7.7 1.9 convolution_bitcast_fusion.1
  9.6 1.9 convolution_bitcast_fusion
  11.6 1.8 pad_maximum_fusion.1
  20.3 1.9 convolution_bitcast_fusion.3
  22.3 1.9 convolution_bitcast_fusion.7
  24.2 1.9 convolution_bitcast_fusion.6
  26.3 2.2 %maximum_add_fusion = f32[2,2,512,384]{3,2,1,0:T(8,128)S(1)} fusion(f32[2,2,512,384]{3,2,1,0:T(8,128)} %collective-permute-done, f32[1,2,512,384]{3,2,1,0:T(8,128)S(1)} %convolution_bitcast_fusion.6, f32[1,2,512,384]{3,2,1,0:T(8,128)S(1)} %convolution_bitcast_fusion.7), kind=kLoop, calls=%fused_computation.11 | loop fusion | flops 1572864 | bytes 9437184 | tf_op jit(solution)/shard_map/add | solution.py:72
  30.7 1.9 convolution_bitcast_fusion.2
  33.4 2.2 %maximum_add_fusion.1 = f32[2,2,512,384]{3,2,1,0:T(8,128)S(1)} fusion(f32[2,2,512,384]{3,2,1,0:T(8,128)} %collective-permute-done.2, f32[1,2,512,384]{3,2,1,0:T(8,128)S(1)} %convolution_bitcast_fusion.2, f32[1,2,512,384]{3,2,1,0:T(8,128)S(1)} %convolution_bitcast_fusion.3), kind=kLoop, calls=%fused_computation.13 | loop fusion | flops 1572864 | bytes 9437184 | tf_op jit(solution)/shard_map/add | solution.py:72
  35.6 12.5 %collective-permute-done.1 = f32[2,256,384]{2,1,0:T(8,128)S(1)} collective-permute-done((f32[2,256,384]{2,1,0:T(8,128)S(1)}, f32[2,256,384]{2,1,0:T(8,128)S(1)}, u32[]{:S(2)}, u32[]{:S(2)}) %collective-permute-start.1) | collective-permute-done | bytes 786464 | tf_op jit(solution)/shard_map/ppermute | solution.py:46
  55.9 13.5 %collective-permute-done.3 = f32[2,256,384]{2,1,0:T(8,128)} collective-permute-done((f32[2,256,384]{2,1,0:T(8,128)}, f32[2,256,384]{2,1,0:T(8,128)}, u32[]{:S(2)}, u32[]{:S(2)}) %collective-permute-start.3) | collective-permute-done | bytes 786464 | tf_op jit(solution)/shard_map/ppermute | solution.py:46
  70.9 2.0 fusion.36
  73.3 1.7 collective-permute-start.7
  77.7 12.6 %collective-permute-done.4 = f32[2,256,384]{2,1,0:T(8,128)S(1)} collective-permute-done((f32[2,256,384]{2,1,0:T(8,128)S(1)}, f32[2,256,384]{2,1,0:T(8,128)S(1)}, u32[]{:S(2)}, u32[]{:S(2)}) %collective-permute-start.4) | collective-permute-done | bytes 786464 | tf_op jit(solution)/shard_map/ppermute | solution.py:46
  92.3 3.5 %collective-permute-start.8 = (f32[512,384]{1,0:T(8,128)S(1)}, f32[512,384]{1,0:T(8,128)S(1)}, u32[]{:S(2)}, u32[]{:S(2)}) collective-permute-start(f32[512,384]{1,0:T(8,128)S(1)} %dynamic-slice_bitcast_fusion), channel_id=1, source_target_pairs={{0,8},{1,9},{2,10},{3,11},{4,12},{5,13},{6,14},{7,15},{8,0},{9,1},... | collective-permute-start | bytes 2359304 | tf_op jit(solution)/shard_map/ppermute | solution.py:83
  96.4 5.4 %all-to-all-start = ((bf16[8,6,512]{2,1,0:T(8,128)(2,1)}), bf16[8,6,512]{2,1,0:T(8,128)(2,1)S(1)}, u32[]{:S(2)}, u32[]{:S(2)}) async-start(bf16[8,6,512]{2,1,0:T(8,128)(2,1)} %copy.103), calls=%async_computation | async-start | bytes 131072 | tf_op jit(solution)/shard_map/all_to_all | solution.py:176
  101.9 13.2 %all-to-all-done = bf16[8,6,512]{2,1,0:T(8,128)(2,1)S(1)} async-done(((bf16[8,6,512]{2,1,0:T(8,128)(2,1)}), bf16[8,6,512]{2,1,0:T(8,128)(2,1)S(1)}, u32[]{:S(2)}, u32[]{:S(2)}) %all-to-all-start) | async-done | bytes 49184 | tf_op jit(solution)/shard_map/all_to_all | solution.py:176
  117.4 1.9 collective-permute-start.9
  119.2 7.4 %collective-permute-done.9 = bf16[512,384]{1,0:T(8,128)(2,1)S(1)} collective-permute-done((bf16[512,384]{1,0:T(8,128)(2,1)S(1)}, bf16[512,384]{1,0:T(8,128)(2,1)S(1)}, u32[]{:S(2)}, u32[]{:S(2)}) %collective-permute-start.9) | collective-permute-done | bytes 393248 | tf_op jit(solution)/shard_map/ppermute | solution.py:88
  129.6 9.0 %collective-permute-done.10 = bf16[2,256,384]{2,1,0:T(8,128)(2,1)S(1)} collective-permute-done((bf16[2,256,384]{2,1,0:T(8,128)(2,1)S(1)}, bf16[2,256,384]{2,1,0:T(8,128)(2,1)S(1)}, u32[]{:S(2)}, u32[]{:S(2)}) %collective-permute-start.10) | collective-permute-done | bytes 393248 | tf_op jit(solution)/shard_map/ppermute | solution.py:59
  140.8 9.4 %collective-permute-done.11 = bf16[2,256,384]{2,1,0:T(8,128)(2,1)S(1)} collective-permute-done((bf16[2,256,384]{2,1,0:T(8,128)(2,1)S(1)}, bf16[2,256,384]{2,1,0:T(8,128)(2,1)S(1)}, u32[]{:S(2)}, u32[]{:S(2)}) %collective-permute-start.11) | collective-permute-done | bytes 393248 | tf_op jit(solution)/shard_map/ppermute | solution.py:59
  152.4 5.6 %collective-permute-done.12 = bf16[2,256,384]{2,1,0:T(8,128)(2,1)S(1)} collective-permute-done((bf16[2,256,384]{2,1,0:T(8,128)(2,1)S(1)}, bf16[2,256,384]{2,1,0:T(8,128)(2,1)S(1)}, u32[]{:S(2)}, u32[]{:S(2)}) %collective-permute-start.12) | collective-permute-done | bytes 393248 | tf_op jit(solution)/shard_map/ppermute | solution.py:59
  158.1 2.8 %collective-permute-done.15 = bf16[2,256,384]{2,1,0:T(8,128)(2,1)S(1)} collective-permute-done((bf16[2,256,384]{2,1,0:T(8,128)(2,1)S(1)}, bf16[2,256,384]{2,1,0:T(8,128)(2,1)S(1)}, u32[]{:S(2)}, u32[]{:S(2)}) %collective-permute-start.15) | collective-permute-done | bytes 393248 | tf_op jit(solution)/shard_map/ppermute | solution.py:59
  161.4 5.6 %collective-permute-done.16 = bf16[2,4,512,384]{3,2,1,0:T(8,128)(2,1)S(1)} collective-permute-done((bf16[2,4,512,384]{3,2,1,0:T(8,128)(2,1)S(1)}, bf16[2,4,512,384]{3,2,1,0:T(8,128)(2,1)S(1)}, u32[]{:S(2)}, u32[]{:S(2)}) %collective-permute-start.16) | collective-permute-done | bytes 3145760 | tf_op jit(solution)/shard_map/ppermute | solution.py:94
  167.1 2.4 %fusion.9 = f32[512,384]{1,0:T(8,128)S(1)} fusion(bf16[2,4,512,384]{3,2,1,0:T(8,128)(2,1)S(1)} %collective-permute-done.16, bf16[2,4,2,512,512]{4,3,2,1,0:T(8,128)(2,1)S(1)} %bitcast.214, s32[]{:T(128)S(6)} %select_n.209), kind=kOutput, calls=%fused_computation.26 | convolution fusion | flops 1610612736 | bytes 8126468 | tf_op jit(solution)/shard_map/dot_general | solution.py:191
  169.5 2.4 %fusion.12 = f32[512,384]{1,0:T(8,128)S(1)} fusion(f32[512,384]{1,0:T(8,128)S(1)} %fusion.9, bf16[2,4,2,512,512]{4,3,2,1,0:T(8,128)(2,1)S(1)} %bitcast.215, s32[]{:T(128)S(6)} %select_n.204, bf16[4,2,256,384]{3,2,0,1:T(8,128)(2,1)S(1)} %bitcast_dynamic-update-slice_fusion.7, bf16[4,2,256,384]{3,2,0,1:T(8,128)(2,1)S(1)} %bitcast_dynamic-update-slice_fusion.3), kind=kOutput, calls=%fused_computation.27 | convolution fusion | flops 1617100800 | bytes 8912900 | tf_op jit(solution)/shard_map/dot_general | solution.py:190
  173.6 17.3 %all_to_all.15 = f32[8,70,384]{2,1,0:T(8,128)S(1)} all-to-all(f32[8,70,384]{2,1,0:T(8,128)S(1)} %pad_maximum_fusion.3), channel_id=1, replica_groups=mesh['br'=8,'bus'=16] {'br'}, dimensions={0} | all-to-all | bytes 1720320 | tf_op jit(solution)/shard_map/all_to_all | solution.py:199
  192.2 3.5 %all-to-all-start.2 = ((f32[8,64,384]{2,1,0:T(8,128)}), f32[8,64,384]{2,1,0:T(8,128)S(1)}, u32[]{:S(2)}, u32[]{:S(2)}) async-start(f32[8,64,384]{2,1,0:T(8,128)} %broadcast_in_dim.153), calls=%async_computation.2 | async-start | bytes 1572864 | tf_op jit(solution)/shard_map/all_to_all | solution.py:204
  198.1 9.0 %all-to-all-done.2 = f32[8,64,384]{2,1,0:T(8,128)S(1)} async-done(((f32[8,64,384]{2,1,0:T(8,128)}), f32[8,64,384]{2,1,0:T(8,128)S(1)}, u32[]{:S(2)}, u32[]{:S(2)}) %all-to-all-start.2) | async-done | bytes 786464 | tf_op jit(solution)/shard_map/all_to_all | solution.py:204
  (150 shorter events, 42.0 us)
Async XLA Ops:
  7.7 18.6 %collective-permute-start = (f32[2,2,512,384]{3,2,1,0:T(8,128)}, f32[2,2,512,384]{3,2,1,0:T(8,128)}, u32[]{:S(2)}, u32[]{:S(2)}) collective-permute-start(f32[2,2,512,384]{3,2,1,0:T(8,128)} %pad_maximum_fusion), channel_id=1, source_target_pairs={{0,1},{1,0},{2,3},{3,2},{4,5},{5,4},{6,7},{7,6},{8,9},{9,8},{10,11... | collective-permute-start | bytes 9437192 | tf_op jit(solution)/shard_map/ppermute | solution.py:72
  11.6 6.4 %copy-start.11 = (s32[1024,3]{0,1:T(4,128)S(1)}, s32[1024,3]{0,1:T(4,128)}, u32[]{:S(2)}) copy-start(s32[1024,3]{0,1:T(4,128)} %param.26) | copy-start | bytes 36868
  13.5 20.0 %collective-permute-start.2 = (f32[2,2,512,384]{3,2,1,0:T(8,128)}, f32[2,2,512,384]{3,2,1,0:T(8,128)}, u32[]{:S(2)}, u32[]{:S(2)}) collective-permute-start(f32[2,2,512,384]{3,2,1,0:T(8,128)} %pad_maximum_fusion.1), channel_id=1, source_target_pairs={{0,1},{1,0},{2,3},{3,2},{4,5},{5,4},{6,7},{7,6},{8,9},{9,8},{10,11... | collective-permute-start | bytes 9437192 | tf_op jit(solution)/shard_map/ppermute | solution.py:72
  14.4 9.8 %copy-start.8 = (s32[128,24]{1,0:T(8,128)}, s32[128,24]{1,0:T(8,128)S(1)}, u32[]{:S(2)}) copy-start(s32[128,24]{1,0:T(8,128)S(1)} %reshape.196) | copy-start | bytes 36868
  20.3 5.8 %copy-start.15 = (s32[24]{0:T(128)}, s32[24]{0:T(128)S(1)}, u32[]{:S(2)}) copy-start(s32[24]{0:T(128)S(1)} %convert_reduce_fusion.1) | copy-start | bytes 292
  28.5 22.2 %copy-start = (f32[2,2,512,384]{3,2,1,0:T(8,128)}, f32[2,2,512,384]{3,2,1,0:T(8,128)S(1)}, u32[]{:S(2)}) copy-start(f32[2,2,512,384]{3,2,1,0:T(8,128)S(1)} %maximum_add_fusion) | copy-start | bytes 9437188
  28.7 19.5 %collective-permute-start.1 = (f32[2,256,384]{2,1,0:T(8,128)S(1)}, f32[2,256,384]{2,1,0:T(8,128)S(1)}, u32[]{:S(2)}, u32[]{:S(2)}) collective-permute-start(f32[2,256,384]{2,1,0:T(8,128)S(1)} %get-tuple-element.34), channel_id=1, source_target_pairs={{0,2},{1,3},{2,4},{3,5},{4,6},{5,7},{6,0},{7,1},{8,10},{9,11},{10,... | collective-permute-start | bytes 2359304 | tf_op jit(solution)/shard_map/ppermute | solution.py:46
  29.1 20.4 %collective-permute-start.5 = (f32[2,256,384]{2,1,0:T(8,128)S(1)}, f32[2,256,384]{2,1,0:T(8,128)S(1)}, u32[]{:S(2)}, u32[]{:S(2)}) collective-permute-start(f32[2,256,384]{2,1,0:T(8,128)S(1)} %get-tuple-element.35), channel_id=1, source_target_pairs={{0,6},{1,7},{2,0},{3,1},{4,2},{5,3},{6,4},{7,5},{8,14},{9,15},{10,... | collective-permute-start | bytes 2359304 | tf_op jit(solution)/shard_map/ppermute | solution.py:46
  35.6 17.8 %copy-start.12 = (s32[384]{0:T(512)S(1)}, s32[384]{0:T(512)}, u32[]{:S(2)}) copy-start(s32[384]{0:T(512)} %param.24) | copy-start | bytes 4612
  50.8 18.6 %collective-permute-start.3 = (f32[2,256,384]{2,1,0:T(8,128)}, f32[2,256,384]{2,1,0:T(8,128)}, u32[]{:S(2)}, u32[]{:S(2)}) collective-permute-start(f32[2,256,384]{2,1,0:T(8,128)} %get-tuple-element.13), channel_id=1, source_target_pairs={{0,2},{1,3},{2,4},{3,5},{4,6},{5,7},{6,0},{7,1},{8,10},{9,11},{10,... | collective-permute-start | bytes 2359304 | tf_op jit(solution)/shard_map/ppermute | solution.py:46
  51.2 19.7 %collective-permute-start.6 = (f32[2,256,384]{2,1,0:T(8,128)}, f32[2,256,384]{2,1,0:T(8,128)}, u32[]{:S(2)}, u32[]{:S(2)}) collective-permute-start(f32[2,256,384]{2,1,0:T(8,128)} %get-tuple-element.33), channel_id=1, source_target_pairs={{0,6},{1,7},{2,0},{3,1},{4,2},{5,3},{6,4},{7,5},{8,14},{9,15},{10,... | collective-permute-start | bytes 2359304 | tf_op jit(solution)/shard_map/ppermute | solution.py:46
  55.1 21.8 %copy-start.4 = (f32[384,64]{1,0:T(8,128)S(1)}, f32[384,64]{1,0:T(8,128)}, u32[]{:S(2)}) copy-start(f32[384,64]{1,0:T(8,128)} %gather_fusion.1) | copy-start | bytes 294916
  72.9 17.4 %collective-permute-start.4 = (f32[2,256,384]{2,1,0:T(8,128)S(1)}, f32[2,256,384]{2,1,0:T(8,128)S(1)}, u32[]{:S(2)}, u32[]{:S(2)}) collective-permute-start(f32[2,256,384]{2,1,0:T(8,128)S(1)} %get-tuple-element.30), channel_id=1, source_target_pairs={{0,2},{1,3},{2,4},{3,5},{4,6},{5,7},{6,0},{7,1},{8,10},{9,11},{10,... | collective-permute-start | bytes 2359304 | tf_op jit(solution)/shard_map/ppermute | solution.py:46
  73.3 18.6 %collective-permute-start.7 = (f32[2,256,384]{2,1,0:T(8,128)S(1)}, f32[2,256,384]{2,1,0:T(8,128)S(1)}, u32[]{:S(2)}, u32[]{:S(2)}) collective-permute-start(f32[2,256,384]{2,1,0:T(8,128)S(1)} %get-tuple-element.31), channel_id=1, source_target_pairs={{0,6},{1,7},{2,0},{3,1},{4,2},{5,3},{6,4},{7,5},{8,14},{9,15},{10,... | collective-permute-start | bytes 2359304 | tf_op jit(solution)/shard_map/ppermute | solution.py:46
  92.3 23.9 %collective-permute-start.8 = (f32[512,384]{1,0:T(8,128)S(1)}, f32[512,384]{1,0:T(8,128)S(1)}, u32[]{:S(2)}, u32[]{:S(2)}) collective-permute-start(f32[512,384]{1,0:T(8,128)S(1)} %dynamic-slice_bitcast_fusion), channel_id=1, source_target_pairs={{0,8},{1,9},{2,10},{3,11},{4,12},{5,13},{6,14},{7,15},{8,0},{9,1},... | collective-permute-start | bytes 2359304 | tf_op jit(solution)/shard_map/ppermute | solution.py:83
  96.4 18.7 %all-to-all-start = ((bf16[8,6,512]{2,1,0:T(8,128)(2,1)}), bf16[8,6,512]{2,1,0:T(8,128)(2,1)S(1)}, u32[]{:S(2)}, u32[]{:S(2)}) async-start(bf16[8,6,512]{2,1,0:T(8,128)(2,1)} %copy.103), calls=%async_computation | async-start | bytes 131072 | tf_op jit(solution)/shard_map/all_to_all | solution.py:176
  117.4 9.3 %collective-permute-start.9 = (bf16[512,384]{1,0:T(8,128)(2,1)S(1)}, bf16[512,384]{1,0:T(8,128)(2,1)S(1)}, u32[]{:S(2)}, u32[]{:S(2)}) collective-permute-start(bf16[512,384]{1,0:T(8,128)(2,1)S(1)} %get-tuple-element.22), channel_id=1, source_target_pairs={{0,8},{1,9},{2,10},{3,11},{4,12},{5,13},{6,14},{7,15},{8,0},{9,1},... | collective-permute-start | bytes 1179656 | tf_op jit(solution)/shard_map/ppermute | solution.py:88
  126.9 11.7 %collective-permute-start.10 = (bf16[2,256,384]{2,1,0:T(8,128)(2,1)S(1)}, bf16[2,256,384]{2,1,0:T(8,128)(2,1)S(1)}, u32[]{:S(2)}, u32[]{:S(2)}) collective-permute-start(bf16[2,256,384]{2,1,0:T(8,128)(2,1)S(1)} %get-tuple-element.36), channel_id=1, source_target_pairs={{0,2},{1,3},{2,4},{3,5},{4,6},{5,7},{6,0},{7,1},{8,10},{9,11},{10,... | collective-permute-start | bytes 1179656 | tf_op jit(solution)/shard_map/ppermute | solution.py:59
  127.7 11.6 %collective-permute-start.13 = (bf16[2,256,384]{2,1,0:T(8,128)(2,1)S(1)}, bf16[2,256,384]{2,1,0:T(8,128)(2,1)S(1)}, u32[]{:S(2)}, u32[]{:S(2)}) collective-permute-start(bf16[2,256,384]{2,1,0:T(8,128)(2,1)S(1)} %get-tuple-element.37), channel_id=1, source_target_pairs={{0,6},{1,7},{2,0},{3,1},{4,2},{5,3},{6,4},{7,5},{8,14},{9,15},{10,... | collective-permute-start | bytes 1179656 | tf_op jit(solution)/shard_map/ppermute | solution.py:59
  129.2 37.9 %slice-start = ((s8[8388608]{0:T(1024)(128)(4,1)}), s8[4194304]{0:T(1024)(128)(4,1)S(1)}, s32[]{:S(2)}) async-start(s8[8388608]{0:T(1024)(128)(4,1)} %bitcast.212), calls=%async_computation.3 | async-start | bytes 8388608
  138.6 11.6 %collective-permute-start.11 = (bf16[2,256,384]{2,1,0:T(8,128)(2,1)S(1)}, bf16[2,256,384]{2,1,0:T(8,128)(2,1)S(1)}, u32[]{:S(2)}, u32[]{:S(2)}) collective-permute-start(bf16[2,256,384]{2,1,0:T(8,128)(2,1)S(1)} %collective-permute-done.10), channel_id=1, source_target_pairs={{0,2},{1,3},{2,4},{3,5},{4,6},{5,7},{6,0},{7,1},{8,10},{9,11},{10,... | collective-permute-start | bytes 1179656 | tf_op jit(solution)/shard_map/ppermute | solution.py:59
  139.2 12.7 %collective-permute-start.14 = (bf16[2,256,384]{2,1,0:T(8,128)(2,1)S(1)}, bf16[2,256,384]{2,1,0:T(8,128)(2,1)S(1)}, u32[]{:S(2)}, u32[]{:S(2)}) collective-permute-start(bf16[2,256,384]{2,1,0:T(8,128)(2,1)S(1)} %collective-permute-done.13), channel_id=1, source_target_pairs={{0,6},{1,7},{2,0},{3,1},{4,2},{5,3},{6,4},{7,5},{8,14},{9,15},{10,... | collective-permute-start | bytes 1179656 | tf_op jit(solution)/shard_map/ppermute | solution.py:59
  150.3 7.8 %collective-permute-start.12 = (bf16[2,256,384]{2,1,0:T(8,128)(2,1)S(1)}, bf16[2,256,384]{2,1,0:T(8,128)(2,1)S(1)}, u32[]{:S(2)}, u32[]{:S(2)}) collective-permute-start(bf16[2,256,384]{2,1,0:T(8,128)(2,1)S(1)} %collective-permute-done.11), channel_id=1, source_target_pairs={{0,2},{1,3},{2,4},{3,5},{4,6},{5,7},{6,0},{7,1},{8,10},{9,11},{10,... | collective-permute-start | bytes 1179656 | tf_op jit(solution)/shard_map/ppermute | solution.py:59
  152.0 9.0 %collective-permute-start.15 = (bf16[2,256,384]{2,1,0:T(8,128)(2,1)S(1)}, bf16[2,256,384]{2,1,0:T(8,128)(2,1)S(1)}, u32[]{:S(2)}, u32[]{:S(2)}) collective-permute-start(bf16[2,256,384]{2,1,0:T(8,128)(2,1)S(1)} %collective-permute-done.14), channel_id=1, source_target_pairs={{0,6},{1,7},{2,0},{3,1},{4,2},{5,3},{6,4},{7,5},{8,14},{9,15},{10,... | collective-permute-start | bytes 1179656 | tf_op jit(solution)/shard_map/ppermute | solution.py:59
  152.3 14.7 %slice-start.1 = ((s8[8388608]{0:T(1024)(128)(4,1)}), s8[4194304]{0:T(1024)(128)(4,1)S(1)}, s32[]{:S(2)}) async-start(s8[8388608]{0:T(1024)(128)(4,1)} %bitcast.212), calls=%async_computation.4 | async-start | bytes 8388608
  161.3 5.7 %collective-permute-start.16 = (bf16[2,4,512,384]{3,2,1,0:T(8,128)(2,1)S(1)}, bf16[2,4,512,384]{3,2,1,0:T(8,128)(2,1)S(1)}, u32[]{:S(2)}, u32[]{:S(2)}) collective-permute-start(bf16[2,4,512,384]{3,2,1,0:T(8,128)(2,1)S(1)} %maximum_bitcast_fusion), channel_id=1, source_target_pairs={{0,1},{1,0},{2,3},{3,2},{4,5},{5,4},{6,7},{7,6},{8,9},{9,8},{10,11... | collective-permute-start | bytes 9437192 | tf_op jit(solution)/shard_map/ppermute | solution.py:94
  173.5 17.6 %copy-start.1 = (f32[64,384]{0,1:T(8,128)S(1)}, f32[64,384]{0,1:T(8,128)}, u32[]{:S(2)}) copy-start(f32[64,384]{0,1:T(8,128)} %broadcast_subtract_fusion) | copy-start | bytes 294916
  173.5 17.6 %copy-start.2 = (f32[64,384]{0,1:T(8,128)S(1)}, f32[64,384]{0,1:T(8,128)}, u32[]{:S(2)}) copy-start(f32[64,384]{0,1:T(8,128)} %multiply_bitcast_fusion) | copy-start | bytes 294916
  173.5 17.6 %copy-start.17 = (f32[64,1]{0,1:T(1,128)S(1)}, f32[64,1]{0,1:T(1,128)}, u32[]{:S(2)}) copy-start(f32[64,1]{0,1:T(1,128)} %negate_bitcast_fusion) | copy-start | bytes 772
  173.6 22.2 %copy-start.16 = (s32[24]{0:T(128)S(1)}, s32[24]{0:T(128)}, u32[]{:S(2)}) copy-start(s32[24]{0:T(128)} %copy-done.15) | copy-start | bytes 292
  173.6 22.3 %copy-start.14 = (s32[24]{0:T(128)S(1)}, s32[24]{0:T(128)}, u32[]{:S(2)}) copy-start(s32[24]{0:T(128)} %get-tuple-element.40) | copy-start | bytes 292
  192.2 14.8 %all-to-all-start.2 = ((f32[8,64,384]{2,1,0:T(8,128)}), f32[8,64,384]{2,1,0:T(8,128)S(1)}, u32[]{:S(2)}, u32[]{:S(2)}) async-start(f32[8,64,384]{2,1,0:T(8,128)} %broadcast_in_dim.153), calls=%async_computation.2 | async-start | bytes 1572864 | tf_op jit(solution)/shard_map/all_to_all | solution.py:204
  (7 other events, 17.6 us)

commit v12 on v8

--- a/solution.py
+++ b/solution.py
@@ -71,11 +71,16 @@
         keep = jnp.stack([flow_part(x, True) for x in group])
         summed.append(keep + lax.ppermute(send, "bus", CORE_SWAP))
     a, b = summed
-    half = a.shape[2] // 2
-    cw, rider = ring_scatter([a[0, :, :half], b[0, :, :half], a[1, :, :half], b[1, :, :half]], True, rider)
-    ccw, _ = ring_scatter([a[1, :, half:], b[0, :, half:], a[0, :, half:], b[1, :, half:]], False)
-    z = jnp.concatenate([cw, ccw], axis=1)
-    return z, rider
+    q = a.shape[2] // 4
+    half = 2 * q
+    cw, rider = ring_scatter([a[0, :, :q], b[0, :, :q], a[1, :, :q], b[1, :, :q]], True, rider)
+    ccw, _ = ring_scatter([a[1, :, q:half], b[0, :, q:half], a[0, :, q:half], b[1, :, q:half]], False)
+    late = jnp.concatenate([a[:, :, half:], b[:, :, half:]], axis=0)
+    late = pick(late, yh, 1) + lax.ppermute(pick(late, 1 - yh, 1), "bus", Y_SWAP)
+    cw_late, _ = ring_scatter([late[0, :q], late[2, :q], late[1, :q], late[3, :q]], True)
+    ccw_late, _ = ring_scatter([late[1, q:], late[2, q:], late[0, q:], late[3, q:]], False)
+    early = bus_pair_sum(jnp.concatenate([cw, ccw], axis=1))
+    return jnp.concatenate([early, cw_late, ccw_late], axis=0), rider
 
 
 def bus_pair_sum(z):
@@ -178,10 +183,9 @@
     masked = masked.reshape(slab_axis * CAP, YHI, XR, CORES, -1)
     masked_keep = pick(masked, core, 3)
     masked_send = pick(masked, 1 - core, 3)
-    ring_out, masked_keep, masked_send, upper, lower, base = lax.optimization_barrier(
+    flow, masked_keep, masked_send, upper, lower, base = lax.optimization_barrier(
         (ring_out, masked_keep, masked_send, upper, lower, base)
     )
-    flow = bus_pair_sum(ring_out)
     moved = prices + step_dual * flow
     bound = step_dual * limits[:, None]
     new_prices = moved - jnp.clip(moved, -bound, bound)

time: 206 us -> 207 us (level)
  waiting for transfers between devices: 99.6 us -> 83.9 us
  starting transfers between devices: 28.9 us -> 37.1 us
  other arithmetic: 21.7 us -> 26.9 us
  local copies, waits for them, and re-layouts: 11.8 us -> 16.6 us
  blocking collectives: 20.6 us -> 17.6 us
    ppermute x1, waiting for transfers between devices: 15 us -> 0.01 us  [bus_pair_sum(): return pick(z, yh, 0) + lax.ppermute(pick(z, 1 - yh, 0), 'bus', Y_SWAP)]
    ppermute x6 -> x12, starting transfers between devices: 6.22 us -> 12.6 us  [ring_scatter(): acc = lax.ppermute(acc, 'bus', perm) + more]
    all_to_all x1, waiting for transfers between devices: 5.59 us -> 9.74 us  [per_device(): arrived_w = lax.all_to_all(outgoing_w, 'br', 0, 0, tiled=True)]
    ppermute x6 -> x12, waiting for transfers between devices: 31.4 us -> 27.4 us  [ring_scatter(): acc = lax.ppermute(acc, 'bus', perm) + more]
    ppermute x0 -> x1, starting transfers between devices: none -> 3.21 us  [bus_reduce_scatter(): lax.ppermute(pick(late, 1 - yh, 1), 'bus', Y_SWAP)]
    all_to_all x1, blocking collectives: 20.6 us -> 17.6 us  [per_device(): gathered = lax.all_to_all(outgoing, 'br', 0, 0, tiled=True)]
    ppermute x6, starting transfers between devices: 5.33 us -> 8.2 us  [ring_gather(): cur = lax.ppermute(cur, 'bus', perm)]
    ppermute x6, waiting for transfers between devices: 27 us -> 24.3 us  [ring_gather(): cur = lax.ppermute(cur, 'bus', perm)]
  transfers between devices with their start and end apart: 19 -> 26, of which waited for: 16 -> 16; matrix products, arithmetic and copies ran while one was open for 16% -> 21% of each run, Pallas kernels for 0% -> 0%
where the time goes in v12:
time: 207 us; the launch traced here: 206 us
  waiting for transfers between devices  83.9 us (41%)
  starting transfers between devices  37.1 us (18%)
  other arithmetic  26.9 us (13%)
  matrix products  22.2 us (11%)
  blocking collectives  17.6 us (9%)
  local copies, waits for them, and re-layouts  16.6 us (8%)
    ppermute x12, waiting for transfers between devices, ring_scatter(): acc = lax.ppermute(acc, 'bus', perm) + more  27.4 us
    ppermute x6, waiting for transfers between devices, ring_gather(): cur = lax.ppermute(cur, 'bus', perm)  24.3 us
    all_to_all x1, blocking collectives, per_device(): gathered = lax.all_to_all(outgoing, 'br', 0, 0, tiled=True)  17.6 us
    dot_general x8, matrix products, flow_part(): return jnp.dot(rows, inject_half, preferred_element_type=jnp.float32)  15.5 us
    ppermute x12, starting transfers between devices, ring_scatter(): acc = lax.ppermute(acc, 'bus', perm) + more  12.6 us
    all_to_all x1, waiting for transfers between devices, per_device(): arrived_w = lax.all_to_all(outgoing_w, 'br', 0, 0, tiled=True)  9.74 us
    all_to_all x1, waiting for transfers between devices, per_device(): lax.all_to_all(jnp.broadcast_to(my_new[None], (slab_axis, share_rows, sce...  8.97 us
    ppermute x6, starting transfers between devices, ring_gather(): cur = lax.ppermute(cur, 'bus', perm)  8.2 us
  transfers between devices with their start and end apart: 26, of which 16 were waited for; matrix products, arithmetic and copies ran while one was open for 21% of the time, Pallas kernels for 0%

profile of v12, /device:TPU:6, one launch (start us, length us, event | category | flops | bytes accessed | tf_op | source)
XLA Modules:
  0.0 205.7 jit_solution(4622745021474427112)
XLA Ops:
  1.9 1.9 convolution_bitcast_fusion.1
  3.8 1.9 convolution_bitcast_fusion
  9.6 1.9 convolution_bitcast_fusion.4
  19.2 1.9 convolution_bitcast_fusion.3
  21.2 1.9 convolution_bitcast_fusion.2
  23.2 1.9 convolution_bitcast_fusion.7
  25.1 1.9 convolution_bitcast_fusion.6
  29.1 2.2 %maximum_add_fusion.1 = f32[2,2,512,384]{3,2,1,0:T(8,128)S(1)} fusion(f32[2,2,512,384]{3,2,1,0:T(8,128)} %collective-permute-done.2, f32[1,2,512,384]{3,2,1,0:T(8,128)S(1)} %convolution_bitcast_fusion.2, f32[1,2,512,384]{3,2,1,0:T(8,128)S(1)} %convolution_bitcast_fusion.3), kind=kLoop, calls=%fused_computation.17 | loop fusion | flops 1572864 | bytes 9437184 | tf_op jit(solution)/shard_map/add | solution.py:72
  33.0 2.2 %maximum_add_fusion = f32[2,2,512,384]{3,2,1,0:T(8,128)S(1)} fusion(f32[2,2,512,384]{3,2,1,0:T(8,128)} %collective-permute-done, f32[1,2,512,384]{3,2,1,0:T(8,128)S(1)} %convolution_bitcast_fusion.6, f32[1,2,512,384]{3,2,1,0:T(8,128)S(1)} %convolution_bitcast_fusion.7), kind=kLoop, calls=%fused_computation.15 | loop fusion | flops 1572864 | bytes 9437184 | tf_op jit(solution)/shard_map/add | solution.py:72
  36.7 3.2 %collective-permute-start.9 = (f32[4,256,384]{2,1,0:T(8,128)}, f32[4,256,384]{2,1,0:T(8,128)}, u32[]{:S(2)}, u32[]{:S(2)}) collective-permute-start(f32[4,256,384]{2,1,0:T(8,128)} %fusion.7), channel_id=1, source_target_pairs={{0,8},{1,9},{2,10},{3,11},{4,12},{5,13},{6,14},{7,15},{8,0},{9,1},... | collective-permute-start | bytes 4718600 | tf_op jit(solution)/shard_map/ppermute | solution.py:79
  44.7 7.2 %collective-permute-done.1 = f32[2,128,384]{2,1,0:T(8,128)} collective-permute-done((f32[2,128,384]{2,1,0:T(8,128)}, f32[2,128,384]{2,1,0:T(8,128)}, u32[]{:S(2)}, u32[]{:S(2)}) %collective-permute-start.1) | collective-permute-done | bytes 393248 | tf_op jit(solution)/shard_map/ppermute | solution.py:46
  53.3 2.3 %fusion.44 = (f32[2,128,384]{2,1,0:T(8,128)}, f32[2,128,384]{2,1,0:T(8,128)}) fusion(f32[2,128,384]{2,1,0:T(8,128)} %collective-permute-done.5, f32[2,2,512,384]{3,2,1,0:T(8,128)} %copy-done.1, f32[2,128,384]{2,1,0:T(8,128)} %collective-permute-done.1), kind=kLoop, calls=%fused_computation.76 | loop fusion | flops 196608 | bytes 2359296 | tf_op jit(solution)/shard_map/add | solution.py:46
  63.4 5.4 %all-to-all-start = ((bf16[8,6,512]{2,1,0:T(8,128)(2,1)}), bf16[8,6,512]{2,1,0:T(8,128)(2,1)}, u32[]{:S(2)}, u32[]{:S(2)}) async-start(bf16[8,6,512]{2,1,0:T(8,128)(2,1)} %copy.99), calls=%async_computation | async-start | bytes 131072 | tf_op jit(solution)/shard_map/all_to_all | solution.py:181
  69.5 9.7 %all-to-all-done = bf16[8,6,512]{2,1,0:T(8,128)(2,1)} async-done(((bf16[8,6,512]{2,1,0:T(8,128)(2,1)}), bf16[8,6,512]{2,1,0:T(8,128)(2,1)}, u32[]{:S(2)}, u32[]{:S(2)}) %all-to-all-start) | async-done | bytes 49184 | tf_op jit(solution)/shard_map/all_to_all | solution.py:181
  88.0 6.2 %collective-permute-done.4 = f32[2,128,384]{2,1,0:T(8,128)S(1)} collective-permute-done((f32[2,128,384]{2,1,0:T(8,128)S(1)}, f32[2,128,384]{2,1,0:T(8,128)S(1)}, u32[]{:S(2)}, u32[]{:S(2)}) %collective-permute-start.4) | collective-permute-done | bytes 393248 | tf_op jit(solution)/shard_map/ppermute | solution.py:46
  101.4 3.8 %collective-permute-done.11 = f32[128,384]{1,0:T(8,128)S(1)} collective-permute-done((f32[128,384]{1,0:T(8,128)S(1)}, f32[128,384]{1,0:T(8,128)S(1)}, u32[]{:S(2)}, u32[]{:S(2)}) %collective-permute-start.11) | collective-permute-done | bytes 196640 | tf_op jit(solution)/shard_map/ppermute | solution.py:46
  109.1 3.6 %collective-permute-done.12 = f32[128,384]{1,0:T(8,128)S(1)} collective-permute-done((f32[128,384]{1,0:T(8,128)S(1)}, f32[128,384]{1,0:T(8,128)S(1)}, u32[]{:S(2)}, u32[]{:S(2)}) %collective-permute-start.12) | collective-permute-done | bytes 196640 | tf_op jit(solution)/shard_map/ppermute | solution.py:46
  112.6 2.1 %collective-permute-done.15 = f32[128,384]{1,0:T(8,128)S(1)} collective-permute-done((f32[128,384]{1,0:T(8,128)S(1)}, f32[128,384]{1,0:T(8,128)S(1)}, u32[]{:S(2)}, u32[]{:S(2)}) %collective-permute-start.15) | collective-permute-done | bytes 196640 | tf_op jit(solution)/shard_map/ppermute | solution.py:46
  117.6 7.7 %collective-permute-done.16 = bf16[512,384]{1,0:T(8,128)(2,1)S(1)} collective-permute-done((bf16[512,384]{1,0:T(8,128)(2,1)S(1)}, bf16[512,384]{1,0:T(8,128)(2,1)S(1)}, u32[]{:S(2)}, u32[]{:S(2)}) %collective-permute-start.16) | collective-permute-done | bytes 393248 | tf_op jit(solution)/shard_map/ppermute | solution.py:93
  125.6 2.0 collective-permute-start.20
  128.1 7.7 %collective-permute-done.17 = bf16[2,256,384]{2,1,0:T(8,128)(2,1)S(1)} collective-permute-done((bf16[2,256,384]{2,1,0:T(8,128)(2,1)S(1)}, bf16[2,256,384]{2,1,0:T(8,128)(2,1)S(1)}, u32[]{:S(2)}, u32[]{:S(2)}) %collective-permute-start.17) | collective-permute-done | bytes 393248 | tf_op jit(solution)/shard_map/ppermute | solution.py:59
  135.8 2.4 %collective-permute-start.18 = (bf16[2,256,384]{2,1,0:T(8,128)(2,1)S(1)}, bf16[2,256,384]{2,1,0:T(8,128)(2,1)S(1)}, u32[]{:S(2)}, u32[]{:S(2)}) collective-permute-start(bf16[2,256,384]{2,1,0:T(8,128)(2,1)S(1)} %collective-permute-done.17), channel_id=1, source_target_pairs={{0,2},{1,3},{2,4},{3,5},{4,6},{5,7},{6,0},{7,1},{8,10},{9,11},{10,... | collective-permute-start | bytes 1179656 | tf_op jit(solution)/shard_map/ppermute | solution.py:59
  138.3 7.9 %collective-permute-done.18 = bf16[2,256,384]{2,1,0:T(8,128)(2,1)S(1)} collective-permute-done((bf16[2,256,384]{2,1,0:T(8,128)(2,1)S(1)}, bf16[2,256,384]{2,1,0:T(8,128)(2,1)S(1)}, u32[]{:S(2)}, u32[]{:S(2)}) %collective-permute-start.18) | collective-permute-done | bytes 393248 | tf_op jit(solution)/shard_map/ppermute | solution.py:59
  146.2 3.7 %collective-permute-start.19 = (bf16[2,256,384]{2,1,0:T(8,128)(2,1)S(1)}, bf16[2,256,384]{2,1,0:T(8,128)(2,1)S(1)}, u32[]{:S(2)}, u32[]{:S(2)}) collective-permute-start(bf16[2,256,384]{2,1,0:T(8,128)(2,1)S(1)} %collective-permute-done.18), channel_id=1, source_target_pairs={{0,2},{1,3},{2,4},{3,5},{4,6},{5,7},{6,0},{7,1},{8,10},{9,11},{10,... | collective-permute-start | bytes 1179656 | tf_op jit(solution)/shard_map/ppermute | solution.py:59
  150.1 5.1 %collective-permute-done.19 = bf16[2,256,384]{2,1,0:T(8,128)(2,1)S(1)} collective-permute-done((bf16[2,256,384]{2,1,0:T(8,128)(2,1)S(1)}, bf16[2,256,384]{2,1,0:T(8,128)(2,1)S(1)}, u32[]{:S(2)}, u32[]{:S(2)}) %collective-permute-start.19) | collective-permute-done | bytes 393248 | tf_op jit(solution)/shard_map/ppermute | solution.py:59
  155.3 3.6 %collective-permute-done.22 = bf16[2,256,384]{2,1,0:T(8,128)(2,1)S(1)} collective-permute-done((bf16[2,256,384]{2,1,0:T(8,128)(2,1)S(1)}, bf16[2,256,384]{2,1,0:T(8,128)(2,1)S(1)}, u32[]{:S(2)}, u32[]{:S(2)}) %collective-permute-start.22) | collective-permute-done | bytes 393248 | tf_op jit(solution)/shard_map/ppermute | solution.py:59
  159.4 5.6 %collective-permute-done.23 = bf16[2,4,512,384]{3,2,1,0:T(8,128)(2,1)S(1)} collective-permute-done((bf16[2,4,512,384]{3,2,1,0:T(8,128)(2,1)S(1)}, bf16[2,4,512,384]{3,2,1,0:T(8,128)(2,1)S(1)}, u32[]{:S(2)}, u32[]{:S(2)}) %collective-permute-start.23) | collective-permute-done | bytes 3145760 | tf_op jit(solution)/shard_map/ppermute | solution.py:99
  165.0 2.4 %fusion.14 = f32[512,384]{1,0:T(8,128)S(1)} fusion(bf16[2,4,512,384]{3,2,1,0:T(8,128)(2,1)S(1)} %collective-permute-done.23, bf16[2,4,2,512,512]{4,3,2,1,0:T(8,128)(2,1)S(1)} %bitcast.250, s32[]{:T(128)S(6)} %select_n.213), kind=kOutput, calls=%fused_computation.34 | convolution fusion | flops 1610612736 | bytes 8126468 | tf_op jit(solution)/shard_map/dot_general | solution.py:196
  167.4 2.4 %fusion.17 = f32[512,384]{1,0:T(8,128)S(1)} fusion(f32[512,384]{1,0:T(8,128)S(1)} %fusion.14, bf16[2,4,2,512,512]{4,3,2,1,0:T(8,128)(2,1)S(1)} %bitcast.251, s32[]{:T(128)S(6)} %select_n.208, bf16[4,2,256,384]{3,2,0,1:T(8,128)(2,1)S(1)} %bitcast_dynamic-update-slice_fusion.7, bf16[4,2,256,384]{3,2,0,1:T(8,128)(2,1)S(1)} %bitcast_dynamic-update-slice_fusion.3), kind=kOutput, calls=%fused_computation.35 | convolution fusion | flops 1617100800 | bytes 8912900 | tf_op jit(solution)/shard_map/dot_general | solution.py:195
  171.1 17.6 %all_to_all.15 = f32[8,70,384]{2,1,0:T(8,128)S(1)} all-to-all(f32[8,70,384]{2,1,0:T(8,128)S(1)} %pad_maximum_fusion.2), channel_id=1, replica_groups=mesh['br'=8,'bus'=16] {'br'}, dimensions={0} | all-to-all | bytes 1720320 | tf_op jit(solution)/shard_map/all_to_all | solution.py:204
  190.1 3.5 %all-to-all-start.2 = ((f32[8,64,384]{2,1,0:T(8,128)}), f32[8,64,384]{2,1,0:T(8,128)S(1)}, u32[]{:S(2)}, u32[]{:S(2)}) async-start(f32[8,64,384]{2,1,0:T(8,128)} %broadcast_in_dim.153), calls=%async_computation.2 | async-start | bytes 1572864 | tf_op jit(solution)/shard_map/all_to_all | solution.py:209
  195.9 9.0 %all-to-all-done.2 = f32[8,64,384]{2,1,0:T(8,128)S(1)} async-done(((f32[8,64,384]{2,1,0:T(8,128)}), f32[8,64,384]{2,1,0:T(8,128)S(1)}, u32[]{:S(2)}, u32[]{:S(2)}) %all-to-all-start.2) | async-done | bytes 786464 | tf_op jit(solution)/shard_map/all_to_all | solution.py:209
  (164 shorter events, 62.0 us)
Async XLA Ops:
  7.6 21.5 %collective-permute-start.2 = (f32[2,2,512,384]{3,2,1,0:T(8,128)}, f32[2,2,512,384]{3,2,1,0:T(8,128)}, u32[]{:S(2)}, u32[]{:S(2)}) collective-permute-start(f32[2,2,512,384]{3,2,1,0:T(8,128)} %pad_maximum_fusion.1), channel_id=1, source_target_pairs={{0,1},{1,0},{2,3},{3,2},{4,5},{5,4},{6,7},{7,6},{8,9},{9,8},{10,11... | collective-permute-start | bytes 9437192 | tf_op jit(solution)/shard_map/ppermute | solution.py:72
  13.4 19.5 %collective-permute-start = (f32[2,2,512,384]{3,2,1,0:T(8,128)}, f32[2,2,512,384]{3,2,1,0:T(8,128)}, u32[]{:S(2)}, u32[]{:S(2)}) collective-permute-start(f32[2,2,512,384]{3,2,1,0:T(8,128)} %pad_maximum_fusion), channel_id=1, source_target_pairs={{0,1},{1,0},{2,3},{3,2},{4,5},{5,4},{6,7},{7,6},{8,9},{9,8},{10,11... | collective-permute-start | bytes 9437192 | tf_op jit(solution)/shard_map/ppermute | solution.py:72
  36.7 47.6 %collective-permute-start.9 = (f32[4,256,384]{2,1,0:T(8,128)}, f32[4,256,384]{2,1,0:T(8,128)}, u32[]{:S(2)}, u32[]{:S(2)}) collective-permute-start(f32[4,256,384]{2,1,0:T(8,128)} %fusion.7), channel_id=1, source_target_pairs={{0,8},{1,9},{2,10},{3,11},{4,12},{5,13},{6,14},{7,15},{8,0},{9,1},... | collective-permute-start | bytes 4718600 | tf_op jit(solution)/shard_map/ppermute | solution.py:79
  40.9 11.1 %collective-permute-start.1 = (f32[2,128,384]{2,1,0:T(8,128)}, f32[2,128,384]{2,1,0:T(8,128)}, u32[]{:S(2)}, u32[]{:S(2)}) collective-permute-start(f32[2,128,384]{2,1,0:T(8,128)} %get-tuple-element.33), channel_id=1, source_target_pairs={{0,2},{1,3},{2,4},{3,5},{4,6},{5,7},{6,0},{7,1},{8,10},{9,11},{10,... | collective-permute-start | bytes 1179656 | tf_op jit(solution)/shard_map/ppermute | solution.py:46
  41.3 12.0 %collective-permute-start.5 = (f32[2,128,384]{2,1,0:T(8,128)}, f32[2,128,384]{2,1,0:T(8,128)}, u32[]{:S(2)}, u32[]{:S(2)}) collective-permute-start(f32[2,128,384]{2,1,0:T(8,128)} %get-tuple-element.32), channel_id=1, source_target_pairs={{0,6},{1,7},{2,0},{3,1},{4,2},{5,3},{6,4},{7,5},{8,14},{9,15},{10,... | collective-permute-start | bytes 1179656 | tf_op jit(solution)/shard_map/ppermute | solution.py:46
  55.6 25.1 %collective-permute-start.3 = (f32[2,128,384]{2,1,0:T(8,128)}, f32[2,128,384]{2,1,0:T(8,128)}, u32[]{:S(2)}, u32[]{:S(2)}) collective-permute-start(f32[2,128,384]{2,1,0:T(8,128)} %get-tuple-element.12), channel_id=1, source_target_pairs={{0,2},{1,3},{2,4},{3,5},{4,6},{5,7},{6,0},{7,1},{8,10},{9,11},{10,... | collective-permute-start | bytes 1179656 | tf_op jit(solution)/shard_map/ppermute | solution.py:46
  55.9 24.8 %collective-permute-start.6 = (f32[2,128,384]{2,1,0:T(8,128)}, f32[2,128,384]{2,1,0:T(8,128)}, u32[]{:S(2)}, u32[]{:S(2)}) collective-permute-start(f32[2,128,384]{2,1,0:T(8,128)} %get-tuple-element.30), channel_id=1, source_target_pairs={{0,6},{1,7},{2,0},{3,1},{4,2},{5,3},{6,4},{7,5},{8,14},{9,15},{10,... | collective-permute-start | bytes 1179656 | tf_op jit(solution)/shard_map/ppermute | solution.py:46
  63.4 15.9 %all-to-all-start = ((bf16[8,6,512]{2,1,0:T(8,128)(2,1)}), bf16[8,6,512]{2,1,0:T(8,128)(2,1)}, u32[]{:S(2)}, u32[]{:S(2)}) async-start(bf16[8,6,512]{2,1,0:T(8,128)(2,1)} %copy.99), calls=%async_computation | async-start | bytes 131072 | tf_op jit(solution)/shard_map/all_to_all | solution.py:181
  82.2 12.0 %collective-permute-start.4 = (f32[2,128,384]{2,1,0:T(8,128)S(1)}, f32[2,128,384]{2,1,0:T(8,128)S(1)}, u32[]{:S(2)}, u32[]{:S(2)}) collective-permute-start(f32[2,128,384]{2,1,0:T(8,128)S(1)} %get-tuple-element.29), channel_id=1, source_target_pairs={{0,2},{1,3},{2,4},{3,5},{4,6},{5,7},{6,0},{7,1},{8,10},{9,11},{10,... | collective-permute-start | bytes 1179656 | tf_op jit(solution)/shard_map/ppermute | solution.py:46
  82.7 12.8 %collective-permute-start.7 = (f32[2,128,384]{2,1,0:T(8,128)S(1)}, f32[2,128,384]{2,1,0:T(8,128)S(1)}, u32[]{:S(2)}, u32[]{:S(2)}) collective-permute-start(f32[2,128,384]{2,1,0:T(8,128)S(1)} %get-tuple-element.28), channel_id=1, source_target_pairs={{0,6},{1,7},{2,0},{3,1},{4,2},{5,3},{6,4},{7,5},{8,14},{9,15},{10,... | collective-permute-start | bytes 1179656 | tf_op jit(solution)/shard_map/ppermute | solution.py:46
  85.9 15.2 %copy-start.4 = (bf16[48,512]{1,0:T(8,128)(2,1)S(1)}, bf16[48,512]{1,0:T(8,128)(2,1)}, u32[]{:S(2)}) copy-start(bf16[48,512]{1,0:T(8,128)(2,1)} %broadcast_in_dim.136) | copy-start | bytes 147460
  85.9 12.8 %collective-permute-start.10 = (f32[128,384]{1,0:T(8,128)S(1)}, f32[128,384]{1,0:T(8,128)S(1)}, u32[]{:S(2)}, u32[]{:S(2)}) collective-permute-start(f32[128,384]{1,0:T(8,128)S(1)} %get-tuple-element.40), channel_id=1, source_target_pairs={{0,2},{1,3},{2,4},{3,5},{4,6},{5,7},{6,0},{7,1},{8,10},{9,11},{10,... | collective-permute-start | bytes 589832 | tf_op jit(solution)/shard_map/ppermute | solution.py:46
  87.7 11.1 %collective-permute-start.13 = (f32[128,384]{1,0:T(8,128)S(1)}, f32[128,384]{1,0:T(8,128)S(1)}, u32[]{:S(2)}, u32[]{:S(2)}) collective-permute-start(f32[128,384]{1,0:T(8,128)S(1)} %get-tuple-element.41), channel_id=1, source_target_pairs={{0,6},{1,7},{2,0},{3,1},{4,2},{5,3},{6,4},{7,5},{8,14},{9,15},{10,... | collective-permute-start | bytes 589832 | tf_op jit(solution)/shard_map/ppermute | solution.py:46
  96.8 12.2 %collective-permute-start.8 = (f32[256,384]{1,0:T(8,128)S(1)}, f32[256,384]{1,0:T(8,128)S(1)}, u32[]{:S(2)}, u32[]{:S(2)}) collective-permute-start(f32[256,384]{1,0:T(8,128)S(1)} %fusion.38), channel_id=1, source_target_pairs={{0,8},{1,9},{2,10},{3,11},{4,12},{5,13},{6,14},{7,15},{8,0},{9,1},... | collective-permute-start | bytes 1179656 | tf_op jit(solution)/shard_map/ppermute | solution.py:88
  98.8 6.3 %collective-permute-start.11 = (f32[128,384]{1,0:T(8,128)S(1)}, f32[128,384]{1,0:T(8,128)S(1)}, u32[]{:S(2)}, u32[]{:S(2)}) collective-permute-start(f32[128,384]{1,0:T(8,128)S(1)} %get-tuple-element.38), channel_id=1, source_target_pairs={{0,2},{1,3},{2,4},{3,5},{4,6},{5,7},{6,0},{7,1},{8,10},{9,11},{10,... | collective-permute-start | bytes 589832 | tf_op jit(solution)/shard_map/ppermute | solution.py:46
  99.4 7.5 %collective-permute-start.14 = (f32[128,384]{1,0:T(8,128)S(1)}, f32[128,384]{1,0:T(8,128)S(1)}, u32[]{:S(2)}, u32[]{:S(2)}) collective-permute-start(f32[128,384]{1,0:T(8,128)S(1)} %get-tuple-element.39), channel_id=1, source_target_pairs={{0,6},{1,7},{2,0},{3,1},{4,2},{5,3},{6,4},{7,5},{8,14},{9,15},{10,... | collective-permute-start | bytes 589832 | tf_op jit(solution)/shard_map/ppermute | solution.py:46
  101.3 13.6 %copy-start.2 = (f32[512,384]{1,0:T(8,128)S(1)}, f32[512,384]{1,0:T(8,128)}, u32[]{:S(2)}) copy-start(f32[512,384]{1,0:T(8,128)} %param.17) | copy-start | bytes 2359300
  106.9 5.7 %collective-permute-start.12 = (f32[128,384]{1,0:T(8,128)S(1)}, f32[128,384]{1,0:T(8,128)S(1)}, u32[]{:S(2)}, u32[]{:S(2)}) collective-permute-start(f32[128,384]{1,0:T(8,128)S(1)} %get-tuple-element.36), channel_id=1, source_target_pairs={{0,2},{1,3},{2,4},{3,5},{4,6},{5,7},{6,0},{7,1},{8,10},{9,11},{10,... | collective-permute-start | bytes 589832 | tf_op jit(solution)/shard_map/ppermute | solution.py:46
  107.9 6.9 %collective-permute-start.15 = (f32[128,384]{1,0:T(8,128)S(1)}, f32[128,384]{1,0:T(8,128)S(1)}, u32[]{:S(2)}, u32[]{:S(2)}) collective-permute-start(f32[128,384]{1,0:T(8,128)S(1)} %get-tuple-element.37), channel_id=1, source_target_pairs={{0,6},{1,7},{2,0},{3,1},{4,2},{5,3},{6,4},{7,5},{8,14},{9,15},{10,... | collective-permute-start | bytes 589832 | tf_op jit(solution)/shard_map/ppermute | solution.py:46
  116.0 9.3 %collective-permute-start.16 = (bf16[512,384]{1,0:T(8,128)(2,1)S(1)}, bf16[512,384]{1,0:T(8,128)(2,1)S(1)}, u32[]{:S(2)}, u32[]{:S(2)}) collective-permute-start(bf16[512,384]{1,0:T(8,128)(2,1)S(1)} %get-tuple-element.20), channel_id=1, source_target_pairs={{0,8},{1,9},{2,10},{3,11},{4,12},{5,13},{6,14},{7,15},{8,0},{9,1},... | collective-permute-start | bytes 1179656 | tf_op jit(solution)/shard_map/ppermute | solution.py:93
  125.5 10.2 %collective-permute-start.17 = (bf16[2,256,384]{2,1,0:T(8,128)(2,1)S(1)}, bf16[2,256,384]{2,1,0:T(8,128)(2,1)S(1)}, u32[]{:S(2)}, u32[]{:S(2)}) collective-permute-start(bf16[2,256,384]{2,1,0:T(8,128)(2,1)S(1)} %get-tuple-element.42), channel_id=1, source_target_pairs={{0,2},{1,3},{2,4},{3,5},{4,6},{5,7},{6,0},{7,1},{8,10},{9,11},{10,... | collective-permute-start | bytes 1179656 | tf_op jit(solution)/shard_map/ppermute | solution.py:59
  125.6 12.6 %collective-permute-start.20 = (bf16[2,256,384]{2,1,0:T(8,128)(2,1)S(1)}, bf16[2,256,384]{2,1,0:T(8,128)(2,1)S(1)}, u32[]{:S(2)}, u32[]{:S(2)}) collective-permute-start(bf16[2,256,384]{2,1,0:T(8,128)(2,1)S(1)} %get-tuple-element.43), channel_id=1, source_target_pairs={{0,6},{1,7},{2,0},{3,1},{4,2},{5,3},{6,4},{7,5},{8,14},{9,15},{10,... | collective-permute-start | bytes 1179656 | tf_op jit(solution)/shard_map/ppermute | solution.py:59
  127.6 37.4 %slice-start = ((s8[8388608]{0:T(1024)(128)(4,1)}), s8[4194304]{0:T(1024)(128)(4,1)S(1)}, s32[]{:S(2)}) async-start(s8[8388608]{0:T(1024)(128)(4,1)} %bitcast.248), calls=%async_computation.3 | async-start | bytes 8388608
  135.8 10.4 %collective-permute-start.18 = (bf16[2,256,384]{2,1,0:T(8,128)(2,1)S(1)}, bf16[2,256,384]{2,1,0:T(8,128)(2,1)S(1)}, u32[]{:S(2)}, u32[]{:S(2)}) collective-permute-start(bf16[2,256,384]{2,1,0:T(8,128)(2,1)S(1)} %collective-permute-done.17), channel_id=1, source_target_pairs={{0,2},{1,3},{2,4},{3,5},{4,6},{5,7},{6,0},{7,1},{8,10},{9,11},{10,... | collective-permute-start | bytes 1179656 | tf_op jit(solution)/shard_map/ppermute | solution.py:59
  138.2 11.7 %collective-permute-start.21 = (bf16[2,256,384]{2,1,0:T(8,128)(2,1)S(1)}, bf16[2,256,384]{2,1,0:T(8,128)(2,1)S(1)}, u32[]{:S(2)}, u32[]{:S(2)}) collective-permute-start(bf16[2,256,384]{2,1,0:T(8,128)(2,1)S(1)} %collective-permute-done.20), channel_id=1, source_target_pairs={{0,6},{1,7},{2,0},{3,1},{4,2},{5,3},{6,4},{7,5},{8,14},{9,15},{10,... | collective-permute-start | bytes 1179656 | tf_op jit(solution)/shard_map/ppermute | solution.py:59
  146.2 9.0 %collective-permute-start.19 = (bf16[2,256,384]{2,1,0:T(8,128)(2,1)S(1)}, bf16[2,256,384]{2,1,0:T(8,128)(2,1)S(1)}, u32[]{:S(2)}, u32[]{:S(2)}) collective-permute-start(bf16[2,256,384]{2,1,0:T(8,128)(2,1)S(1)} %collective-permute-done.18), channel_id=1, source_target_pairs={{0,2},{1,3},{2,4},{3,5},{4,6},{5,7},{6,0},{7,1},{8,10},{9,11},{10,... | collective-permute-start | bytes 1179656 | tf_op jit(solution)/shard_map/ppermute | solution.py:59
  149.9 9.0 %collective-permute-start.22 = (bf16[2,256,384]{2,1,0:T(8,128)(2,1)S(1)}, bf16[2,256,384]{2,1,0:T(8,128)(2,1)S(1)}, u32[]{:S(2)}, u32[]{:S(2)}) collective-permute-start(bf16[2,256,384]{2,1,0:T(8,128)(2,1)S(1)} %collective-permute-done.21), channel_id=1, source_target_pairs={{0,6},{1,7},{2,0},{3,1},{4,2},{5,3},{6,4},{7,5},{8,14},{9,15},{10,... | collective-permute-start | bytes 1179656 | tf_op jit(solution)/shard_map/ppermute | solution.py:59
  150.0 15.1 %slice-start.1 = ((s8[8388608]{0:T(1024)(128)(4,1)}), s8[4194304]{0:T(1024)(128)(4,1)S(1)}, s32[]{:S(2)}) async-start(s8[8388608]{0:T(1024)(128)(4,1)} %bitcast.248), calls=%async_computation.4 | async-start | bytes 8388608
  159.3 5.7 %collective-permute-start.23 = (bf16[2,4,512,384]{3,2,1,0:T(8,128)(2,1)S(1)}, bf16[2,4,512,384]{3,2,1,0:T(8,128)(2,1)S(1)}, u32[]{:S(2)}, u32[]{:S(2)}) collective-permute-start(bf16[2,4,512,384]{3,2,1,0:T(8,128)(2,1)S(1)} %maximum_bitcast_fusion), channel_id=1, source_target_pairs={{0,1},{1,0},{2,3},{3,2},{4,5},{5,4},{6,7},{7,6},{8,9},{9,8},{10,11... | collective-permute-start | bytes 9437192 | tf_op jit(solution)/shard_map/ppermute | solution.py:99
  171.1 22.5 %copy-start.12 = (s32[24]{0:T(128)S(1)}, s32[24]{0:T(128)}, u32[]{:S(2)}) copy-start(s32[24]{0:T(128)} %copy-done.11) | copy-start | bytes 292
  171.1 22.6 %copy-start.13 = (s32[24]{0:T(128)S(1)}, s32[24]{0:T(128)}, u32[]{:S(2)}) copy-start(s32[24]{0:T(128)} %get-tuple-element.46) | copy-start | bytes 292
  190.1 14.8 %all-to-all-start.2 = ((f32[8,64,384]{2,1,0:T(8,128)}), f32[8,64,384]{2,1,0:T(8,128)S(1)}, u32[]{:S(2)}, u32[]{:S(2)}) async-start(f32[8,64,384]{2,1,0:T(8,128)} %broadcast_in_dim.153), calls=%async_computation.2 | async-start | bytes 1572864 | tf_op jit(solution)/shard_map/all_to_all | solution.py:209
  (10 other events, 48.9 us)

commit v13 on v12

--- a/solution.py
+++ b/solution.py
@@ -44,7 +44,7 @@
     acc = contribs[0]
     for k, more in enumerate(contribs[1:]):
         acc = lax.ppermute(acc, "bus", perm) + more
-        if k == 0 and rider is not None:
+        if k == 1 and rider is not None:
             acc, rider = lax.optimization_barrier((acc, rider))
     return acc, rider
 

time: 207 us -> 215 us (1.039)
  local copies, waits for them, and re-layouts: 16.6 us -> 25.7 us
  waiting for transfers between devices: 83.9 us -> 80 us
  other arithmetic: 26.9 us -> 30.4 us
    ppermute x12, waiting for transfers between devices: 27.4 us -> 22.5 us  [ring_scatter(): acc = lax.ppermute(acc, 'bus', perm) + more]
    unnamed x37 -> x41, local copies, waits for them, and re-layouts: 3.24 us -> 6.58 us
  transfers between devices with their start and end apart: 26 -> 26, of which waited for: 16 -> 17; matrix products, arithmetic and copies ran while one was open for 21% -> 28% of each run, Pallas kernels for 0% -> 0%
where the time goes in v13:
time: 215 us; the launch traced here: 214 us
  waiting for transfers between devices  80 us (37%)
  starting transfers between devices  36.9 us (17%)
  other arithmetic  30.4 us (14%)
  local copies, waits for them, and re-layouts  25.7 us (12%)
  matrix products  22.2 us (10%)
  blocking collectives  17.3 us (8%)
    ppermute x6, waiting for transfers between devices, ring_gather(): cur = lax.ppermute(cur, 'bus', perm)  26.3 us
    ppermute x12, waiting for transfers between devices, ring_scatter(): acc = lax.ppermute(acc, 'bus', perm) + more  22.5 us
    all_to_all x1, blocking collectives, per_device(): gathered = lax.all_to_all(outgoing, 'br', 0, 0, tiled=True)  17.3 us
    dot_general x8, matrix products, flow_part(): return jnp.dot(rows, inject_half, preferred_element_type=jnp.float32)  15.5 us
    ppermute x12, starting transfers between devices, ring_scatter(): acc = lax.ppermute(acc, 'bus', perm) + more  12.6 us
    all_to_all x1, waiting for transfers between devices, per_device(): arrived_w = lax.all_to_all(outgoing_w, 'br', 0, 0, tiled=True)  9.39 us
    all_to_all x1, waiting for transfers between devices, per_device(): lax.all_to_all(jnp.broadcast_to(my_new[None], (slab_axis, share_rows, sce...  8.96 us
    ppermute x6, starting transfers between devices, ring_gather(): cur = lax.ppermute(cur, 'bus', perm)  7.62 us
  transfers between devices with their start and end apart: 26, of which 17 were waited for; matrix products, arithmetic and copies ran while one was open for 28% of the time, Pallas kernels for 0%

profile of v13, /device:TPU:6, one launch (start us, length us, event | category | flops | bytes accessed | tf_op | source)
XLA Modules:
  0.0 213.9 jit_solution(16998445962216154764)
XLA Ops:
  1.9 1.9 convolution_bitcast_fusion.1
  3.8 1.9 convolution_bitcast_fusion
  29.6 2.0 copy.100
  32.8 2.2 %gather_fusion = f32[64,64]{1,0:T(8,128)} fusion(f32[64,1024]{0,1:T(8,128)} %copy.100, s32[1024]{0:T(1024)S(1)} %pad_clamp_fusion.2), kind=kCustom, calls=%fused_computation.2 | custom fusion | bytes 33024 | tf_op jit(solution)/shard_map/jit(_take)/gather | solution.py:165
  40.0 1.9 convolution_bitcast_fusion.2
  42.0 1.9 convolution_bitcast_fusion.7
  43.9 1.9 convolution_bitcast_fusion.6
  51.0 2.2 %maximum_add_fusion.1 = f32[2,2,512,384]{3,2,1,0:T(8,128)S(1)} fusion(f32[2,2,512,384]{3,2,1,0:T(8,128)} %collective-permute-done.2, f32[1,2,512,384]{3,2,1,0:T(8,128)S(1)} %convolution_bitcast_fusion.2, f32[1,2,512,384]{3,2,1,0:T(8,128)S(1)} %convolution_bitcast_fusion.3), kind=kLoop, calls=%fused_computation.17 | loop fusion | flops 1572864 | bytes 9437184 | tf_op jit(solution)/shard_map/add | solution.py:72
  55.4 3.2 %collective-permute-start.9 = (f32[4,256,384]{2,1,0:T(8,128)}, f32[4,256,384]{2,1,0:T(8,128)}, u32[]{:S(2)}, u32[]{:S(2)}) collective-permute-start(f32[4,256,384]{2,1,0:T(8,128)} %fusion.7), channel_id=1, source_target_pairs={{0,8},{1,9},{2,10},{3,11},{4,12},{5,13},{6,14},{7,15},{8,0},{9,1},... | collective-permute-start | bytes 4718600 | tf_op jit(solution)/shard_map/ppermute | solution.py:79
  67.2 7.1 %collective-permute-done.3 = f32[2,128,384]{2,1,0:T(8,128)S(1)} collective-permute-done((f32[2,128,384]{2,1,0:T(8,128)S(1)}, f32[2,128,384]{2,1,0:T(8,128)S(1)}, u32[]{:S(2)}, u32[]{:S(2)}) %collective-permute-start.3) | collective-permute-done | bytes 393248 | tf_op jit(solution)/shard_map/ppermute | solution.py:46
  74.3 2.6 %collective-permute-done.6 = f32[2,128,384]{2,1,0:T(8,128)S(1)} collective-permute-done((f32[2,128,384]{2,1,0:T(8,128)S(1)}, f32[2,128,384]{2,1,0:T(8,128)S(1)}, u32[]{:S(2)}, u32[]{:S(2)}) %collective-permute-start.6) | collective-permute-done | bytes 393248 | tf_op jit(solution)/shard_map/ppermute | solution.py:46
  76.9 2.1 fusion.43
  79.7 5.4 %all-to-all-start = ((bf16[8,6,512]{2,1,0:T(8,128)(2,1)}), bf16[8,6,512]{2,1,0:T(8,128)(2,1)S(1)}, u32[]{:S(2)}, u32[]{:S(2)}) async-start(bf16[8,6,512]{2,1,0:T(8,128)(2,1)} %copy.99), calls=%async_computation | async-start | bytes 131072 | tf_op jit(solution)/shard_map/all_to_all | solution.py:181
  87.9 9.4 %all-to-all-done = bf16[8,6,512]{2,1,0:T(8,128)(2,1)S(1)} async-done(((bf16[8,6,512]{2,1,0:T(8,128)(2,1)}), bf16[8,6,512]{2,1,0:T(8,128)(2,1)S(1)}, u32[]{:S(2)}, u32[]{:S(2)}) %all-to-all-start) | async-done | bytes 49184 | tf_op jit(solution)/shard_map/all_to_all | solution.py:181
  104.7 2.9 %collective-permute-done.13 = f32[128,384]{1,0:T(8,128)S(1)} collective-permute-done((f32[128,384]{1,0:T(8,128)S(1)}, f32[128,384]{1,0:T(8,128)S(1)}, u32[]{:S(2)}, u32[]{:S(2)}) %collective-permute-start.13) | collective-permute-done | bytes 196640 | tf_op jit(solution)/shard_map/ppermute | solution.py:46
  107.9 2.0 collective-permute-start.14
  110.1 3.5 %collective-permute-done.11 = f32[128,384]{1,0:T(8,128)S(1)} collective-permute-done((f32[128,384]{1,0:T(8,128)S(1)}, f32[128,384]{1,0:T(8,128)S(1)}, u32[]{:S(2)}, u32[]{:S(2)}) %collective-permute-start.11) | collective-permute-done | bytes 196640 | tf_op jit(solution)/shard_map/ppermute | solution.py:46
  115.0 2.0 collective-permute-start.15
  117.1 3.6 %collective-permute-done.12 = f32[128,384]{1,0:T(8,128)S(1)} collective-permute-done((f32[128,384]{1,0:T(8,128)S(1)}, f32[128,384]{1,0:T(8,128)S(1)}, u32[]{:S(2)}, u32[]{:S(2)}) %collective-permute-start.12) | collective-permute-done | bytes 196640 | tf_op jit(solution)/shard_map/ppermute | solution.py:46
  123.2 2.0 collective-permute-start.16
  125.2 7.3 %collective-permute-done.16 = bf16[512,384]{1,0:T(8,128)(2,1)S(1)} collective-permute-done((bf16[512,384]{1,0:T(8,128)(2,1)S(1)}, bf16[512,384]{1,0:T(8,128)(2,1)S(1)}, u32[]{:S(2)}, u32[]{:S(2)}) %collective-permute-start.16) | collective-permute-done | bytes 393248 | tf_op jit(solution)/shard_map/ppermute | solution.py:93
  135.2 8.8 %collective-permute-done.17 = bf16[2,256,384]{2,1,0:T(8,128)(2,1)S(1)} collective-permute-done((bf16[2,256,384]{2,1,0:T(8,128)(2,1)S(1)}, bf16[2,256,384]{2,1,0:T(8,128)(2,1)S(1)}, u32[]{:S(2)}, u32[]{:S(2)}) %collective-permute-start.17) | collective-permute-done | bytes 393248 | tf_op jit(solution)/shard_map/ppermute | solution.py:59
  146.2 8.4 %collective-permute-done.18 = bf16[2,256,384]{2,1,0:T(8,128)(2,1)S(1)} collective-permute-done((bf16[2,256,384]{2,1,0:T(8,128)(2,1)S(1)}, bf16[2,256,384]{2,1,0:T(8,128)(2,1)S(1)}, u32[]{:S(2)}, u32[]{:S(2)}) %collective-permute-start.18) | collective-permute-done | bytes 393248 | tf_op jit(solution)/shard_map/ppermute | solution.py:59
  154.7 3.7 %collective-permute-start.19 = (bf16[2,256,384]{2,1,0:T(8,128)(2,1)S(1)}, bf16[2,256,384]{2,1,0:T(8,128)(2,1)S(1)}, u32[]{:S(2)}, u32[]{:S(2)}) collective-permute-start(bf16[2,256,384]{2,1,0:T(8,128)(2,1)S(1)} %collective-permute-done.18), channel_id=1, source_target_pairs={{0,2},{1,3},{2,4},{3,5},{4,6},{5,7},{6,0},{7,1},{8,10},{9,11},{10,... | collective-permute-start | bytes 1179656 | tf_op jit(solution)/shard_map/ppermute | solution.py:59
  158.6 5.1 %collective-permute-done.19 = bf16[2,256,384]{2,1,0:T(8,128)(2,1)S(1)} collective-permute-done((bf16[2,256,384]{2,1,0:T(8,128)(2,1)S(1)}, bf16[2,256,384]{2,1,0:T(8,128)(2,1)S(1)}, u32[]{:S(2)}, u32[]{:S(2)}) %collective-permute-start.19) | collective-permute-done | bytes 393248 | tf_op jit(solution)/shard_map/ppermute | solution.py:59
  163.7 3.7 %collective-permute-done.22 = bf16[2,256,384]{2,1,0:T(8,128)(2,1)S(1)} collective-permute-done((bf16[2,256,384]{2,1,0:T(8,128)(2,1)S(1)}, bf16[2,256,384]{2,1,0:T(8,128)(2,1)S(1)}, u32[]{:S(2)}, u32[]{:S(2)}) %collective-permute-start.22) | collective-permute-done | bytes 393248 | tf_op jit(solution)/shard_map/ppermute | solution.py:59
  167.9 5.6 %collective-permute-done.23 = bf16[2,4,512,384]{3,2,1,0:T(8,128)(2,1)S(1)} collective-permute-done((bf16[2,4,512,384]{3,2,1,0:T(8,128)(2,1)S(1)}, bf16[2,4,512,384]{3,2,1,0:T(8,128)(2,1)S(1)}, u32[]{:S(2)}, u32[]{:S(2)}) %collective-permute-start.23) | collective-permute-done | bytes 3145760 | tf_op jit(solution)/shard_map/ppermute | solution.py:99
  173.5 2.4 %fusion.14 = f32[512,384]{1,0:T(8,128)S(1)} fusion(bf16[2,4,512,384]{3,2,1,0:T(8,128)(2,1)S(1)} %collective-permute-done.23, bf16[2,4,2,512,512]{4,3,2,1,0:T(8,128)(2,1)S(1)} %bitcast.250, s32[]{:T(128)S(6)} %select_n.213), kind=kOutput, calls=%fused_computation.34 | convolution fusion | flops 1610612736 | bytes 8126468 | tf_op jit(solution)/shard_map/dot_general | solution.py:196
  175.9 2.4 %fusion.17 = f32[512,384]{1,0:T(8,128)S(1)} fusion(f32[512,384]{1,0:T(8,128)S(1)} %fusion.14, bf16[2,4,2,512,512]{4,3,2,1,0:T(8,128)(2,1)S(1)} %bitcast.251, s32[]{:T(128)S(6)} %select_n.208, bf16[4,2,256,384]{3,2,0,1:T(8,128)(2,1)S(1)} %bitcast_dynamic-update-slice_fusion.7, bf16[4,2,256,384]{3,2,0,1:T(8,128)(2,1)S(1)} %bitcast_dynamic-update-slice_fusion.3), kind=kOutput, calls=%fused_computation.35 | convolution fusion | flops 1617100800 | bytes 8912900 | tf_op jit(solution)/shard_map/dot_general | solution.py:195
  179.6 17.3 %all_to_all.15 = f32[8,70,384]{2,1,0:T(8,128)S(1)} all-to-all(f32[8,70,384]{2,1,0:T(8,128)S(1)} %pad_maximum_fusion.2), channel_id=1, replica_groups=mesh['br'=8,'bus'=16] {'br'}, dimensions={0} | all-to-all | bytes 1720320 | tf_op jit(solution)/shard_map/all_to_all | solution.py:204
  198.2 3.5 %all-to-all-start.2 = ((f32[8,64,384]{2,1,0:T(8,128)}), f32[8,64,384]{2,1,0:T(8,128)S(1)}, u32[]{:S(2)}, u32[]{:S(2)}) async-start(f32[8,64,384]{2,1,0:T(8,128)} %broadcast_in_dim.153), calls=%async_computation.2 | async-start | bytes 1572864 | tf_op jit(solution)/shard_map/all_to_all | solution.py:209
  204.0 9.0 %all-to-all-done.2 = f32[8,64,384]{2,1,0:T(8,128)S(1)} async-done(((f32[8,64,384]{2,1,0:T(8,128)}), f32[8,64,384]{2,1,0:T(8,128)S(1)}, u32[]{:S(2)}, u32[]{:S(2)}) %all-to-all-start.2) | async-done | bytes 786464 | tf_op jit(solution)/shard_map/all_to_all | solution.py:209
  (168 shorter events, 73.5 us)
Async XLA Ops:
  7.6 43.4 %collective-permute-start.2 = (f32[2,2,512,384]{3,2,1,0:T(8,128)}, f32[2,2,512,384]{3,2,1,0:T(8,128)}, u32[]{:S(2)}, u32[]{:S(2)}) collective-permute-start(f32[2,2,512,384]{3,2,1,0:T(8,128)} %pad_maximum_fusion.1), channel_id=1, source_target_pairs={{0,1},{1,0},{2,3},{3,2},{4,5},{5,4},{6,7},{7,6},{8,9},{9,8},{10,11... | collective-permute-start | bytes 9437192 | tf_op jit(solution)/shard_map/ppermute | solution.py:72
  13.4 34.0 %collective-permute-start = (f32[2,2,512,384]{3,2,1,0:T(8,128)}, f32[2,2,512,384]{3,2,1,0:T(8,128)S(1)}, u32[]{:S(2)}, u32[]{:S(2)}) collective-permute-start(f32[2,2,512,384]{3,2,1,0:T(8,128)} %pad_maximum_fusion), channel_id=1, source_target_pairs={{0,1},{1,0},{2,3},{3,2},{4,5},{5,4},{6,7},{7,6},{8,9},{9,8},{10,11... | collective-permute-start | bytes 9437192 | tf_op jit(solution)/shard_map/ppermute | solution.py:72
  49.0 13.7 %collective-permute-start.1 = (f32[2,128,384]{2,1,0:T(8,128)}, f32[2,128,384]{2,1,0:T(8,128)}, u32[]{:S(2)}, u32[]{:S(2)}) collective-permute-start(f32[2,128,384]{2,1,0:T(8,128)} %get-tuple-element.33), channel_id=1, source_target_pairs={{0,2},{1,3},{2,4},{3,5},{4,6},{5,7},{6,0},{7,1},{8,10},{9,11},{10,... | collective-permute-start | bytes 1179656 | tf_op jit(solution)/shard_map/ppermute | solution.py:46
  49.3 13.3 %collective-permute-start.5 = (f32[2,128,384]{2,1,0:T(8,128)}, f32[2,128,384]{2,1,0:T(8,128)}, u32[]{:S(2)}, u32[]{:S(2)}) collective-permute-start(f32[2,128,384]{2,1,0:T(8,128)} %get-tuple-element.32), channel_id=1, source_target_pairs={{0,6},{1,7},{2,0},{3,1},{4,2},{5,3},{6,4},{7,5},{8,14},{9,15},{10,... | collective-permute-start | bytes 1179656 | tf_op jit(solution)/shard_map/ppermute | solution.py:46
  55.4 41.9 %collective-permute-start.9 = (f32[4,256,384]{2,1,0:T(8,128)}, f32[4,256,384]{2,1,0:T(8,128)}, u32[]{:S(2)}, u32[]{:S(2)}) collective-permute-start(f32[4,256,384]{2,1,0:T(8,128)} %fusion.7), channel_id=1, source_target_pairs={{0,8},{1,9},{2,10},{3,11},{4,12},{5,13},{6,14},{7,15},{8,0},{9,1},... | collective-permute-start | bytes 4718600 | tf_op jit(solution)/shard_map/ppermute | solution.py:79
  61.2 17.8 %copy-start.5 = (bf16[8,6,512]{2,0,1:T(8,128)(2,1)S(1)}, bf16[8,6,512]{2,0,1:T(8,128)(2,1)}, u32[]{:S(2)}) copy-start(bf16[8,6,512]{2,0,1:T(8,128)(2,1)} %convolution_convert_fusion) | copy-start | bytes 147460
  64.1 10.2 %collective-permute-start.3 = (f32[2,128,384]{2,1,0:T(8,128)S(1)}, f32[2,128,384]{2,1,0:T(8,128)S(1)}, u32[]{:S(2)}, u32[]{:S(2)}) collective-permute-start(f32[2,128,384]{2,1,0:T(8,128)S(1)} %get-tuple-element.31), channel_id=1, source_target_pairs={{0,2},{1,3},{2,4},{3,5},{4,6},{5,7},{6,0},{7,1},{8,10},{9,11},{10,... | collective-permute-start | bytes 1179656 | tf_op jit(solution)/shard_map/ppermute | solution.py:46
  65.8 11.1 %collective-permute-start.6 = (f32[2,128,384]{2,1,0:T(8,128)S(1)}, f32[2,128,384]{2,1,0:T(8,128)S(1)}, u32[]{:S(2)}, u32[]{:S(2)}) collective-permute-start(f32[2,128,384]{2,1,0:T(8,128)S(1)} %get-tuple-element.30), channel_id=1, source_target_pairs={{0,6},{1,7},{2,0},{3,1},{4,2},{5,3},{6,4},{7,5},{8,14},{9,15},{10,... | collective-permute-start | bytes 1179656 | tf_op jit(solution)/shard_map/ppermute | solution.py:46
  79.7 17.6 %all-to-all-start = ((bf16[8,6,512]{2,1,0:T(8,128)(2,1)}), bf16[8,6,512]{2,1,0:T(8,128)(2,1)S(1)}, u32[]{:S(2)}, u32[]{:S(2)}) async-start(bf16[8,6,512]{2,1,0:T(8,128)(2,1)} %copy.99), calls=%async_computation | async-start | bytes 131072 | tf_op jit(solution)/shard_map/all_to_all | solution.py:181
  85.9 15.2 %collective-permute-start.4 = (f32[2,128,384]{2,1,0:T(8,128)}, f32[2,128,384]{2,1,0:T(8,128)}, u32[]{:S(2)}, u32[]{:S(2)}) collective-permute-start(f32[2,128,384]{2,1,0:T(8,128)} %get-tuple-element.12), channel_id=1, source_target_pairs={{0,2},{1,3},{2,4},{3,5},{4,6},{5,7},{6,0},{7,1},{8,10},{9,11},{10,... | collective-permute-start | bytes 1179656 | tf_op jit(solution)/shard_map/ppermute | solution.py:46
  86.1 14.9 %collective-permute-start.7 = (f32[2,128,384]{2,1,0:T(8,128)}, f32[2,128,384]{2,1,0:T(8,128)}, u32[]{:S(2)}, u32[]{:S(2)}) collective-permute-start(f32[2,128,384]{2,1,0:T(8,128)} %get-tuple-element.28), channel_id=1, source_target_pairs={{0,6},{1,7},{2,0},{3,1},{4,2},{5,3},{6,4},{7,5},{8,14},{9,15},{10,... | collective-permute-start | bytes 1179656 | tf_op jit(solution)/shard_map/ppermute | solution.py:46
  98.9 5.7 %collective-permute-start.10 = (f32[128,384]{1,0:T(8,128)S(1)}, f32[128,384]{1,0:T(8,128)S(1)}, u32[]{:S(2)}, u32[]{:S(2)}) collective-permute-start(f32[128,384]{1,0:T(8,128)S(1)} %get-tuple-element.40), channel_id=1, source_target_pairs={{0,2},{1,3},{2,4},{3,5},{4,6},{5,7},{6,0},{7,1},{8,10},{9,11},{10,... | collective-permute-start | bytes 589832 | tf_op jit(solution)/shard_map/ppermute | solution.py:46
  100.7 6.9 %collective-permute-start.13 = (f32[128,384]{1,0:T(8,128)S(1)}, f32[128,384]{1,0:T(8,128)S(1)}, u32[]{:S(2)}, u32[]{:S(2)}) collective-permute-start(f32[128,384]{1,0:T(8,128)S(1)} %get-tuple-element.41), channel_id=1, source_target_pairs={{0,6},{1,7},{2,0},{3,1},{4,2},{5,3},{6,4},{7,5},{8,14},{9,15},{10,... | collective-permute-start | bytes 589832 | tf_op jit(solution)/shard_map/ppermute | solution.py:46
  102.5 14.5 %collective-permute-start.8 = (f32[256,384]{1,0:T(8,128)S(1)}, f32[256,384]{1,0:T(8,128)S(1)}, u32[]{:S(2)}, u32[]{:S(2)}) collective-permute-start(f32[256,384]{1,0:T(8,128)S(1)} %fusion.38), channel_id=1, source_target_pairs={{0,8},{1,9},{2,10},{3,11},{4,12},{5,13},{6,14},{7,15},{8,0},{9,1},... | collective-permute-start | bytes 1179656 | tf_op jit(solution)/shard_map/ppermute | solution.py:88
  107.6 6.0 %collective-permute-start.11 = (f32[128,384]{1,0:T(8,128)S(1)}, f32[128,384]{1,0:T(8,128)S(1)}, u32[]{:S(2)}, u32[]{:S(2)}) collective-permute-start(f32[128,384]{1,0:T(8,128)S(1)} %get-tuple-element.38), channel_id=1, source_target_pairs={{0,2},{1,3},{2,4},{3,5},{4,6},{5,7},{6,0},{7,1},{8,10},{9,11},{10,... | collective-permute-start | bytes 589832 | tf_op jit(solution)/shard_map/ppermute | solution.py:46
  107.9 7.0 %collective-permute-start.14 = (f32[128,384]{1,0:T(8,128)S(1)}, f32[128,384]{1,0:T(8,128)S(1)}, u32[]{:S(2)}, u32[]{:S(2)}) collective-permute-start(f32[128,384]{1,0:T(8,128)S(1)} %get-tuple-element.39), channel_id=1, source_target_pairs={{0,6},{1,7},{2,0},{3,1},{4,2},{5,3},{6,4},{7,5},{8,14},{9,15},{10,... | collective-permute-start | bytes 589832 | tf_op jit(solution)/shard_map/ppermute | solution.py:46
  114.9 5.7 %collective-permute-start.12 = (f32[128,384]{1,0:T(8,128)S(1)}, f32[128,384]{1,0:T(8,128)S(1)}, u32[]{:S(2)}, u32[]{:S(2)}) collective-permute-start(f32[128,384]{1,0:T(8,128)S(1)} %get-tuple-element.36), channel_id=1, source_target_pairs={{0,2},{1,3},{2,4},{3,5},{4,6},{5,7},{6,0},{7,1},{8,10},{9,11},{10,... | collective-permute-start | bytes 589832 | tf_op jit(solution)/shard_map/ppermute | solution.py:46
  115.0 6.9 %collective-permute-start.15 = (f32[128,384]{1,0:T(8,128)S(1)}, f32[128,384]{1,0:T(8,128)S(1)}, u32[]{:S(2)}, u32[]{:S(2)}) collective-permute-start(f32[128,384]{1,0:T(8,128)S(1)} %get-tuple-element.37), channel_id=1, source_target_pairs={{0,6},{1,7},{2,0},{3,1},{4,2},{5,3},{6,4},{7,5},{8,14},{9,15},{10,... | collective-permute-start | bytes 589832 | tf_op jit(solution)/shard_map/ppermute | solution.py:46
  123.2 9.3 %collective-permute-start.16 = (bf16[512,384]{1,0:T(8,128)(2,1)S(1)}, bf16[512,384]{1,0:T(8,128)(2,1)S(1)}, u32[]{:S(2)}, u32[]{:S(2)}) collective-permute-start(bf16[512,384]{1,0:T(8,128)(2,1)S(1)} %get-tuple-element.20), channel_id=1, source_target_pairs={{0,8},{1,9},{2,10},{3,11},{4,12},{5,13},{6,14},{7,15},{8,0},{9,1},... | collective-permute-start | bytes 1179656 | tf_op jit(solution)/shard_map/ppermute | solution.py:93
  132.7 11.3 %collective-permute-start.17 = (bf16[2,256,384]{2,1,0:T(8,128)(2,1)S(1)}, bf16[2,256,384]{2,1,0:T(8,128)(2,1)S(1)}, u32[]{:S(2)}, u32[]{:S(2)}) collective-permute-start(bf16[2,256,384]{2,1,0:T(8,128)(2,1)S(1)} %get-tuple-element.42), channel_id=1, source_target_pairs={{0,2},{1,3},{2,4},{3,5},{4,6},{5,7},{6,0},{7,1},{8,10},{9,11},{10,... | collective-permute-start | bytes 1179656 | tf_op jit(solution)/shard_map/ppermute | solution.py:59
  133.1 12.9 %collective-permute-start.20 = (bf16[2,256,384]{2,1,0:T(8,128)(2,1)S(1)}, bf16[2,256,384]{2,1,0:T(8,128)(2,1)S(1)}, u32[]{:S(2)}, u32[]{:S(2)}) collective-permute-start(bf16[2,256,384]{2,1,0:T(8,128)(2,1)S(1)} %get-tuple-element.43), channel_id=1, source_target_pairs={{0,6},{1,7},{2,0},{3,1},{4,2},{5,3},{6,4},{7,5},{8,14},{9,15},{10,... | collective-permute-start | bytes 1179656 | tf_op jit(solution)/shard_map/ppermute | solution.py:59
  134.8 38.7 %slice-start = ((s8[8388608]{0:T(1024)(128)(4,1)}), s8[4194304]{0:T(1024)(128)(4,1)S(1)}, s32[]{:S(2)}) async-start(s8[8388608]{0:T(1024)(128)(4,1)} %bitcast.248), calls=%async_computation.3 | async-start | bytes 8388608
  144.1 10.6 %collective-permute-start.18 = (bf16[2,256,384]{2,1,0:T(8,128)(2,1)S(1)}, bf16[2,256,384]{2,1,0:T(8,128)(2,1)S(1)}, u32[]{:S(2)}, u32[]{:S(2)}) collective-permute-start(bf16[2,256,384]{2,1,0:T(8,128)(2,1)S(1)} %collective-permute-done.17), channel_id=1, source_target_pairs={{0,2},{1,3},{2,4},{3,5},{4,6},{5,7},{6,0},{7,1},{8,10},{9,11},{10,... | collective-permute-start | bytes 1179656 | tf_op jit(solution)/shard_map/ppermute | solution.py:59
  146.1 12.3 %collective-permute-start.21 = (bf16[2,256,384]{2,1,0:T(8,128)(2,1)S(1)}, bf16[2,256,384]{2,1,0:T(8,128)(2,1)S(1)}, u32[]{:S(2)}, u32[]{:S(2)}) collective-permute-start(bf16[2,256,384]{2,1,0:T(8,128)(2,1)S(1)} %collective-permute-done.20), channel_id=1, source_target_pairs={{0,6},{1,7},{2,0},{3,1},{4,2},{5,3},{6,4},{7,5},{8,14},{9,15},{10,... | collective-permute-start | bytes 1179656 | tf_op jit(solution)/shard_map/ppermute | solution.py:59
  154.7 9.0 %collective-permute-start.19 = (bf16[2,256,384]{2,1,0:T(8,128)(2,1)S(1)}, bf16[2,256,384]{2,1,0:T(8,128)(2,1)S(1)}, u32[]{:S(2)}, u32[]{:S(2)}) collective-permute-start(bf16[2,256,384]{2,1,0:T(8,128)(2,1)S(1)} %collective-permute-done.18), channel_id=1, source_target_pairs={{0,2},{1,3},{2,4},{3,5},{4,6},{5,7},{6,0},{7,1},{8,10},{9,11},{10,... | collective-permute-start | bytes 1179656 | tf_op jit(solution)/shard_map/ppermute | solution.py:59
  158.4 9.0 %collective-permute-start.22 = (bf16[2,256,384]{2,1,0:T(8,128)(2,1)S(1)}, bf16[2,256,384]{2,1,0:T(8,128)(2,1)S(1)}, u32[]{:S(2)}, u32[]{:S(2)}) collective-permute-start(bf16[2,256,384]{2,1,0:T(8,128)(2,1)S(1)} %collective-permute-done.21), channel_id=1, source_target_pairs={{0,6},{1,7},{2,0},{3,1},{4,2},{5,3},{6,4},{7,5},{8,14},{9,15},{10,... | collective-permute-start | bytes 1179656 | tf_op jit(solution)/shard_map/ppermute | solution.py:59
  158.5 15.1 %slice-start.1 = ((s8[8388608]{0:T(1024)(128)(4,1)}), s8[4194304]{0:T(1024)(128)(4,1)S(1)}, s32[]{:S(2)}) async-start(s8[8388608]{0:T(1024)(128)(4,1)} %bitcast.248), calls=%async_computation.4 | async-start | bytes 8388608
  167.8 5.7 %collective-permute-start.23 = (bf16[2,4,512,384]{3,2,1,0:T(8,128)(2,1)S(1)}, bf16[2,4,512,384]{3,2,1,0:T(8,128)(2,1)S(1)}, u32[]{:S(2)}, u32[]{:S(2)}) collective-permute-start(bf16[2,4,512,384]{3,2,1,0:T(8,128)(2,1)S(1)} %maximum_bitcast_fusion), channel_id=1, source_target_pairs={{0,1},{1,0},{2,3},{3,2},{4,5},{5,4},{6,7},{7,6},{8,9},{9,8},{10,11... | collective-permute-start | bytes 9437192 | tf_op jit(solution)/shard_map/ppermute | solution.py:99
  179.5 17.6 %copy-start.2 = (f32[64,384]{0,1:T(8,128)S(1)}, f32[64,384]{0,1:T(8,128)}, u32[]{:S(2)}) copy-start(f32[64,384]{0,1:T(8,128)} %broadcast_subtract_fusion) | copy-start | bytes 294916
  179.6 22.2 %copy-start.14 = (s32[24]{0:T(128)S(1)}, s32[24]{0:T(128)}, u32[]{:S(2)}) copy-start(s32[24]{0:T(128)} %copy-done.13) | copy-start | bytes 292
  179.6 22.2 %copy-start.15 = (s32[24]{0:T(128)S(1)}, s32[24]{0:T(128)}, u32[]{:S(2)}) copy-start(s32[24]{0:T(128)} %get-tuple-element.46) | copy-start | bytes 292
  198.2 14.8 %all-to-all-start.2 = ((f32[8,64,384]{2,1,0:T(8,128)}), f32[8,64,384]{2,1,0:T(8,128)S(1)}, u32[]{:S(2)}, u32[]{:S(2)}) async-start(f32[8,64,384]{2,1,0:T(8,128)} %broadcast_in_dim.153), calls=%async_computation.2 | async-start | bytes 1572864 | tf_op jit(solution)/shard_map/all_to_all | solution.py:209
  (12 other events, 65.3 us)

commit v14 on v7

--- a/solution.py
+++ b/solution.py
@@ -195,13 +195,16 @@
     partial_rent = partial_rent + lax.dot_general(masked_send, prices_send, contract_w, preferred_element_type=jnp.float32)
 
     gathered = lax.all_to_all(partial_grad.reshape(slab_axis, share_rows, scenarios), "br", 0, 0, tiled=True)
-    returned = lax.all_to_all(partial_rent.reshape(slab_axis, CAP, scenarios), "br", 0, 0, tiled=True)
     gradient = jnp.sum(gathered, axis=0)
     trial = base - step_primal * gradient
     my_new = jnp.minimum(jnp.maximum(trial, lower), upper)
-    new_injections = lax.all_to_all(
-        jnp.broadcast_to(my_new[None], (slab_axis, share_rows, scenarios)), "br", 0, 0, tiled=True
-    ).reshape(bus_rows, scenarios)
+    outgoing = jnp.concatenate(
+        [jnp.broadcast_to(my_new[None], (slab_axis, share_rows, scenarios)), partial_rent.reshape(slab_axis, CAP, scenarios)],
+        axis=1,
+    )
+    arrived = lax.all_to_all(outgoing, "br", 0, 0, tiled=True)
+    new_injections = arrived[:, :share_rows].reshape(bus_rows, scenarios)
+    returned = arrived[:, share_rows:]
 
     lookup = own_slab * CAP + own_slot
     fetched = jnp.take(returned.reshape(slab_axis * CAP, scenarios), lookup, axis=0)

time: 215 us -> 210 us (0.977)
  starting transfers between devices: 38.8 us -> 35.2 us
    all_to_all x2 -> x1, starting transfers between devices: 7.18 us -> 3.63 us  [per_device(): arrived = lax.all_to_all(outgoing, 'br', 0, 0, tiled=True)]
    all_to_all x2 -> x1, waiting for transfers between devices: 13.9 us -> 12.3 us  [per_device(): arrived = lax.all_to_all(outgoing, 'br', 0, 0, tiled=True)]
  transfers between devices with their start and end apart: 21 -> 20, of which waited for: 18 -> 17; matrix products, arithmetic and copies ran while one was open for 19% -> 18% of each run, Pallas kernels for 0% -> 0%
where the time goes in v14:
time: 210 us; the launch traced here: 209 us
  waiting for transfers between devices  111 us (53%)
  starting transfers between devices  35.2 us (17%)
  matrix products  25 us (12%)
  other arithmetic  23.9 us (11%)
  local copies, waits for them, and re-layouts  13.1 us (6%)
    ppermute x6, waiting for transfers between devices, ring_scatter(): acc = lax.ppermute(acc, 'bus', perm) + more  31.4 us
    ppermute x6, waiting for transfers between devices, ring_gather(): cur = lax.ppermute(cur, 'bus', perm)  27.1 us
    dot_general x8, matrix products, flow_part(): return jnp.dot(rows, inject_half, preferred_element_type=jnp.float32)  15.5 us
    ppermute x1, waiting for transfers between devices, bus_pair_sum(): return pick(z, yh, 0) + lax.ppermute(pick(z, 1 - yh, 0), 'bus', Y_SWAP)  15 us
    all_to_all x1, waiting for transfers between devices, per_device(): arrived = lax.all_to_all(outgoing, 'br', 0, 0, tiled=True)  12.3 us
    all_to_all x1, waiting for transfers between devices, per_device(): lax.all_to_all(partial_grad.reshape(slab_axis, share_rows, scenarios), 'b...  7.71 us
    all_to_all x1, starting transfers between devices, per_device(): arrived_w = lax.all_to_all(outgoing_w, 'br', 0, 0, tiled=True)  6.43 us
    all_to_all x1, starting transfers between devices, per_device(): lax.all_to_all(partial_grad.reshape(slab_axis, share_rows, scenarios), 'b...  6.3 us
  transfers between devices with their start and end apart: 20, of which 17 were waited for; matrix products, arithmetic and copies ran while one was open for 18% of the time, Pallas kernels for 0%

profile of v14, /device:TPU:6, one launch (start us, length us, event | category | flops | bytes accessed | tf_op | source)
XLA Modules:
  0.0 209.3 jit_solution(9771043449869074091)
XLA Ops:
  1.9 1.9 convolution_bitcast_fusion.5
  3.9 1.9 convolution_bitcast_fusion.4
  7.6 1.9 convolution_bitcast_fusion.1
  9.6 1.9 convolution_bitcast_fusion
  11.6 1.9 pad_maximum_fusion.1
  20.6 1.9 convolution_bitcast_fusion.3
  22.5 1.9 convolution_bitcast_fusion.7
  24.5 1.9 convolution_bitcast_fusion.6
  26.5 2.2 %maximum_add_fusion = f32[2,2,512,384]{3,2,1,0:T(8,128)S(1)} fusion(f32[2,2,512,384]{3,2,1,0:T(8,128)} %collective-permute-done, f32[1,2,512,384]{3,2,1,0:T(8,128)S(1)} %convolution_bitcast_fusion.6, f32[1,2,512,384]{3,2,1,0:T(8,128)S(1)} %convolution_bitcast_fusion.7), kind=kLoop, calls=%fused_computation.11 | loop fusion | flops 1572864 | bytes 9437184 | tf_op jit(solution)/shard_map/add | solution.py:72
  30.9 1.9 convolution_bitcast_fusion.2
  33.0 2.2 %maximum_add_fusion.1 = f32[2,2,512,384]{3,2,1,0:T(8,128)S(1)} fusion(f32[2,2,512,384]{3,2,1,0:T(8,128)} %collective-permute-done.2, f32[1,2,512,384]{3,2,1,0:T(8,128)S(1)} %convolution_bitcast_fusion.2, f32[1,2,512,384]{3,2,1,0:T(8,128)S(1)} %convolution_bitcast_fusion.3), kind=kLoop, calls=%fused_computation.13 | loop fusion | flops 1572864 | bytes 9437184 | tf_op jit(solution)/shard_map/add | solution.py:72
  35.2 13.1 %collective-permute-done.1 = f32[2,256,384]{2,1,0:T(8,128)S(1)} collective-permute-done((f32[2,256,384]{2,1,0:T(8,128)S(1)}, f32[2,256,384]{2,1,0:T(8,128)S(1)}, u32[]{:S(2)}, u32[]{:S(2)}) %collective-permute-start.1) | collective-permute-done | bytes 786464 | tf_op jit(solution)/shard_map/ppermute | solution.py:46
  53.4 14.7 %collective-permute-done.3 = f32[2,256,384]{2,1,0:T(8,128)S(1)} collective-permute-done((f32[2,256,384]{2,1,0:T(8,128)S(1)}, f32[2,256,384]{2,1,0:T(8,128)S(1)}, u32[]{:S(2)}, u32[]{:S(2)}) %collective-permute-start.3) | collective-permute-done | bytes 786464 | tf_op jit(solution)/shard_map/ppermute | solution.py:46
  75.7 6.4 %all-to-all-start = ((bf16[8,6,512]{2,1,0:T(8,128)(2,1)}), bf16[8,6,512]{2,1,0:T(8,128)(2,1)S(1)}, u32[]{:S(2)}, u32[]{:S(2)}) async-start(bf16[8,6,512]{2,1,0:T(8,128)(2,1)} %copy.99), calls=%async_computation | async-start | bytes 131072 | tf_op jit(solution)/shard_map/all_to_all | solution.py:176
  82.9 5.6 %all-to-all-done = bf16[8,6,512]{2,1,0:T(8,128)(2,1)S(1)} async-done(((bf16[8,6,512]{2,1,0:T(8,128)(2,1)}), bf16[8,6,512]{2,1,0:T(8,128)(2,1)S(1)}, u32[]{:S(2)}, u32[]{:S(2)}) %all-to-all-start) | async-done | bytes 49184 | tf_op jit(solution)/shard_map/all_to_all | solution.py:176
  92.0 3.5 %collective-permute-start.8 = (f32[512,384]{1,0:T(8,128)S(1)}, f32[512,384]{1,0:T(8,128)}, u32[]{:S(2)}, u32[]{:S(2)}) collective-permute-start(f32[512,384]{1,0:T(8,128)S(1)} %dynamic-slice_bitcast_fusion), channel_id=1, source_target_pairs={{0,8},{1,9},{2,10},{3,11},{4,12},{5,13},{6,14},{7,15},{8,0},{9,1},... | collective-permute-start | bytes 2359304 | tf_op jit(solution)/shard_map/ppermute | solution.py:83
  95.4 15.0 %collective-permute-done.8 = f32[512,384]{1,0:T(8,128)} collective-permute-done((f32[512,384]{1,0:T(8,128)S(1)}, f32[512,384]{1,0:T(8,128)}, u32[]{:S(2)}, u32[]{:S(2)}) %collective-permute-start.8) | collective-permute-done | bytes 786464 | tf_op jit(solution)/shard_map/ppermute | solution.py:83
  110.4 2.2 %fusion.65 = (bf16[512,384]{1,0:T(8,128)(2,1)S(1)}, f32[512,384]{1,0:T(8,128)}) fusion(f32[512]{0:T(512)S(1)} %get-tuple-element.41, f32[512]{0:T(512)S(1)} %get-tuple-element.40, f32[512,384]{1,0:T(8,128)S(1)} %copy-done.3, f32[512,384]{1,0:T(8,128)} %collective-permute-done.8, f32[2,512,384]{2,1,0:T(8,128)S(1)} %pad_maximum_fusion.2, s32[]{:T(128)S(6)} %select_n.226), kind=kLoop, calls=%fused_computation.142 | loop fusion | flops 1376256 | bytes 3543044 | tf_op jit(solution)/shard_map/convert_element_type | solution.py:188
  112.6 3.2 %collective-permute-start.9 = (bf16[512,384]{1,0:T(8,128)(2,1)S(1)}, bf16[512,384]{1,0:T(8,128)(2,1)S(1)}, u32[]{:S(2)}, u32[]{:S(2)}) collective-permute-start(bf16[512,384]{1,0:T(8,128)(2,1)S(1)} %get-tuple-element.20), channel_id=1, source_target_pairs={{0,8},{1,9},{2,10},{3,11},{4,12},{5,13},{6,14},{7,15},{8,0},{9,1},... | collective-permute-start | bytes 1179656 | tf_op jit(solution)/shard_map/ppermute | solution.py:88
  115.9 6.0 %collective-permute-done.9 = bf16[512,384]{1,0:T(8,128)(2,1)S(1)} collective-permute-done((bf16[512,384]{1,0:T(8,128)(2,1)S(1)}, bf16[512,384]{1,0:T(8,128)(2,1)S(1)}, u32[]{:S(2)}, u32[]{:S(2)}) %collective-permute-start.9) | collective-permute-done | bytes 393248 | tf_op jit(solution)/shard_map/ppermute | solution.py:88
  124.7 8.6 %collective-permute-done.10 = bf16[2,256,384]{2,1,0:T(8,128)(2,1)S(1)} collective-permute-done((bf16[2,256,384]{2,1,0:T(8,128)(2,1)S(1)}, bf16[2,256,384]{2,1,0:T(8,128)(2,1)S(1)}, u32[]{:S(2)}, u32[]{:S(2)}) %collective-permute-start.10) | collective-permute-done | bytes 393248 | tf_op jit(solution)/shard_map/ppermute | solution.py:59
  135.4 9.7 %collective-permute-done.11 = bf16[2,256,384]{2,1,0:T(8,128)(2,1)S(1)} collective-permute-done((bf16[2,256,384]{2,1,0:T(8,128)(2,1)S(1)}, bf16[2,256,384]{2,1,0:T(8,128)(2,1)S(1)}, u32[]{:S(2)}, u32[]{:S(2)}) %collective-permute-start.11) | collective-permute-done | bytes 393248 | tf_op jit(solution)/shard_map/ppermute | solution.py:59
  147.3 5.6 %collective-permute-done.12 = bf16[2,256,384]{2,1,0:T(8,128)(2,1)S(1)} collective-permute-done((bf16[2,256,384]{2,1,0:T(8,128)(2,1)S(1)}, bf16[2,256,384]{2,1,0:T(8,128)(2,1)S(1)}, u32[]{:S(2)}, u32[]{:S(2)}) %collective-permute-start.12) | collective-permute-done | bytes 393248 | tf_op jit(solution)/shard_map/ppermute | solution.py:59
  153.0 2.4 %collective-permute-done.15 = bf16[2,256,384]{2,1,0:T(8,128)(2,1)S(1)} collective-permute-done((bf16[2,256,384]{2,1,0:T(8,128)(2,1)S(1)}, bf16[2,256,384]{2,1,0:T(8,128)(2,1)S(1)}, u32[]{:S(2)}, u32[]{:S(2)}) %collective-permute-start.15) | collective-permute-done | bytes 393248 | tf_op jit(solution)/shard_map/ppermute | solution.py:59
  155.9 5.6 %collective-permute-done.16 = bf16[2,4,512,384]{3,2,1,0:T(8,128)(2,1)S(1)} collective-permute-done((bf16[2,4,512,384]{3,2,1,0:T(8,128)(2,1)S(1)}, bf16[2,4,512,384]{3,2,1,0:T(8,128)(2,1)S(1)}, u32[]{:S(2)}, u32[]{:S(2)}) %collective-permute-start.16) | collective-permute-done | bytes 3145760 | tf_op jit(solution)/shard_map/ppermute | solution.py:94
  163.1 2.4 %fusion.9 = f32[512,384]{1,0:T(8,128)S(1)} fusion(bf16[2,4,512,384]{3,2,1,0:T(8,128)(2,1)S(1)} %collective-permute-done.16, bf16[2,4,2,512,512]{4,3,2,1,0:T(8,128)(2,1)S(1)} %bitcast.221, s32[]{:T(128)S(6)} %select_n.209), kind=kOutput, calls=%fused_computation.26 | convolution fusion | flops 1610612736 | bytes 8126468 | tf_op jit(solution)/shard_map/dot_general | solution.py:192
  165.5 3.4 %fusion.12 = f32[512,384]{1,0:T(8,128)} fusion(f32[512,384]{1,0:T(8,128)S(1)} %fusion.9, bf16[2,4,2,512,512]{4,3,2,1,0:T(8,128)(2,1)S(1)} %bitcast.222, s32[]{:T(128)S(6)} %select_n.204, bf16[4,2,256,384]{3,2,0,1:T(8,128)(2,1)S(1)} %bitcast_dynamic-update-slice_fusion.7, bf16[4,2,256,384]{3,2,0,1:T(8,128)(2,1)S(1)} %bitcast_dynamic-update-slice_fusion.3), kind=kOutput, calls=%fused_computation.27 | convolution fusion | flops 1617100800 | bytes 8912900 | tf_op jit(solution)/shard_map/dot_general | solution.py:191
  168.9 6.3 %all-to-all-start.1 = ((f32[8,64,384]{2,1,0:T(8,128)}), f32[8,64,384]{2,1,0:T(8,128)}, u32[]{:S(2)}, u32[]{:S(2)}) async-start(f32[8,64,384]{2,1,0:T(8,128)} %bitcast.225), calls=%async_computation.1 | async-start | bytes 1572864 | tf_op jit(solution)/shard_map/all_to_all | solution.py:197
  175.2 2.5 %convolution_bitcast_fusion.8 = f32[48,384]{1,0:T(8,128)S(1)} fusion(bf16[48,2,4,512]{3,0,2,1:T(8,128)(2,1)S(1)} %get-tuple-element.19, bf16[2,4,512,384]{3,2,1,0:T(8,128)(2,1)} %copy-done), kind=kOutput, calls=%fused_computation.28 | convolution fusion | flops 150994944 | bytes 3612672 | tf_op jit(solution)/shard_map/dot_general | solution.py:195
  179.9 7.7 %all-to-all-done.1 = f32[8,64,384]{2,1,0:T(8,128)} async-done(((f32[8,64,384]{2,1,0:T(8,128)}), f32[8,64,384]{2,1,0:T(8,128)}, u32[]{:S(2)}, u32[]{:S(2)}) %all-to-all-start.1) | async-done | bytes 786464 | tf_op jit(solution)/shard_map/all_to_all | solution.py:197
  190.1 3.6 %all-to-all-start.2 = ((f32[8,70,384]{2,1,0:T(8,128)}), f32[8,70,384]{2,1,0:T(8,128)S(1)}, u32[]{:S(2)}, u32[]{:S(2)}) async-start(f32[8,70,384]{2,1,0:T(8,128)} %pad_maximum_fusion.3), calls=%async_computation.2 | async-start | bytes 1769472 | tf_op jit(solution)/shard_map/all_to_all | solution.py:205
  194.6 12.3 %all-to-all-done.2 = f32[8,70,384]{2,1,0:T(8,128)S(1)} async-done(((f32[8,70,384]{2,1,0:T(8,128)}), f32[8,70,384]{2,1,0:T(8,128)S(1)}, u32[]{:S(2)}, u32[]{:S(2)}) %all-to-all-start.2) | async-done | bytes 860192 | tf_op jit(solution)/shard_map/all_to_all | solution.py:205
  (138 shorter events, 46.3 us)
Async XLA Ops:
  7.6 18.9 %collective-permute-start = (f32[2,2,512,384]{3,2,1,0:T(8,128)}, f32[2,2,512,384]{3,2,1,0:T(8,128)}, u32[]{:S(2)}, u32[]{:S(2)}) collective-permute-start(f32[2,2,512,384]{3,2,1,0:T(8,128)} %pad_maximum_fusion), channel_id=1, source_target_pairs={{0,1},{1,0},{2,3},{3,2},{4,5},{5,4},{6,7},{7,6},{8,9},{9,8},{10,11... | collective-permute-start | bytes 9437192 | tf_op jit(solution)/shard_map/ppermute | solution.py:72
  11.5 2.9 %copy-start.7 = (bf16[8,1536]{1,0:T(8,128)(2,1)S(1)}, bf16[8,1536]{1,0:T(8,128)(2,1)}, u32[]{:S(2)}) copy-start(bf16[8,1536]{1,0:T(8,128)(2,1)} %param.27) | copy-start | bytes 73732
  11.5 2.9 %copy-start.9 = (s32[1024,3]{0,1:T(4,128)S(1)}, s32[1024,3]{0,1:T(4,128)}, u32[]{:S(2)}) copy-start(s32[1024,3]{0,1:T(4,128)} %param.26) | copy-start | bytes 36868
  11.5 5.3 %copy-start.5 = (f32[64,1024]{1,0:T(8,128)S(1)}, f32[64,1024]{1,0:T(8,128)}, u32[]{:S(2)}) copy-start(f32[64,1024]{1,0:T(8,128)} %param.22) | copy-start | bytes 786436
  13.5 19.5 %collective-permute-start.2 = (f32[2,2,512,384]{3,2,1,0:T(8,128)}, f32[2,2,512,384]{3,2,1,0:T(8,128)}, u32[]{:S(2)}, u32[]{:S(2)}) collective-permute-start(f32[2,2,512,384]{3,2,1,0:T(8,128)} %pad_maximum_fusion.1), channel_id=1, source_target_pairs={{0,1},{1,0},{2,3},{3,2},{4,5},{5,4},{6,7},{7,6},{8,9},{9,8},{10,11... | collective-permute-start | bytes 9437192 | tf_op jit(solution)/shard_map/ppermute | solution.py:72
  14.4 10.1 %copy-start.6 = (s32[128,24]{1,0:T(8,128)}, s32[128,24]{1,0:T(8,128)S(1)}, u32[]{:S(2)}) copy-start(s32[128,24]{1,0:T(8,128)S(1)} %reshape.196) | copy-start | bytes 36868
  22.5 3.9 %copy-start.10 = (s32[384]{0:T(512)S(1)}, s32[384]{0:T(512)}, u32[]{:S(2)}) copy-start(s32[384]{0:T(512)} %param.24) | copy-start | bytes 4612
  28.8 19.5 %collective-permute-start.1 = (f32[2,256,384]{2,1,0:T(8,128)S(1)}, f32[2,256,384]{2,1,0:T(8,128)S(1)}, u32[]{:S(2)}, u32[]{:S(2)}) collective-permute-start(f32[2,256,384]{2,1,0:T(8,128)S(1)} %get-tuple-element.32), channel_id=1, source_target_pairs={{0,2},{1,3},{2,4},{3,5},{4,6},{5,7},{6,0},{7,1},{8,10},{9,11},{10,... | collective-permute-start | bytes 2359304 | tf_op jit(solution)/shard_map/ppermute | solution.py:46
  29.2 20.4 %collective-permute-start.5 = (f32[2,256,384]{2,1,0:T(8,128)S(1)}, f32[2,256,384]{2,1,0:T(8,128)S(1)}, u32[]{:S(2)}, u32[]{:S(2)}) collective-permute-start(f32[2,256,384]{2,1,0:T(8,128)S(1)} %get-tuple-element.33), channel_id=1, source_target_pairs={{0,6},{1,7},{2,0},{3,1},{4,2},{5,3},{6,4},{7,5},{8,14},{9,15},{10,... | collective-permute-start | bytes 2359304 | tf_op jit(solution)/shard_map/ppermute | solution.py:46
  49.8 18.4 %collective-permute-start.3 = (f32[2,256,384]{2,1,0:T(8,128)S(1)}, f32[2,256,384]{2,1,0:T(8,128)S(1)}, u32[]{:S(2)}, u32[]{:S(2)}) collective-permute-start(f32[2,256,384]{2,1,0:T(8,128)S(1)} %get-tuple-element.12), channel_id=1, source_target_pairs={{0,2},{1,3},{2,4},{3,5},{4,6},{5,7},{6,0},{7,1},{8,10},{9,11},{10,... | collective-permute-start | bytes 2359304 | tf_op jit(solution)/shard_map/ppermute | solution.py:46
  50.2 19.4 %collective-permute-start.6 = (f32[2,256,384]{2,1,0:T(8,128)S(1)}, f32[2,256,384]{2,1,0:T(8,128)S(1)}, u32[]{:S(2)}, u32[]{:S(2)}) collective-permute-start(f32[2,256,384]{2,1,0:T(8,128)S(1)} %get-tuple-element.31), channel_id=1, source_target_pairs={{0,6},{1,7},{2,0},{3,1},{4,2},{5,3},{6,4},{7,5},{8,14},{9,15},{10,... | collective-permute-start | bytes 2359304 | tf_op jit(solution)/shard_map/ppermute | solution.py:46
  71.1 18.5 %collective-permute-start.4 = (f32[2,256,384]{2,1,0:T(8,128)}, f32[2,256,384]{2,1,0:T(8,128)}, u32[]{:S(2)}, u32[]{:S(2)}) collective-permute-start(f32[2,256,384]{2,1,0:T(8,128)} %get-tuple-element.28), channel_id=1, source_target_pairs={{0,2},{1,3},{2,4},{3,5},{4,6},{5,7},{6,0},{7,1},{8,10},{9,11},{10,... | collective-permute-start | bytes 2359304 | tf_op jit(solution)/shard_map/ppermute | solution.py:46
  71.3 18.9 %collective-permute-start.7 = (f32[2,256,384]{2,1,0:T(8,128)}, f32[2,256,384]{2,1,0:T(8,128)}, u32[]{:S(2)}, u32[]{:S(2)}) collective-permute-start(f32[2,256,384]{2,1,0:T(8,128)} %get-tuple-element.29), channel_id=1, source_target_pairs={{0,6},{1,7},{2,0},{3,1},{4,2},{5,3},{6,4},{7,5},{8,14},{9,15},{10,... | collective-permute-start | bytes 2359304 | tf_op jit(solution)/shard_map/ppermute | solution.py:46
  75.7 12.8 %all-to-all-start = ((bf16[8,6,512]{2,1,0:T(8,128)(2,1)}), bf16[8,6,512]{2,1,0:T(8,128)(2,1)S(1)}, u32[]{:S(2)}, u32[]{:S(2)}) async-start(bf16[8,6,512]{2,1,0:T(8,128)(2,1)} %copy.99), calls=%async_computation | async-start | bytes 131072 | tf_op jit(solution)/shard_map/all_to_all | solution.py:176
  91.8 3.7 %copy-start.11 = (f32[512]{0:T(512)S(1)}, f32[512]{0:T(512)}, u32[]{:S(2)}) copy-start(f32[512]{0:T(512)} %param.18) | copy-start | bytes 6148
  91.8 18.6 %copy-start.3 = (f32[512,384]{1,0:T(8,128)S(1)}, f32[512,384]{1,0:T(8,128)}, u32[]{:S(2)}) copy-start(f32[512,384]{1,0:T(8,128)} %param.17) | copy-start | bytes 2359300
  92.0 18.4 %collective-permute-start.8 = (f32[512,384]{1,0:T(8,128)S(1)}, f32[512,384]{1,0:T(8,128)}, u32[]{:S(2)}, u32[]{:S(2)}) collective-permute-start(f32[512,384]{1,0:T(8,128)S(1)} %dynamic-slice_bitcast_fusion), channel_id=1, source_target_pairs={{0,8},{1,9},{2,10},{3,11},{4,12},{5,13},{6,14},{7,15},{8,0},{9,1},... | collective-permute-start | bytes 2359304 | tf_op jit(solution)/shard_map/ppermute | solution.py:83
  112.6 9.3 %collective-permute-start.9 = (bf16[512,384]{1,0:T(8,128)(2,1)S(1)}, bf16[512,384]{1,0:T(8,128)(2,1)S(1)}, u32[]{:S(2)}, u32[]{:S(2)}) collective-permute-start(bf16[512,384]{1,0:T(8,128)(2,1)S(1)} %get-tuple-element.20), channel_id=1, source_target_pairs={{0,8},{1,9},{2,10},{3,11},{4,12},{5,13},{6,14},{7,15},{8,0},{9,1},... | collective-permute-start | bytes 1179656 | tf_op jit(solution)/shard_map/ppermute | solution.py:88
  122.1 11.1 %collective-permute-start.10 = (bf16[2,256,384]{2,1,0:T(8,128)(2,1)S(1)}, bf16[2,256,384]{2,1,0:T(8,128)(2,1)S(1)}, u32[]{:S(2)}, u32[]{:S(2)}) collective-permute-start(bf16[2,256,384]{2,1,0:T(8,128)(2,1)S(1)} %get-tuple-element.34), channel_id=1, source_target_pairs={{0,2},{1,3},{2,4},{3,5},{4,6},{5,7},{6,0},{7,1},{8,10},{9,11},{10,... | collective-permute-start | bytes 1179656 | tf_op jit(solution)/shard_map/ppermute | solution.py:59
  122.8 11.2 %collective-permute-start.13 = (bf16[2,256,384]{2,1,0:T(8,128)(2,1)S(1)}, bf16[2,256,384]{2,1,0:T(8,128)(2,1)S(1)}, u32[]{:S(2)}, u32[]{:S(2)}) collective-permute-start(bf16[2,256,384]{2,1,0:T(8,128)(2,1)S(1)} %get-tuple-element.35), channel_id=1, source_target_pairs={{0,6},{1,7},{2,0},{3,1},{4,2},{5,3},{6,4},{7,5},{8,14},{9,15},{10,... | collective-permute-start | bytes 1179656 | tf_op jit(solution)/shard_map/ppermute | solution.py:59
  124.2 38.9 %slice-start = ((s8[8388608]{0:T(1024)(128)(4,1)}), s8[4194304]{0:T(1024)(128)(4,1)S(1)}, s32[]{:S(2)}) async-start(s8[8388608]{0:T(1024)(128)(4,1)} %bitcast.219), calls=%async_computation.3 | async-start | bytes 8388608
  133.3 11.9 %collective-permute-start.11 = (bf16[2,256,384]{2,1,0:T(8,128)(2,1)S(1)}, bf16[2,256,384]{2,1,0:T(8,128)(2,1)S(1)}, u32[]{:S(2)}, u32[]{:S(2)}) collective-permute-start(bf16[2,256,384]{2,1,0:T(8,128)(2,1)S(1)} %collective-permute-done.10), channel_id=1, source_target_pairs={{0,2},{1,3},{2,4},{3,5},{4,6},{5,7},{6,0},{7,1},{8,10},{9,11},{10,... | collective-permute-start | bytes 1179656 | tf_op jit(solution)/shard_map/ppermute | solution.py:59
  134.0 12.4 %collective-permute-start.14 = (bf16[2,256,384]{2,1,0:T(8,128)(2,1)S(1)}, bf16[2,256,384]{2,1,0:T(8,128)(2,1)S(1)}, u32[]{:S(2)}, u32[]{:S(2)}) collective-permute-start(bf16[2,256,384]{2,1,0:T(8,128)(2,1)S(1)} %collective-permute-done.13), channel_id=1, source_target_pairs={{0,6},{1,7},{2,0},{3,1},{4,2},{5,3},{6,4},{7,5},{8,14},{9,15},{10,... | collective-permute-start | bytes 1179656 | tf_op jit(solution)/shard_map/ppermute | solution.py:59
  145.1 7.8 %collective-permute-start.12 = (bf16[2,256,384]{2,1,0:T(8,128)(2,1)S(1)}, bf16[2,256,384]{2,1,0:T(8,128)(2,1)S(1)}, u32[]{:S(2)}, u32[]{:S(2)}) collective-permute-start(bf16[2,256,384]{2,1,0:T(8,128)(2,1)S(1)} %collective-permute-done.11), channel_id=1, source_target_pairs={{0,2},{1,3},{2,4},{3,5},{4,6},{5,7},{6,0},{7,1},{8,10},{9,11},{10,... | collective-permute-start | bytes 1179656 | tf_op jit(solution)/shard_map/ppermute | solution.py:59
  146.4 9.0 %collective-permute-start.15 = (bf16[2,256,384]{2,1,0:T(8,128)(2,1)S(1)}, bf16[2,256,384]{2,1,0:T(8,128)(2,1)S(1)}, u32[]{:S(2)}, u32[]{:S(2)}) collective-permute-start(bf16[2,256,384]{2,1,0:T(8,128)(2,1)S(1)} %collective-permute-done.14), channel_id=1, source_target_pairs={{0,6},{1,7},{2,0},{3,1},{4,2},{5,3},{6,4},{7,5},{8,14},{9,15},{10,... | collective-permute-start | bytes 1179656 | tf_op jit(solution)/shard_map/ppermute | solution.py:59
  147.2 15.9 %slice-start.1 = ((s8[8388608]{0:T(1024)(128)(4,1)}), s8[4194304]{0:T(1024)(128)(4,1)S(1)}, s32[]{:S(2)}) async-start(s8[8388608]{0:T(1024)(128)(4,1)} %bitcast.219), calls=%async_computation.4 | async-start | bytes 8388608
  155.8 5.7 %collective-permute-start.16 = (bf16[2,4,512,384]{3,2,1,0:T(8,128)(2,1)S(1)}, bf16[2,4,512,384]{3,2,1,0:T(8,128)(2,1)S(1)}, u32[]{:S(2)}, u32[]{:S(2)}) collective-permute-start(bf16[2,4,512,384]{3,2,1,0:T(8,128)(2,1)S(1)} %maximum_bitcast_fusion), channel_id=1, source_target_pairs={{0,1},{1,0},{2,3},{3,2},{4,5},{5,4},{6,7},{7,6},{8,9},{9,8},{10,11... | collective-permute-start | bytes 9437192 | tf_op jit(solution)/shard_map/ppermute | solution.py:94
  168.9 18.7 %all-to-all-start.1 = ((f32[8,64,384]{2,1,0:T(8,128)}), f32[8,64,384]{2,1,0:T(8,128)}, u32[]{:S(2)}, u32[]{:S(2)}) async-start(f32[8,64,384]{2,1,0:T(8,128)} %bitcast.225), calls=%async_computation.1 | async-start | bytes 1572864 | tf_op jit(solution)/shard_map/all_to_all | solution.py:197
  175.2 2.5 %copy-start.4 = (bf16[48,2,4,512]{3,0,2,1:T(8,128)(2,1)S(1)}, bf16[48,2,4,512]{3,0,2,1:T(8,128)(2,1)}, u32[]{:S(2)}) copy-start(bf16[48,2,4,512]{3,0,2,1:T(8,128)(2,1)} %get-tuple-element.18) | copy-start | bytes 1179652
  177.7 11.2 %copy-start.1 = (f32[64,384]{0,1:T(8,128)S(1)}, f32[64,384]{0,1:T(8,128)}, u32[]{:S(2)}) copy-start(f32[64,384]{0,1:T(8,128)} %broadcast_subtract_fusion) | copy-start | bytes 294916
  177.7 11.2 %copy-start.2 = (f32[64,384]{0,1:T(8,128)S(1)}, f32[64,384]{0,1:T(8,128)}, u32[]{:S(2)}) copy-start(f32[64,384]{0,1:T(8,128)} %multiply_bitcast_fusion) | copy-start | bytes 294916
  190.1 16.9 %all-to-all-start.2 = ((f32[8,70,384]{2,1,0:T(8,128)}), f32[8,70,384]{2,1,0:T(8,128)S(1)}, u32[]{:S(2)}, u32[]{:S(2)}) async-start(f32[8,70,384]{2,1,0:T(8,128)} %pad_maximum_fusion.3), calls=%async_computation.2 | async-start | bytes 1769472 | tf_op jit(solution)/shard_map/all_to_all | solution.py:205
  (2 other events, 4.1 us)
